TPU v7x, 256 devices: a whole 4x4x8 slice. The times are simulated.
256 devices in a mesh: mom: 64 (over x, y, z_lo, core), spin: 4 (over z_hi).
Axes of the slice: x: 4, y: 4, z: 8 (z_hi: 4, z_lo: 2; z = z_hi * 2 + z_lo), core: 2. Of those that a mesh axis runs over, the one named last changes fastest.
Arguments:
- vertex_start: bfloat16 [64, 4, 768, 768], P('mom', 'spin'), may hold values from -6 to 6
- bare_vertex: bfloat16 [64, 4, 768, 768], P('mom', 'spin'), may hold values from -6 to 6
- bubble: bfloat16 [64, 4, 64, 12, 12], P('mom', 'spin'), may hold values from -0.011962891 to 0.011962891
- form_mix: bfloat16 [2, 12, 12], replicated, may hold values from -0.59765625 to 0.59765625
- cross_tables: int32 [2, 64, 64], replicated, may hold values from 0 to 63, as said below
- freq_perm: int32 [2, 64], replicated, may hold values from 0 to 63, each once within a row
Outputs:
- vertex_final: bfloat16 [64, 4, 768, 768], P('mom', 'spin')
Inputs may be any that keep to these rules, and one draw needn't show every extreme that they name: `cross_tables`: for each crossing and frequency, the entries over the 64 momenta are a permutation of the momenta; for each crossing and momentum, every momentum appears exactly once over the 64 frequencies.
All inputs are finite; a program needn't handle non-finite values.
Results may differ from a plain program's by a relative error of at most 0.0085.
Values may be sent and summed in bfloat16 or wider, within the bound.
No kernel may reach another device: no remote copies, remote signals or barrier semaphores. Data moves between devices by JAX's collectives and lax.ppermute only.
A program may use at most 64 MiB of HBM per device.

v0:
```python
import jax
import jax.numpy as jnp
from jax import lax
from jax.sharding import PartitionSpec as P

INNER = 2


COEF_SELF = (-0.5, 0.5, 0.5, 0.5)
COEF_PAIR = (-1.5, -0.5, 1.5, -0.5)


def partner_2(value, axis, stride):
    mask = 2**stride
    pairs = [(source, source ^ mask) for source in range(lax.axis_size(axis))]
    return lax.ppermute(value, axis, pairs)


def make_orders(table, frequency_perm, momentum, momenta, per_peer, freqs):
    freq_range = jnp.arange(freqs, dtype=jnp.int32)
    own_row = jnp.take(table, momentum, axis=0)
    send_order = jnp.argsort(own_row * freqs + freq_range)
    hit_mask = (table == momentum).astype(jnp.int32)
    source = jnp.sum(hit_mask * jnp.arange(momenta, dtype=jnp.int32)[:, None], axis=0)
    within = jnp.sum(hit_mask * (jnp.cumsum(hit_mask, axis=1) - 1), axis=0)
    position = source * per_peer + within
    freq_of = jnp.argsort(frequency_perm)
    return (send_order, jnp.take(position, freq_of, axis=0))


def pack_blocks(matrix, send_order, momenta, per_peer, freqs, forms):
    order_len = matrix.shape[1]
    blocks = jnp.take(matrix.reshape(freqs, forms, order_len), send_order, axis=0)
    return blocks.reshape(momenta, per_peer, forms, order_len)


def unpack_blocks(received, recv_order, mixing, freqs, forms):
    order_len = received.shape[-1]
    gathered = jnp.take(received.reshape(freqs, forms, order_len), recv_order, axis=0)
    mixed = jnp.einsum("lm,fmb->flb", mixing, gathered, preferred_element_type=jnp.float32)
    return mixed.reshape(freqs * forms, order_len)


def local(vertex_start, bare_vertex, bubble, form_mix, cross_tables, freq_perm):
    current = vertex_start[0, 0]
    bare_mat = bare_vertex[0, 0]
    bubble_mat = bubble[0, 0]
    freqs, forms = (bubble_mat.shape[0], bubble_mat.shape[1])
    order_len = current.shape[0]
    momenta = lax.axis_size("mom")
    per_peer = freqs // momenta
    momentum = lax.axis_index("mom")
    channel = lax.axis_index("spin")
    coef_self = jnp.take(jnp.array(COEF_SELF, jnp.float32), channel)
    coef_pair = jnp.take(jnp.array(COEF_PAIR, jnp.float32), channel)
    orders_first = make_orders(cross_tables[0], freq_perm[0], momentum, momenta, per_peer, freqs)
    orders_second = make_orders(cross_tables[1], freq_perm[1], momentum, momenta, per_peer, freqs)
    partner = partner_2(current, "spin", 0)
    stacked = jnp.stack(
        [
            pack_blocks(current, orders_first[0], momenta, per_peer, freqs, forms),
            pack_blocks(partner, orders_first[0], momenta, per_peer, freqs, forms),
            pack_blocks(current, orders_second[0], momenta, per_peer, freqs, forms),
            pack_blocks(partner, orders_second[0], momenta, per_peer, freqs, forms),
        ]
    )
    received = lax.all_to_all(stacked, "mom", split_axis=1, concat_axis=1, tiled=True)
    own_sum = unpack_blocks(received[0], orders_first[1], form_mix[0], freqs, forms)
    own_sum = own_sum + unpack_blocks(received[2], orders_second[1], form_mix[1], freqs, forms)
    other_sum = unpack_blocks(received[1], orders_first[1], form_mix[0], freqs, forms)
    other_sum = other_sum + unpack_blocks(received[3], orders_second[1], form_mix[1], freqs, forms)
    own_round = own_sum.astype(jnp.bfloat16)
    other_round = other_sum.astype(jnp.bfloat16)
    reducible = (
        coef_self * own_round.astype(jnp.float32) + coef_pair * other_round.astype(jnp.float32)
    ).astype(jnp.bfloat16)
    base_sum = bare_mat.astype(jnp.float32) + reducible.astype(jnp.float32)
    for inner_step in range(INNER):
        carried = jnp.einsum(
            "fln,fnb->flb",
            bubble_mat,
            current.reshape(freqs, forms, order_len),
            preferred_element_type=jnp.float32,
        )
        carried = carried.reshape(order_len, order_len).astype(jnp.bfloat16)
        total = base_sum + jnp.dot(bare_mat, carried, preferred_element_type=jnp.float32)
        total = total + jnp.dot(reducible, carried, preferred_element_type=jnp.float32)
        current = total.astype(jnp.bfloat16)
    return current[None, None]


def solution(mesh):
    in_specs = (
        P("mom", "spin", None, None),
        P("mom", "spin", None, None),
        P("mom", "spin", None, None, None),
        P(),
        P(),
        P(),
    )
    out_specs = P("mom", "spin", None, None)
    return jax.shard_map(local, mesh=mesh, in_specs=in_specs, out_specs=out_specs, check_vma=False)
```

profile of v0, /device:TPU:1, one launch (start us, length us, event | category | flops | bytes accessed | tf_op | source)
XLA Modules:
  0.0 200.5 jit_solution(17556819864388075838)
XLA Ops:
  0.0 3.8 %collective-permute-start = (bf16[768,768]{1,0:T(8,128)(2,1)}, bf16[768,768]{1,0:T(8,128)(2,1)}, u32[]{:S(2)}, u32[]{:S(2)}) collective-permute-start(bf16[768,768]{1,0:T(8,128)(2,1)} %bitcast.108), channel_id=1, source_target_pairs={{0,1},{1,0},{2,3},{3,2},{4,5},{5,4},{6,7},{7,6},{8,9},{9,8},{10,11... | collective-permute-start | bytes 3538952 | tf_op jit(solution)/shard_map/ppermute | solution.py:16
  3.8 2.2 %reshape_squeeze.17 = bf16[64,12,768]{2,1,0:T(8,128)(2,1)S(1)} reshape(bf16[1,1,768,768]{3,2,1,0:T(8,128)(2,1)} %param.14) | data formatting | bytes 2359296 | tf_op jit(solution)/shard_map/reshape;squeeze | solution.py:33
  6.0 0.0 copy-done.11
  6.1 2.0 %sort.60 = (s32[64]{0:T(128)}, s32[64]{0:T(128)S(1)}) sort(s32[64]{0:T(128)S(1)} %fusion.29, s32[64]{0:T(128)S(1)} %iota.27), dimensions={0}, to_apply=%region_1.0 | sort | flops 384 | bytes 1024 | tf_op jit(solution)/shard_map/jit(argsort)/sort | solution.py:22
  8.1 2.0 %sort.59 = (s32[64]{0:T(128)}, s32[64]{0:T(128)S(1)}) sort(s32[64]{0:T(128)S(1)} %fusion.26, s32[64]{0:T(128)S(1)} %iota.25), dimensions={0}, to_apply=%region_0.0 | sort | flops 384 | bytes 1024 | tf_op jit(solution)/shard_map/jit(argsort)/sort | solution.py:22
  10.2 1.8 gather_fusion.2
  12.0 1.8 gather_fusion
  13.8 40.7 %collective-permute-done = bf16[768,768]{1,0:T(8,128)(2,1)} collective-permute-done((bf16[768,768]{1,0:T(8,128)(2,1)}, bf16[768,768]{1,0:T(8,128)(2,1)}, u32[]{:S(2)}, u32[]{:S(2)}) %collective-permute-start) | collective-permute-done | bytes 1179680 | tf_op jit(solution)/shard_map/ppermute | solution.py:16
  54.5 2.2 %reshape.41 = bf16[64,12,768]{2,1,0:T(8,128)(2,1)S(1)} reshape(bf16[768,768]{1,0:T(8,128)(2,1)} %collective-permute-done) | data formatting | bytes 2359296 | tf_op jit(solution)/shard_map/reshape | solution.py:33
  56.6 1.8 gather_fusion.1
  58.4 1.8 gather_fusion.3
  60.3 2.4 %select_bitcast_fusion.1 = (bf16[1,64,1,12,768]{4,3,1,2,0:T(8,128)(2,1)S(1)}, bf16[1,64,1,12,768]{4,3,1,2,0:T(8,128)(2,1)S(1)}) fusion(bf16[64,12,768]{2,1,0:T(8,128)(2,1)} %gather_fusion.2, pred[64]{0:T(512)(128)(4,1)S(1)} %get-tuple-element.99, bf16[64,12,768]{2,1,0:T(8,128)(2,1)} %gather_fusion.3), kind=kLoop, calls=%fused_computation.35 | loop fusion | flops 1179648 | bytes 4718656 | tf_op jit(solution)/shard_map/stack;reshape | solution.py:59
  62.6 0.4 copy-done.3
  63.1 0.3 select_bitcast_fusion.3
  63.4 1.1 pad_maximum_fusion
  64.6 8.2 %copy.39 = bf16[4,64,1,12,768]{4,0,3,2,1:T(4,128)(2,1)} copy(bf16[4,64,1,12,768]{4,3,1,2,0:T(8,128)(2,1)S(1)} %pad_maximum_fusion) | data formatting | bytes 9437184 | tf_op jit(solution)/shard_map/stack | solution.py:59
  72.8 9.8 %all-to-all-start = ((bf16[4,64,1,12,768]{4,0,3,2,1:T(4,128)(2,1)}), bf16[4,64,1,12,768]{4,0,3,2,1:T(4,128)(2,1)}, u32[]{:S(2)}, u32[]{:S(2)}) async-start(bf16[4,64,1,12,768]{4,0,3,2,1:T(4,128)(2,1)} %copy.39), calls=%async_computation | async-start | bytes 9437184 | tf_op jit(solution)/shard_map/all_to_all | solution.py:67
  82.6 0.6 dynamic-slice.14
  83.2 0.0 copy-done.17
  83.2 0.7 dynamic-slice.13
  85.2 0.2 reduce_window_sum.18
  85.4 0.2 reduce_window_sum.17
  85.7 0.3 copy.50
  86.0 0.5 convolution_convert_fusion.1
  86.5 0.0 copy-start.14
  86.5 0.0 copy-start.13
  86.5 1.2 convert_element_type.92
  87.7 2.0 %sort.62 = (s32[64]{0:T(128)}, s32[64]{0:T(128)S(1)}) sort(s32[64]{0:T(128)S(1)} %get-tuple-element.89, s32[64]{0:T(128)S(1)} %iota.29), dimensions={0}, to_apply=%region_9.13 | sort | flops 384 | bytes 1024 | tf_op jit(solution)/shard_map/jit(argsort)/sort | solution.py:27
  89.7 2.0 %sort.61 = (s32[64]{0:T(128)}, s32[64]{0:T(128)S(1)}) sort(s32[64]{0:T(128)S(1)} %get-tuple-element.90, s32[64]{0:T(128)S(1)} %iota.28), dimensions={0}, to_apply=%region_5.8 | sort | flops 384 | bytes 1024 | tf_op jit(solution)/shard_map/jit(argsort)/sort | solution.py:27
  91.9 0.8 gather_fusion.6
  92.6 0.8 gather_fusion.4
  93.5 48.4 %all-to-all-done = bf16[4,64,1,12,768]{4,0,3,2,1:T(4,128)(2,1)} async-done(((bf16[4,64,1,12,768]{4,0,3,2,1:T(4,128)(2,1)}), bf16[4,64,1,12,768]{4,0,3,2,1:T(4,128)(2,1)}, u32[]{:S(2)}, u32[]{:S(2)}) %all-to-all-start) | async-done | bytes 4718624 | tf_op jit(solution)/shard_map/all_to_all | solution.py:67
  141.9 15.4 %fusion.36 = (bf16[1,64,1,12,768]{4,0,3,2,1:T(2,128)(2,1)S(1)}, bf16[1,64,1,12,768]{4,0,3,2,1:T(2,128)(2,1)S(1)}, bf16[1,64,1,12,768]{4,0,3,2,1:T(2,128)(2,1)S(1)}, bf16[1,64,1,12,768]{4,0,3,2,1:T(2,128)(2,1)}) fusion(bf16[4,64,1,12,768]{4,0,3,2,1:T(4,128)(2,1)} %all-to-all-done), kind=kLoop, calls=%fused_computation.94 | loop fusion | bytes 9437184 | tf_op jit(solution)/shard_map/slice | solution.py:69
  157.3 1.5 copy.76
  158.8 0.4 copy.75
  159.1 0.4 copy.77
  159.5 1.8 gather_fusion.8
  161.3 1.8 gather_fusion.5
  163.1 2.2 %fusion.5 = f32[64,768,12]{1,2,0:T(8,128)S(1)} fusion(bf16[64,12,768]{2,1,0:T(8,128)(2,1)} %gather_fusion.8, pred[64]{0:T(512)(128)(4,1)S(1)} %get-tuple-element.75, bf16[1,12,12]{2,0,1:T(2,128)(2,1)S(1)} %get-tuple-element.88), kind=kOutput, calls=%fused_computation.29 | convolution fusion | flops 14745600 | bytes 3539296 | tf_op jit(solution)/shard_map/lm,fmb->flb/dot_general | solution.py:40
  165.3 0.0 copy-done.4
  165.3 0.0 copy-start.1
  165.3 2.3 %fusion.8 = f32[64,768,12]{1,2,0:T(8,128)} fusion(bf16[64,12,768]{2,1,0:T(8,128)(2,1)S(1)} %copy-done.4, pred[64]{0:T(512)(128)(4,1)S(1)} %get-tuple-element.75, bf16[1,12,12]{2,0,1:T(2,128)(2,1)S(1)} %get-tuple-element.88), kind=kOutput, calls=%fused_computation.32 | convolution fusion | flops 14745600 | bytes 3539296 | tf_op jit(solution)/shard_map/lm,fmb->flb/dot_general | solution.py:40
  167.6 0.0 copy-done.1
  167.6 1.5 copy.74
  169.1 3.2 %gather_fusion.7 = bf16[64,12,768]{2,1,0:T(8,128)(2,1)} fusion(bf16[64,12,768]{2,1,0:T(8,128)(2,1)} %bitcast.104, s32[1024]{0:T(1024)S(1)} %pad_clamp_fusion), kind=kCustom, calls=%fused_computation.6.clone | custom fusion | bytes 2359552 | tf_op jit(solution)/shard_map/jit(_take)/gather | solution.py:39
  172.3 3.2 %gather_fusion.9 = bf16[64,12,768]{2,1,0:T(8,128)(2,1)} fusion(bf16[64,12,768]{2,1,0:T(8,128)(2,1)} %bitcast.106, s32[1024]{0:T(1024)S(1)} %pad_clamp_fusion), kind=kCustom, calls=%fused_computation.8.clone | custom fusion | bytes 2359552 | tf_op jit(solution)/shard_map/jit(_take)/gather | solution.py:39
  175.5 2.2 %add_convert_fusion.1 = bf16[64,768,12]{1,2,0:T(8,128)(2,1)S(1)} fusion(f32[64,768,12]{1,2,0:T(8,128)S(1)} %fusion.5, bf16[64,12,768]{2,1,0:T(8,128)(2,1)} %gather_fusion.9, pred[64]{0:T(512)(128)(4,1)S(1)} %get-tuple-element.71, bf16[1,12,12]{2,0,1:T(2,128)(2,1)S(1)} %get-tuple-element.87), kind=kOutput, calls=%fused_computation.13 | convolution fusion | flops 15925248 | bytes 4718944 | tf_op jit(solution)/shard_map/lm,fmb->flb/dot_general | solution.py:40
  177.8 0.1 copy-done
  177.9 0.5 copy-done.5
  178.4 1.1 add_convert_fusion
  179.4 2.1 %convert_bitcast_fusion = f32[64,12,768]{2,1,0:T(8,128)} fusion(bf16[64,768,12]{1,2,0:T(8,128)(2,1)S(1)} %add_convert_fusion), kind=kLoop, calls=%fused_computation.11 | loop fusion | flops 589824 | bytes 3538944 | tf_op jit(solution)/shard_map/convert_element_type | solution.py:77
  181.5 1.1 convert_element_type.94
  182.7 2.6 %reshape.145 = f32[768,768]{1,0:T(8,128)S(1)} reshape(f32[64,12,768]{2,1,0:T(8,128)} %convert_bitcast_fusion) | data formatting | bytes 4718592 | tf_op jit(solution)/shard_map/convert_element_type | solution.py:77
  185.3 0.0 copy-start.15
  185.3 3.6 %fusion.38 = f32[768,768]{1,0:T(8,128)S(1)} fusion(bf16[768,768]{1,0:T(8,128)(2,1)} %convert_element_type.94, bf16[768,768]{1,0:T(8,128)(2,1)} %convert_element_type.92), kind=kOutput, calls=%fused_computation.96 | convolution fusion | flops 905969664 | bytes 4718592 | tf_op jit(solution)/shard_map/dot_general | solution.py:87
  189.0 2.2 %fusion.3 = bf16[768,768]{1,0:T(8,128)(2,1)} fusion(f32[768,768]{1,0:T(8,128)S(1)} %fusion.38, bf16[768,768]{1,0:T(8,128)(2,1)S(1)} %copy-done.8, f32[768,768]{1,0:T(8,128)S(1)} %reshape.145, bf16[1,1,768,768]{3,2,1,0:T(8,128)(2,1)S(1)} %copy-done.15), kind=kOutput, calls=%fused_computation.20 | convolution fusion | flops 908918784 | bytes 8257536 | tf_op jit(solution)/shard_map/dot_general | solution.py:86
  191.2 2.2 %reshape.42 = bf16[64,12,768]{2,1,0:T(8,128)(2,1)S(1)} reshape(bf16[768,768]{1,0:T(8,128)(2,1)} %fusion.3) | data formatting | bytes 2359296 | tf_op jit(solution)/shard_map/reshape | solution.py:82
  193.4 0.5 fusion.14
  193.9 0.0 copy-start.9
  193.9 1.2 convert_element_type.98
  195.1 0.5 copy-done.9
  195.6 2.5 %fusion.39 = f32[768,768]{1,0:T(8,128)S(1)} fusion(bf16[768,768]{1,0:T(8,128)(2,1)S(1)} %copy-done.9, bf16[768,768]{1,0:T(8,128)(2,1)} %convert_element_type.98), kind=kOutput, calls=%fused_computation.97 | convolution fusion | flops 905969664 | bytes 4718592 | tf_op jit(solution)/shard_map/dot_general | solution.py:87
  198.2 0.2 copy-done.16
  198.3 2.2 %fusion.15 = bf16[1,1,768,768]{3,2,1,0:T(8,128)(2,1)} fusion(f32[768,768]{1,0:T(8,128)S(1)} %fusion.39, bf16[768,768]{1,0:T(8,128)(2,1)S(1)} %copy-done.10, f32[768,768]{1,0:T(8,128)S(1)} %copy-done.7, bf16[1,1,768,768]{3,2,1,0:T(8,128)(2,1)S(1)} %copy-done.16), kind=kOutput, calls=%fused_computation.43 | convolution fusion | flops 908918784 | bytes 8257536 | tf_op jit(solution)/shard_map/dot_general | solution.py:86
  (48 shorter events, 0.2 us)
Async XLA Ops:
  0.0 6.0 %copy-start.11 = (s32[2,64,64]{2,1,0:T(8,128)S(1)}, s32[2,64,64]{2,1,0:T(8,128)}, u32[]{:S(2)}) copy-start(s32[2,64,64]{2,1,0:T(8,128)} %param.18) | copy-start | bytes 98308
  0.0 54.5 %collective-permute-start = (bf16[768,768]{1,0:T(8,128)(2,1)}, bf16[768,768]{1,0:T(8,128)(2,1)}, u32[]{:S(2)}, u32[]{:S(2)}) collective-permute-start(bf16[768,768]{1,0:T(8,128)(2,1)} %bitcast.108), channel_id=1, source_target_pairs={{0,1},{1,0},{2,3},{3,2},{4,5},{5,4},{6,7},{7,6},{8,9},{9,8},{10,11... | collective-permute-start | bytes 3538952 | tf_op jit(solution)/shard_map/ppermute | solution.py:16
  60.2 2.4 %copy-start.2 = (bf16[64,12,768]{2,1,0:T(8,128)(2,1)S(1)}, bf16[64,12,768]{2,1,0:T(8,128)(2,1)}, u32[]{:S(2)}) copy-start(bf16[64,12,768]{2,1,0:T(8,128)(2,1)} %gather_fusion) | copy-start | bytes 3538948
  60.2 2.8 %copy-start.3 = (bf16[64,12,768]{2,1,0:T(8,128)(2,1)S(1)}, bf16[64,12,768]{2,1,0:T(8,128)(2,1)}, u32[]{:S(2)}) copy-start(bf16[64,12,768]{2,1,0:T(8,128)(2,1)} %gather_fusion.1) | copy-start | bytes 3538948
  72.8 9.8 %copy-start.18 = (f32[4]{0:T(128)S(1)}, f32[4]{0:T(128)}, u32[]{:S(2)}) copy-start(f32[4]{0:T(128)} %constant.83.clone..sunk.2) | copy-start | bytes 52
  72.8 10.4 %copy-start.17 = (f32[4]{0:T(128)S(1)}, f32[4]{0:T(128)}, u32[]{:S(2)}) copy-start(f32[4]{0:T(128)} %constant.82.clone..sunk.2) | copy-start | bytes 52
  72.8 12.9 %copy-start.12 = (bf16[1,1,64,12,12]{2,4,3,1,0:T(8,128)(2,1)S(1)}, bf16[1,1,64,12,12]{2,4,3,1,0:T(8,128)(2,1)}, u32[]{:S(2)}) copy-start(bf16[1,1,64,12,12]{2,4,3,1,0:T(8,128)(2,1)} %param.16) | copy-start | bytes 55300
  72.8 69.1 %all-to-all-start = ((bf16[4,64,1,12,768]{4,0,3,2,1:T(4,128)(2,1)}), bf16[4,64,1,12,768]{4,0,3,2,1:T(4,128)(2,1)}, u32[]{:S(2)}, u32[]{:S(2)}) async-start(bf16[4,64,1,12,768]{4,0,3,2,1:T(4,128)(2,1)} %copy.39), calls=%async_computation | async-start | bytes 9437184 | tf_op jit(solution)/shard_map/all_to_all | solution.py:67
  86.5 1.2 copy-start.14
  86.5 7.0 %copy-start.13 = (bf16[2,12,12]{2,0,1:T(2,128)(2,1)S(1)}, bf16[2,12,12]{2,0,1:T(2,128)(2,1)}, u32[]{:S(2)}) copy-start(bf16[2,12,12]{2,0,1:T(2,128)(2,1)} %param.17) | copy-start | bytes 1732
  163.1 2.2 %copy-start.4 = (bf16[64,12,768]{2,1,0:T(8,128)(2,1)S(1)}, bf16[64,12,768]{2,1,0:T(8,128)(2,1)}, u32[]{:S(2)}) copy-start(bf16[64,12,768]{2,1,0:T(8,128)(2,1)} %gather_fusion.5) | copy-start | bytes 3538948
  165.3 2.3 %copy-start.1 = (bf16[1,64,1,12,768]{4,0,3,2,1:T(2,128)(2,1)S(1)}, bf16[1,64,1,12,768]{4,0,3,2,1:T(2,128)(2,1)}, u32[]{:S(2)}) copy-start(bf16[1,64,1,12,768]{4,0,3,2,1:T(2,128)(2,1)} %get-tuple-element.82) | copy-start | bytes 3538948
  175.5 2.4 %copy-start = (f32[64,768,12]{1,2,0:T(8,128)S(1)}, f32[64,768,12]{1,2,0:T(8,128)}, u32[]{:S(2)}) copy-start(f32[64,768,12]{1,2,0:T(8,128)} %fusion.8) | copy-start | bytes 7077892
  175.5 2.8 %copy-start.5 = (bf16[64,12,768]{2,1,0:T(8,128)(2,1)S(1)}, bf16[64,12,768]{2,1,0:T(8,128)(2,1)}, u32[]{:S(2)}) copy-start(bf16[64,12,768]{2,1,0:T(8,128)(2,1)} %gather_fusion.7) | copy-start | bytes 3538948
  185.3 3.6 %copy-start.6 = (f32[768,768]{1,0:T(8,128)}, f32[768,768]{1,0:T(8,128)S(1)}, u32[]{:S(2)}) copy-start(f32[768,768]{1,0:T(8,128)S(1)} %reshape.145) | copy-start | bytes 7077892
  185.3 3.6 %copy-start.8 = (bf16[768,768]{1,0:T(8,128)(2,1)S(1)}, bf16[768,768]{1,0:T(8,128)(2,1)}, u32[]{:S(2)}) copy-start(bf16[768,768]{1,0:T(8,128)(2,1)} %convert_element_type.92) | copy-start | bytes 3538948
  185.3 3.6 %copy-start.15 = (bf16[1,1,768,768]{3,2,1,0:T(8,128)(2,1)S(1)}, bf16[1,1,768,768]{3,2,1,0:T(8,128)(2,1)}, u32[]{:S(2)}) copy-start(bf16[1,1,768,768]{3,2,1,0:T(8,128)(2,1)} %param.15) | copy-start | bytes 3538948
  193.9 1.7 copy-start.9
  195.6 2.5 %copy-start.7 = (f32[768,768]{1,0:T(8,128)S(1)}, f32[768,768]{1,0:T(8,128)}, u32[]{:S(2)}) copy-start(f32[768,768]{1,0:T(8,128)} %copy-done.6) | copy-start | bytes 7077892
  195.6 2.5 %copy-start.10 = (bf16[768,768]{1,0:T(8,128)(2,1)S(1)}, bf16[768,768]{1,0:T(8,128)(2,1)}, u32[]{:S(2)}) copy-start(bf16[768,768]{1,0:T(8,128)(2,1)} %convert_element_type.98) | copy-start | bytes 3538948
  195.6 2.7 %copy-start.16 = (bf16[1,1,768,768]{3,2,1,0:T(8,128)(2,1)S(1)}, bf16[1,1,768,768]{3,2,1,0:T(8,128)(2,1)}, u32[]{:S(2)}) copy-start(bf16[1,1,768,768]{3,2,1,0:T(8,128)(2,1)} %param.15) | copy-start | bytes 3538948
where the time goes:
time: 204 us; the launch traced here: 200 us
  waiting for transfers between devices  89.1 us (44%)
  local copies, waits for them, and re-layouts  62 us (30%)
  matrix products  19.4 us (10%)
  other arithmetic  14.7 us (7%)
  starting transfers between devices  13.6 us (7%)
    all_to_all x1, waiting for transfers between devices, local(): lax.all_to_all(stacked, 'mom', split_axis=1, concat_axis=1, tiled=True)  48.4 us
    ppermute x1, waiting for transfers between devices, partner_2(): return lax.ppermute(value, axis, pairs)  40.7 us
    slice x1, local copies, waits for them, and re-layouts, local(): received[2]  15.4 us
    gather x4, local copies, waits for them, and re-layouts, unpack_blocks(): jnp.take(received.reshape(freqs, forms, order_len), recv_order, axis=0)  10 us
    all_to_all x1, starting transfers between devices, local(): lax.all_to_all(stacked, 'mom', split_axis=1, concat_axis=1, tiled=True)  9.8 us
    another operation x1, local copies, waits for them, and re-layouts, local(): jnp.stack([pack_blocks(current, orders_first[0], momenta, per_peer, freqs...  8.24 us
    dot_general x4, matrix products, unpack_blocks(): jnp.einsum('lm,fmb->flb', mixing, gathered, preferred_element_type=jnp.fl...  7.81 us
    gather x4, local copies, waits for them, and re-layouts, pack_blocks(): jnp.take(matrix.reshape(freqs, forms, order_len), send_order, axis=0)  7.2 us
  transfers between devices with their start and end apart: 2, of which 2 were waited for; matrix products, arithmetic and copies ran while one was open for 10% of the time, Pallas kernels for 0%

commit v1 on v0

v1 whole, which is shorter than its diff:
```python
import jax
import jax.numpy as jnp
from jax import lax
from jax.sharding import PartitionSpec as P

INNER = 2
NCHUNK = 3

COEF_SELF = (-0.5, 0.5, 0.5, 0.5)
COEF_PAIR = (-1.5, -0.5, 1.5, -0.5)


def partner_2(value, axis, stride):
    mask = 2**stride
    pairs = [(source, source ^ mask) for source in range(lax.axis_size(axis))]
    return lax.ppermute(value, axis, pairs)


def inverse_perm(perm, size):
    idx = jnp.arange(size, dtype=jnp.int32)
    return jnp.sum(jnp.where(perm[None, :] == idx[:, None], idx[None, :], 0), axis=1)


def crossing_plan(table, frequency_perm, momentum, freqs):
    idx = jnp.arange(freqs, dtype=jnp.int32)
    own_row = jnp.take(table, momentum, axis=0)
    send_order = inverse_perm(own_row, freqs)
    hit = table == momentum
    source = jnp.sum(jnp.where(hit, idx[:, None], 0), axis=0)
    freq_of = inverse_perm(frequency_perm, freqs)
    return send_order, jnp.take(source, freq_of, axis=0)


def mix_matrix(slots, mixing, freqs):
    forms = mixing.shape[0]
    idx = jnp.arange(freqs, dtype=jnp.int32)
    onehot = (slots[:, None] == idx[None, :]).astype(mixing.dtype)
    full = onehot[:, None, :, None] * mixing[None, :, None, :]
    return full.reshape(freqs * forms, freqs * forms)


def local(vertex_start, bare_vertex, bubble, form_mix, cross_tables, freq_perm):
    current = vertex_start[0, 0]
    bare_mat = bare_vertex[0, 0]
    bubble_mat = bubble[0, 0]
    freqs, forms = (bubble_mat.shape[0], bubble_mat.shape[1])
    order_len = current.shape[0]
    momenta = lax.axis_size("mom")
    assert freqs == momenta
    momentum = lax.axis_index("mom")
    channel = lax.axis_index("spin")
    coef_self = jnp.take(jnp.array(COEF_SELF, jnp.float32), channel)
    coef_pair = jnp.take(jnp.array(COEF_PAIR, jnp.float32), channel)

    blocks = current.reshape(freqs, forms, order_len)
    packs = []
    mixes = []
    for r in range(2):
        send_order, recv_slots = crossing_plan(cross_tables[r], freq_perm[r], momentum, freqs)
        packs.append(jnp.take(blocks, send_order, axis=0))
        mixes.append(mix_matrix(recv_slots, form_mix[r], freqs))
    stacked = jnp.stack(packs)
    mix = jnp.concatenate(mixes, axis=1)

    def carry_of(mat):
        carried = jnp.einsum(
            "fln,fnb->flb",
            bubble_mat,
            mat.reshape(freqs, forms, order_len),
            preferred_element_type=jnp.float32,
        )
        return carried.reshape(order_len, order_len).astype(jnp.bfloat16)

    carried = carry_of(current)
    bare_part = jnp.dot(bare_mat, carried, preferred_element_type=jnp.float32)

    width = order_len // NCHUNK
    red_chunks = []
    for k in range(NCHUNK):
        cols = slice(k * width, (k + 1) * width)
        received = lax.all_to_all(stacked[..., cols], "mom", split_axis=1, concat_axis=1, tiled=True)
        summed = jnp.dot(
            mix, received.reshape(2 * order_len, width), preferred_element_type=jnp.float32
        ).astype(jnp.bfloat16)
        other = partner_2(summed, "spin", 0)
        red_chunks.append(
            (coef_self * summed.astype(jnp.float32) + coef_pair * other.astype(jnp.float32)).astype(
                jnp.bfloat16
            )
        )
    reducible = jnp.concatenate(red_chunks, axis=1)
    base_sum = bare_mat.astype(jnp.float32) + reducible.astype(jnp.float32)

    total = base_sum + bare_part
    for k in range(NCHUNK):
        rows = slice(k * width, (k + 1) * width)
        total = total + jnp.dot(red_chunks[k], carried[rows], preferred_element_type=jnp.float32)
    current = total.astype(jnp.bfloat16)
    for inner_step in range(1, INNER):
        carried = carry_of(current)
        total = base_sum + jnp.dot(bare_mat, carried, preferred_element_type=jnp.float32)
        total = total + jnp.dot(reducible, carried, preferred_element_type=jnp.float32)
        current = total.astype(jnp.bfloat16)
    return current[None, None]


def solution(mesh):
    in_specs = (
        P("mom", "spin", None, None),
        P("mom", "spin", None, None),
        P("mom", "spin", None, None, None),
        P(),
        P(),
        P(),
    )
    out_specs = P("mom", "spin", None, None)
    return jax.shard_map(local, mesh=mesh, in_specs=in_specs, out_specs=out_specs, check_vma=False)
```

time: 204 us -> 188 us (0.922); the launches traced: 200 us -> 187 us
  waiting for transfers between devices: 89.1 us -> 36.3 us
  starting transfers between devices: 13.6 us -> 34.1 us
  local copies, waits for them, and re-layouts: 62 us -> 78.2 us
  other arithmetic: 14.7 us -> 17.8 us
    mul x0 -> x3, local copies, waits for them, and re-layouts: none -> 48.5 us  [mix_matrix(): full = onehot[:, None, :, None] * mixing[None, :, None, :]]
    all_to_all x1 -> x3, waiting for transfers between devices: 48.4 us -> 0.01 us  [local(): lax.all_to_all(stacked[..., cols], 'mom', split_axis=1, concat_axis=1, ti...]
    all_to_all x1 -> x3, starting transfers between devices: 9.8 us -> 28.3 us  [local(): lax.all_to_all(stacked[..., cols], 'mom', split_axis=1, concat_axis=1, ti...]
    gather x10 -> x4, local copies, waits for them, and re-layouts: 18.8 us -> 4.02 us  [the longest x2 2.46 us: local(): packs.append(jnp.take(blocks, send_order, axis=0))]
    another operation x6 -> x1, local copies, waits for them, and re-layouts: 14.1 us -> 2.16 us  [local(): blocks = current.reshape(freqs, forms, order_len)]
    mul x0 -> x2, other arithmetic: none -> 11.4 us  [mix_matrix(): full = onehot[:, None, :, None] * mixing[None, :, None, :]]
    slice x2 -> x4, local copies, waits for them, and re-layouts: 15.4 us -> 6.35 us  [the longest x3 6.34 us: local(): stacked[..., cols]]
    sort x4 -> x0, other arithmetic: 8.14 us -> none  [the longest x2 4.07 us: make_orders(): freq_of = jnp.argsort(frequency_perm)]
  transfers between devices with their start and end apart: 2 -> 6, of which waited for: 2 -> 3; matrix products, arithmetic and copies ran while one was open for 10% -> 48% of each run, Pallas kernels for 0% -> 0%
where the time goes in v1:
time: 188 us; the launch traced here: 187 us
  local copies, waits for them, and re-layouts  78.2 us (42%)
  waiting for transfers between devices  36.3 us (19%)
  starting transfers between devices  34.1 us (18%)
  matrix products  18.8 us (10%)
  other arithmetic  17.8 us (9%)
    mul x3, local copies, waits for them, and re-layouts, mix_matrix(): full = onehot[:, None, :, None] * mixing[None, :, None, :]  48.5 us
    ppermute x3, waiting for transfers between devices, partner_2(): return lax.ppermute(value, axis, pairs)  36.3 us
    all_to_all x3, starting transfers between devices, local(): lax.all_to_all(stacked[..., cols], 'mom', split_axis=1, concat_axis=1, ti...  28.3 us
    mul x2, other arithmetic, mix_matrix(): full = onehot[:, None, :, None] * mixing[None, :, None, :]  11.4 us
    dot_general x3, matrix products, local(): jnp.dot(mix, received.reshape(2 * order_len, width), preferred_element_ty...  8.19 us
    slice x3, local copies, waits for them, and re-layouts, local(): stacked[..., cols]  6.34 us
    ppermute x3, starting transfers between devices, partner_2(): return lax.ppermute(value, axis, pairs)  5.75 us
    unnamed x44, local copies, waits for them, and re-layouts  5 us
  transfers between devices with their start and end apart: 6, of which 3 were waited for; matrix products, arithmetic and copies ran while one was open for 48% of the time, Pallas kernels for 0%

profile of v1, /device:TPU:1, one launch (start us, length us, event | category | flops | bytes accessed | tf_op | source)
XLA Modules:
  0.0 186.9 jit_solution(12353021071223536853)
XLA Ops:
  0.0 0.8 slice_bitcast_fusion
  0.8 0.1 select_reduce_fusion
  0.9 0.1 select_reduce_fusion.1
  1.1 2.2 %reshape_squeeze.4 = bf16[64,12,768]{2,1,0:T(8,128)(2,1)S(1)} reshape(bf16[1,1,768,768]{3,2,1,0:T(8,128)(2,1)} %param.14) | data formatting | bytes 2359296 | tf_op jit(solution)/shard_map/reshape;squeeze | solution.py:55
  3.3 1.8 gather_fusion.3
  5.1 0.6 gather_fusion.2
  5.7 1.6 select_bitcast_fusion
  7.4 0.2 select_bitcast_fusion.1
  7.6 1.4 pad_maximum_fusion.1
  9.0 1.7 copy.36
  10.7 10.3 %all-to-all-start.1 = ((bf16[2,64,12,256]{3,0,2,1:T(2,128)(2,1)}), bf16[2,64,12,256]{3,0,2,1:T(2,128)(2,1)S(1)}, u32[]{:S(2)}, u32[]{:S(2)}) async-start(bf16[2,64,12,256]{3,0,2,1:T(2,128)(2,1)} %copy.36), calls=%async_computation.1 | async-start | bytes 1572864 | tf_op jit(solution)/shard_map/all_to_all | solution.py:81
  21.1 0.1 select_reduce_fusion.2
  21.3 0.8 gather_fusion
  22.1 0.1 fusion.19
  22.2 5.7 %broadcast_multiply_fusion.1 = bf16[64,12,64,12]{3,2,1,0:T(8,128)(2,1)} fusion(bf16[12,12]{1,0:T(8,128)(2,1)S(1)} %get-tuple-element.71, bf16[64,64]{1,0:T(8,128)(2,1)S(1)} %fusion.19), kind=kLoop, calls=%fused_computation.5 | loop fusion | flops 589824 | bytes 1188128 | tf_op jit(solution)/shard_map/mul | solution.py:38
  27.8 24.2 %mul.71 = bf16[768,768]{1,0:T(8,128)(2,1)} reshape(bf16[64,12,64,12]{3,2,1,0:T(8,128)(2,1)} %broadcast_multiply_fusion.1) | data formatting | bytes 2359296 | tf_op jit(solution)/shard_map/mul | solution.py:38
  52.1 2.9 %copy.34 = bf16[2,64,12,256]{3,0,2,1:T(2,128)(2,1)} copy(bf16[2,64,12,256]{3,2,1,0:T(8,128)(2,1)} %get-tuple-element.62) | data formatting | bytes 1572864 | tf_op jit(solution)/shard_map/slice | solution.py:81
  55.0 9.0 %all-to-all-start = ((bf16[2,64,12,256]{3,0,2,1:T(2,128)(2,1)}), bf16[2,64,12,256]{3,0,2,1:T(2,128)(2,1)}, u32[]{:S(2)}, u32[]{:S(2)}) async-start(bf16[2,64,12,256]{3,0,2,1:T(2,128)(2,1)} %copy.34), calls=%async_computation | async-start | bytes 1572864 | tf_op jit(solution)/shard_map/all_to_all | solution.py:81
  64.1 0.8 gather_fusion.1
  64.9 0.1 fusion.20
  64.9 5.7 %broadcast_multiply_fusion = bf16[64,12,64,12]{3,2,1,0:T(8,128)(2,1)} fusion(bf16[12,12]{1,0:T(8,128)(2,1)S(1)} %get-tuple-element.70, bf16[64,64]{1,0:T(8,128)(2,1)S(1)} %fusion.20), kind=kLoop, calls=%fused_computation.4 | loop fusion | flops 589824 | bytes 1188128 | tf_op jit(solution)/shard_map/mul | solution.py:38
  70.6 24.3 %mul.76 = bf16[768,768]{1,0:T(8,128)(2,1)} reshape(bf16[64,12,64,12]{3,2,1,0:T(8,128)(2,1)} %broadcast_multiply_fusion) | data formatting | bytes 2359296 | tf_op jit(solution)/shard_map/mul | solution.py:38
  94.9 0.6 dynamic-slice.14
  95.5 0.7 dynamic-slice.13
  97.4 0.3 copy.40
  97.7 1.7 copy.38
  99.4 9.0 %all-to-all-start.2 = ((bf16[2,64,12,256]{3,0,2,1:T(2,128)(2,1)}), bf16[2,64,12,256]{3,0,2,1:T(2,128)(2,1)}, u32[]{:S(2)}, u32[]{:S(2)}) async-start(bf16[2,64,12,256]{3,0,2,1:T(2,128)(2,1)} %copy.38), calls=%async_computation.2 | async-start | bytes 1572864 | tf_op jit(solution)/shard_map/all_to_all | solution.py:81
  108.4 0.5 convolution_convert_fusion.1
  109.0 0.3 convert_element_type.97
  109.3 0.0 copy-start
  109.3 2.5 %copy.31 = bf16[1,1,768,768]{2,3,1,0:T(8,128)(2,1)} copy(bf16[1,1,768,768]{3,2,1,0:T(8,128)(2,1)} %param.15) | data formatting | bytes 2359296 | tf_op args[1]
  111.8 0.1 constant_dynamic-update-slice_fusion.1
  111.9 1.2 copy-done.3
  113.1 0.1 constant_dynamic-update-slice_fusion
  113.1 1.2 copy-done.12
  114.3 2.6 %fusion.10 = f32[768,768]{1,0:T(8,128)} fusion(bf16[768,768]{1,0:T(8,128)(2,1)S(1)} %convert_element_type.97, bf16[1,1,768,768]{3,2,1,0:T(8,128)(2,1)S(1)} %copy-done.12), kind=kOutput, calls=%fused_computation.31 | convolution fusion | flops 905969664 | bytes 4718592 | tf_op jit(solution)/shard_map/dot_general | solution.py:75
  116.9 0.2 copy.37
  117.1 0.2 reshape.85
  117.3 2.5 %convolution_convert_fusion.3 = bf16[768,256]{0,1:T(8,128)(2,1)S(1)} fusion(bf16[768,1536]{1,0:T(8,128)(2,1)} %copy-done.14, bf16[1536,256]{1,0:T(8,128)(2,1)S(1)} %reshape.85), kind=kOutput, calls=%fused_computation.26 | convolution fusion | flops 604176384 | bytes 3538944 | tf_op jit(solution)/shard_map/dot_general | solution.py:82
  119.7 3.1 %collective-permute-start.1 = (bf16[768,256]{0,1:T(8,128)(2,1)S(1)}, bf16[768,256]{0,1:T(8,128)(2,1)}, u32[]{:S(2)}, u32[]{:S(2)}) collective-permute-start(bf16[768,256]{0,1:T(8,128)(2,1)S(1)} %convolution_convert_fusion.3), channel_id=1, source_target_pairs={{0,1},{1,0},{2,3},{3,2},{4,5},{5,4},{6,7},{7,6},{8,9},{9,8},{10,11... | collective-permute-start | bytes 1179656 | tf_op jit(solution)/shard_map/ppermute | solution.py:16
  122.8 1.3 copy.35
  124.1 0.2 reshape.84
  124.3 3.2 %convolution_convert_fusion.4 = bf16[768,256]{0,1:T(8,128)(2,1)} fusion(bf16[768,1536]{1,0:T(8,128)(2,1)} %copy-done.14, bf16[1536,256]{1,0:T(8,128)(2,1)S(1)} %reshape.84), kind=kOutput, calls=%fused_computation.27 | convolution fusion | flops 604176384 | bytes 3538944 | tf_op jit(solution)/shard_map/dot_general | solution.py:82
  127.5 0.0 collective-permute-start
  127.6 1.3 copy.39
  128.8 0.2 reshape.86
  129.0 2.5 %convolution_convert_fusion.2 = bf16[768,256]{0,1:T(8,128)(2,1)S(1)} fusion(bf16[768,1536]{1,0:T(8,128)(2,1)} %copy-done.14, bf16[1536,256]{1,0:T(8,128)(2,1)S(1)} %reshape.86), kind=kOutput, calls=%fused_computation.25 | convolution fusion | flops 604176384 | bytes 3538944 | tf_op jit(solution)/shard_map/dot_general | solution.py:82
  131.5 2.6 %collective-permute-start.2 = (bf16[768,256]{0,1:T(8,128)(2,1)S(1)}, bf16[768,256]{0,1:T(8,128)(2,1)S(1)}, u32[]{:S(2)}, u32[]{:S(2)}) collective-permute-start(bf16[768,256]{0,1:T(8,128)(2,1)S(1)} %convolution_convert_fusion.2), channel_id=1, source_target_pairs={{0,1},{1,0},{2,3},{3,2},{4,5},{5,4},{6,7},{7,6},{8,9},{9,8},{10,11... | collective-permute-start | bytes 1179656 | tf_op jit(solution)/shard_map/ppermute | solution.py:16
  134.2 23.0 %collective-permute-done.1 = bf16[768,256]{0,1:T(8,128)(2,1)} collective-permute-done((bf16[768,256]{0,1:T(8,128)(2,1)S(1)}, bf16[768,256]{0,1:T(8,128)(2,1)}, u32[]{:S(2)}, u32[]{:S(2)}) %collective-permute-start.1) | collective-permute-done | bytes 393248 | tf_op jit(solution)/shard_map/ppermute | solution.py:16
  157.2 1.1 add_convert_fusion.1
  158.3 0.5 fusion.15
  158.8 6.8 %collective-permute-done = bf16[768,256]{0,1:T(8,128)(2,1)} collective-permute-done((bf16[768,256]{0,1:T(8,128)(2,1)}, bf16[768,256]{0,1:T(8,128)(2,1)}, u32[]{:S(2)}, u32[]{:S(2)}) %collective-permute-start) | collective-permute-done | bytes 393248 | tf_op jit(solution)/shard_map/ppermute | solution.py:16
  165.6 1.3 add_convert_fusion.2
  166.9 0.5 fusion.17
  167.4 6.5 %collective-permute-done.2 = bf16[768,256]{0,1:T(8,128)(2,1)S(1)} collective-permute-done((bf16[768,256]{0,1:T(8,128)(2,1)S(1)}, bf16[768,256]{0,1:T(8,128)(2,1)S(1)}, u32[]{:S(2)}, u32[]{:S(2)}) %collective-permute-start.2) | collective-permute-done | bytes 393248 | tf_op jit(solution)/shard_map/ppermute | solution.py:16
  173.9 0.1 add_convert_fusion
  174.1 0.9 fusion.5
  175.0 1.5 copy.45
  176.5 2.2 %reshape.87 = bf16[64,12,768]{2,1,0:T(8,128)(2,1)S(1)} reshape(bf16[768,768]{1,0:T(8,128)(2,1)} %copy.45) | data formatting | bytes 2359296 | tf_op jit(solution)/shard_map/reshape | solution.py:69
  178.6 1.5 fusion.6
  180.1 1.2 convert_element_type.101
  181.3 2.9 %fusion.8 = f32[768,768]{1,0:T(8,128)S(1)} fusion(bf16[768,768]{1,0:T(8,128)(2,1)} %convert_element_type.101, bf16[1,1,768,768]{3,2,1,0:T(8,128)(2,1)} %param.15), kind=kOutput, calls=%fused_computation.29 | convolution fusion | flops 905969664 | bytes 4718592 | tf_op jit(solution)/shard_map/dot_general | solution.py:101
  184.2 1.2 fusion.7
  185.5 1.5 copy.48
  (58 shorter events, 0.2 us)
Async XLA Ops:
  9.0 12.1 %copy-start.15 = (s32[2,64,64]{2,1,0:T(8,128)S(1)}, s32[2,64,64]{2,1,0:T(8,128)}, u32[]{:S(2)}) copy-start(s32[2,64,64]{2,1,0:T(8,128)} %param.18) | copy-start | bytes 98308
  9.0 12.1 %copy-start.18 = (s32[2,64]{1,0:T(2,128)S(1)}, s32[2,64]{1,0:T(2,128)}, u32[]{:S(2)}) copy-start(s32[2,64]{1,0:T(2,128)} %param.19) | copy-start | bytes 1540
  9.0 13.0 %copy-start.17 = (bf16[2,12,12]{2,0,1:T(2,128)(2,1)S(1)}, bf16[2,12,12]{2,0,1:T(2,128)(2,1)}, u32[]{:S(2)}) copy-start(bf16[2,12,12]{2,0,1:T(2,128)(2,1)} %param.17) | copy-start | bytes 1732
  10.7 44.3 %all-to-all-start.1 = ((bf16[2,64,12,256]{3,0,2,1:T(2,128)(2,1)}), bf16[2,64,12,256]{3,0,2,1:T(2,128)(2,1)S(1)}, u32[]{:S(2)}, u32[]{:S(2)}) async-start(bf16[2,64,12,256]{3,0,2,1:T(2,128)(2,1)} %copy.36), calls=%async_computation.1 | async-start | bytes 1572864 | tf_op jit(solution)/shard_map/all_to_all | solution.py:81
  55.0 15.6 %copy-start.6 = (bf16[2,64,12,256]{3,0,2,1:T(2,128)(2,1)}, bf16[2,64,12,256]{3,0,2,1:T(2,128)(2,1)S(1)}, u32[]{:S(2)}) copy-start(bf16[2,64,12,256]{3,0,2,1:T(2,128)(2,1)S(1)} %all-to-all-done.1) | copy-start | bytes 2359300
  55.0 44.4 %all-to-all-start = ((bf16[2,64,12,256]{3,0,2,1:T(2,128)(2,1)}), bf16[2,64,12,256]{3,0,2,1:T(2,128)(2,1)}, u32[]{:S(2)}, u32[]{:S(2)}) async-start(bf16[2,64,12,256]{3,0,2,1:T(2,128)(2,1)} %copy.34), calls=%async_computation | async-start | bytes 1572864 | tf_op jit(solution)/shard_map/all_to_all | solution.py:81
  70.6 24.3 %copy-start.20 = (f32[4]{0:T(128)S(1)}, f32[4]{0:T(128)}, u32[]{:S(2)}) copy-start(f32[4]{0:T(128)} %constant.69.clone..sunk.2) | copy-start | bytes 52
  70.6 24.9 %copy-start.19 = (f32[4]{0:T(128)S(1)}, f32[4]{0:T(128)}, u32[]{:S(2)}) copy-start(f32[4]{0:T(128)} %constant.68.clone..sunk.2) | copy-start | bytes 52
  70.6 26.8 %copy-start.16 = (bf16[1,1,64,12,12]{2,4,3,1,0:T(8,128)(2,1)S(1)}, bf16[1,1,64,12,12]{2,4,3,1,0:T(8,128)(2,1)}, u32[]{:S(2)}) copy-start(bf16[1,1,64,12,12]{2,4,3,1,0:T(8,128)(2,1)} %param.16) | copy-start | bytes 55300
  97.7 10.7 %copy-start.9 = (bf16[64,12,12]{2,1,0:T(8,128)(2,1)}, bf16[64,12,12]{2,1,0:T(8,128)(2,1)S(1)}, u32[]{:S(2)}) copy-start(bf16[64,12,12]{2,1,0:T(8,128)(2,1)S(1)} %copy.40) | copy-start | bytes 55300
  99.4 28.1 %all-to-all-start.2 = ((bf16[2,64,12,256]{3,0,2,1:T(2,128)(2,1)}), bf16[2,64,12,256]{3,0,2,1:T(2,128)(2,1)}, u32[]{:S(2)}, u32[]{:S(2)}) async-start(bf16[2,64,12,256]{3,0,2,1:T(2,128)(2,1)} %copy.38), calls=%async_computation.2 | async-start | bytes 1572864 | tf_op jit(solution)/shard_map/all_to_all | solution.py:81
  109.3 2.5 %copy-start = (bf16[768,768]{1,0:T(8,128)(2,1)S(1)}, bf16[768,768]{1,0:T(8,128)(2,1)}, u32[]{:S(2)}) copy-start(bf16[768,768]{1,0:T(8,128)(2,1)} %mul.71) | copy-start | bytes 3538948
  111.8 1.3 copy-start.3
  113.1 1.3 copy-start.12
  114.3 2.6 %copy-start.14 = (bf16[768,1536]{1,0:T(8,128)(2,1)}, bf16[768,1536]{1,0:T(8,128)(2,1)S(1)}, u32[]{:S(2)}) copy-start(bf16[768,1536]{1,0:T(8,128)(2,1)S(1)} %constant_dynamic-update-slice_fusion) | copy-start | bytes 7077892
  114.3 2.6 %copy-start.7 = (bf16[2,64,12,256]{3,0,2,1:T(2,128)(2,1)S(1)}, bf16[2,64,12,256]{3,0,2,1:T(2,128)(2,1)}, u32[]{:S(2)}) copy-start(bf16[2,64,12,256]{3,0,2,1:T(2,128)(2,1)} %copy-done.6) | copy-start | bytes 2359300
  119.7 37.4 %collective-permute-start.1 = (bf16[768,256]{0,1:T(8,128)(2,1)S(1)}, bf16[768,256]{0,1:T(8,128)(2,1)}, u32[]{:S(2)}, u32[]{:S(2)}) collective-permute-start(bf16[768,256]{0,1:T(8,128)(2,1)S(1)} %convolution_convert_fusion.3), channel_id=1, source_target_pairs={{0,1},{1,0},{2,3},{3,2},{4,5},{5,4},{6,7},{7,6},{8,9},{9,8},{10,11... | collective-permute-start | bytes 1179656 | tf_op jit(solution)/shard_map/ppermute | solution.py:16
  127.5 38.1 %collective-permute-start = (bf16[768,256]{0,1:T(8,128)(2,1)}, bf16[768,256]{0,1:T(8,128)(2,1)}, u32[]{:S(2)}, u32[]{:S(2)}) collective-permute-start(bf16[768,256]{0,1:T(8,128)(2,1)} %convolution_convert_fusion.4), channel_id=1, source_target_pairs={{0,1},{1,0},{2,3},{3,2},{4,5},{5,4},{6,7},{7,6},{8,9},{9,8},{10,11... | collective-permute-start | bytes 1179656 | tf_op jit(solution)/shard_map/ppermute | solution.py:16
  131.5 42.4 %collective-permute-start.2 = (bf16[768,256]{0,1:T(8,128)(2,1)S(1)}, bf16[768,256]{0,1:T(8,128)(2,1)S(1)}, u32[]{:S(2)}, u32[]{:S(2)}) collective-permute-start(bf16[768,256]{0,1:T(8,128)(2,1)S(1)} %convolution_convert_fusion.2), channel_id=1, source_target_pairs={{0,1},{1,0},{2,3},{3,2},{4,5},{5,4},{6,7},{7,6},{8,9},{9,8},{10,11... | collective-permute-start | bytes 1179656 | tf_op jit(solution)/shard_map/ppermute | solution.py:16
  166.9 7.2 %copy-start.4 = (bf16[768,256]{0,1:T(8,128)(2,1)}, bf16[768,256]{0,1:T(8,128)(2,1)S(1)}, u32[]{:S(2)}) copy-start(bf16[768,256]{0,1:T(8,128)(2,1)S(1)} %add_convert_fusion.2) | copy-start | bytes 1179652
  166.9 7.2 %copy-start.1 = (bf16[1,1,768,768]{2,3,1,0:T(8,128)(2,1)S(1)}, bf16[1,1,768,768]{2,3,1,0:T(8,128)(2,1)}, u32[]{:S(2)}) copy-start(bf16[1,1,768,768]{2,3,1,0:T(8,128)(2,1)} %copy.31) | copy-start | bytes 3538948
  166.9 7.2 %copy-start.8 = (f32[768,768]{1,0:T(8,128)S(1)}, f32[768,768]{1,0:T(8,128)}, u32[]{:S(2)}) copy-start(f32[768,768]{1,0:T(8,128)} %fusion.10) | copy-start | bytes 7077892
  174.1 0.9 copy-start.10
  181.3 2.9 %copy-start.2 = (bf16[1,1,768,768]{2,3,1,0:T(8,128)(2,1)S(1)}, bf16[1,1,768,768]{2,3,1,0:T(8,128)(2,1)}, u32[]{:S(2)}) copy-start(bf16[1,1,768,768]{2,3,1,0:T(8,128)(2,1)} %copy.31) | copy-start | bytes 3538948
  181.3 2.9 %copy-start.5 = (bf16[768,256]{0,1:T(8,128)(2,1)S(1)}, bf16[768,256]{0,1:T(8,128)(2,1)}, u32[]{:S(2)}) copy-start(bf16[768,256]{0,1:T(8,128)(2,1)} %copy-done.4) | copy-start | bytes 1179652
  181.3 2.9 %copy-start.11 = (bf16[768,256]{0,1:T(8,128)(2,1)S(1)}, bf16[768,256]{0,1:T(8,128)(2,1)}, u32[]{:S(2)}) copy-start(bf16[768,256]{0,1:T(8,128)(2,1)} %copy-done.10) | copy-start | bytes 1179652
  181.3 2.9 %copy-start.13 = (bf16[768,768]{1,0:T(8,128)(2,1)S(1)}, bf16[768,768]{1,0:T(8,128)(2,1)}, u32[]{:S(2)}) copy-start(bf16[768,768]{1,0:T(8,128)(2,1)} %convert_element_type.101) | copy-start | bytes 3538948

commit v2 on v1

--- a/solution.py
+++ b/solution.py
@@ -4,7 +4,7 @@
 from jax.sharding import PartitionSpec as P
 
 INNER = 2
-NCHUNK = 3
+NCHUNK = 2
 
 COEF_SELF = (-0.5, 0.5, 0.5, 0.5)
 COEF_PAIR = (-1.5, -0.5, 1.5, -0.5)
@@ -31,12 +31,29 @@
     return send_order, jnp.take(source, freq_of, axis=0)
 
 
-def mix_matrix(slots, mixing, freqs):
-    forms = mixing.shape[0]
+def block_rows(order_len, freqs):
+    forms = order_len // freqs
+    rows = lax.broadcasted_iota(jnp.int32, (order_len, freqs), 0) // forms
+    cols = lax.broadcasted_iota(jnp.int32, (order_len, freqs), 1)
+    return (rows == cols).astype(jnp.bfloat16)
+
+
+def form_rows(order_len, forms):
+    rows = lax.broadcasted_iota(jnp.int32, (order_len, forms), 0) % forms
+    cols = lax.broadcasted_iota(jnp.int32, (order_len, forms), 1)
+    return (rows == cols).astype(jnp.bfloat16)
+
+
+def exact_dot(a, b):
+    return jnp.dot(a, b, preferred_element_type=jnp.float32).astype(jnp.bfloat16)
+
+
+def mix_matrix(slots, mixing, freqs, expand, forms_expand):
     idx = jnp.arange(freqs, dtype=jnp.int32)
-    onehot = (slots[:, None] == idx[None, :]).astype(mixing.dtype)
-    full = onehot[:, None, :, None] * mixing[None, :, None, :]
-    return full.reshape(freqs * forms, freqs * forms)
+    onehot = (slots[:, None] == idx[None, :]).astype(jnp.bfloat16)
+    select = exact_dot(exact_dot(expand, onehot), expand.T)
+    tiled = exact_dot(exact_dot(forms_expand, mixing), forms_expand.T)
+    return select * tiled
 
 
 def local(vertex_start, bare_vertex, bubble, form_mix, cross_tables, freq_perm):
@@ -53,23 +70,23 @@
     coef_pair = jnp.take(jnp.array(COEF_PAIR, jnp.float32), channel)
 
     blocks = current.reshape(freqs, forms, order_len)
+    expand = block_rows(order_len, freqs)
+    forms_expand = form_rows(order_len, forms)
     packs = []
     mixes = []
     for r in range(2):
         send_order, recv_slots = crossing_plan(cross_tables[r], freq_perm[r], momentum, freqs)
         packs.append(jnp.take(blocks, send_order, axis=0))
-        mixes.append(mix_matrix(recv_slots, form_mix[r], freqs))
+        mixes.append(mix_matrix(recv_slots, form_mix[r], freqs, expand, forms_expand))
     stacked = jnp.stack(packs)
     mix = jnp.concatenate(mixes, axis=1)
 
+    bubble_tall = bubble_mat.reshape(order_len, forms)
+    block_mask = exact_dot(expand, expand.T)
+    bubble_full = exact_dot(bubble_tall, forms_expand.T) * block_mask
+
     def carry_of(mat):
-        carried = jnp.einsum(
-            "fln,fnb->flb",
-            bubble_mat,
-            mat.reshape(freqs, forms, order_len),
-            preferred_element_type=jnp.float32,
-        )
-        return carried.reshape(order_len, order_len).astype(jnp.bfloat16)
+        return exact_dot(bubble_full, mat)
 
     carried = carry_of(current)
     bare_part = jnp.dot(bare_mat, carried, preferred_element_type=jnp.float32)

time: 188 us -> 142 us (0.76)
  local copies, waits for them, and re-layouts: 78.2 us -> 22 us
  waiting for transfers between devices: 36.3 us -> 55.6 us
  matrix products: 18.8 us -> 34.8 us
  starting transfers between devices: 34.1 us -> 19.1 us
  other arithmetic: 17.8 us -> 7.99 us
    mul x3 -> x0, local copies, waits for them, and re-layouts: 48.5 us -> none  [mix_matrix(): full = onehot[:, None, :, None] * mixing[None, :, None, :]]
    dot_general x2 -> x8, matrix products: 2.03 us -> 21.2 us  [exact_dot(): jnp.dot(a, b, preferred_element_type=jnp.float32).astype(jnp.bfloat16)]
    all_to_all x3 -> x2, waiting for transfers between devices: 0.01 us -> 15.3 us  [local(): lax.all_to_all(stacked[..., cols], 'mom', split_axis=1, concat_axis=1, ti...]
    all_to_all x3 -> x2, starting transfers between devices: 28.3 us -> 15.8 us  [local(): lax.all_to_all(stacked[..., cols], 'mom', split_axis=1, concat_axis=1, ti...]
    mul x2 -> x0, other arithmetic: 11.4 us -> none  [mix_matrix(): full = onehot[:, None, :, None] * mixing[None, :, None, :]]
    ppermute x3 -> x2, waiting for transfers between devices: 36.3 us -> 40.3 us  [partner_2(): return lax.ppermute(value, axis, pairs)]
    dot_general x3 -> x2, matrix products: 8.19 us -> 4.86 us  [local(): jnp.dot(mix, received.reshape(2 * order_len, width), preferred_element_ty...]
    convert_element_type x3 -> x0, local copies, waits for them, and re-layouts: 2.92 us -> none  [the longest x2 1.47 us: carry_of(): return carried.reshape(order_len, order_len).astype(jnp.bfloat16)]
  transfers between devices with their start and end apart: 6 -> 4, of which waited for: 3 -> 4; matrix products, arithmetic and copies ran while one was open for 48% -> 24% of each run, Pallas kernels for 0% -> 0%
where the time goes in v2:
time: 142 us; the launch traced here: 141 us
  waiting for transfers between devices  55.6 us (39%)
  matrix products  34.8 us (25%)
  local copies, waits for them, and re-layouts  22 us (15%)
  starting transfers between devices  19.1 us (13%)
  other arithmetic  7.99 us (6%)
  between operations  1.63 us (1%)
    ppermute x2, waiting for transfers between devices, partner_2(): return lax.ppermute(value, axis, pairs)  40.3 us
    dot_general x8, matrix products, exact_dot(): jnp.dot(a, b, preferred_element_type=jnp.float32).astype(jnp.bfloat16)  21.2 us
    all_to_all x2, starting transfers between devices, local(): lax.all_to_all(stacked[..., cols], 'mom', split_axis=1, concat_axis=1, ti...  15.8 us
    all_to_all x2, waiting for transfers between devices, local(): lax.all_to_all(stacked[..., cols], 'mom', split_axis=1, concat_axis=1, ti...  15.3 us
    dot_general x2, matrix products, local(): jnp.dot(mix, received.reshape(2 * order_len, width), preferred_element_ty...  4.86 us
    slice x2, local copies, waits for them, and re-layouts, local(): stacked[..., cols]  4.46 us
    convert_element_type x2, other arithmetic, local(): (coef_self * summed.astype(jnp.float32) + coef_pair * other.astype(jnp.fl...  3.55 us
    ppermute x2, starting transfers between devices, partner_2(): return lax.ppermute(value, axis, pairs)  3.32 us
  transfers between devices with their start and end apart: 4, of which 4 were waited for; matrix products, arithmetic and copies ran while one was open for 24% of the time, Pallas kernels for 0%

profile of v2, /device:TPU:1, one launch (start us, length us, event | category | flops | bytes accessed | tf_op | source)
XLA Modules:
  0.0 141.1 jit_solution(2454567124618929003)
XLA Ops:
  0.0 0.8 slice_bitcast_fusion
  0.8 0.1 select_reduce_fusion
  0.9 0.1 select_reduce_fusion.1
  1.1 2.2 %reshape_squeeze.6 = bf16[64,12,768]{2,1,0:T(8,128)(2,1)S(1)} reshape(bf16[1,1,768,768]{3,2,1,0:T(8,128)(2,1)} %param.14) | data formatting | bytes 2359296 | tf_op jit(solution)/shard_map/reshape;squeeze | solution.py:72
  3.3 1.8 %gather_fusion.3 = bf16[64,12,768]{2,1,0:T(8,128)(2,1)} fusion(bf16[64,12,768]{2,1,0:T(8,128)(2,1)S(1)} %reshape_squeeze.6, s32[1024]{0:T(1024)S(1)} %pad_clamp_fusion), kind=kCustom, calls=%fused_computation.3.clone | custom fusion | bytes 2359552 | tf_op jit(solution)/shard_map/jit(_take)/gather | solution.py:79
  5.1 0.6 gather_fusion.2
  5.7 1.6 %select_bitcast_fusion = bf16[1,64,12,768]{3,2,1,0:T(8,128)(2,1)S(1)} fusion(bf16[64,12,768]{2,1,0:T(8,128)(2,1)} %gather_fusion.3, pred[64]{0:T(512)(128)(4,1)S(1)} %get-tuple-element.75), kind=kLoop, calls=%fused_computation.17 | loop fusion | flops 589824 | bytes 2359360 | tf_op jit(solution)/shard_map/stack | solution.py:81
  7.4 0.2 select_bitcast_fusion.1
  7.6 0.4 pad_maximum_fusion.1
  8.0 2.2 %copy.25 = bf16[2,64,12,384]{3,0,2,1:T(2,128)(2,1)} copy(bf16[2,64,12,384]{3,2,1,0:T(8,128)(2,1)S(1)} %get-tuple-element.61) | data formatting | bytes 2359296 | tf_op jit(solution)/shard_map/slice | solution.py:98
  10.3 10.3 %all-to-all-start.1 = ((bf16[2,64,12,384]{3,0,2,1:T(2,128)(2,1)}), bf16[2,64,12,384]{3,0,2,1:T(2,128)(2,1)S(1)}, u32[]{:S(2)}, u32[]{:S(2)}) async-start(bf16[2,64,12,384]{3,0,2,1:T(2,128)(2,1)} %copy.25), calls=%async_computation.1 | async-start | bytes 2359296 | tf_op jit(solution)/shard_map/all_to_all | solution.py:98
  20.6 0.0 copy-start.14
  20.6 0.0 copy-start.8
  20.6 2.2 %copy.23 = bf16[2,64,12,384]{3,0,2,1:T(2,128)(2,1)} copy(bf16[2,64,12,384]{3,2,1,0:T(8,128)(2,1)S(1)} %get-tuple-element.62) | data formatting | bytes 2359296 | tf_op jit(solution)/shard_map/slice | solution.py:98
  22.9 0.0 copy-done.14
  22.9 0.1 select_reduce_fusion.2
  23.0 0.1 select_reduce_fusion.4
  23.1 0.0 copy-done.8
  23.2 0.8 gather_fusion.1
  23.9 0.8 gather_fusion
  24.8 0.5 and_select_fusion
  25.3 0.5 and_select_fusion.1
  25.8 14.5 %all-to-all-done.1 = bf16[2,64,12,384]{3,0,2,1:T(2,128)(2,1)S(1)} async-done(((bf16[2,64,12,384]{3,0,2,1:T(2,128)(2,1)}), bf16[2,64,12,384]{3,0,2,1:T(2,128)(2,1)S(1)}, u32[]{:S(2)}, u32[]{:S(2)}) %all-to-all-start.1) | async-done | bytes 1179680 | tf_op jit(solution)/shard_map/all_to_all | solution.py:98
  40.3 5.5 %all-to-all-start = ((bf16[2,64,12,384]{3,0,2,1:T(2,128)(2,1)}), bf16[2,64,12,384]{3,0,2,1:T(2,128)(2,1)}, u32[]{:S(2)}, u32[]{:S(2)}) async-start(bf16[2,64,12,384]{3,0,2,1:T(2,128)(2,1)} %copy.23), calls=%async_computation | async-start | bytes 2359296 | tf_op jit(solution)/shard_map/all_to_all | solution.py:98
  45.8 0.6 fusion.62
  46.4 0.0 copy-done.9
  46.4 0.2 copy.27
  46.6 0.9 reshape_squeeze.7
  47.4 0.0 copy-done.13
  47.4 0.6 fusion.70
  48.0 0.0 copy-done.12
  48.0 1.0 convolution_convert_fusion.6
  49.1 1.8 %convolution_convert_fusion.7 = bf16[768,768]{0,1:T(8,128)(2,1)S(1)} fusion(s32[768]{0:T(1024)S(1)} %get-tuple-element.69, s32[768]{0:T(1024)S(1)} %get-tuple-element.70, pred[768]{0:T(1024)(128)(4,1)} %copy-done.12, bf16[1,12,12]{2,0,1:T(2,128)(2,1)} %get-tuple-element.65), kind=kOutput, calls=%fused_computation.26 | convolution fusion | flops 15012864 | bytes 1186848 | tf_op jit(solution)/shard_map/dot_general | solution.py:48
  50.8 0.0 copy-start.10
  50.9 2.1 %fusion.8 = bf16[768,768]{0,1:T(8,128)(2,1)S(1)} fusion(bf16[768,12]{0,1:T(8,128)(2,1)} %reshape_squeeze.7, s32[768]{0:T(1024)S(1)} %get-tuple-element.69, s32[768]{0:T(1024)S(1)} %get-tuple-element.70, pred[768]{0:T(1024)(128)(4,1)} %copy-done.12), kind=kOutput, calls=%fused_computation.29 | convolution fusion | flops 14764032 | bytes 1204992 | tf_op jit(solution)/shard_map/dot_general | solution.py:48
  53.0 2.0 %fusion.11 = bf16[768,768]{0,1:T(8,128)(2,1)} fusion(bf16[768,768]{0,1:T(8,128)(2,1)S(1)} %fusion.8, s32[768]{0:T(1024)S(1)} %iota_divide_fusion, s32[768]{0:T(1024)S(1)} %broadcast_add_fusion, pred[768]{0:T(1024)(128)(4,1)S(1)} %copy-done.10), kind=kOutput, calls=%fused_computation.32 | convolution fusion | flops 76775424 | bytes 2366208 | tf_op jit(solution)/shard_map/dot_general | solution.py:48
  55.0 2.7 %fusion.10 = bf16[768,768]{0,1:T(8,128)(2,1)} fusion(bf16[768,768]{0,1:T(8,128)(2,1)S(1)} %convolution_convert_fusion.6, s32[768]{0:T(1024)S(1)} %iota_divide_fusion, s32[768]{0:T(1024)S(1)} %broadcast_add_fusion, pred[768]{0:T(1024)(128)(4,1)S(1)} %copy-done.11, s32[64]{0:T(128)} %and_select_fusion), kind=kOutput, calls=%fused_computation.31 | convolution fusion | flops 84987904 | bytes 2366464 | tf_op jit(solution)/shard_map/dot_general | solution.py:48
  57.7 2.1 %fusion.9 = bf16[768,768]{0,1:T(8,128)(2,1)} fusion(bf16[768,768]{0,1:T(8,128)(2,1)S(1)} %convolution_convert_fusion.7, s32[768]{0:T(1024)S(1)} %iota_divide_fusion, s32[768]{0:T(1024)S(1)} %broadcast_add_fusion, pred[768]{0:T(1024)(128)(4,1)S(1)} %copy-done.11, s32[64]{0:T(128)S(1)} %copy-done.15), kind=kOutput, calls=%fused_computation.30 | convolution fusion | flops 84987904 | bytes 2366464 | tf_op jit(solution)/shard_map/dot_general | solution.py:48
  59.8 3.4 %convolution_convert_fusion.1 = bf16[768,768]{1,0:T(8,128)(2,1)} fusion(bf16[768,768]{0,1:T(8,128)(2,1)S(1)} %copy-done.1, bf16[1,1,768,768]{3,2,1,0:T(8,128)(2,1)} %param.14), kind=kOutput, calls=%fused_computation.20 | convolution fusion | flops 906559488 | bytes 3538944 | tf_op jit(solution)/shard_map/dot_general | solution.py:48
  63.3 0.2 copy.26
  63.5 1.2 reshape.23
  64.7 0.8 all-to-all-done
  65.5 1.5 %copy.24 = bf16[2,64,12,384]{3,2,1,0:T(8,128)(2,1)S(1)} copy(bf16[2,64,12,384]{3,0,2,1:T(2,128)(2,1)} %all-to-all-done) | data formatting | bytes 2359296 | tf_op jit(solution)/shard_map/all_to_all | solution.py:98
  67.0 1.2 reshape.22
  68.2 0.5 copy-done.3
  68.7 3.7 %fusion.13 = bf16[768,384]{0,1:T(8,128)(2,1)} fusion(bf16[1536,384]{1,0:T(8,128)(2,1)} %reshape.22, bf16[768,768]{0,1:T(8,128)(2,1)S(1)} %copy-done.3, bf16[768,768]{0,1:T(8,128)(2,1)} %fusion.9), kind=kOutput, calls=%fused_computation.34 | convolution fusion | flops 910983168 | bytes 4128768 | tf_op jit(solution)/shard_map/dot_general | solution.py:99
  72.4 3.0 %collective-permute-start = (bf16[768,384]{0,1:T(8,128)(2,1)}, bf16[768,384]{0,1:T(8,128)(2,1)}, u32[]{:S(2)}, u32[]{:S(2)}) collective-permute-start(bf16[768,384]{0,1:T(8,128)(2,1)} %fusion.13), channel_id=1, source_target_pairs={{0,1},{1,0},{2,3},{3,2},{4,5},{5,4},{6,7},{7,6},{8,9},{9,8},{10,11... | collective-permute-start | bytes 1769480 | tf_op jit(solution)/shard_map/ppermute | solution.py:16
  75.4 0.0 copy-done.4
  75.4 1.2 fusion.14
  76.6 0.3 collective-permute-start.1
  76.9 0.0 copy-done.7
  76.9 2.5 %fusion.17 = f32[768,768]{1,0:T(8,128)} fusion(bf16[768,768]{1,0:T(8,128)(2,1)S(1)} %copy-done.7, bf16[1,1,768,768]{3,2,1,0:T(8,128)(2,1)S(1)} %copy-done), kind=kOutput, calls=%fused_computation.39 | convolution fusion | flops 905969664 | bytes 4718592 | tf_op jit(solution)/shard_map/dot_general | solution.py:92
  79.4 1.5 %copy.20 = bf16[1,1,768,768]{2,3,1,0:T(8,128)(2,1)} copy(bf16[1,1,768,768]{3,2,1,0:T(8,128)(2,1)S(1)} %copy-done) | data formatting | bytes 2359296 | tf_op args[1]
  80.9 0.6 dynamic-slice.14
  81.5 0.6 dynamic-slice.13
  83.5 31.0 %collective-permute-done = bf16[768,384]{0,1:T(8,128)(2,1)} collective-permute-done((bf16[768,384]{0,1:T(8,128)(2,1)}, bf16[768,384]{0,1:T(8,128)(2,1)}, u32[]{:S(2)}, u32[]{:S(2)}) %collective-permute-start) | collective-permute-done | bytes 589856 | tf_op jit(solution)/shard_map/ppermute | solution.py:16
  114.5 1.5 %add_convert_fusion.1 = bf16[768,384]{0,1:T(8,128)(2,1)S(1)} fusion(bf16[768,384]{0,1:T(8,128)(2,1)} %collective-permute-done, bf16[768,384]{0,1:T(8,128)(2,1)} %fusion.13, f32[]{:T(128)} %bitcast.13, f32[]{:T(128)} %bitcast.2), kind=kLoop, calls=%fused_computation.43 | loop fusion | flops 1769472 | bytes 1769480 | tf_op jit(solution)/shard_map/convert_element_type | solution.py:104
  116.0 1.9 %fusion.22 = f32[768,768]{0,1:T(8,128)S(1)} fusion(bf16[768,384]{0,1:T(8,128)(2,1)S(1)} %add_convert_fusion.1, bf16[768,768]{1,0:T(8,128)(2,1)} %convolution_convert_fusion.1), kind=kOutput, calls=%fused_computation.49 | convolution fusion | flops 452984832 | bytes 3538944 | tf_op jit(solution)/shard_map/dot_general | solution.py:114
  117.9 9.3 %collective-permute-done.1 = bf16[768,384]{0,1:T(8,128)(2,1)} collective-permute-done((bf16[768,384]{0,1:T(8,128)(2,1)S(1)}, bf16[768,384]{0,1:T(8,128)(2,1)}, u32[]{:S(2)}, u32[]{:S(2)}) %collective-permute-start.1) | collective-permute-done | bytes 589856 | tf_op jit(solution)/shard_map/ppermute | solution.py:16
  127.1 2.1 %add_convert_fusion = bf16[768,384]{0,1:T(8,128)(2,1)} fusion(bf16[768,384]{0,1:T(8,128)(2,1)} %collective-permute-done.1, bf16[768,384]{0,1:T(8,128)(2,1)S(1)} %fusion.14, f32[]{:T(128)} %bitcast.13, f32[]{:T(128)} %bitcast.2), kind=kLoop, calls=%fused_computation.42 | loop fusion | flops 1769472 | bytes 1769480 | tf_op jit(solution)/shard_map/convert_element_type | solution.py:104
  129.2 6.1 %convolution_convert_fusion = bf16[768,768]{1,0:T(8,128)(2,1)} fusion(bf16[768,768]{0,1:T(8,128)(2,1)} %fusion.11, f32[768,768]{0,1:T(8,128)S(1)} %fusion.22, f32[768,768]{1,0:T(8,128)} %fusion.17, bf16[768,384]{0,1:T(8,128)(2,1)} %add_convert_fusion, bf16[1,1,768,768]{2,3,1,0:T(8,128)(2,1)} %copy.20, bf16[768,384]{0,1:T(8,128)(2,1)S(1)} %add_convert_fusion.1, ...), kind=kOutput, calls=%fused_computation.19 | convolution fusion | flops 1365442560 | bytes 10616832 | tf_op jit(solution)/shard_map/dot_general | solution.py:48
  135.3 2.9 %fusion.15 = f32[768,768]{1,0:T(8,128)S(1)} fusion(bf16[768,768]{1,0:T(8,128)(2,1)} %convolution_convert_fusion, bf16[1,1,768,768]{3,2,1,0:T(8,128)(2,1)} %param.15), kind=kOutput, calls=%fused_computation.37 | convolution fusion | flops 905969664 | bytes 4718592 | tf_op jit(solution)/shard_map/dot_general | solution.py:118
  138.2 1.4 fusion.12
  139.7 1.5 %copy.32 = bf16[1,1,768,768]{3,2,1,0:T(8,128)(2,1)} copy(bf16[1,1,768,768]{2,3,1,0:T(8,128)(2,1)S(1)} %fusion.12) | data formatting | bytes 2359296 | tf_op jit(solution)/shard_map/broadcast_in_dim | solution.py:121
  (42 shorter events, 0.2 us)
Async XLA Ops:
  10.3 30.0 %all-to-all-start.1 = ((bf16[2,64,12,384]{3,0,2,1:T(2,128)(2,1)}), bf16[2,64,12,384]{3,0,2,1:T(2,128)(2,1)S(1)}, u32[]{:S(2)}, u32[]{:S(2)}) async-start(bf16[2,64,12,384]{3,0,2,1:T(2,128)(2,1)} %copy.25), calls=%async_computation.1 | async-start | bytes 2359296 | tf_op jit(solution)/shard_map/all_to_all | solution.py:98
  20.6 2.3 %copy-start.14 = (s32[2,64]{1,0:T(2,128)S(1)}, s32[2,64]{1,0:T(2,128)}, u32[]{:S(2)}) copy-start(s32[2,64]{1,0:T(2,128)} %param.19) | copy-start | bytes 1540
  20.6 2.5 %copy-start.8 = (s32[2,64,64]{2,1,0:T(8,128)S(1)}, s32[2,64,64]{2,1,0:T(8,128)}, u32[]{:S(2)}) copy-start(s32[2,64,64]{2,1,0:T(8,128)} %param.18) | copy-start | bytes 98308
  24.7 23.3 %copy-start.12 = (pred[768]{0:T(1024)(128)(4,1)}, pred[768]{0:T(1024)(128)(4,1)S(1)}, u32[]{:S(2)}) copy-start(pred[768]{0:T(1024)(128)(4,1)S(1)} %fusion.61) | copy-start | bytes 2308
  25.8 20.6 %copy-start.9 = (bf16[1,1,64,12,12]{2,4,3,1,0:T(8,128)(2,1)S(1)}, bf16[1,1,64,12,12]{2,4,3,1,0:T(8,128)(2,1)}, u32[]{:S(2)}) copy-start(bf16[1,1,64,12,12]{2,4,3,1,0:T(8,128)(2,1)} %param.16) | copy-start | bytes 55300
  25.8 21.7 %copy-start.13 = (bf16[2,12,12]{2,0,1:T(2,128)(2,1)S(1)}, bf16[2,12,12]{2,0,1:T(2,128)(2,1)}, u32[]{:S(2)}) copy-start(bf16[2,12,12]{2,0,1:T(2,128)(2,1)} %param.17) | copy-start | bytes 1732
  40.3 25.2 %all-to-all-start = ((bf16[2,64,12,384]{3,0,2,1:T(2,128)(2,1)}), bf16[2,64,12,384]{3,0,2,1:T(2,128)(2,1)}, u32[]{:S(2)}, u32[]{:S(2)}) async-start(bf16[2,64,12,384]{3,0,2,1:T(2,128)(2,1)} %copy.23), calls=%async_computation | async-start | bytes 2359296 | tf_op jit(solution)/shard_map/all_to_all | solution.py:98
  50.8 2.1 %copy-start.10 = (pred[768]{0:T(1024)(128)(4,1)S(1)}, pred[768]{0:T(1024)(128)(4,1)}, u32[]{:S(2)}) copy-start(pred[768]{0:T(1024)(128)(4,1)} %fusion.62) | copy-start | bytes 2308
  53.0 2.0 %copy-start.11 = (pred[768]{0:T(1024)(128)(4,1)S(1)}, pred[768]{0:T(1024)(128)(4,1)}, u32[]{:S(2)}) copy-start(pred[768]{0:T(1024)(128)(4,1)} %fusion.62) | copy-start | bytes 2308
  55.0 2.7 %copy-start.15 = (s32[64]{0:T(128)S(1)}, s32[64]{0:T(128)}, u32[]{:S(2)}) copy-start(s32[64]{0:T(128)} %and_select_fusion.1) | copy-start | bytes 772
  57.7 2.1 %copy-start.1 = (bf16[768,768]{0,1:T(8,128)(2,1)S(1)}, bf16[768,768]{0,1:T(8,128)(2,1)}, u32[]{:S(2)}) copy-start(bf16[768,768]{0,1:T(8,128)(2,1)} %fusion.11) | copy-start | bytes 3538948
  67.0 1.7 %copy-start.3 = (bf16[768,768]{0,1:T(8,128)(2,1)S(1)}, bf16[768,768]{0,1:T(8,128)(2,1)}, u32[]{:S(2)}) copy-start(bf16[768,768]{0,1:T(8,128)(2,1)} %fusion.10) | copy-start | bytes 3538948
  68.7 6.7 %copy-start.4 = (bf16[768,768]{0,1:T(8,128)(2,1)S(1)}, bf16[768,768]{0,1:T(8,128)(2,1)}, u32[]{:S(2)}) copy-start(bf16[768,768]{0,1:T(8,128)(2,1)} %fusion.9) | copy-start | bytes 3538948
  68.7 6.7 %copy-start.5 = (bf16[1536,384]{1,0:T(8,128)(2,1)S(1)}, bf16[1536,384]{1,0:T(8,128)(2,1)}, u32[]{:S(2)}) copy-start(bf16[1536,384]{1,0:T(8,128)(2,1)} %reshape.23) | copy-start | bytes 3538948
  72.4 4.5 %copy-start = (bf16[1,1,768,768]{3,2,1,0:T(8,128)(2,1)S(1)}, bf16[1,1,768,768]{3,2,1,0:T(8,128)(2,1)}, u32[]{:S(2)}) copy-start(bf16[1,1,768,768]{3,2,1,0:T(8,128)(2,1)} %param.15) | copy-start | bytes 3538948
  72.4 4.5 %copy-start.7 = (bf16[768,768]{1,0:T(8,128)(2,1)S(1)}, bf16[768,768]{1,0:T(8,128)(2,1)}, u32[]{:S(2)}) copy-start(bf16[768,768]{1,0:T(8,128)(2,1)} %convolution_convert_fusion.1) | copy-start | bytes 3538948
  72.4 42.1 %collective-permute-start = (bf16[768,384]{0,1:T(8,128)(2,1)}, bf16[768,384]{0,1:T(8,128)(2,1)}, u32[]{:S(2)}, u32[]{:S(2)}) collective-permute-start(bf16[768,384]{0,1:T(8,128)(2,1)} %fusion.13), channel_id=1, source_target_pairs={{0,1},{1,0},{2,3},{3,2},{4,5},{5,4},{6,7},{7,6},{8,9},{9,8},{10,11... | collective-permute-start | bytes 1769480 | tf_op jit(solution)/shard_map/ppermute | solution.py:16
  76.6 50.6 %collective-permute-start.1 = (bf16[768,384]{0,1:T(8,128)(2,1)S(1)}, bf16[768,384]{0,1:T(8,128)(2,1)}, u32[]{:S(2)}, u32[]{:S(2)}) collective-permute-start(bf16[768,384]{0,1:T(8,128)(2,1)S(1)} %fusion.14), channel_id=1, source_target_pairs={{0,1},{1,0},{2,3},{3,2},{4,5},{5,4},{6,7},{7,6},{8,9},{9,8},{10,11... | collective-permute-start | bytes 1769480 | tf_op jit(solution)/shard_map/ppermute | solution.py:16
  79.4 1.5 %copy-start.17 = (f32[4]{0:T(128)S(1)}, f32[4]{0:T(128)}, u32[]{:S(2)}) copy-start(f32[4]{0:T(128)} %constant.88.clone..sunk.2) | copy-start | bytes 52
  79.4 2.1 %copy-start.16 = (f32[4]{0:T(128)S(1)}, f32[4]{0:T(128)}, u32[]{:S(2)}) copy-start(f32[4]{0:T(128)} %constant.87.clone..sunk.2) | copy-start | bytes 52
  135.3 2.9 %copy-start.2 = (bf16[1,1,768,768]{2,3,1,0:T(8,128)(2,1)S(1)}, bf16[1,1,768,768]{2,3,1,0:T(8,128)(2,1)}, u32[]{:S(2)}) copy-start(bf16[1,1,768,768]{2,3,1,0:T(8,128)(2,1)} %copy.20) | copy-start | bytes 3538948
  135.3 2.9 %copy-start.6 = (bf16[768,384]{0,1:T(8,128)(2,1)S(1)}, bf16[768,384]{0,1:T(8,128)(2,1)}, u32[]{:S(2)}) copy-start(bf16[768,384]{0,1:T(8,128)(2,1)} %add_convert_fusion) | copy-start | bytes 1769476
  135.3 2.9 %copy-start.18 = (bf16[768,768]{1,0:T(8,128)(2,1)S(1)}, bf16[768,768]{1,0:T(8,128)(2,1)}, u32[]{:S(2)}) copy-start(bf16[768,768]{1,0:T(8,128)(2,1)} %convolution_convert_fusion) | copy-start | bytes 3538948

commit v3 on v2

--- a/solution.py
+++ b/solution.py
@@ -93,12 +93,14 @@
 
     width = order_len // NCHUNK
     red_chunks = []
+    pieces = [stacked[..., k * width:(k + 1) * width] for k in range(NCHUNK)]
     for k in range(NCHUNK):
-        cols = slice(k * width, (k + 1) * width)
-        received = lax.all_to_all(stacked[..., cols], "mom", split_axis=1, concat_axis=1, tiled=True)
+        received = lax.all_to_all(pieces[k], "mom", split_axis=1, concat_axis=1, tiled=True)
         summed = jnp.dot(
             mix, received.reshape(2 * order_len, width), preferred_element_type=jnp.float32
         ).astype(jnp.bfloat16)
+        if k + 1 < NCHUNK:
+            summed, pieces[k + 1] = lax.optimization_barrier((summed, pieces[k + 1]))
         other = partner_2(summed, "spin", 0)
         red_chunks.append(
             (coef_self * summed.astype(jnp.float32) + coef_pair * other.astype(jnp.float32)).astype(

time: 142 us -> 125 us (0.88)
  waiting for transfers between devices: 55.6 us -> 46.1 us
  local copies, waits for them, and re-layouts: 22 us -> 17.9 us
  other arithmetic: 7.99 us -> 5.6 us
    ppermute x2, waiting for transfers between devices: 40.3 us -> 16.9 us  [partner_2(): return lax.ppermute(value, axis, pairs)]
    all_to_all x2, waiting for transfers between devices: 15.3 us -> 29.3 us  [local(): lax.all_to_all(pieces[k], 'mom', split_axis=1, concat_axis=1, tiled=True)]
    dot_general x8, matrix products: 21.2 us -> 18.2 us  [exact_dot(): jnp.dot(a, b, preferred_element_type=jnp.float32).astype(jnp.bfloat16)]
    dot_general x2, matrix products: 4.86 us -> 7.43 us  [local(): jnp.dot(mix, received.reshape(2 * order_len, width), preferred_element_ty...]
    slice x2 -> x1, local copies, waits for them, and re-layouts: 4.46 us -> 2.23 us  [local(): pieces = [stacked[..., k * width:(k + 1) * width] for k in range(NCHUNK)]]
    optimization_barrier x0 -> x1, local copies, waits for them, and re-layouts: none -> 2.24 us  [local(): summed, pieces[k + 1] = lax.optimization_barrier((summed, pieces[k + 1]))]
    broadcast_in_dim x1 -> x0, local copies, waits for them, and re-layouts: 1.45 us -> none  [local(): return current[None, None]]
  transfers between devices with their start and end apart: 4 -> 4, of which waited for: 4 -> 4; matrix products, arithmetic and copies ran while one was open for 24% -> 22% of each run, Pallas kernels for 0% -> 0%
where the time goes in v3:
time: 125 us; the launch traced here: 124 us
  waiting for transfers between devices  46.1 us (37%)
  matrix products  34.7 us (28%)
  starting transfers between devices  18.5 us (15%)
  local copies, waits for them, and re-layouts  17.9 us (14%)
  other arithmetic  5.6 us (4%)
  between operations  1.49 us (1%)
    all_to_all x2, waiting for transfers between devices, local(): lax.all_to_all(pieces[k], 'mom', split_axis=1, concat_axis=1, tiled=True)  29.3 us
    dot_general x8, matrix products, exact_dot(): jnp.dot(a, b, preferred_element_type=jnp.float32).astype(jnp.bfloat16)  18.2 us
    ppermute x2, waiting for transfers between devices, partner_2(): return lax.ppermute(value, axis, pairs)  16.9 us
    all_to_all x2, starting transfers between devices, local(): lax.all_to_all(pieces[k], 'mom', split_axis=1, concat_axis=1, tiled=True)  15.5 us
    dot_general x2, matrix products, local(): jnp.dot(mix, received.reshape(2 * order_len, width), preferred_element_ty...  7.43 us
    ppermute x2, starting transfers between devices, partner_2(): return lax.ppermute(value, axis, pairs)  2.99 us
    convert_element_type x2, other arithmetic, local(): (coef_self * summed.astype(jnp.float32) + coef_pair * other.astype(jnp.fl...  2.76 us
    dot_general x1, matrix products, local(): jnp.dot(reducible, carried, preferred_element_type=jnp.float32)  2.5 us
  transfers between devices with their start and end apart: 4, of which 4 were waited for; matrix products, arithmetic and copies ran while one was open for 22% of the time, Pallas kernels for 0%

profile of v3, /device:TPU:1, one launch (start us, length us, event | category | flops | bytes accessed | tf_op | source)
XLA Modules:
  0.0 124.3 jit_solution(14904410584247705741)
XLA Ops:
  0.0 0.8 slice_bitcast_fusion
  0.8 0.1 select_reduce_fusion
  0.9 0.1 select_reduce_fusion.1
  1.1 2.2 %reshape_squeeze.6 = bf16[64,12,768]{2,1,0:T(8,128)(2,1)S(1)} reshape(bf16[1,1,768,768]{3,2,1,0:T(8,128)(2,1)} %param.14) | data formatting | bytes 2359296 | tf_op jit(solution)/shard_map/reshape;squeeze | solution.py:72
  3.3 1.8 %gather_fusion.3 = bf16[64,12,768]{2,1,0:T(8,128)(2,1)} fusion(bf16[64,12,768]{2,1,0:T(8,128)(2,1)S(1)} %reshape_squeeze.6, s32[1024]{0:T(1024)S(1)} %pad_clamp_fusion), kind=kCustom, calls=%fused_computation.3.clone | custom fusion | bytes 2359552 | tf_op jit(solution)/shard_map/jit(_take)/gather | solution.py:79
  5.1 0.6 gather_fusion.2
  5.7 1.6 %select_bitcast_fusion = bf16[1,64,12,768]{3,2,1,0:T(8,128)(2,1)S(1)} fusion(bf16[64,12,768]{2,1,0:T(8,128)(2,1)} %gather_fusion.3, pred[64]{0:T(512)(128)(4,1)S(1)} %get-tuple-element.81), kind=kLoop, calls=%fused_computation.17 | loop fusion | flops 589824 | bytes 2359360 | tf_op jit(solution)/shard_map/stack | solution.py:81
  7.3 0.2 select_bitcast_fusion.1
  7.6 0.4 pad_maximum_fusion.1
  8.0 2.2 %copy.20 = bf16[2,64,12,384]{3,0,2,1:T(2,128)(2,1)} copy(bf16[2,64,12,384]{3,2,1,0:T(8,128)(2,1)S(1)} %get-tuple-element.66) | data formatting | bytes 2359296 | tf_op jit(solution)/shard_map/slice | solution.py:96
  10.2 0.0 copy-start.4
  10.2 0.0 copy-start.7
  10.2 10.6 %all-to-all-start = ((bf16[2,64,12,384]{3,0,2,1:T(2,128)(2,1)}), bf16[2,64,12,384]{3,0,2,1:T(2,128)(2,1)}, u32[]{:S(2)}, u32[]{:S(2)}) async-start(bf16[2,64,12,384]{3,0,2,1:T(2,128)(2,1)} %copy.20), calls=%async_computation | async-start | bytes 2359296 | tf_op jit(solution)/shard_map/all_to_all | solution.py:98
  20.9 0.0 copy-done.4
  20.9 0.0 copy-done.7
  20.9 0.1 select_reduce_fusion.2
  21.0 0.1 select_reduce_fusion.4
  21.2 0.8 gather_fusion.1
  22.0 0.8 gather_fusion
  22.8 0.0 copy-done.6
  22.8 1.0 convolution_convert_fusion.6
  23.9 2.1 %convolution_convert_fusion.7 = bf16[768,768]{0,1:T(8,128)(2,1)} fusion(s32[768]{0:T(1024)S(1)} %get-tuple-element.73, s32[768]{0:T(1024)S(1)} %get-tuple-element.74, pred[768]{0:T(1024)(128)(4,1)S(1)} %fusion.61, bf16[1,12,12]{2,0,1:T(2,128)(2,1)S(1)} %get-tuple-element.69), kind=kOutput, calls=%fused_computation.26 | convolution fusion | flops 15012864 | bytes 1186848 | tf_op jit(solution)/shard_map/dot_general | solution.py:48
  25.9 2.1 %fusion.10 = bf16[768,768]{0,1:T(8,128)(2,1)} fusion(bf16[768,768]{0,1:T(8,128)(2,1)S(1)} %convolution_convert_fusion.6, s32[768]{0:T(1024)S(1)} %get-tuple-element.75, s32[768]{0:T(1024)S(1)} %get-tuple-element.76, pred[768]{0:T(1024)(128)(4,1)S(1)} %fusion.62, s32[64]{0:T(128)S(1)} %and_select_fusion), kind=kOutput, calls=%fused_computation.31 | convolution fusion | flops 84987904 | bytes 2366464 | tf_op jit(solution)/shard_map/dot_general | solution.py:48
  28.0 3.4 %fusion.9 = bf16[768,768]{0,1:T(8,128)(2,1)} fusion(bf16[768,768]{0,1:T(8,128)(2,1)} %convolution_convert_fusion.7, s32[768]{0:T(1024)S(1)} %get-tuple-element.75, s32[768]{0:T(1024)S(1)} %get-tuple-element.76, pred[768]{0:T(1024)(128)(4,1)S(1)} %fusion.62, s32[64]{0:T(128)S(1)} %and_select_fusion.1), kind=kOutput, calls=%fused_computation.30 | convolution fusion | flops 84987904 | bytes 2366464 | tf_op jit(solution)/shard_map/dot_general | solution.py:48
  31.4 9.1 %all-to-all-done = bf16[2,64,12,384]{3,0,2,1:T(2,128)(2,1)} async-done(((bf16[2,64,12,384]{3,0,2,1:T(2,128)(2,1)}), bf16[2,64,12,384]{3,0,2,1:T(2,128)(2,1)}, u32[]{:S(2)}, u32[]{:S(2)}) %all-to-all-start) | async-done | bytes 1179680 | tf_op jit(solution)/shard_map/all_to_all | solution.py:98
  40.5 1.5 %copy.21 = bf16[2,64,12,384]{3,2,1,0:T(8,128)(2,1)S(1)} copy(bf16[2,64,12,384]{3,0,2,1:T(2,128)(2,1)} %all-to-all-done) | data formatting | bytes 2359296 | tf_op jit(solution)/shard_map/all_to_all | solution.py:98
  42.0 1.2 reshape.22
  43.2 3.4 %fusion.13 = bf16[768,384]{1,0:T(8,128)(2,1)S(1)} fusion(bf16[1536,384]{1,0:T(8,128)(2,1)} %reshape.22, bf16[768,768]{0,1:T(8,128)(2,1)} %fusion.10, bf16[768,768]{0,1:T(8,128)(2,1)} %fusion.9), kind=kOutput, calls=%fused_computation.34 | convolution fusion | flops 910983168 | bytes 4128768 | tf_op jit(solution)/shard_map/dot_general | solution.py:99
  46.6 2.2 %copy.22 = bf16[2,64,12,384]{3,0,2,1:T(2,128)(2,1)} copy(bf16[2,64,12,384]{3,2,1,0:T(8,128)(2,1)S(1)} %get-tuple-element.11) | data formatting | bytes 2359296 | tf_op jit(solution)/shard_map/optimization_barrier | solution.py:103
  48.8 4.9 %all-to-all-start.1 = ((bf16[2,64,12,384]{3,0,2,1:T(2,128)(2,1)}), bf16[2,64,12,384]{3,0,2,1:T(2,128)(2,1)S(1)}, u32[]{:S(2)}, u32[]{:S(2)}) async-start(bf16[2,64,12,384]{3,0,2,1:T(2,128)(2,1)} %copy.22), calls=%async_computation.1 | async-start | bytes 2359296 | tf_op jit(solution)/shard_map/all_to_all | solution.py:98
  53.6 0.0 copy-done.5
  53.7 0.2 copy.25
  53.8 0.3 reshape_squeeze.7
  54.1 1.1 fusion.8
  55.3 0.0 copy-start.2
  55.3 1.0 fusion.11
  56.3 0.2 copy-done.2
  56.5 2.2 %convolution_convert_fusion.1 = bf16[768,768]{1,0:T(8,128)(2,1)} fusion(bf16[768,768]{0,1:T(8,128)(2,1)S(1)} %fusion.11, bf16[1,1,768,768]{3,2,1,0:T(8,128)(2,1)S(1)} %copy-done.2), kind=kOutput, calls=%fused_computation.20 | convolution fusion | flops 906559488 | bytes 3538944 | tf_op jit(solution)/shard_map/dot_general | solution.py:48
  58.7 0.0 copy-done
  58.7 3.0 %collective-permute-start = (bf16[768,384]{1,0:T(8,128)(2,1)S(1)}, bf16[768,384]{1,0:T(8,128)(2,1)}, u32[]{:S(2)}, u32[]{:S(2)}) collective-permute-start(bf16[768,384]{1,0:T(8,128)(2,1)S(1)} %fusion.13), channel_id=1, source_target_pairs={{0,1},{1,0},{2,3},{3,2},{4,5},{5,4},{6,7},{7,6},{8,9},{9,8},{10,11... | collective-permute-start | bytes 1769480 | tf_op jit(solution)/shard_map/ppermute | solution.py:16
  61.7 20.2 %all-to-all-done.1 = bf16[2,64,12,384]{3,0,2,1:T(2,128)(2,1)S(1)} async-done(((bf16[2,64,12,384]{3,0,2,1:T(2,128)(2,1)}), bf16[2,64,12,384]{3,0,2,1:T(2,128)(2,1)S(1)}, u32[]{:S(2)}, u32[]{:S(2)}) %all-to-all-start.1) | async-done | bytes 1179680 | tf_op jit(solution)/shard_map/all_to_all | solution.py:98
  81.8 0.2 copy.23
  82.1 0.0 copy-start.1
  82.1 1.2 reshape.23
  83.3 0.5 copy-done.1
  83.8 4.0 %fusion.14 = bf16[768,384]{1,0:T(8,128)(2,1)} fusion(bf16[1536,384]{1,0:T(8,128)(2,1)} %reshape.23, bf16[768,768]{0,1:T(8,128)(2,1)S(1)} %copy-done.1, bf16[768,768]{0,1:T(8,128)(2,1)} %fusion.9), kind=kOutput, calls=%fused_computation.35 | convolution fusion | flops 910983168 | bytes 4128768 | tf_op jit(solution)/shard_map/dot_general | solution.py:99
  87.8 0.0 collective-permute-start.1
  87.8 0.0 copy-done.3
  87.8 0.0 copy-done.8
  87.8 2.5 %fusion.16 = f32[768,768]{0,1:T(8,128)} fusion(bf16[768,768]{1,0:T(8,128)(2,1)S(1)} %copy-done.3, bf16[1,1,768,768]{3,2,1,0:T(8,128)(2,1)S(1)} %copy-done.8), kind=kOutput, calls=%fused_computation.38 | convolution fusion | flops 905969664 | bytes 4718592 | tf_op jit(solution)/shard_map/dot_general | solution.py:92
  90.3 0.0 copy-done.11
  90.3 0.6 dynamic-slice.14
  90.9 0.0 copy-done.10
  90.9 0.6 dynamic-slice.13
  92.7 7.4 %collective-permute-done = bf16[768,384]{1,0:T(8,128)(2,1)} collective-permute-done((bf16[768,384]{1,0:T(8,128)(2,1)S(1)}, bf16[768,384]{1,0:T(8,128)(2,1)}, u32[]{:S(2)}, u32[]{:S(2)}) %collective-permute-start) | collective-permute-done | bytes 589856 | tf_op jit(solution)/shard_map/ppermute | solution.py:16
  100.1 1.3 %add_convert_fusion.1 = bf16[768,384]{1,0:T(8,128)(2,1)S(1)} fusion(bf16[768,384]{1,0:T(8,128)(2,1)} %collective-permute-done, bf16[768,384]{1,0:T(8,128)(2,1)S(1)} %fusion.13, f32[]{:T(128)} %bitcast.13, f32[]{:T(128)} %bitcast.2), kind=kLoop, calls=%fused_computation.42 | loop fusion | flops 1769472 | bytes 1769480 | tf_op jit(solution)/shard_map/convert_element_type | solution.py:106
  101.4 1.8 %fusion.22 = f32[768,768]{1,0:T(8,128)S(1)} fusion(bf16[768,384]{1,0:T(8,128)(2,1)S(1)} %add_convert_fusion.1, bf16[768,768]{1,0:T(8,128)(2,1)} %convolution_convert_fusion.1), kind=kOutput, calls=%fused_computation.49 | convolution fusion | flops 452984832 | bytes 3538944 | tf_op jit(solution)/shard_map/dot_general | solution.py:116
  103.2 9.5 %collective-permute-done.1 = bf16[768,384]{1,0:T(8,128)(2,1)} collective-permute-done((bf16[768,384]{1,0:T(8,128)(2,1)}, bf16[768,384]{1,0:T(8,128)(2,1)}, u32[]{:S(2)}, u32[]{:S(2)}) %collective-permute-start.1) | collective-permute-done | bytes 589856 | tf_op jit(solution)/shard_map/ppermute | solution.py:16
  112.7 1.5 %add_convert_fusion = bf16[768,384]{1,0:T(8,128)(2,1)S(1)} fusion(bf16[768,384]{1,0:T(8,128)(2,1)} %collective-permute-done.1, bf16[768,384]{1,0:T(8,128)(2,1)} %fusion.14, f32[]{:T(128)} %bitcast.13, f32[]{:T(128)} %bitcast.2), kind=kLoop, calls=%fused_computation.41 | loop fusion | flops 1769472 | bytes 1769480 | tf_op jit(solution)/shard_map/convert_element_type | solution.py:106
  114.2 5.4 %convolution_convert_fusion = bf16[768,768]{1,0:T(8,128)(2,1)} fusion(bf16[768,768]{0,1:T(8,128)(2,1)} %copy-done, f32[768,768]{1,0:T(8,128)S(1)} %fusion.22, f32[768,768]{0,1:T(8,128)} %fusion.16, bf16[768,384]{1,0:T(8,128)(2,1)S(1)} %add_convert_fusion, bf16[1,1,768,768]{3,2,1,0:T(8,128)(2,1)} %param.15, bf16[768,384]{1,0:T(8,128)(2,1)S(1)} %add_convert_fusion.1, ...), kind=kOutput, calls=%fused_computation.19 | convolution fusion | flops 1365442560 | bytes 10616832 | tf_op jit(solution)/shard_map/dot_general | solution.py:48
  119.6 2.5 %fusion.19 = f32[768,768]{1,0:T(8,128)S(1)} fusion(bf16[768,768]{1,0:T(8,128)(2,1)} %convolution_convert_fusion, bf16[768,384]{1,0:T(8,128)(2,1)S(1)} %add_convert_fusion, bf16[768,384]{1,0:T(8,128)(2,1)S(1)} %add_convert_fusion.1), kind=kOutput, calls=%fused_computation.47 | convolution fusion | flops 908328960 | bytes 4718592 | tf_op jit(solution)/shard_map/dot_general | solution.py:121
  122.1 0.0 copy-done.9
  122.1 0.0 copy-done.12
  122.1 2.2 %fusion.12 = bf16[1,1,768,768]{3,2,1,0:T(8,128)(2,1)} fusion(f32[768,768]{1,0:T(8,128)S(1)} %fusion.19, bf16[768,768]{1,0:T(8,128)(2,1)S(1)} %copy-done.12, bf16[1,1,768,768]{3,2,1,0:T(8,128)(2,1)S(1)} %copy-done.9, bf16[768,384]{1,0:T(8,128)(2,1)S(1)} %add_convert_fusion, bf16[768,384]{1,0:T(8,128)(2,1)S(1)} %add_convert_fusion.1), kind=kOutput, calls=%fused_computation.33 | convolution fusion | flops 911278080 | bytes 7077888 | tf_op jit(solution)/shard_map/dot_general | solution.py:120
  (27 shorter events, 0.2 us)
Async XLA Ops:
  10.2 10.6 %copy-start.4 = (s32[2,64,64]{2,1,0:T(8,128)S(1)}, s32[2,64,64]{2,1,0:T(8,128)}, u32[]{:S(2)}) copy-start(s32[2,64,64]{2,1,0:T(8,128)} %param.18) | copy-start | bytes 98308
  10.2 10.7 %copy-start.7 = (s32[2,64]{1,0:T(2,128)S(1)}, s32[2,64]{1,0:T(2,128)}, u32[]{:S(2)}) copy-start(s32[2,64]{1,0:T(2,128)} %param.19) | copy-start | bytes 1540
  10.2 12.6 %copy-start.6 = (bf16[2,12,12]{2,0,1:T(2,128)(2,1)S(1)}, bf16[2,12,12]{2,0,1:T(2,128)(2,1)}, u32[]{:S(2)}) copy-start(bf16[2,12,12]{2,0,1:T(2,128)(2,1)} %param.17) | copy-start | bytes 1732
  10.2 30.3 %all-to-all-start = ((bf16[2,64,12,384]{3,0,2,1:T(2,128)(2,1)}), bf16[2,64,12,384]{3,0,2,1:T(2,128)(2,1)}, u32[]{:S(2)}, u32[]{:S(2)}) async-start(bf16[2,64,12,384]{3,0,2,1:T(2,128)(2,1)} %copy.20), calls=%async_computation | async-start | bytes 2359296 | tf_op jit(solution)/shard_map/all_to_all | solution.py:98
  48.8 4.9 %copy-start.5 = (bf16[1,1,64,12,12]{2,4,3,1,0:T(8,128)(2,1)S(1)}, bf16[1,1,64,12,12]{2,4,3,1,0:T(8,128)(2,1)}, u32[]{:S(2)}) copy-start(bf16[1,1,64,12,12]{2,4,3,1,0:T(8,128)(2,1)} %param.16) | copy-start | bytes 55300
  48.8 33.0 %all-to-all-start.1 = ((bf16[2,64,12,384]{3,0,2,1:T(2,128)(2,1)}), bf16[2,64,12,384]{3,0,2,1:T(2,128)(2,1)S(1)}, u32[]{:S(2)}, u32[]{:S(2)}) async-start(bf16[2,64,12,384]{3,0,2,1:T(2,128)(2,1)} %copy.22), calls=%async_computation.1 | async-start | bytes 2359296 | tf_op jit(solution)/shard_map/all_to_all | solution.py:98
  55.3 1.3 %copy-start.2 = (bf16[1,1,768,768]{3,2,1,0:T(8,128)(2,1)S(1)}, bf16[1,1,768,768]{3,2,1,0:T(8,128)(2,1)}, u32[]{:S(2)}) copy-start(bf16[1,1,768,768]{3,2,1,0:T(8,128)(2,1)} %param.14) | copy-start | bytes 3538948
  56.5 2.2 %copy-start = (bf16[768,768]{0,1:T(8,128)(2,1)}, bf16[768,768]{0,1:T(8,128)(2,1)S(1)}, u32[]{:S(2)}) copy-start(bf16[768,768]{0,1:T(8,128)(2,1)S(1)} %fusion.11) | copy-start | bytes 3538948
  58.7 41.4 %collective-permute-start = (bf16[768,384]{1,0:T(8,128)(2,1)S(1)}, bf16[768,384]{1,0:T(8,128)(2,1)}, u32[]{:S(2)}, u32[]{:S(2)}) collective-permute-start(bf16[768,384]{1,0:T(8,128)(2,1)S(1)} %fusion.13), channel_id=1, source_target_pairs={{0,1},{1,0},{2,3},{3,2},{4,5},{5,4},{6,7},{7,6},{8,9},{9,8},{10,11... | collective-permute-start | bytes 1769480 | tf_op jit(solution)/shard_map/ppermute | solution.py:16
  82.1 1.7 %copy-start.1 = (bf16[768,768]{0,1:T(8,128)(2,1)S(1)}, bf16[768,768]{0,1:T(8,128)(2,1)}, u32[]{:S(2)}) copy-start(bf16[768,768]{0,1:T(8,128)(2,1)} %fusion.10) | copy-start | bytes 3538948
  83.8 4.1 %copy-start.3 = (bf16[768,768]{1,0:T(8,128)(2,1)S(1)}, bf16[768,768]{1,0:T(8,128)(2,1)}, u32[]{:S(2)}) copy-start(bf16[768,768]{1,0:T(8,128)(2,1)} %convolution_convert_fusion.1) | copy-start | bytes 3538948
  83.8 4.1 %copy-start.8 = (bf16[1,1,768,768]{3,2,1,0:T(8,128)(2,1)S(1)}, bf16[1,1,768,768]{3,2,1,0:T(8,128)(2,1)}, u32[]{:S(2)}) copy-start(bf16[1,1,768,768]{3,2,1,0:T(8,128)(2,1)} %param.15) | copy-start | bytes 3538948
  87.8 2.5 %copy-start.11 = (f32[4]{0:T(128)S(1)}, f32[4]{0:T(128)}, u32[]{:S(2)}) copy-start(f32[4]{0:T(128)} %constant.88.clone..sunk.2) | copy-start | bytes 52
  87.8 3.1 %copy-start.10 = (f32[4]{0:T(128)S(1)}, f32[4]{0:T(128)}, u32[]{:S(2)}) copy-start(f32[4]{0:T(128)} %constant.87.clone..sunk.2) | copy-start | bytes 52
  87.8 24.9 %collective-permute-start.1 = (bf16[768,384]{1,0:T(8,128)(2,1)}, bf16[768,384]{1,0:T(8,128)(2,1)}, u32[]{:S(2)}, u32[]{:S(2)}) collective-permute-start(bf16[768,384]{1,0:T(8,128)(2,1)} %fusion.14), channel_id=1, source_target_pairs={{0,1},{1,0},{2,3},{3,2},{4,5},{5,4},{6,7},{7,6},{8,9},{9,8},{10,11... | collective-permute-start | bytes 1769480 | tf_op jit(solution)/shard_map/ppermute | solution.py:16
  119.6 2.5 %copy-start.9 = (bf16[1,1,768,768]{3,2,1,0:T(8,128)(2,1)S(1)}, bf16[1,1,768,768]{3,2,1,0:T(8,128)(2,1)}, u32[]{:S(2)}) copy-start(bf16[1,1,768,768]{3,2,1,0:T(8,128)(2,1)} %param.15) | copy-start | bytes 3538948
  119.6 2.5 %copy-start.12 = (bf16[768,768]{1,0:T(8,128)(2,1)S(1)}, bf16[768,768]{1,0:T(8,128)(2,1)}, u32[]{:S(2)}) copy-start(bf16[768,768]{1,0:T(8,128)(2,1)} %convolution_convert_fusion) | copy-start | bytes 3538948

commit v4 on v3

--- a/solution.py
+++ b/solution.py
@@ -1,7 +1,7 @@
 import jax
 import jax.numpy as jnp
 from jax import lax
-from jax.sharding import PartitionSpec as P
+from jax.sharding import Mesh, PartitionSpec as P
 
 INNER = 2
 NCHUNK = 2
@@ -62,9 +62,13 @@
     bubble_mat = bubble[0, 0]
     freqs, forms = (bubble_mat.shape[0], bubble_mat.shape[1])
     order_len = current.shape[0]
-    momenta = lax.axis_size("mom")
+    n_xy = lax.axis_size("xy")
+    n_zc = lax.axis_size("zc")
+    momenta = n_xy * n_zc
     assert freqs == momenta
-    momentum = lax.axis_index("mom")
+    momentum = lax.axis_index("xy") * n_zc + lax.axis_index("zc")
+    slot = jnp.arange(momenta, dtype=jnp.int32)
+    momentum_of_slot = (slot % n_xy) * n_zc + slot // n_xy
     channel = lax.axis_index("spin")
     coef_self = jnp.take(jnp.array(COEF_SELF, jnp.float32), channel)
     coef_pair = jnp.take(jnp.array(COEF_PAIR, jnp.float32), channel)
@@ -76,8 +80,9 @@
     mixes = []
     for r in range(2):
         send_order, recv_slots = crossing_plan(cross_tables[r], freq_perm[r], momentum, freqs)
-        packs.append(jnp.take(blocks, send_order, axis=0))
-        mixes.append(mix_matrix(recv_slots, form_mix[r], freqs, expand, forms_expand))
+        packs.append(jnp.take(blocks, jnp.take(send_order, momentum_of_slot), axis=0))
+        recv_at = (recv_slots % n_zc) * n_xy + recv_slots // n_zc
+        mixes.append(mix_matrix(recv_at, form_mix[r], freqs, expand, forms_expand))
     stacked = jnp.stack(packs)
     mix = jnp.concatenate(mixes, axis=1)
 
@@ -95,7 +100,9 @@
     red_chunks = []
     pieces = [stacked[..., k * width:(k + 1) * width] for k in range(NCHUNK)]
     for k in range(NCHUNK):
-        received = lax.all_to_all(pieces[k], "mom", split_axis=1, concat_axis=1, tiled=True)
+        staged = pieces[k].reshape(2, n_zc, n_xy, forms, width)
+        staged = lax.all_to_all(staged, "zc", split_axis=1, concat_axis=1, tiled=True)
+        received = lax.all_to_all(staged, "xy", split_axis=2, concat_axis=2, tiled=True)
         summed = jnp.dot(
             mix, received.reshape(2 * order_len, width), preferred_element_type=jnp.float32
         ).astype(jnp.bfloat16)
@@ -124,13 +131,9 @@
 
 
 def solution(mesh):
-    in_specs = (
-        P("mom", "spin", None, None),
-        P("mom", "spin", None, None),
-        P("mom", "spin", None, None, None),
-        P(),
-        P(),
-        P(),
-    )
-    out_specs = P("mom", "spin", None, None)
-    return jax.shard_map(local, mesh=mesh, in_specs=in_specs, out_specs=out_specs, check_vma=False)
+    momenta, channels = mesh.devices.shape
+    n_zc = 4 if momenta % 4 == 0 else 1
+    staged_mesh = Mesh(mesh.devices.reshape(momenta // n_zc, n_zc, channels), ("xy", "zc", "spin"))
+    vertex = P(("xy", "zc"), "spin", None, None)
+    in_specs = (vertex, vertex, P(("xy", "zc"), "spin", None, None, None), P(), P(), P())
+    return jax.shard_map(local, mesh=staged_mesh, in_specs=in_specs, out_specs=vertex, check_vma=False)

time: 125 us -> 162 us (1.30)
  blocking collectives: 0 us -> 20.5 us
  waiting for transfers between devices: 46.1 us -> 56.3 us
  starting transfers between devices: 18.5 us -> 22 us
  local copies, waits for them, and re-layouts: 17.9 us -> 21.3 us
    all_to_all x0 -> x1, blocking collectives: none -> 20.5 us  [local(): lax.all_to_all(staged, 'zc', split_axis=1, concat_axis=1, tiled=True)]
    ppermute x2, waiting for transfers between devices: 16.9 us -> 26 us  [partner_2(): return lax.ppermute(value, axis, pairs)]
    all_to_all x2 -> x4, local copies, waits for them, and re-layouts: 1.74 us -> 5.59 us  [the longest x2 3.85 us: local(): lax.all_to_all(staged, 'zc', split_axis=1, concat_axis=1, tiled=True)]
    ppermute x2, starting transfers between devices: 2.99 us -> 6.06 us  [partner_2(): return lax.ppermute(value, axis, pairs)]
    optimization_barrier x1 -> x0, local copies, waits for them, and re-layouts: 2.24 us -> none  [local(): summed, pieces[k + 1] = lax.optimization_barrier((summed, pieces[k + 1]))]
    slice x2 -> x1, local copies, waits for them, and re-layouts: 2.24 us -> 0.01 us  [local(): mixes.append(mix_matrix(recv_at, form_mix[r], freqs, expand, forms_expand))]
    gather x2 -> x4, local copies, waits for them, and re-layouts: 2.45 us -> 4.02 us  [the longest x2 2.46 us: local(): jnp.take(blocks, jnp.take(send_order, momentum_of_slot), axis=0)]
    all_to_all x2 -> x3, waiting for transfers between devices: 29.3 us -> 30.3 us  [the longest x2 17.2 us: local(): lax.all_to_all(staged, 'xy', split_axis=2, concat_axis=2, tiled=True)]
  transfers between devices with their start and end apart: 4 -> 5, of which waited for: 4 -> 5; matrix products, arithmetic and copies ran while one was open for 22% -> 17% of each run, Pallas kernels for 0% -> 0%
where the time goes in v4:
time: 162 us
  waiting for transfers between devices  56.3 us (35%)
  matrix products  34.5 us (21%)
  starting transfers between devices  22 us (14%)
  local copies, waits for them, and re-layouts  21.3 us (13%)
  blocking collectives  20.5 us (13%)
  other arithmetic  5.45 us (3%)
    ppermute x2, waiting for transfers between devices, partner_2(): return lax.ppermute(value, axis, pairs)  26 us
    all_to_all x1, blocking collectives, local(): lax.all_to_all(staged, 'zc', split_axis=1, concat_axis=1, tiled=True)  20.5 us
    dot_general x8, matrix products, exact_dot(): jnp.dot(a, b, preferred_element_type=jnp.float32).astype(jnp.bfloat16)  18.5 us
    all_to_all x2, waiting for transfers between devices, local(): lax.all_to_all(staged, 'xy', split_axis=2, concat_axis=2, tiled=True)  17.2 us
    all_to_all x1, waiting for transfers between devices, local(): lax.all_to_all(staged, 'zc', split_axis=1, concat_axis=1, tiled=True)  13 us
    all_to_all x2, starting transfers between devices, local(): lax.all_to_all(staged, 'xy', split_axis=2, concat_axis=2, tiled=True)  9.1 us
    all_to_all x1, starting transfers between devices, local(): lax.all_to_all(staged, 'zc', split_axis=1, concat_axis=1, tiled=True)  6.83 us
    dot_general x2, matrix products, local(): jnp.dot(mix, received.reshape(2 * order_len, width), preferred_element_ty...  6.56 us
  transfers between devices with their start and end apart: 5, of which 5 were waited for; matrix products, arithmetic and copies ran while one was open for 17% of the time, Pallas kernels for 0%

profile of v4, /device:TPU:1, one launch (start us, length us, event | category | flops | bytes accessed | tf_op | source)
XLA Modules:
  0.0 161.5 jit_solution(14873088509399379552)
XLA Ops:
  0.0 0.8 slice_bitcast_fusion
  0.8 0.1 select_reduce_fusion
  0.9 0.8 slice_bitcast_fusion.3
  1.7 0.1 select_reduce_fusion.2
  1.8 0.8 gather_fusion.4
  2.6 2.2 %reshape_squeeze.6 = bf16[64,12,768]{2,1,0:T(8,128)(2,1)S(1)} reshape(bf16[1,1,768,768]{3,2,1,0:T(8,128)(2,1)} %param.16) | data formatting | bytes 2359296 | tf_op jit(solution)/shard_map/reshape;squeeze | solution.py:76
  4.8 0.1 select_reduce_fusion.1
  4.9 0.8 gather_fusion.2
  5.7 1.8 %gather_fusion.5 = bf16[64,12,768]{2,1,0:T(8,128)(2,1)} fusion(bf16[64,12,768]{2,1,0:T(8,128)(2,1)S(1)} %reshape_squeeze.6, s32[1024]{0:T(1024)S(1)} %pad_clamp_fusion), kind=kCustom, calls=%fused_computation.5.clone | custom fusion | bytes 2359552 | tf_op jit(solution)/shard_map/jit(_take)/gather | solution.py:83
  7.5 0.6 gather_fusion.3
  8.2 1.6 select_bitcast_fusion
  9.8 0.2 select_bitcast_fusion.1
  10.0 0.4 pad_maximum_fusion.1
  10.5 1.3 copy.20
  11.7 6.8 %all-to-all-start = ((bf16[2,4,16,12,384]{4,2,3,0,1:T(8,128)(2,1)}), bf16[2,4,16,12,384]{4,2,3,0,1:T(8,128)(2,1)S(1)}, u32[]{:S(2)}, u32[]{:S(2)}) async-start(bf16[2,4,16,12,384]{4,2,3,0,1:T(8,128)(2,1)} %copy.20), calls=%async_computation | async-start | bytes 2359296 | tf_op jit(solution)/shard_map/all_to_all | solution.py:104
  18.6 0.8 gather_fusion.1
  19.4 0.1 select_reduce_fusion.4
  19.5 0.8 gather_fusion
  20.4 13.0 %all-to-all-done = bf16[2,4,16,12,384]{4,2,3,0,1:T(8,128)(2,1)S(1)} async-done(((bf16[2,4,16,12,384]{4,2,3,0,1:T(8,128)(2,1)}), bf16[2,4,16,12,384]{4,2,3,0,1:T(8,128)(2,1)S(1)}, u32[]{:S(2)}, u32[]{:S(2)}) %all-to-all-start) | async-done | bytes 1179680 | tf_op jit(solution)/shard_map/all_to_all | solution.py:104
  33.4 1.9 %copy.21 = bf16[2,4,16,12,384]{4,1,3,0,2:T(4,128)(2,1)} copy(bf16[2,4,16,12,384]{4,2,3,0,1:T(8,128)(2,1)S(1)} %all-to-all-done) | data formatting | bytes 2359296 | tf_op jit(solution)/shard_map/all_to_all | solution.py:104
  35.4 5.1 %all-to-all-start.1 = ((bf16[2,4,16,12,384]{4,1,3,0,2:T(4,128)(2,1)}), bf16[2,4,16,12,384]{4,1,3,0,2:T(4,128)(2,1)}, u32[]{:S(2)}, u32[]{:S(2)}) async-start(bf16[2,4,16,12,384]{4,1,3,0,2:T(4,128)(2,1)} %copy.21), calls=%async_computation.1 | async-start | bytes 2359296 | tf_op jit(solution)/shard_map/all_to_all | solution.py:105
  40.5 1.0 convolution_convert_fusion.6
  41.5 2.1 %convolution_convert_fusion.7 = bf16[768,768]{0,1:T(8,128)(2,1)} fusion(s32[768]{0:T(1024)S(1)} %get-tuple-element.78, s32[768]{0:T(1024)S(1)} %get-tuple-element.79, pred[768]{0:T(1024)(128)(4,1)S(1)} %fusion.61, bf16[1,12,12]{2,0,1:T(2,128)(2,1)S(1)} %get-tuple-element.74), kind=kOutput, calls=%fused_computation.28 | convolution fusion | flops 15012864 | bytes 1186848 | tf_op jit(solution)/shard_map/dot_general | solution.py:48
  43.6 2.1 %fusion.10 = bf16[768,768]{0,1:T(8,128)(2,1)} fusion(bf16[768,768]{0,1:T(8,128)(2,1)S(1)} %convolution_convert_fusion.6, s32[768]{0:T(1024)S(1)} %get-tuple-element.80, s32[768]{0:T(1024)S(1)} %get-tuple-element.81, pred[768]{0:T(1024)(128)(4,1)S(1)} %fusion.62, s32[64]{0:T(128)S(1)} %fusion.71), kind=kOutput, calls=%fused_computation.33 | convolution fusion | flops 84987904 | bytes 2366464 | tf_op jit(solution)/shard_map/dot_general | solution.py:48
  45.7 3.4 %fusion.9 = bf16[768,768]{0,1:T(8,128)(2,1)} fusion(bf16[768,768]{0,1:T(8,128)(2,1)} %convolution_convert_fusion.7, s32[768]{0:T(1024)S(1)} %get-tuple-element.80, s32[768]{0:T(1024)S(1)} %get-tuple-element.81, pred[768]{0:T(1024)(128)(4,1)S(1)} %fusion.62, s32[64]{0:T(128)S(1)} %fusion.69), kind=kOutput, calls=%fused_computation.32 | convolution fusion | flops 84987904 | bytes 2366464 | tf_op jit(solution)/shard_map/dot_general | solution.py:48
  49.0 8.4 %all-to-all-done.1 = bf16[2,4,16,12,384]{4,1,3,0,2:T(4,128)(2,1)} async-done(((bf16[2,4,16,12,384]{4,1,3,0,2:T(4,128)(2,1)}), bf16[2,4,16,12,384]{4,1,3,0,2:T(4,128)(2,1)}, u32[]{:S(2)}, u32[]{:S(2)}) %all-to-all-start.1) | async-done | bytes 1179680 | tf_op jit(solution)/shard_map/all_to_all | solution.py:105
  57.4 1.5 copy.22
  58.9 1.2 reshape.34
  60.1 3.4 %fusion.13 = bf16[768,384]{1,0:T(8,128)(2,1)S(1)} fusion(bf16[1536,384]{1,0:T(8,128)(2,1)} %reshape.34, bf16[768,768]{0,1:T(8,128)(2,1)} %fusion.10, bf16[768,768]{0,1:T(8,128)(2,1)} %fusion.9), kind=kOutput, calls=%fused_computation.36 | convolution fusion | flops 910983168 | bytes 4128768 | tf_op jit(solution)/shard_map/dot_general | solution.py:106
  63.5 0.3 copy.23
  63.8 20.5 %all_to_all.20 = bf16[2,4,16,12,384]{4,2,3,0,1:T(8,128)(2,1)S(1)} all-to-all(bf16[2,4,16,12,384]{4,2,3,0,1:T(8,128)(2,1)S(1)} %copy.23), channel_id=1, replica_groups=mesh['xy'=16,'zc'=4,'spin'=4] {'zc'}, dimensions={1} | all-to-all | bytes 2359296 | tf_op jit(solution)/shard_map/all_to_all | solution.py:104
  84.3 1.9 %copy.24 = bf16[2,4,16,12,384]{4,1,3,0,2:T(4,128)(2,1)} copy(bf16[2,4,16,12,384]{4,2,3,0,1:T(8,128)(2,1)S(1)} %all_to_all.20) | data formatting | bytes 2359296 | tf_op jit(solution)/shard_map/all_to_all | solution.py:104
  86.2 4.0 %all-to-all-start.3 = ((bf16[2,4,16,12,384]{4,1,3,0,2:T(4,128)(2,1)}), bf16[2,4,16,12,384]{4,1,3,0,2:T(4,128)(2,1)S(1)}, u32[]{:S(2)}, u32[]{:S(2)}) async-start(bf16[2,4,16,12,384]{4,1,3,0,2:T(4,128)(2,1)} %copy.24), calls=%async_computation.3 | async-start | bytes 2359296 | tf_op jit(solution)/shard_map/all_to_all | solution.py:105
  90.2 0.0 copy-done.7
  90.2 0.2 copy.27
  90.4 0.3 reshape_squeeze.7
  90.7 1.1 fusion.8
  91.8 0.0 copy-start.3
  91.8 1.0 fusion.11
  92.9 0.2 copy-done.3
  93.1 2.2 %convolution_convert_fusion.1 = bf16[768,768]{1,0:T(8,128)(2,1)} fusion(bf16[768,768]{0,1:T(8,128)(2,1)S(1)} %fusion.11, bf16[1,1,768,768]{3,2,1,0:T(8,128)(2,1)S(1)} %copy-done.3), kind=kOutput, calls=%fused_computation.22 | convolution fusion | flops 906559488 | bytes 3538944 | tf_op jit(solution)/shard_map/dot_general | solution.py:48
  95.3 0.0 copy-done
  95.3 3.0 %collective-permute-start = (bf16[768,384]{1,0:T(8,128)(2,1)S(1)}, bf16[768,384]{1,0:T(8,128)(2,1)}, u32[]{:S(2)}, u32[]{:S(2)}) collective-permute-start(bf16[768,384]{1,0:T(8,128)(2,1)S(1)} %fusion.13), channel_id=1, source_target_pairs={{0,1},{1,0},{2,3},{3,2},{4,5},{5,4},{6,7},{7,6},{8,9},{9,8},{10,11... | collective-permute-start | bytes 1769480 | tf_op jit(solution)/shard_map/ppermute | solution.py:16
  98.2 8.8 %all-to-all-done.3 = bf16[2,4,16,12,384]{4,1,3,0,2:T(4,128)(2,1)S(1)} async-done(((bf16[2,4,16,12,384]{4,1,3,0,2:T(4,128)(2,1)}), bf16[2,4,16,12,384]{4,1,3,0,2:T(4,128)(2,1)S(1)}, u32[]{:S(2)}, u32[]{:S(2)}) %all-to-all-start.3) | async-done | bytes 1179680 | tf_op jit(solution)/shard_map/all_to_all | solution.py:105
  107.1 0.2 copy.25
  107.3 0.0 copy-start.2
  107.3 1.2 reshape.36
  108.5 0.5 copy-done.2
  109.0 3.2 %fusion.14 = bf16[768,384]{1,0:T(8,128)(2,1)S(1)} fusion(bf16[1536,384]{1,0:T(8,128)(2,1)} %reshape.36, bf16[768,768]{0,1:T(8,128)(2,1)S(1)} %copy-done.2, bf16[768,768]{0,1:T(8,128)(2,1)} %fusion.9), kind=kOutput, calls=%fused_computation.37 | convolution fusion | flops 910983168 | bytes 4128768 | tf_op jit(solution)/shard_map/dot_general | solution.py:106
  112.2 0.0 copy-start.12
  112.2 0.0 copy-start.11
  112.2 3.1 %collective-permute-start.1 = (bf16[768,384]{1,0:T(8,128)(2,1)S(1)}, bf16[768,384]{1,0:T(8,128)(2,1)}, u32[]{:S(2)}, u32[]{:S(2)}) collective-permute-start(bf16[768,384]{1,0:T(8,128)(2,1)S(1)} %fusion.14), channel_id=1, source_target_pairs={{0,1},{1,0},{2,3},{3,2},{4,5},{5,4},{6,7},{7,6},{8,9},{9,8},{10,11... | collective-permute-start | bytes 1769480 | tf_op jit(solution)/shard_map/ppermute | solution.py:16
  115.3 0.0 copy-done.4
  115.3 2.5 %fusion.16 = f32[768,768]{0,1:T(8,128)} fusion(bf16[768,768]{1,0:T(8,128)(2,1)S(1)} %copy-done.4, bf16[1,1,768,768]{3,2,1,0:T(8,128)(2,1)S(1)} %copy-done.9), kind=kOutput, calls=%fused_computation.40 | convolution fusion | flops 905969664 | bytes 4718592 | tf_op jit(solution)/shard_map/dot_general | solution.py:97
  117.8 0.6 dynamic-slice.14
  118.5 0.6 dynamic-slice.13
  120.3 16.8 %collective-permute-done = bf16[768,384]{1,0:T(8,128)(2,1)} collective-permute-done((bf16[768,384]{1,0:T(8,128)(2,1)S(1)}, bf16[768,384]{1,0:T(8,128)(2,1)}, u32[]{:S(2)}, u32[]{:S(2)}) %collective-permute-start) | collective-permute-done | bytes 589856 | tf_op jit(solution)/shard_map/ppermute | solution.py:16
  137.2 1.3 add_convert_fusion.1
  138.5 2.2 %fusion.22 = f32[768,768]{1,0:T(8,128)} fusion(bf16[768,384]{1,0:T(8,128)(2,1)S(1)} %add_convert_fusion.1, bf16[768,768]{1,0:T(8,128)(2,1)S(1)} %copy-done.5), kind=kOutput, calls=%fused_computation.51 | convolution fusion | flops 452984832 | bytes 3538944 | tf_op jit(solution)/shard_map/dot_general | solution.py:123
  140.7 9.1 %collective-permute-done.1 = bf16[768,384]{1,0:T(8,128)(2,1)} collective-permute-done((bf16[768,384]{1,0:T(8,128)(2,1)S(1)}, bf16[768,384]{1,0:T(8,128)(2,1)}, u32[]{:S(2)}, u32[]{:S(2)}) %collective-permute-start.1) | collective-permute-done | bytes 589856 | tf_op jit(solution)/shard_map/ppermute | solution.py:16
  149.8 1.3 add_convert_fusion
  151.1 5.7 %convolution_convert_fusion = bf16[768,768]{1,0:T(8,128)(2,1)} fusion(bf16[768,768]{0,1:T(8,128)(2,1)S(1)} %copy-done.1, f32[768,768]{1,0:T(8,128)} %fusion.22, f32[768,768]{0,1:T(8,128)} %fusion.16, bf16[768,384]{1,0:T(8,128)(2,1)S(1)} %add_convert_fusion, bf16[1,1,768,768]{3,2,1,0:T(8,128)(2,1)} %param.17, bf16[768,384]{1,0:T(8,128)(2,1)S(1)} %add_convert_fusion.1, ...), kind=kOutput, calls=%fused_computation.21 | convolution fusion | flops 1365442560 | bytes 10616832 | tf_op jit(solution)/shard_map/dot_general | solution.py:48
  156.8 2.5 %fusion.19 = f32[768,768]{1,0:T(8,128)S(1)} fusion(bf16[768,768]{1,0:T(8,128)(2,1)} %convolution_convert_fusion, bf16[768,384]{1,0:T(8,128)(2,1)S(1)} %add_convert_fusion, bf16[768,384]{1,0:T(8,128)(2,1)S(1)} %add_convert_fusion.1), kind=kOutput, calls=%fused_computation.49 | convolution fusion | flops 908328960 | bytes 4718592 | tf_op jit(solution)/shard_map/dot_general | solution.py:128
  159.3 2.2 %fusion.12 = bf16[1,1,768,768]{3,2,1,0:T(8,128)(2,1)} fusion(f32[768,768]{1,0:T(8,128)S(1)} %fusion.19, bf16[768,768]{1,0:T(8,128)(2,1)S(1)} %copy-done.13, bf16[1,1,768,768]{3,2,1,0:T(8,128)(2,1)S(1)} %copy-done.10, bf16[768,384]{1,0:T(8,128)(2,1)S(1)} %add_convert_fusion, bf16[768,384]{1,0:T(8,128)(2,1)S(1)} %add_convert_fusion.1), kind=kOutput, calls=%fused_computation.35 | convolution fusion | flops 911278080 | bytes 7077888 | tf_op jit(solution)/shard_map/dot_general | solution.py:127
  (37 shorter events, 0.2 us)
Async XLA Ops:
  11.7 6.8 %copy-start.6 = (s32[2,64,64]{2,1,0:T(8,128)S(1)}, s32[2,64,64]{2,1,0:T(8,128)}, u32[]{:S(2)}) copy-start(s32[2,64,64]{2,1,0:T(8,128)} %param.20) | copy-start | bytes 98308
  11.7 8.6 %copy-start.8 = (bf16[2,12,12]{2,0,1:T(2,128)(2,1)S(1)}, bf16[2,12,12]{2,0,1:T(2,128)(2,1)}, u32[]{:S(2)}) copy-start(bf16[2,12,12]{2,0,1:T(2,128)(2,1)} %param.19) | copy-start | bytes 1732
  11.7 21.7 %all-to-all-start = ((bf16[2,4,16,12,384]{4,2,3,0,1:T(8,128)(2,1)}), bf16[2,4,16,12,384]{4,2,3,0,1:T(8,128)(2,1)S(1)}, u32[]{:S(2)}, u32[]{:S(2)}) async-start(bf16[2,4,16,12,384]{4,2,3,0,1:T(8,128)(2,1)} %copy.20), calls=%async_computation | async-start | bytes 2359296 | tf_op jit(solution)/shard_map/all_to_all | solution.py:104
  35.4 22.1 %all-to-all-start.1 = ((bf16[2,4,16,12,384]{4,1,3,0,2:T(4,128)(2,1)}), bf16[2,4,16,12,384]{4,1,3,0,2:T(4,128)(2,1)}, u32[]{:S(2)}, u32[]{:S(2)}) async-start(bf16[2,4,16,12,384]{4,1,3,0,2:T(4,128)(2,1)} %copy.21), calls=%async_computation.1 | async-start | bytes 2359296 | tf_op jit(solution)/shard_map/all_to_all | solution.py:105
  86.2 4.0 %copy-start.7 = (bf16[1,1,64,12,12]{2,4,3,1,0:T(8,128)(2,1)S(1)}, bf16[1,1,64,12,12]{2,4,3,1,0:T(8,128)(2,1)}, u32[]{:S(2)}) copy-start(bf16[1,1,64,12,12]{2,4,3,1,0:T(8,128)(2,1)} %param.18) | copy-start | bytes 55300
  86.2 20.9 %all-to-all-start.3 = ((bf16[2,4,16,12,384]{4,1,3,0,2:T(4,128)(2,1)}), bf16[2,4,16,12,384]{4,1,3,0,2:T(4,128)(2,1)S(1)}, u32[]{:S(2)}, u32[]{:S(2)}) async-start(bf16[2,4,16,12,384]{4,1,3,0,2:T(4,128)(2,1)} %copy.24), calls=%async_computation.3 | async-start | bytes 2359296 | tf_op jit(solution)/shard_map/all_to_all | solution.py:105
  91.8 1.3 copy-start.3
  93.1 2.2 %copy-start = (bf16[768,768]{0,1:T(8,128)(2,1)}, bf16[768,768]{0,1:T(8,128)(2,1)S(1)}, u32[]{:S(2)}) copy-start(bf16[768,768]{0,1:T(8,128)(2,1)S(1)} %fusion.11) | copy-start | bytes 3538948
  95.3 41.9 %collective-permute-start = (bf16[768,384]{1,0:T(8,128)(2,1)S(1)}, bf16[768,384]{1,0:T(8,128)(2,1)}, u32[]{:S(2)}, u32[]{:S(2)}) collective-permute-start(bf16[768,384]{1,0:T(8,128)(2,1)S(1)} %fusion.13), channel_id=1, source_target_pairs={{0,1},{1,0},{2,3},{3,2},{4,5},{5,4},{6,7},{7,6},{8,9},{9,8},{10,11... | collective-permute-start | bytes 1769480 | tf_op jit(solution)/shard_map/ppermute | solution.py:16
  107.3 1.7 %copy-start.2 = (bf16[768,768]{0,1:T(8,128)(2,1)S(1)}, bf16[768,768]{0,1:T(8,128)(2,1)}, u32[]{:S(2)}) copy-start(bf16[768,768]{0,1:T(8,128)(2,1)} %fusion.10) | copy-start | bytes 3538948
  109.0 6.3 %copy-start.4 = (bf16[768,768]{1,0:T(8,128)(2,1)S(1)}, bf16[768,768]{1,0:T(8,128)(2,1)}, u32[]{:S(2)}) copy-start(bf16[768,768]{1,0:T(8,128)(2,1)} %convolution_convert_fusion.1) | copy-start | bytes 3538948
  109.0 6.3 %copy-start.9 = (bf16[1,1,768,768]{3,2,1,0:T(8,128)(2,1)S(1)}, bf16[1,1,768,768]{3,2,1,0:T(8,128)(2,1)}, u32[]{:S(2)}) copy-start(bf16[1,1,768,768]{3,2,1,0:T(8,128)(2,1)} %param.17) | copy-start | bytes 3538948
  112.2 5.6 %copy-start.12 = (f32[4]{0:T(128)S(1)}, f32[4]{0:T(128)}, u32[]{:S(2)}) copy-start(f32[4]{0:T(128)} %constant.161.clone..sunk.2) | copy-start | bytes 52
  112.2 6.3 %copy-start.11 = (f32[4]{0:T(128)S(1)}, f32[4]{0:T(128)}, u32[]{:S(2)}) copy-start(f32[4]{0:T(128)} %constant.160.clone..sunk.2) | copy-start | bytes 52
  112.2 37.6 %collective-permute-start.1 = (bf16[768,384]{1,0:T(8,128)(2,1)S(1)}, bf16[768,384]{1,0:T(8,128)(2,1)}, u32[]{:S(2)}, u32[]{:S(2)}) collective-permute-start(bf16[768,384]{1,0:T(8,128)(2,1)S(1)} %fusion.14), channel_id=1, source_target_pairs={{0,1},{1,0},{2,3},{3,2},{4,5},{5,4},{6,7},{7,6},{8,9},{9,8},{10,11... | collective-permute-start | bytes 1769480 | tf_op jit(solution)/shard_map/ppermute | solution.py:16
  117.8 20.6 %copy-start.5 = (bf16[768,768]{1,0:T(8,128)(2,1)S(1)}, bf16[768,768]{1,0:T(8,128)(2,1)}, u32[]{:S(2)}) copy-start(bf16[768,768]{1,0:T(8,128)(2,1)} %convolution_convert_fusion.1) | copy-start | bytes 3538948
  140.7 10.4 %copy-start.1 = (bf16[768,768]{0,1:T(8,128)(2,1)S(1)}, bf16[768,768]{0,1:T(8,128)(2,1)}, u32[]{:S(2)}) copy-start(bf16[768,768]{0,1:T(8,128)(2,1)} %copy-done) | copy-start | bytes 3538948
  156.8 2.5 %copy-start.10 = (bf16[1,1,768,768]{3,2,1,0:T(8,128)(2,1)S(1)}, bf16[1,1,768,768]{3,2,1,0:T(8,128)(2,1)}, u32[]{:S(2)}) copy-start(bf16[1,1,768,768]{3,2,1,0:T(8,128)(2,1)} %param.17) | copy-start | bytes 3538948
  156.8 2.5 %copy-start.13 = (bf16[768,768]{1,0:T(8,128)(2,1)S(1)}, bf16[768,768]{1,0:T(8,128)(2,1)}, u32[]{:S(2)}) copy-start(bf16[768,768]{1,0:T(8,128)(2,1)} %convolution_convert_fusion) | copy-start | bytes 3538948

commit v5 on v3

--- a/solution.py
+++ b/solution.py
@@ -4,7 +4,7 @@
 from jax.sharding import PartitionSpec as P
 
 INNER = 2
-NCHUNK = 2
+WIDTHS = (256, 512)
 
 COEF_SELF = (-0.5, 0.5, 0.5, 0.5)
 COEF_PAIR = (-1.5, -0.5, 1.5, -0.5)
@@ -91,15 +91,16 @@
     carried = carry_of(current)
     bare_part = jnp.dot(bare_mat, carried, preferred_element_type=jnp.float32)
 
-    width = order_len // NCHUNK
+    assert sum(WIDTHS) == order_len
+    starts = [sum(WIDTHS[:k]) for k in range(len(WIDTHS))]
     red_chunks = []
-    pieces = [stacked[..., k * width:(k + 1) * width] for k in range(NCHUNK)]
-    for k in range(NCHUNK):
+    pieces = [stacked[..., starts[k]:starts[k] + WIDTHS[k]] for k in range(len(WIDTHS))]
+    for k in range(len(WIDTHS)):
         received = lax.all_to_all(pieces[k], "mom", split_axis=1, concat_axis=1, tiled=True)
         summed = jnp.dot(
-            mix, received.reshape(2 * order_len, width), preferred_element_type=jnp.float32
+            mix, received.reshape(2 * order_len, WIDTHS[k]), preferred_element_type=jnp.float32
         ).astype(jnp.bfloat16)
-        if k + 1 < NCHUNK:
+        if k + 1 < len(WIDTHS):
             summed, pieces[k + 1] = lax.optimization_barrier((summed, pieces[k + 1]))
         other = partner_2(summed, "spin", 0)
         red_chunks.append(
@@ -111,8 +112,8 @@
     base_sum = bare_mat.astype(jnp.float32) + reducible.astype(jnp.float32)
 
     total = base_sum + bare_part
-    for k in range(NCHUNK):
-        rows = slice(k * width, (k + 1) * width)
+    for k in range(len(WIDTHS)):
+        rows = slice(starts[k], starts[k] + WIDTHS[k])
         total = total + jnp.dot(red_chunks[k], carried[rows], preferred_element_type=jnp.float32)
     current = total.astype(jnp.bfloat16)
     for inner_step in range(1, INNER):

time: 125 us -> 137 us (1.096)
  local copies, waits for them, and re-layouts: 17.9 us -> 23.7 us
  waiting for transfers between devices: 46.1 us -> 49.9 us
  other arithmetic: 5.6 us -> 7.98 us
  matrix products: 34.7 us -> 32.6 us
  starting transfers between devices: 18.5 us -> 20.2 us
    ppermute x2, waiting for transfers between devices: 16.9 us -> 26.5 us  [partner_2(): return lax.ppermute(value, axis, pairs)]
    all_to_all x2, waiting for transfers between devices: 29.3 us -> 23.4 us  [local(): lax.all_to_all(pieces[k], 'mom', split_axis=1, concat_axis=1, tiled=True)]
    unnamed x27 -> x46, local copies, waits for them, and re-layouts: 0.99 us -> 2.91 us
    broadcast_in_dim x0 -> x1, local copies, waits for them, and re-layouts: none -> 1.45 us  [local(): return current[None, None]]
    all_to_all x2, starting transfers between devices: 15.5 us -> 16.9 us  [local(): lax.all_to_all(pieces[k], 'mom', split_axis=1, concat_axis=1, tiled=True)]
    all_to_all x2, local copies, waits for them, and re-layouts: 1.74 us -> 3.14 us  [local(): lax.all_to_all(pieces[k], 'mom', split_axis=1, concat_axis=1, tiled=True)]
  transfers between devices with their start and end apart: 4 -> 4, of which waited for: 4 -> 3; matrix products, arithmetic and copies ran while one was open for 22% -> 24% of each run, Pallas kernels for 0% -> 0%
where the time goes in v5:
time: 137 us; the launch traced here: 136 us
  waiting for transfers between devices  49.9 us (36%)
  matrix products  32.6 us (24%)
  local copies, waits for them, and re-layouts  23.7 us (17%)
  starting transfers between devices  20.2 us (15%)
  other arithmetic  7.98 us (6%)
  between operations  1.61 us (1%)
    ppermute x2, waiting for transfers between devices, partner_2(): return lax.ppermute(value, axis, pairs)  26.5 us
    all_to_all x2, waiting for transfers between devices, local(): lax.all_to_all(pieces[k], 'mom', split_axis=1, concat_axis=1, tiled=True)  23.4 us
    dot_general x8, matrix products, exact_dot(): jnp.dot(a, b, preferred_element_type=jnp.float32).astype(jnp.bfloat16)  18 us
    all_to_all x2, starting transfers between devices, local(): lax.all_to_all(pieces[k], 'mom', split_axis=1, concat_axis=1, tiled=True)  16.9 us
    dot_general x2, matrix products, local(): jnp.dot(mix, received.reshape(2 * order_len, WIDTHS[k]), preferred_elemen...  6.55 us
    convert_element_type x2, other arithmetic, local(): (coef_self * summed.astype(jnp.float32) + coef_pair * other.astype(jnp.fl...  3.58 us
    ppermute x2, starting transfers between devices, partner_2(): return lax.ppermute(value, axis, pairs)  3.31 us
    all_to_all x2, local copies, waits for them, and re-layouts, local(): lax.all_to_all(pieces[k], 'mom', split_axis=1, concat_axis=1, tiled=True)  3.14 us
  transfers between devices with their start and end apart: 4, of which 3 were waited for; matrix products, arithmetic and copies ran while one was open for 24% of the time, Pallas kernels for 0%

profile of v5, /device:TPU:1, one launch (start us, length us, event | category | flops | bytes accessed | tf_op | source)
XLA Modules:
  0.0 136.0 jit_solution(6671203565616688775)
XLA Ops:
  0.0 0.8 slice_bitcast_fusion.1
  0.8 0.1 select_reduce_fusion
  0.9 0.1 select_reduce_fusion.1
  1.1 2.2 %reshape_squeeze.6 = bf16[64,12,768]{2,1,0:T(8,128)(2,1)S(1)} reshape(bf16[1,1,768,768]{3,2,1,0:T(8,128)(2,1)} %param.14) | data formatting | bytes 2359296 | tf_op jit(solution)/shard_map/reshape;squeeze | solution.py:72
  3.3 0.6 gather_fusion.3
  3.9 1.8 %gather_fusion.2 = bf16[64,12,768]{2,1,0:T(8,128)(2,1)} fusion(bf16[64,12,768]{2,1,0:T(8,128)(2,1)S(1)} %reshape_squeeze.6, s32[1024]{0:T(1024)S(1)} %pad_clamp_fusion.1), kind=kCustom, calls=%fused_computation.1.clone | custom fusion | bytes 2359552 | tf_op jit(solution)/shard_map/jit(_take)/gather | solution.py:79
  5.7 0.2 select_bitcast_fusion
  6.0 1.2 copy-done.1
  7.1 0.2 select_bitcast_fusion.1
  7.4 0.1 pad_maximum_fusion.10
  7.5 0.0 copy-start.11
  7.5 1.7 %copy.25 = bf16[2,64,12,256]{3,0,2,1:T(2,128)(2,1)} copy(bf16[2,64,12,256]{3,2,1,0:T(8,128)(2,1)S(1)} %pad_maximum_fusion.10) | data formatting | bytes 1572864 | tf_op jit(solution)/shard_map/slice | solution.py:97
  9.2 10.5 %all-to-all-start = ((bf16[2,64,12,256]{3,0,2,1:T(2,128)(2,1)}), bf16[2,64,12,256]{3,0,2,1:T(2,128)(2,1)}, u32[]{:S(2)}, u32[]{:S(2)}) async-start(bf16[2,64,12,256]{3,0,2,1:T(2,128)(2,1)} %copy.25), calls=%async_computation | async-start | bytes 1572864 | tf_op jit(solution)/shard_map/all_to_all | solution.py:99
  19.8 0.0 copy-start.15
  19.8 0.0 copy-start.18
  19.8 0.0 copy-start.17
  19.8 1.7 %pad_maximum_fusion.1 = bf16[2,64,12,512]{3,2,1,0:T(8,128)(2,1)} fusion(bf16[1,64,12,768]{3,2,1,0:T(8,128)(2,1)S(1)} %select_bitcast_fusion, bf16[1,64,12,768]{3,2,1,0:T(8,128)(2,1)S(1)} %select_bitcast_fusion.1), kind=kLoop, calls=%fused_computation.13 | loop fusion | flops 3145728 | bytes 3932160 | tf_op jit(solution)/shard_map/stack | solution.py:81
  21.5 0.1 select_reduce_fusion.2
  21.6 0.1 select_reduce_fusion.4
  21.8 0.8 gather_fusion
  22.5 0.6 and_select_fusion.1
  23.1 0.5 fusion.62
  23.7 0.8 gather_fusion.1
  24.4 0.5 and_select_fusion
  25.0 1.0 convolution_convert_fusion.7
  26.0 1.7 %convolution_convert_fusion.6 = bf16[768,768]{0,1:T(8,128)(2,1)S(1)} fusion(s32[768]{0:T(1024)S(1)} %get-tuple-element.71, s32[768]{0:T(1024)S(1)} %get-tuple-element.72, pred[768]{0:T(1024)(128)(4,1)} %copy-done.15, bf16[1,12,12]{2,0,1:T(2,128)(2,1)S(1)} %get-tuple-element.68), kind=kOutput, calls=%fused_computation.23 | convolution fusion | flops 15012864 | bytes 1186848 | tf_op jit(solution)/shard_map/dot_general | solution.py:48
  27.7 1.8 %fusion.8 = bf16[768,768]{0,1:T(8,128)(2,1)S(1)} fusion(bf16[768,768]{0,1:T(8,128)(2,1)S(1)} %convolution_convert_fusion.7, s32[768]{0:T(1024)S(1)} %get-tuple-element.73, s32[768]{0:T(1024)S(1)} %get-tuple-element.74, pred[768]{0:T(1024)(128)(4,1)} %fusion.62, s32[64]{0:T(128)} %and_select_fusion.1), kind=kOutput, calls=%fused_computation.28 | convolution fusion | flops 84987904 | bytes 2366464 | tf_op jit(solution)/shard_map/dot_general | solution.py:48
  29.5 2.8 %fusion.9 = bf16[768,768]{0,1:T(8,128)(2,1)} fusion(bf16[768,768]{0,1:T(8,128)(2,1)S(1)} %convolution_convert_fusion.6, s32[768]{0:T(1024)S(1)} %get-tuple-element.73, s32[768]{0:T(1024)S(1)} %get-tuple-element.74, pred[768]{0:T(1024)(128)(4,1)} %fusion.62, s32[64]{0:T(128)} %and_select_fusion), kind=kOutput, calls=%fused_computation.29 | convolution fusion | flops 84987904 | bytes 2366464 | tf_op jit(solution)/shard_map/dot_general | solution.py:48
  32.3 2.9 %all-to-all-done = bf16[2,64,12,256]{3,0,2,1:T(2,128)(2,1)} async-done(((bf16[2,64,12,256]{3,0,2,1:T(2,128)(2,1)}), bf16[2,64,12,256]{3,0,2,1:T(2,128)(2,1)}, u32[]{:S(2)}, u32[]{:S(2)}) %all-to-all-start) | async-done | bytes 786464 | tf_op jit(solution)/shard_map/all_to_all | solution.py:99
  35.2 1.3 copy.26
  36.5 1.1 reshape.22
  37.5 0.0 copy-done.5
  37.5 2.9 %fusion.13 = bf16[768,256]{1,0:T(8,128)(2,1)} fusion(bf16[1536,256]{1,0:T(8,128)(2,1)} %reshape.22, bf16[768,768]{0,1:T(8,128)(2,1)S(1)} %copy-done.5, bf16[768,768]{0,1:T(8,128)(2,1)S(1)} %fusion.8), kind=kOutput, calls=%fused_computation.33 | convolution fusion | flops 608894976 | bytes 3538944 | tf_op jit(solution)/shard_map/dot_general | solution.py:100
  40.4 0.0 copy-done
  40.4 2.8 %copy.27 = bf16[2,64,12,512]{3,0,2,1:T(2,128)(2,1)} copy(bf16[2,64,12,512]{3,2,1,0:T(8,128)(2,1)S(1)} %copy-done) | data formatting | bytes 3145728 | tf_op jit(solution)/shard_map/optimization_barrier | solution.py:104
  43.2 6.4 %all-to-all-start.1 = ((bf16[2,64,12,512]{3,0,2,1:T(2,128)(2,1)}), bf16[2,64,12,512]{3,0,2,1:T(2,128)(2,1)}, u32[]{:S(2)}, u32[]{:S(2)}) async-start(bf16[2,64,12,512]{3,0,2,1:T(2,128)(2,1)} %copy.27), calls=%async_computation.1 | async-start | bytes 3145728 | tf_op jit(solution)/shard_map/all_to_all | solution.py:99
  49.6 0.0 copy-start.16
  49.6 0.6 dynamic-slice.14
  50.2 0.0 copy-done.19
  50.2 0.6 dynamic-slice.13
  52.0 0.2 copy.30
  52.2 0.3 reshape_squeeze.7
  52.5 1.4 %copy.22 = bf16[1,1,768,768]{2,3,1,0:T(8,128)(2,1)} copy(bf16[1,1,768,768]{3,2,1,0:T(8,128)(2,1)S(1)} %copy-done.2) | data formatting | bytes 2359296 | tf_op args[1]
  53.9 1.1 fusion.7
  55.0 1.0 fusion.10
  56.1 0.0 copy-start.7
  56.1 2.2 %convolution_convert_fusion.1 = bf16[768,768]{1,0:T(8,128)(2,1)} fusion(bf16[768,768]{0,1:T(8,128)(2,1)S(1)} %fusion.10, bf16[1,1,768,768]{3,2,1,0:T(8,128)(2,1)S(1)} %copy-done.8), kind=kOutput, calls=%fused_computation.18 | convolution fusion | flops 906559488 | bytes 3538944 | tf_op jit(solution)/shard_map/dot_general | solution.py:48
  58.2 3.0 %collective-permute-start = (bf16[768,256]{1,0:T(8,128)(2,1)}, bf16[768,256]{1,0:T(8,128)(2,1)}, u32[]{:S(2)}, u32[]{:S(2)}) collective-permute-start(bf16[768,256]{1,0:T(8,128)(2,1)} %fusion.13), channel_id=1, source_target_pairs={{0,1},{1,0},{2,3},{3,2},{4,5},{5,4},{6,7},{7,6},{8,9},{9,8},{10,11... | collective-permute-start | bytes 1179656 | tf_op jit(solution)/shard_map/ppermute | solution.py:16
  61.2 20.6 %all-to-all-done.1 = bf16[2,64,12,512]{3,0,2,1:T(2,128)(2,1)} async-done(((bf16[2,64,12,512]{3,0,2,1:T(2,128)(2,1)}), bf16[2,64,12,512]{3,0,2,1:T(2,128)(2,1)}, u32[]{:S(2)}, u32[]{:S(2)}) %all-to-all-start.1) | async-done | bytes 1572896 | tf_op jit(solution)/shard_map/all_to_all | solution.py:99
  81.8 1.9 %copy.28 = bf16[2,64,12,512]{3,2,1,0:T(8,128)(2,1)S(1)} copy(bf16[2,64,12,512]{3,0,2,1:T(2,128)(2,1)} %all-to-all-done.1) | data formatting | bytes 3145728 | tf_op jit(solution)/shard_map/all_to_all | solution.py:99
  83.7 1.4 %reshape.23 = bf16[1536,512]{1,0:T(8,128)(2,1)} reshape(bf16[2,64,12,512]{3,2,1,0:T(8,128)(2,1)S(1)} %copy.28) | data formatting | bytes 3145728 | tf_op jit(solution)/shard_map/reshape | solution.py:101
  85.0 3.6 %fusion.11 = bf16[768,512]{0,1:T(8,128)(2,1)S(1)} fusion(bf16[1536,512]{1,0:T(8,128)(2,1)} %reshape.23, bf16[768,768]{0,1:T(8,128)(2,1)} %fusion.9, bf16[768,768]{0,1:T(8,128)(2,1)} %copy-done.4), kind=kOutput, calls=%fused_computation.31 | convolution fusion | flops 1213071360 | bytes 4718592 | tf_op jit(solution)/shard_map/dot_general | solution.py:100
  88.7 0.3 collective-permute-start.1
  89.0 2.6 %fusion.16 = f32[768,768]{1,0:T(8,128)} fusion(bf16[768,768]{1,0:T(8,128)(2,1)S(1)} %copy-done.12, bf16[1,1,768,768]{3,2,1,0:T(8,128)(2,1)S(1)} %copy-done.2), kind=kOutput, calls=%fused_computation.37 | convolution fusion | flops 905969664 | bytes 4718592 | tf_op jit(solution)/shard_map/dot_general | solution.py:92
  91.6 0.0 collective-permute-done
  91.6 1.3 add_convert_fusion.1
  92.8 0.9 copy.29
  93.8 1.5 %fusion.22 = f32[768,768]{0,1:T(8,128)S(1)} fusion(bf16[768,256]{1,0:T(8,128)(2,1)S(1)} %add_convert_fusion.1, bf16[768,768]{1,0:T(8,128)(2,1)} %convolution_convert_fusion.1), kind=kOutput, calls=%fused_computation.47 | convolution fusion | flops 301989888 | bytes 3145728 | tf_op jit(solution)/shard_map/dot_general | solution.py:117
  95.3 26.5 %collective-permute-done.1 = bf16[768,512]{0,1:T(8,128)(2,1)} collective-permute-done((bf16[768,512]{0,1:T(8,128)(2,1)S(1)}, bf16[768,512]{0,1:T(8,128)(2,1)}, u32[]{:S(2)}, u32[]{:S(2)}) %collective-permute-start.1) | collective-permute-done | bytes 786464 | tf_op jit(solution)/shard_map/ppermute | solution.py:16
  121.8 2.3 %add_convert_fusion = bf16[768,512]{0,1:T(8,128)(2,1)} fusion(bf16[768,512]{0,1:T(8,128)(2,1)} %collective-permute-done.1, bf16[768,512]{0,1:T(8,128)(2,1)S(1)} %fusion.11, f32[]{:T(128)} %bitcast.13, f32[]{:T(128)} %bitcast.2), kind=kLoop, calls=%fused_computation.16 | loop fusion | flops 2359296 | bytes 2359304 | tf_op jit(solution)/shard_map/convert_element_type | solution.py:107
  124.1 6.4 %convolution_convert_fusion = bf16[768,768]{1,0:T(8,128)(2,1)} fusion(bf16[768,768]{0,1:T(8,128)(2,1)} %copy-done.7, f32[768,768]{0,1:T(8,128)S(1)} %fusion.22, f32[768,768]{1,0:T(8,128)} %fusion.16, bf16[768,512]{0,1:T(8,128)(2,1)} %add_convert_fusion, bf16[1,1,768,768]{2,3,1,0:T(8,128)(2,1)} %copy.22, bf16[768,256]{0,1:T(8,128)(2,1)} %copy.29, ...), kind=kOutput, calls=%fused_computation.17 | convolution fusion | flops 1516437504 | bytes 11010048 | tf_op jit(solution)/shard_map/dot_general | solution.py:48
  130.6 2.5 %fusion.14 = f32[768,768]{1,0:T(8,128)S(1)} fusion(bf16[768,768]{1,0:T(8,128)(2,1)} %convolution_convert_fusion, bf16[1,1,768,768]{3,2,1,0:T(8,128)(2,1)S(1)} %copy-done.3), kind=kOutput, calls=%fused_computation.35 | convolution fusion | flops 905969664 | bytes 4718592 | tf_op jit(solution)/shard_map/dot_general | solution.py:121
  133.2 1.4 %fusion.12 = bf16[1,1,768,768]{2,3,1,0:T(8,128)(2,1)S(1)} fusion(bf16[768,768]{1,0:T(8,128)(2,1)S(1)} %copy-done.21, f32[768,768]{1,0:T(8,128)S(1)} %fusion.14, bf16[1,1,768,768]{2,3,1,0:T(8,128)(2,1)S(1)} %copy-done.6, bf16[768,512]{0,1:T(8,128)(2,1)S(1)} %copy-done.9, bf16[768,256]{0,1:T(8,128)(2,1)S(1)} %copy-done.10), kind=kOutput, calls=%fused_computation.32 | convolution fusion | flops 913637376 | bytes 7077888 | tf_op jit(solution)/shard_map/dot_general | solution.py:122
  134.6 1.5 %copy.35 = bf16[1,1,768,768]{3,2,1,0:T(8,128)(2,1)} copy(bf16[1,1,768,768]{2,3,1,0:T(8,128)(2,1)S(1)} %fusion.12) | data formatting | bytes 2359296 | tf_op jit(solution)/shard_map/broadcast_in_dim | solution.py:124
  (49 shorter events, 0.2 us)
Async XLA Ops:
  5.7 1.4 %copy-start.1 = (bf16[64,12,768]{2,1,0:T(8,128)(2,1)S(1)}, bf16[64,12,768]{2,1,0:T(8,128)(2,1)}, u32[]{:S(2)}) copy-start(bf16[64,12,768]{2,1,0:T(8,128)(2,1)} %gather_fusion.2) | copy-start | bytes 3538948
  7.5 12.2 %copy-start.11 = (s32[2,64,64]{2,1,0:T(8,128)S(1)}, s32[2,64,64]{2,1,0:T(8,128)}, u32[]{:S(2)}) copy-start(s32[2,64,64]{2,1,0:T(8,128)} %param.18) | copy-start | bytes 98308
  9.2 26.0 %all-to-all-start = ((bf16[2,64,12,256]{3,0,2,1:T(2,128)(2,1)}), bf16[2,64,12,256]{3,0,2,1:T(2,128)(2,1)}, u32[]{:S(2)}, u32[]{:S(2)}) async-start(bf16[2,64,12,256]{3,0,2,1:T(2,128)(2,1)} %copy.25), calls=%async_computation | async-start | bytes 1572864 | tf_op jit(solution)/shard_map/all_to_all | solution.py:99
  19.8 5.2 %copy-start.15 = (pred[768]{0:T(1024)(128)(4,1)}, pred[768]{0:T(1024)(128)(4,1)S(1)}, u32[]{:S(2)}) copy-start(pred[768]{0:T(1024)(128)(4,1)S(1)} %fusion.61) | copy-start | bytes 2308
  19.8 1.7 %copy-start.18 = (s32[2,64]{1,0:T(2,128)S(1)}, s32[2,64]{1,0:T(2,128)}, u32[]{:S(2)}) copy-start(s32[2,64]{1,0:T(2,128)} %param.19) | copy-start | bytes 1540
  19.8 5.1 %copy-start.17 = (bf16[2,12,12]{2,0,1:T(2,128)(2,1)S(1)}, bf16[2,12,12]{2,0,1:T(2,128)(2,1)}, u32[]{:S(2)}) copy-start(bf16[2,12,12]{2,0,1:T(2,128)(2,1)} %param.17) | copy-start | bytes 1732
  29.5 8.1 %copy-start.4 = (bf16[768,768]{0,1:T(8,128)(2,1)}, bf16[768,768]{0,1:T(8,128)(2,1)S(1)}, u32[]{:S(2)}) copy-start(bf16[768,768]{0,1:T(8,128)(2,1)S(1)} %fusion.8) | copy-start | bytes 3538948
  32.3 5.2 %copy-start.5 = (bf16[768,768]{0,1:T(8,128)(2,1)S(1)}, bf16[768,768]{0,1:T(8,128)(2,1)}, u32[]{:S(2)}) copy-start(bf16[768,768]{0,1:T(8,128)(2,1)} %fusion.9) | copy-start | bytes 3538948
  37.5 2.9 %copy-start = (bf16[2,64,12,512]{3,2,1,0:T(8,128)(2,1)S(1)}, bf16[2,64,12,512]{3,2,1,0:T(8,128)(2,1)}, u32[]{:S(2)}) copy-start(bf16[2,64,12,512]{3,2,1,0:T(8,128)(2,1)} %pad_maximum_fusion.1) | copy-start | bytes 4718596
  43.2 6.4 %copy-start.20 = (f32[4]{0:T(128)S(1)}, f32[4]{0:T(128)}, u32[]{:S(2)}) copy-start(f32[4]{0:T(128)} %constant.88.clone..sunk.2) | copy-start | bytes 52
  43.2 7.0 %copy-start.19 = (f32[4]{0:T(128)S(1)}, f32[4]{0:T(128)}, u32[]{:S(2)}) copy-start(f32[4]{0:T(128)} %constant.87.clone..sunk.2) | copy-start | bytes 52
  43.2 8.8 %copy-start.13 = (bf16[1,1,64,12,12]{2,4,3,1,0:T(8,128)(2,1)S(1)}, bf16[1,1,64,12,12]{2,4,3,1,0:T(8,128)(2,1)}, u32[]{:S(2)}) copy-start(bf16[1,1,64,12,12]{2,4,3,1,0:T(8,128)(2,1)} %param.16) | copy-start | bytes 55300
  43.2 9.2 %copy-start.2 = (bf16[1,1,768,768]{3,2,1,0:T(8,128)(2,1)S(1)}, bf16[1,1,768,768]{3,2,1,0:T(8,128)(2,1)}, u32[]{:S(2)}) copy-start(bf16[1,1,768,768]{3,2,1,0:T(8,128)(2,1)} %param.15) | copy-start | bytes 3538948
  43.2 38.6 %all-to-all-start.1 = ((bf16[2,64,12,512]{3,0,2,1:T(2,128)(2,1)}), bf16[2,64,12,512]{3,0,2,1:T(2,128)(2,1)}, u32[]{:S(2)}, u32[]{:S(2)}) async-start(bf16[2,64,12,512]{3,0,2,1:T(2,128)(2,1)} %copy.27), calls=%async_computation.1 | async-start | bytes 3145728 | tf_op jit(solution)/shard_map/all_to_all | solution.py:99
  49.6 4.3 %copy-start.16 = (pred[768]{0:T(1024)(128)(4,1)S(1)}, pred[768]{0:T(1024)(128)(4,1)}, u32[]{:S(2)}) copy-start(pred[768]{0:T(1024)(128)(4,1)} %copy-done.15) | copy-start | bytes 2308
  52.4 2.6 %copy-start.14 = (pred[768]{0:T(1024)(128)(4,1)S(1)}, pred[768]{0:T(1024)(128)(4,1)}, u32[]{:S(2)}) copy-start(pred[768]{0:T(1024)(128)(4,1)} %fusion.62) | copy-start | bytes 2308
  53.9 2.1 %copy-start.8 = (bf16[1,1,768,768]{3,2,1,0:T(8,128)(2,1)S(1)}, bf16[1,1,768,768]{3,2,1,0:T(8,128)(2,1)}, u32[]{:S(2)}) copy-start(bf16[1,1,768,768]{3,2,1,0:T(8,128)(2,1)} %param.14) | copy-start | bytes 3538948
  56.1 2.2 %copy-start.7 = (bf16[768,768]{0,1:T(8,128)(2,1)}, bf16[768,768]{0,1:T(8,128)(2,1)S(1)}, u32[]{:S(2)}) copy-start(bf16[768,768]{0,1:T(8,128)(2,1)S(1)} %fusion.10) | copy-start | bytes 3538948
  58.2 33.3 %collective-permute-start = (bf16[768,256]{1,0:T(8,128)(2,1)}, bf16[768,256]{1,0:T(8,128)(2,1)}, u32[]{:S(2)}, u32[]{:S(2)}) collective-permute-start(bf16[768,256]{1,0:T(8,128)(2,1)} %fusion.13), channel_id=1, source_target_pairs={{0,1},{1,0},{2,3},{3,2},{4,5},{5,4},{6,7},{7,6},{8,9},{9,8},{10,11... | collective-permute-start | bytes 1179656 | tf_op jit(solution)/shard_map/ppermute | solution.py:16
  85.0 4.0 %copy-start.12 = (bf16[768,768]{1,0:T(8,128)(2,1)S(1)}, bf16[768,768]{1,0:T(8,128)(2,1)}, u32[]{:S(2)}) copy-start(bf16[768,768]{1,0:T(8,128)(2,1)} %convolution_convert_fusion.1) | copy-start | bytes 3538948
  88.7 33.1 %collective-permute-start.1 = (bf16[768,512]{0,1:T(8,128)(2,1)S(1)}, bf16[768,512]{0,1:T(8,128)(2,1)}, u32[]{:S(2)}, u32[]{:S(2)}) collective-permute-start(bf16[768,512]{0,1:T(8,128)(2,1)S(1)} %fusion.11), channel_id=1, source_target_pairs={{0,1},{1,0},{2,3},{3,2},{4,5},{5,4},{6,7},{7,6},{8,9},{9,8},{10,11... | collective-permute-start | bytes 2359304 | tf_op jit(solution)/shard_map/ppermute | solution.py:16
  124.1 6.4 %copy-start.3 = (bf16[1,1,768,768]{3,2,1,0:T(8,128)(2,1)S(1)}, bf16[1,1,768,768]{3,2,1,0:T(8,128)(2,1)}, u32[]{:S(2)}) copy-start(bf16[1,1,768,768]{3,2,1,0:T(8,128)(2,1)} %param.15) | copy-start | bytes 3538948
  130.5 2.6 %copy-start.6 = (bf16[1,1,768,768]{2,3,1,0:T(8,128)(2,1)S(1)}, bf16[1,1,768,768]{2,3,1,0:T(8,128)(2,1)}, u32[]{:S(2)}) copy-start(bf16[1,1,768,768]{2,3,1,0:T(8,128)(2,1)} %copy.22) | copy-start | bytes 3538948
  130.5 2.6 %copy-start.9 = (bf16[768,512]{0,1:T(8,128)(2,1)S(1)}, bf16[768,512]{0,1:T(8,128)(2,1)}, u32[]{:S(2)}) copy-start(bf16[768,512]{0,1:T(8,128)(2,1)} %add_convert_fusion) | copy-start | bytes 2359300
  130.5 2.6 %copy-start.10 = (bf16[768,256]{0,1:T(8,128)(2,1)S(1)}, bf16[768,256]{0,1:T(8,128)(2,1)}, u32[]{:S(2)}) copy-start(bf16[768,256]{0,1:T(8,128)(2,1)} %copy.29) | copy-start | bytes 1179652
  130.6 2.6 %copy-start.21 = (bf16[768,768]{1,0:T(8,128)(2,1)S(1)}, bf16[768,768]{1,0:T(8,128)(2,1)}, u32[]{:S(2)}) copy-start(bf16[768,768]{1,0:T(8,128)(2,1)} %convolution_convert_fusion) | copy-start | bytes 3538948

commit v6 on v3

--- a/solution.py
+++ b/solution.py
@@ -66,8 +66,8 @@
     assert freqs == momenta
     momentum = lax.axis_index("mom")
     channel = lax.axis_index("spin")
-    coef_self = jnp.take(jnp.array(COEF_SELF, jnp.float32), channel)
-    coef_pair = jnp.take(jnp.array(COEF_PAIR, jnp.float32), channel)
+    coef_self = sum(jnp.where(channel == c, jnp.float32(v), 0.0) for c, v in enumerate(COEF_SELF))
+    coef_pair = sum(jnp.where(channel == c, jnp.float32(v), 0.0) for c, v in enumerate(COEF_PAIR))
 
     blocks = current.reshape(freqs, forms, order_len)
     expand = block_rows(order_len, freqs)
@@ -81,15 +81,12 @@
     stacked = jnp.stack(packs)
     mix = jnp.concatenate(mixes, axis=1)
 
-    bubble_tall = bubble_mat.reshape(order_len, forms)
-    block_mask = exact_dot(expand, expand.T)
-    bubble_full = exact_dot(bubble_tall, forms_expand.T) * block_mask
+    def carry_of(mat, bubble_mat):
+        bubble_tall = bubble_mat.reshape(order_len, forms)
+        block_mask = exact_dot(expand, expand.T)
+        bubble_full = exact_dot(bubble_tall, forms_expand.T) * block_mask
+        return bubble_full, exact_dot(bubble_full, mat)
 
-    def carry_of(mat):
-        return exact_dot(bubble_full, mat)
-
-    carried = carry_of(current)
-    bare_part = jnp.dot(bare_mat, carried, preferred_element_type=jnp.float32)
 
     width = order_len // NCHUNK
     red_chunks = []
@@ -99,14 +96,23 @@
         summed = jnp.dot(
             mix, received.reshape(2 * order_len, width), preferred_element_type=jnp.float32
         ).astype(jnp.bfloat16)
+        if k + 1 == NCHUNK:
+            sums = [pair[0] for pair in red_chunks]
+            summed, current, bubble_mat, sums = lax.optimization_barrier(
+                (summed, current, bubble_mat, sums)
+            )
+            red_chunks = [(sums[c], red_chunks[c][1]) for c in range(k)]
+            bubble_full, carried = carry_of(current, bubble_mat)
+            bare_part = jnp.dot(bare_mat, carried, preferred_element_type=jnp.float32)
         if k + 1 < NCHUNK:
             summed, pieces[k + 1] = lax.optimization_barrier((summed, pieces[k + 1]))
-        other = partner_2(summed, "spin", 0)
-        red_chunks.append(
-            (coef_self * summed.astype(jnp.float32) + coef_pair * other.astype(jnp.float32)).astype(
-                jnp.bfloat16
-            )
+        red_chunks.append((summed, partner_2(summed, "spin", 0)))
+    red_chunks = [
+        (coef_self * summed.astype(jnp.float32) + coef_pair * other.astype(jnp.float32)).astype(
+            jnp.bfloat16
         )
+        for summed, other in red_chunks
+    ]
     reducible = jnp.concatenate(red_chunks, axis=1)
     base_sum = bare_mat.astype(jnp.float32) + reducible.astype(jnp.float32)
 
@@ -116,7 +122,7 @@
         total = total + jnp.dot(red_chunks[k], carried[rows], preferred_element_type=jnp.float32)
     current = total.astype(jnp.bfloat16)
     for inner_step in range(1, INNER):
-        carried = carry_of(current)
+        carried = exact_dot(bubble_full, current)
         total = base_sum + jnp.dot(bare_mat, carried, preferred_element_type=jnp.float32)
         total = total + jnp.dot(reducible, carried, preferred_element_type=jnp.float32)
         current = total.astype(jnp.bfloat16)

time: 125 us -> 129 us (1.032)
  waiting for transfers between devices: 46.1 us -> 53.9 us
  matrix products: 34.7 us -> 32.5 us
    all_to_all x2, waiting for transfers between devices: 29.3 us -> 38.2 us  [local(): lax.all_to_all(pieces[k], 'mom', split_axis=1, concat_axis=1, tiled=True)]
    another operation x3 -> x0, local copies, waits for them, and re-layouts: 1.43 us -> none  [the longest x1 0.59 us: local(): coef_self = jnp.take(jnp.array(COEF_SELF, jnp.float32), channel)]
  transfers between devices with their start and end apart: 4 -> 4, of which waited for: 4 -> 3; matrix products, arithmetic and copies ran while one was open for 22% -> 19% of each run, Pallas kernels for 0% -> 0%
where the time goes in v6:
time: 129 us
  waiting for transfers between devices  53.9 us (42%)
  matrix products  32.5 us (25%)
  starting transfers between devices  18.7 us (14%)
  local copies, waits for them, and re-layouts  17.2 us (13%)
  other arithmetic  5.86 us (5%)
    all_to_all x2, waiting for transfers between devices, local(): lax.all_to_all(pieces[k], 'mom', split_axis=1, concat_axis=1, tiled=True)  38.2 us
    dot_general x8, matrix products, exact_dot(): jnp.dot(a, b, preferred_element_type=jnp.float32).astype(jnp.bfloat16)  17.3 us
    ppermute x2, waiting for transfers between devices, partner_2(): return lax.ppermute(value, axis, pairs)  15.7 us
    all_to_all x2, starting transfers between devices, local(): lax.all_to_all(pieces[k], 'mom', split_axis=1, concat_axis=1, tiled=True)  15.3 us
    dot_general x2, matrix products, local(): jnp.dot(mix, received.reshape(2 * order_len, width), preferred_element_ty...  7.25 us
    ppermute x2, starting transfers between devices, partner_2(): return lax.ppermute(value, axis, pairs)  3.35 us
    convert_element_type x2, other arithmetic, local(): (coef_self * summed.astype(jnp.float32) + coef_pair * other.astype(jnp.fl...  3.02 us
  transfers between devices with their start and end apart: 4, of which 3 were waited for; matrix products, arithmetic and copies ran while one was open for 19% of the time, Pallas kernels for 0%

profile of v6, /device:TPU:1, one launch (start us, length us, event | category | flops | bytes accessed | tf_op | source)
XLA Modules:
  0.0 128.6 jit_solution(7828984554516273655)
XLA Ops:
  0.0 0.8 slice_bitcast_fusion
  0.8 0.1 select_reduce_fusion.1
  0.9 0.1 select_reduce_fusion
  1.1 2.2 %reshape_squeeze.3 = bf16[64,12,768]{2,1,0:T(8,128)(2,1)S(1)} reshape(bf16[1,1,768,768]{3,2,1,0:T(8,128)(2,1)} %param.12) | data formatting | bytes 2359296 | tf_op jit(solution)/shard_map/reshape;squeeze | solution.py:72
  3.3 0.6 gather_fusion.3
  3.9 1.8 %gather_fusion.2 = bf16[64,12,768]{2,1,0:T(8,128)(2,1)} fusion(bf16[64,12,768]{2,1,0:T(8,128)(2,1)S(1)} %reshape_squeeze.3, s32[1024]{0:T(1024)S(1)} %pad_clamp_fusion.1), kind=kCustom, calls=%fused_computation.1.clone | custom fusion | bytes 2359552 | tf_op jit(solution)/shard_map/jit(_take)/gather | solution.py:79
  5.7 1.6 %select_bitcast_fusion.1 = bf16[1,64,12,768]{3,2,1,0:T(8,128)(2,1)S(1)} fusion(bf16[64,12,768]{2,1,0:T(8,128)(2,1)} %gather_fusion.2, pred[64]{0:T(512)(128)(4,1)S(1)} %get-tuple-element.46), kind=kLoop, calls=%fused_computation.18 | loop fusion | flops 589824 | bytes 2359360 | tf_op jit(solution)/shard_map/stack | solution.py:81
  7.3 0.2 select_bitcast_fusion
  7.6 0.4 pad_maximum_fusion.1
  8.0 2.2 %copy.14 = bf16[2,64,12,384]{3,0,2,1:T(2,128)(2,1)} copy(bf16[2,64,12,384]{3,2,1,0:T(8,128)(2,1)S(1)} %get-tuple-element.34) | data formatting | bytes 2359296 | tf_op jit(solution)/shard_map/slice | solution.py:93
  10.2 0.0 copy-start.4
  10.2 0.0 copy-start.7
  10.2 0.0 copy-start.6
  10.2 10.6 %all-to-all-start = ((bf16[2,64,12,384]{3,0,2,1:T(2,128)(2,1)}), bf16[2,64,12,384]{3,0,2,1:T(2,128)(2,1)}, u32[]{:S(2)}, u32[]{:S(2)}) async-start(bf16[2,64,12,384]{3,0,2,1:T(2,128)(2,1)} %copy.14), calls=%async_computation | async-start | bytes 2359296 | tf_op jit(solution)/shard_map/all_to_all | solution.py:95
  20.9 0.0 copy-done.4
  20.9 0.0 copy-done.7
  20.9 0.1 select_reduce_fusion.4
  21.0 0.1 select_reduce_fusion.2
  21.2 0.8 gather_fusion.1
  22.0 0.8 gather_fusion
  22.8 0.0 copy-done.6
  22.9 1.0 convolution_convert_fusion.7
  23.9 2.0 %convolution_convert_fusion.6 = bf16[768,768]{0,1:T(8,128)(2,1)} fusion(s32[768]{0:T(1024)S(1)} %get-tuple-element.47, s32[768]{0:T(1024)S(1)} %get-tuple-element.48, pred[768]{0:T(1024)(128)(4,1)S(1)} %fusion.59, bf16[1,12,12]{2,0,1:T(2,128)(2,1)S(1)} %get-tuple-element.38), kind=kOutput, calls=%fused_computation.25 | convolution fusion | flops 15012864 | bytes 1186848 | tf_op jit(solution)/shard_map/dot_general | solution.py:48
  25.9 2.1 %fusion.8 = bf16[768,768]{0,1:T(8,128)(2,1)} fusion(bf16[768,768]{0,1:T(8,128)(2,1)S(1)} %convolution_convert_fusion.7, s32[768]{0:T(1024)S(1)} %get-tuple-element.49, s32[768]{0:T(1024)S(1)} %get-tuple-element.50, pred[768]{0:T(1024)(128)(4,1)S(1)} %fusion.60, s32[64]{0:T(128)S(1)} %and_select_fusion.1), kind=kOutput, calls=%fused_computation.29 | convolution fusion | flops 84987904 | bytes 2366464 | tf_op jit(solution)/shard_map/dot_general | solution.py:48
  28.0 3.4 %fusion.9 = bf16[768,768]{0,1:T(8,128)(2,1)} fusion(bf16[768,768]{0,1:T(8,128)(2,1)} %convolution_convert_fusion.6, s32[768]{0:T(1024)S(1)} %get-tuple-element.49, s32[768]{0:T(1024)S(1)} %get-tuple-element.50, pred[768]{0:T(1024)(128)(4,1)S(1)} %fusion.60, s32[64]{0:T(128)S(1)} %and_select_fusion), kind=kOutput, calls=%fused_computation.30 | convolution fusion | flops 84987904 | bytes 2366464 | tf_op jit(solution)/shard_map/dot_general | solution.py:48
  31.4 9.1 %all-to-all-done = bf16[2,64,12,384]{3,0,2,1:T(2,128)(2,1)} async-done(((bf16[2,64,12,384]{3,0,2,1:T(2,128)(2,1)}), bf16[2,64,12,384]{3,0,2,1:T(2,128)(2,1)}, u32[]{:S(2)}, u32[]{:S(2)}) %all-to-all-start) | async-done | bytes 1179680 | tf_op jit(solution)/shard_map/all_to_all | solution.py:95
  40.5 1.5 %copy.15 = bf16[2,64,12,384]{3,2,1,0:T(8,128)(2,1)S(1)} copy(bf16[2,64,12,384]{3,0,2,1:T(2,128)(2,1)} %all-to-all-done) | data formatting | bytes 2359296 | tf_op jit(solution)/shard_map/all_to_all | solution.py:95
  42.0 1.2 reshape.24
  43.2 3.4 %fusion.12 = bf16[768,384]{1,0:T(8,128)(2,1)S(1)} fusion(bf16[1536,384]{1,0:T(8,128)(2,1)} %reshape.24, bf16[768,768]{0,1:T(8,128)(2,1)} %fusion.9, bf16[768,768]{0,1:T(8,128)(2,1)} %fusion.8), kind=kOutput, calls=%fused_computation.33 | convolution fusion | flops 910983168 | bytes 4128768 | tf_op jit(solution)/shard_map/dot_general | solution.py:96
  46.6 2.2 %copy.16 = bf16[2,64,12,384]{3,0,2,1:T(2,128)(2,1)} copy(bf16[2,64,12,384]{3,2,1,0:T(8,128)(2,1)S(1)} %get-tuple-element.14) | data formatting | bytes 2359296 | tf_op jit(solution)/shard_map/optimization_barrier | solution.py:108
  48.8 4.7 %all-to-all-start.1 = ((bf16[2,64,12,384]{3,0,2,1:T(2,128)(2,1)}), bf16[2,64,12,384]{3,0,2,1:T(2,128)(2,1)S(1)}, u32[]{:S(2)}, u32[]{:S(2)}) async-start(bf16[2,64,12,384]{3,0,2,1:T(2,128)(2,1)} %copy.16), calls=%async_computation.1 | async-start | bytes 2359296 | tf_op jit(solution)/shard_map/all_to_all | solution.py:95
  53.5 3.3 %collective-permute-start = (bf16[768,384]{1,0:T(8,128)(2,1)S(1)}, bf16[768,384]{1,0:T(8,128)(2,1)}, u32[]{:S(2)}, u32[]{:S(2)}) collective-permute-start(bf16[768,384]{1,0:T(8,128)(2,1)S(1)} %fusion.12), channel_id=1, source_target_pairs={{0,1},{1,0},{2,3},{3,2},{4,5},{5,4},{6,7},{7,6},{8,9},{9,8},{10,11... | collective-permute-start | bytes 1769480 | tf_op jit(solution)/shard_map/ppermute | solution.py:16
  56.8 29.1 %all-to-all-done.1 = bf16[2,64,12,384]{3,0,2,1:T(2,128)(2,1)S(1)} async-done(((bf16[2,64,12,384]{3,0,2,1:T(2,128)(2,1)}), bf16[2,64,12,384]{3,0,2,1:T(2,128)(2,1)S(1)}, u32[]{:S(2)}, u32[]{:S(2)}) %all-to-all-start.1) | async-done | bytes 1179680 | tf_op jit(solution)/shard_map/all_to_all | solution.py:95
  85.9 0.2 copy.17
  86.2 0.0 copy-start
  86.2 1.2 reshape.25
  87.3 0.5 copy-done
  87.9 0.0 copy-start.5
  87.9 3.9 %fusion.13 = bf16[768,384]{1,0:T(8,128)(2,1)} fusion(bf16[1536,384]{1,0:T(8,128)(2,1)} %reshape.25, bf16[768,768]{0,1:T(8,128)(2,1)} %fusion.9, bf16[768,768]{0,1:T(8,128)(2,1)S(1)} %copy-done), kind=kOutput, calls=%fused_computation.34 | convolution fusion | flops 910983168 | bytes 4128768 | tf_op jit(solution)/shard_map/dot_general | solution.py:96
  91.7 0.0 copy-done.5
  91.7 0.2 copy.18
  91.9 0.3 reshape.26
  92.2 0.1 collective-permute-start.1
  92.3 1.3 convolution_convert_fusion.5
  93.6 0.0 copy-start.2
  93.6 1.0 fusion.10
  94.6 0.2 copy-done.2
  94.8 1.1 convolution_convert_fusion.1
  95.9 0.0 copy-done.1
  95.9 0.0 copy-start.3
  96.0 0.0 collective-permute-done
  96.0 1.7 %add_convert_fusion.1 = bf16[768,384]{1,0:T(8,128)(2,1)S(1)} fusion(bf16[768,384]{1,0:T(8,128)(2,1)} %collective-permute-done, bf16[768,384]{1,0:T(8,128)(2,1)S(1)} %fusion.12, f32[]{:T(128)S(6)} %add.80, f32[]{:T(128)S(6)} %add.76), kind=kLoop, calls=%fused_computation.40 | loop fusion | flops 1769472 | bytes 1769480 | tf_op jit(solution)/shard_map/convert_element_type | solution.py:111
  97.7 0.0 copy-start.8
  97.7 0.8 fusion.20
  98.5 0.0 copy-done.3
  98.5 0.5 copy-done.8
  99.0 2.5 %fusion.14 = f32[768,768]{0,1:T(8,128)} fusion(bf16[768,768]{1,0:T(8,128)(2,1)S(1)} %convolution_convert_fusion.1, bf16[1,1,768,768]{3,2,1,0:T(8,128)(2,1)S(1)} %copy-done.8), kind=kOutput, calls=%fused_computation.36 | convolution fusion | flops 905969664 | bytes 4718592 | tf_op jit(solution)/shard_map/dot_general | solution.py:106
  101.5 15.7 %collective-permute-done.1 = bf16[768,384]{1,0:T(8,128)(2,1)S(1)} collective-permute-done((bf16[768,384]{1,0:T(8,128)(2,1)}, bf16[768,384]{1,0:T(8,128)(2,1)S(1)}, u32[]{:S(2)}, u32[]{:S(2)}) %collective-permute-start.1) | collective-permute-done | bytes 589856 | tf_op jit(solution)/shard_map/ppermute | solution.py:16
  117.1 1.3 %add_convert_fusion = bf16[768,384]{1,0:T(8,128)(2,1)S(1)} fusion(bf16[768,384]{1,0:T(8,128)(2,1)S(1)} %collective-permute-done.1, bf16[768,384]{1,0:T(8,128)(2,1)} %fusion.13, f32[]{:T(128)S(6)} %add.80, f32[]{:T(128)S(6)} %add.76), kind=kLoop, calls=%fused_computation.39 | loop fusion | flops 1769472 | bytes 1769480 | tf_op jit(solution)/shard_map/convert_element_type | solution.py:111
  118.5 5.4 %convolution_convert_fusion = bf16[768,768]{1,0:T(8,128)(2,1)} fusion(bf16[768,768]{1,0:T(8,128)(2,1)} %copy-done.1, f32[768,768]{1,0:T(8,128)S(1)} %fusion.20, f32[768,768]{0,1:T(8,128)} %fusion.14, bf16[768,384]{1,0:T(8,128)(2,1)S(1)} %add_convert_fusion, bf16[1,1,768,768]{3,2,1,0:T(8,128)(2,1)} %param.13, bf16[768,384]{1,0:T(8,128)(2,1)S(1)} %add_convert_fusion.1, ...), kind=kOutput, calls=%fused_computation.19 | convolution fusion | flops 1365442560 | bytes 10616832 | tf_op jit(solution)/shard_map/dot_general | solution.py:48
  123.8 2.5 %fusion.17 = f32[768,768]{1,0:T(8,128)S(1)} fusion(bf16[768,768]{1,0:T(8,128)(2,1)} %convolution_convert_fusion, bf16[768,384]{1,0:T(8,128)(2,1)S(1)} %add_convert_fusion, bf16[768,384]{1,0:T(8,128)(2,1)S(1)} %add_convert_fusion.1), kind=kOutput, calls=%fused_computation.45 | convolution fusion | flops 908328960 | bytes 4718592 | tf_op jit(solution)/shard_map/dot_general | solution.py:127
  126.3 0.0 copy-done.9
  126.4 0.0 copy-done.10
  126.4 2.2 %fusion.11 = bf16[1,1,768,768]{3,2,1,0:T(8,128)(2,1)} fusion(f32[768,768]{1,0:T(8,128)S(1)} %fusion.17, bf16[768,768]{1,0:T(8,128)(2,1)S(1)} %copy-done.10, bf16[1,1,768,768]{3,2,1,0:T(8,128)(2,1)S(1)} %copy-done.9, bf16[768,384]{1,0:T(8,128)(2,1)S(1)} %add_convert_fusion, bf16[768,384]{1,0:T(8,128)(2,1)S(1)} %add_convert_fusion.1), kind=kOutput, calls=%fused_computation.32 | convolution fusion | flops 911278080 | bytes 7077888 | tf_op jit(solution)/shard_map/dot_general | solution.py:126
  (21 shorter events, 0.2 us)
Async XLA Ops:
  10.2 10.6 %copy-start.4 = (s32[2,64,64]{2,1,0:T(8,128)S(1)}, s32[2,64,64]{2,1,0:T(8,128)}, u32[]{:S(2)}) copy-start(s32[2,64,64]{2,1,0:T(8,128)} %param.16) | copy-start | bytes 98308
  10.2 10.7 %copy-start.7 = (s32[2,64]{1,0:T(2,128)S(1)}, s32[2,64]{1,0:T(2,128)}, u32[]{:S(2)}) copy-start(s32[2,64]{1,0:T(2,128)} %param.17) | copy-start | bytes 1540
  10.2 12.6 %copy-start.6 = (bf16[2,12,12]{2,0,1:T(2,128)(2,1)S(1)}, bf16[2,12,12]{2,0,1:T(2,128)(2,1)}, u32[]{:S(2)}) copy-start(bf16[2,12,12]{2,0,1:T(2,128)(2,1)} %param.15) | copy-start | bytes 1732
  10.2 30.3 %all-to-all-start = ((bf16[2,64,12,384]{3,0,2,1:T(2,128)(2,1)}), bf16[2,64,12,384]{3,0,2,1:T(2,128)(2,1)}, u32[]{:S(2)}, u32[]{:S(2)}) async-start(bf16[2,64,12,384]{3,0,2,1:T(2,128)(2,1)} %copy.14), calls=%async_computation | async-start | bytes 2359296 | tf_op jit(solution)/shard_map/all_to_all | solution.py:95
  48.8 37.1 %all-to-all-start.1 = ((bf16[2,64,12,384]{3,0,2,1:T(2,128)(2,1)}), bf16[2,64,12,384]{3,0,2,1:T(2,128)(2,1)S(1)}, u32[]{:S(2)}, u32[]{:S(2)}) async-start(bf16[2,64,12,384]{3,0,2,1:T(2,128)(2,1)} %copy.16), calls=%async_computation.1 | async-start | bytes 2359296 | tf_op jit(solution)/shard_map/all_to_all | solution.py:95
  53.5 42.4 %collective-permute-start = (bf16[768,384]{1,0:T(8,128)(2,1)S(1)}, bf16[768,384]{1,0:T(8,128)(2,1)}, u32[]{:S(2)}, u32[]{:S(2)}) collective-permute-start(bf16[768,384]{1,0:T(8,128)(2,1)S(1)} %fusion.12), channel_id=1, source_target_pairs={{0,1},{1,0},{2,3},{3,2},{4,5},{5,4},{6,7},{7,6},{8,9},{9,8},{10,11... | collective-permute-start | bytes 1769480 | tf_op jit(solution)/shard_map/ppermute | solution.py:16
  86.2 1.7 %copy-start = (bf16[768,768]{0,1:T(8,128)(2,1)S(1)}, bf16[768,768]{0,1:T(8,128)(2,1)}, u32[]{:S(2)}) copy-start(bf16[768,768]{0,1:T(8,128)(2,1)} %fusion.8) | copy-start | bytes 3538948
  87.9 3.9 %copy-start.5 = (bf16[1,1,64,12,12]{2,4,3,1,0:T(8,128)(2,1)S(1)}, bf16[1,1,64,12,12]{2,4,3,1,0:T(8,128)(2,1)}, u32[]{:S(2)}) copy-start(bf16[1,1,64,12,12]{2,4,3,1,0:T(8,128)(2,1)} %param.14) | copy-start | bytes 55300
  92.2 25.0 %collective-permute-start.1 = (bf16[768,384]{1,0:T(8,128)(2,1)}, bf16[768,384]{1,0:T(8,128)(2,1)S(1)}, u32[]{:S(2)}, u32[]{:S(2)}) collective-permute-start(bf16[768,384]{1,0:T(8,128)(2,1)} %fusion.13), channel_id=1, source_target_pairs={{0,1},{1,0},{2,3},{3,2},{4,5},{5,4},{6,7},{7,6},{8,9},{9,8},{10,11... | collective-permute-start | bytes 1769480 | tf_op jit(solution)/shard_map/ppermute | solution.py:16
  93.6 1.3 copy-start.2
  94.8 1.1 copy-start.1
  95.9 2.5 %copy-start.3 = (bf16[768,768]{1,0:T(8,128)(2,1)}, bf16[768,768]{1,0:T(8,128)(2,1)S(1)}, u32[]{:S(2)}) copy-start(bf16[768,768]{1,0:T(8,128)(2,1)S(1)} %convolution_convert_fusion.1) | copy-start | bytes 3538948
  97.7 1.3 copy-start.8
  123.8 2.5 %copy-start.9 = (bf16[1,1,768,768]{3,2,1,0:T(8,128)(2,1)S(1)}, bf16[1,1,768,768]{3,2,1,0:T(8,128)(2,1)}, u32[]{:S(2)}) copy-start(bf16[1,1,768,768]{3,2,1,0:T(8,128)(2,1)} %param.13) | copy-start | bytes 3538948
  123.8 2.5 %copy-start.10 = (bf16[768,768]{1,0:T(8,128)(2,1)S(1)}, bf16[768,768]{1,0:T(8,128)(2,1)}, u32[]{:S(2)}) copy-start(bf16[768,768]{1,0:T(8,128)(2,1)} %convolution_convert_fusion) | copy-start | bytes 3538948

commit v7 on v3

--- a/solution.py
+++ b/solution.py
@@ -69,16 +69,18 @@
     coef_self = jnp.take(jnp.array(COEF_SELF, jnp.float32), channel)
     coef_pair = jnp.take(jnp.array(COEF_PAIR, jnp.float32), channel)
 
-    blocks = current.reshape(freqs, forms, order_len)
     expand = block_rows(order_len, freqs)
     forms_expand = form_rows(order_len, forms)
-    packs = []
+    same_form = exact_dot(forms_expand, forms_expand.T)
+    idx = jnp.arange(freqs, dtype=jnp.int32)
+    selects = []
     mixes = []
     for r in range(2):
         send_order, recv_slots = crossing_plan(cross_tables[r], freq_perm[r], momentum, freqs)
-        packs.append(jnp.take(blocks, send_order, axis=0))
+        onehot = (send_order[:, None] == idx[None, :]).astype(jnp.bfloat16)
+        selects.append(exact_dot(exact_dot(expand, onehot), expand.T) * same_form)
         mixes.append(mix_matrix(recv_slots, form_mix[r], freqs, expand, forms_expand))
-    stacked = jnp.stack(packs)
+    select = jnp.concatenate(selects, axis=0)
     mix = jnp.concatenate(mixes, axis=1)
 
     bubble_tall = bubble_mat.reshape(order_len, forms)
@@ -93,7 +95,10 @@
 
     width = order_len // NCHUNK
     red_chunks = []
-    pieces = [stacked[..., k * width:(k + 1) * width] for k in range(NCHUNK)]
+    pieces = [
+        exact_dot(select, current[:, k * width:(k + 1) * width]).reshape(2, freqs, forms, width)
+        for k in range(NCHUNK)
+    ]
     for k in range(NCHUNK):
         received = lax.all_to_all(pieces[k], "mom", split_axis=1, concat_axis=1, tiled=True)
         summed = jnp.dot(

time: 125 us -> 130 us (1.040)
  matrix products: 34.7 us -> 46.7 us
  waiting for transfers between devices: 46.1 us -> 40.7 us
  other arithmetic: 5.6 us -> 3.3 us
    dot_general x8 -> x13, matrix products: 18.2 us -> 30.2 us  [exact_dot(): jnp.dot(a, b, preferred_element_type=jnp.float32).astype(jnp.bfloat16)]
    reshape x0 -> x3, local copies, waits for them, and re-layouts: none -> 6.61 us  [local(): exact_dot(select, current[:, k * width:(k + 1) * width])]
    all_to_all x2, waiting for transfers between devices: 29.3 us -> 23.5 us  [local(): lax.all_to_all(pieces[k], 'mom', split_axis=1, concat_axis=1, tiled=True)]
    gather x2 -> x0, local copies, waits for them, and re-layouts: 2.45 us -> none  [local(): packs.append(jnp.take(blocks, send_order, axis=0))]
    another operation x3 -> x0, other arithmetic: 2.27 us -> none  [local(): stacked = jnp.stack(packs)]
    slice x1 -> x0, local copies, waits for them, and re-layouts: 2.23 us -> none  [local(): pieces = [stacked[..., k * width:(k + 1) * width] for k in range(NCHUNK)]]
    another operation x1 -> x0, local copies, waits for them, and re-layouts: 2.16 us -> none  [local(): blocks = current.reshape(freqs, forms, order_len)]
  transfers between devices with their start and end apart: 4 -> 4, of which waited for: 4 -> 4; matrix products, arithmetic and copies ran while one was open for 22% -> 26% of each run, Pallas kernels for 0% -> 0%
where the time goes in v7:
time: 130 us; the launch traced here: 129 us
  matrix products  46.7 us (36%)
  waiting for transfers between devices  40.7 us (31%)
  starting transfers between devices  19.1 us (15%)
  local copies, waits for them, and re-layouts  17.8 us (14%)
  other arithmetic  3.3 us (3%)
  between operations  1.51 us (1%)
    dot_general x13, matrix products, exact_dot(): jnp.dot(a, b, preferred_element_type=jnp.float32).astype(jnp.bfloat16)  30.2 us
    all_to_all x2, waiting for transfers between devices, local(): lax.all_to_all(pieces[k], 'mom', split_axis=1, concat_axis=1, tiled=True)  23.5 us
    ppermute x2, waiting for transfers between devices, partner_2(): return lax.ppermute(value, axis, pairs)  17.2 us
    all_to_all x2, starting transfers between devices, local(): lax.all_to_all(pieces[k], 'mom', split_axis=1, concat_axis=1, tiled=True)  16.2 us
    dot_general x2, matrix products, local(): jnp.dot(mix, received.reshape(2 * order_len, width), preferred_element_ty...  7.42 us
    reshape x3, local copies, waits for them, and re-layouts, local(): exact_dot(select, current[:, k * width:(k + 1) * width])  6.61 us
    ppermute x2, starting transfers between devices, partner_2(): return lax.ppermute(value, axis, pairs)  2.99 us
    convert_element_type x2, other arithmetic, local(): (coef_self * summed.astype(jnp.float32) + coef_pair * other.astype(jnp.fl...  2.76 us
  transfers between devices with their start and end apart: 4, of which 4 were waited for; matrix products, arithmetic and copies ran while one was open for 26% of the time, Pallas kernels for 0%

profile of v7, /device:TPU:1, one launch (start us, length us, event | category | flops | bytes accessed | tf_op | source)
XLA Modules:
  0.0 129.1 jit_solution(4343377379425876571)
XLA Ops:
  0.0 0.8 slice_bitcast_fusion.1
  0.8 0.1 select_reduce_fusion.1
  1.0 0.1 select_reduce_fusion
  1.1 1.0 convolution_convert_fusion.6
  2.1 1.3 %fusion.10 = bf16[768,768]{1,0:T(8,128)(2,1)S(1)} fusion(bf16[768,768]{1,0:T(8,128)(2,1)S(1)} %convolution_convert_fusion.6, s32[768]{0:T(1024)S(1)} %get-tuple-element.72, s32[768]{0:T(1024)S(1)} %get-tuple-element.73, pred[768]{0:T(1024)(128)(4,1)S(1)} %fusion.83, s32[64]{0:T(128)S(1)} %select_reduce_fusion.1), kind=kOutput, calls=%fused_computation.30 | convolution fusion | flops 84987904 | bytes 2366464 | tf_op jit(solution)/shard_map/dot_general | solution.py:48
  3.4 2.3 %fusion.11 = bf16[768,768]{1,0:T(8,128)(2,1)} fusion(bf16[768,768]{1,0:T(8,128)(2,1)S(1)} %convolution_convert_fusion.6, s32[768]{0:T(1024)S(1)} %get-tuple-element.72, s32[768]{0:T(1024)S(1)} %get-tuple-element.73, pred[768]{0:T(1024)(128)(4,1)S(1)} %fusion.83, s32[64]{0:T(128)S(1)} %select_reduce_fusion), kind=kOutput, calls=%fused_computation.31 | convolution fusion | flops 84987904 | bytes 2366464 | tf_op jit(solution)/shard_map/dot_general | solution.py:48
  5.8 3.8 %convolution_convert_fusion.1 = bf16[1536,384]{1,0:T(8,128)(2,1)} fusion(bf16[768,768]{1,0:T(8,128)(2,1)} %fusion.11, bf16[768,768]{1,0:T(8,128)(2,1)S(1)} %fusion.10, bf16[768,768]{1,0:T(8,128)(2,1)} %bitcast.74), kind=kOutput, calls=%fused_computation.3 | convolution fusion | flops 911278080 | bytes 4128768 | tf_op jit(solution)/shard_map/dot_general | solution.py:48
  9.6 2.2 %reshape.25 = bf16[2,64,12,384]{3,2,1,0:T(8,128)(2,1)S(1)} reshape(bf16[1536,384]{1,0:T(8,128)(2,1)} %convolution_convert_fusion.1) | data formatting | bytes 2359296 | tf_op jit(solution)/shard_map/reshape | solution.py:99
  11.8 2.3 %copy.20 = bf16[2,64,12,384]{3,0,2,1:T(2,128)(2,1)} copy(bf16[2,64,12,384]{3,2,1,0:T(8,128)(2,1)S(1)} %reshape.25) | data formatting | bytes 2359296 | tf_op jit(solution)/shard_map/reshape | solution.py:99
  14.0 10.6 %all-to-all-start = ((bf16[2,64,12,384]{3,0,2,1:T(2,128)(2,1)}), bf16[2,64,12,384]{3,0,2,1:T(2,128)(2,1)}, u32[]{:S(2)}, u32[]{:S(2)}) async-start(bf16[2,64,12,384]{3,0,2,1:T(2,128)(2,1)} %copy.20), calls=%async_computation | async-start | bytes 2359296 | tf_op jit(solution)/shard_map/all_to_all | solution.py:103
  24.7 0.0 copy-done.2
  24.7 0.0 copy-start.7
  24.7 3.5 %convolution_convert_fusion = bf16[1536,384]{1,0:T(8,128)(2,1)} fusion(bf16[768,768]{1,0:T(8,128)(2,1)S(1)} %copy-done.2, bf16[768,768]{1,0:T(8,128)(2,1)S(1)} %fusion.10, bf16[768,768]{1,0:T(8,128)(2,1)} %bitcast.75), kind=kOutput, calls=%fused_computation.2 | convolution fusion | flops 911278080 | bytes 4128768 | tf_op jit(solution)/shard_map/dot_general | solution.py:48
  28.2 0.0 copy-done.7
  28.2 0.1 select_reduce_fusion.2
  28.3 0.1 select_reduce_fusion.4
  28.4 0.0 copy-start.4
  28.4 0.0 copy-start.6
  28.4 2.2 %reshape.27 = bf16[2,64,12,384]{3,2,1,0:T(8,128)(2,1)S(1)} reshape(bf16[1536,384]{1,0:T(8,128)(2,1)} %convolution_convert_fusion) | data formatting | bytes 2359296 | tf_op jit(solution)/shard_map/reshape | solution.py:99
  30.7 0.0 copy-done.4
  30.7 0.8 gather_fusion
  31.5 0.8 gather_fusion.1
  32.3 0.0 copy-done.6
  32.3 1.0 convolution_convert_fusion.12
  33.3 2.0 %convolution_convert_fusion.11 = bf16[768,768]{0,1:T(8,128)(2,1)} fusion(s32[768]{0:T(1024)S(1)} %get-tuple-element.70, s32[768]{0:T(1024)S(1)} %get-tuple-element.71, pred[768]{0:T(1024)(128)(4,1)S(1)} %fusion.82, bf16[1,12,12]{2,0,1:T(2,128)(2,1)S(1)} %get-tuple-element.67), kind=kOutput, calls=%fused_computation.23 | convolution fusion | flops 15012864 | bytes 1186848 | tf_op jit(solution)/shard_map/dot_general | solution.py:48
  35.4 2.1 %fusion.8 = bf16[768,768]{0,1:T(8,128)(2,1)} fusion(bf16[768,768]{0,1:T(8,128)(2,1)S(1)} %convolution_convert_fusion.12, s32[768]{0:T(1024)S(1)} %get-tuple-element.72, s32[768]{0:T(1024)S(1)} %get-tuple-element.73, pred[768]{0:T(1024)(128)(4,1)S(1)} %fusion.83, s32[64]{0:T(128)S(1)} %and_select_fusion.1), kind=kOutput, calls=%fused_computation.28 | convolution fusion | flops 84987904 | bytes 2366464 | tf_op jit(solution)/shard_map/dot_general | solution.py:48
  37.5 3.4 %fusion.9 = bf16[768,768]{0,1:T(8,128)(2,1)} fusion(bf16[768,768]{0,1:T(8,128)(2,1)} %convolution_convert_fusion.11, s32[768]{0:T(1024)S(1)} %get-tuple-element.72, s32[768]{0:T(1024)S(1)} %get-tuple-element.73, pred[768]{0:T(1024)(128)(4,1)S(1)} %fusion.83, s32[64]{0:T(128)S(1)} %and_select_fusion), kind=kOutput, calls=%fused_computation.29 | convolution fusion | flops 84987904 | bytes 2366464 | tf_op jit(solution)/shard_map/dot_general | solution.py:48
  40.8 3.5 %all-to-all-done = bf16[2,64,12,384]{3,0,2,1:T(2,128)(2,1)} async-done(((bf16[2,64,12,384]{3,0,2,1:T(2,128)(2,1)}), bf16[2,64,12,384]{3,0,2,1:T(2,128)(2,1)}, u32[]{:S(2)}, u32[]{:S(2)}) %all-to-all-start) | async-done | bytes 1179680 | tf_op jit(solution)/shard_map/all_to_all | solution.py:103
  44.3 1.5 %copy.21 = bf16[2,64,12,384]{3,2,1,0:T(8,128)(2,1)S(1)} copy(bf16[2,64,12,384]{3,0,2,1:T(2,128)(2,1)} %all-to-all-done) | data formatting | bytes 2359296 | tf_op jit(solution)/shard_map/all_to_all | solution.py:103
  45.8 1.2 reshape.26
  47.0 3.4 %fusion.14 = bf16[768,384]{1,0:T(8,128)(2,1)S(1)} fusion(bf16[1536,384]{1,0:T(8,128)(2,1)} %reshape.26, bf16[768,768]{0,1:T(8,128)(2,1)} %fusion.9, bf16[768,768]{0,1:T(8,128)(2,1)} %fusion.8), kind=kOutput, calls=%fused_computation.34 | convolution fusion | flops 910983168 | bytes 4128768 | tf_op jit(solution)/shard_map/dot_general | solution.py:104
  50.3 2.3 %copy.22 = bf16[2,64,12,384]{3,0,2,1:T(2,128)(2,1)} copy(bf16[2,64,12,384]{3,2,1,0:T(8,128)(2,1)S(1)} %reshape.27) | data formatting | bytes 2359296 | tf_op jit(solution)/shard_map/optimization_barrier | solution.py:108
  52.6 5.5 %all-to-all-start.1 = ((bf16[2,64,12,384]{3,0,2,1:T(2,128)(2,1)}), bf16[2,64,12,384]{3,0,2,1:T(2,128)(2,1)S(1)}, u32[]{:S(2)}, u32[]{:S(2)}) async-start(bf16[2,64,12,384]{3,0,2,1:T(2,128)(2,1)} %copy.22), calls=%async_computation.1 | async-start | bytes 2359296 | tf_op jit(solution)/shard_map/all_to_all | solution.py:103
  58.1 0.0 copy-done.5
  58.1 0.2 copy.25
  58.3 0.3 reshape_squeeze.3
  58.6 1.1 fusion.7
  59.7 0.0 copy-start.8
  59.7 1.0 fusion.12
  60.8 0.2 copy-done.8
  61.0 2.2 %convolution_convert_fusion.3 = bf16[768,768]{1,0:T(8,128)(2,1)} fusion(bf16[768,768]{0,1:T(8,128)(2,1)S(1)} %fusion.12, bf16[1,1,768,768]{3,2,1,0:T(8,128)(2,1)S(1)} %copy-done.8), kind=kOutput, calls=%fused_computation.15 | convolution fusion | flops 906559488 | bytes 3538944 | tf_op jit(solution)/shard_map/dot_general | solution.py:48
  63.2 0.0 copy-done
  63.2 3.0 %collective-permute-start = (bf16[768,384]{1,0:T(8,128)(2,1)S(1)}, bf16[768,384]{1,0:T(8,128)(2,1)}, u32[]{:S(2)}, u32[]{:S(2)}) collective-permute-start(bf16[768,384]{1,0:T(8,128)(2,1)S(1)} %fusion.14), channel_id=1, source_target_pairs={{0,1},{1,0},{2,3},{3,2},{4,5},{5,4},{6,7},{7,6},{8,9},{9,8},{10,11... | collective-permute-start | bytes 1769480 | tf_op jit(solution)/shard_map/ppermute | solution.py:16
  66.2 20.0 %all-to-all-done.1 = bf16[2,64,12,384]{3,0,2,1:T(2,128)(2,1)S(1)} async-done(((bf16[2,64,12,384]{3,0,2,1:T(2,128)(2,1)}), bf16[2,64,12,384]{3,0,2,1:T(2,128)(2,1)S(1)}, u32[]{:S(2)}, u32[]{:S(2)}) %all-to-all-start.1) | async-done | bytes 1179680 | tf_op jit(solution)/shard_map/all_to_all | solution.py:103
  86.2 0.2 copy.23
  86.4 0.0 copy-start.1
  86.4 1.2 reshape.28
  87.6 0.5 copy-done.1
  88.1 4.0 %fusion.15 = bf16[768,384]{1,0:T(8,128)(2,1)} fusion(bf16[1536,384]{1,0:T(8,128)(2,1)} %reshape.28, bf16[768,768]{0,1:T(8,128)(2,1)} %fusion.9, bf16[768,768]{0,1:T(8,128)(2,1)S(1)} %copy-done.1), kind=kOutput, calls=%fused_computation.35 | convolution fusion | flops 910983168 | bytes 4128768 | tf_op jit(solution)/shard_map/dot_general | solution.py:104
  92.2 0.0 collective-permute-start.1
  92.2 0.0 copy-done.3
  92.2 2.5 %fusion.16 = f32[768,768]{0,1:T(8,128)} fusion(bf16[768,768]{1,0:T(8,128)(2,1)S(1)} %copy-done.3, bf16[1,1,768,768]{3,2,1,0:T(8,128)(2,1)S(1)} %copy-done.9), kind=kOutput, calls=%fused_computation.37 | convolution fusion | flops 905969664 | bytes 4718592 | tf_op jit(solution)/shard_map/dot_general | solution.py:94
  94.7 0.6 dynamic-slice.14
  95.3 0.6 dynamic-slice.13
  97.1 7.7 %collective-permute-done = bf16[768,384]{1,0:T(8,128)(2,1)} collective-permute-done((bf16[768,384]{1,0:T(8,128)(2,1)S(1)}, bf16[768,384]{1,0:T(8,128)(2,1)}, u32[]{:S(2)}, u32[]{:S(2)}) %collective-permute-start) | collective-permute-done | bytes 589856 | tf_op jit(solution)/shard_map/ppermute | solution.py:16
  104.8 1.3 add_convert_fusion.1
  106.1 1.8 %fusion.22 = f32[768,768]{1,0:T(8,128)S(1)} fusion(bf16[768,384]{1,0:T(8,128)(2,1)S(1)} %add_convert_fusion.1, bf16[768,768]{1,0:T(8,128)(2,1)} %convolution_convert_fusion.3), kind=kOutput, calls=%fused_computation.50 | convolution fusion | flops 452984832 | bytes 3538944 | tf_op jit(solution)/shard_map/dot_general | solution.py:121
  108.0 9.5 %collective-permute-done.1 = bf16[768,384]{1,0:T(8,128)(2,1)} collective-permute-done((bf16[768,384]{1,0:T(8,128)(2,1)}, bf16[768,384]{1,0:T(8,128)(2,1)}, u32[]{:S(2)}, u32[]{:S(2)}) %collective-permute-start.1) | collective-permute-done | bytes 589856 | tf_op jit(solution)/shard_map/ppermute | solution.py:16
  117.5 1.5 %add_convert_fusion = bf16[768,384]{1,0:T(8,128)(2,1)S(1)} fusion(bf16[768,384]{1,0:T(8,128)(2,1)} %collective-permute-done.1, bf16[768,384]{1,0:T(8,128)(2,1)} %fusion.15, f32[]{:T(128)} %bitcast.12, f32[]{:T(128)} %bitcast.2), kind=kLoop, calls=%fused_computation.40 | loop fusion | flops 1769472 | bytes 1769480 | tf_op jit(solution)/shard_map/convert_element_type | solution.py:111
  118.9 5.4 %convolution_convert_fusion.2 = bf16[768,768]{1,0:T(8,128)(2,1)} fusion(bf16[768,768]{0,1:T(8,128)(2,1)} %copy-done, f32[768,768]{1,0:T(8,128)S(1)} %fusion.22, f32[768,768]{0,1:T(8,128)} %fusion.16, bf16[768,384]{1,0:T(8,128)(2,1)S(1)} %add_convert_fusion, bf16[1,1,768,768]{3,2,1,0:T(8,128)(2,1)} %param.13, bf16[768,384]{1,0:T(8,128)(2,1)S(1)} %add_convert_fusion.1, ...), kind=kOutput, calls=%fused_computation.14 | convolution fusion | flops 1365442560 | bytes 10616832 | tf_op jit(solution)/shard_map/dot_general | solution.py:48
  124.3 2.5 %fusion.19 = f32[768,768]{1,0:T(8,128)S(1)} fusion(bf16[768,768]{1,0:T(8,128)(2,1)} %convolution_convert_fusion.2, bf16[768,384]{1,0:T(8,128)(2,1)S(1)} %add_convert_fusion, bf16[768,384]{1,0:T(8,128)(2,1)S(1)} %add_convert_fusion.1), kind=kOutput, calls=%fused_computation.48 | convolution fusion | flops 908328960 | bytes 4718592 | tf_op jit(solution)/shard_map/dot_general | solution.py:126
  126.8 0.0 copy-done.10
  126.8 0.0 copy-done.13
  126.9 2.2 %fusion.13 = bf16[1,1,768,768]{3,2,1,0:T(8,128)(2,1)} fusion(f32[768,768]{1,0:T(8,128)S(1)} %fusion.19, bf16[768,768]{1,0:T(8,128)(2,1)S(1)} %copy-done.13, bf16[1,1,768,768]{3,2,1,0:T(8,128)(2,1)S(1)} %copy-done.10, bf16[768,384]{1,0:T(8,128)(2,1)S(1)} %add_convert_fusion, bf16[768,384]{1,0:T(8,128)(2,1)S(1)} %add_convert_fusion.1), kind=kOutput, calls=%fused_computation.33 | convolution fusion | flops 911278080 | bytes 7077888 | tf_op jit(solution)/shard_map/dot_general | solution.py:125
  (25 shorter events, 0.1 us)
Async XLA Ops:
  14.0 10.6 %copy-start.2 = (bf16[768,768]{1,0:T(8,128)(2,1)S(1)}, bf16[768,768]{1,0:T(8,128)(2,1)}, u32[]{:S(2)}) copy-start(bf16[768,768]{1,0:T(8,128)(2,1)} %fusion.11) | copy-start | bytes 3538948
  14.0 30.2 %all-to-all-start = ((bf16[2,64,12,384]{3,0,2,1:T(2,128)(2,1)}), bf16[2,64,12,384]{3,0,2,1:T(2,128)(2,1)}, u32[]{:S(2)}, u32[]{:S(2)}) async-start(bf16[2,64,12,384]{3,0,2,1:T(2,128)(2,1)} %copy.20), calls=%async_computation | async-start | bytes 2359296 | tf_op jit(solution)/shard_map/all_to_all | solution.py:103
  24.7 3.5 %copy-start.7 = (s32[2,64]{1,0:T(2,128)S(1)}, s32[2,64]{1,0:T(2,128)}, u32[]{:S(2)}) copy-start(s32[2,64]{1,0:T(2,128)} %param.17) | copy-start | bytes 1540
  28.4 2.3 %copy-start.4 = (s32[2,64,64]{2,1,0:T(8,128)S(1)}, s32[2,64,64]{2,1,0:T(8,128)}, u32[]{:S(2)}) copy-start(s32[2,64,64]{2,1,0:T(8,128)} %param.16) | copy-start | bytes 98308
  28.4 3.9 %copy-start.6 = (bf16[2,12,12]{2,0,1:T(2,128)(2,1)S(1)}, bf16[2,12,12]{2,0,1:T(2,128)(2,1)}, u32[]{:S(2)}) copy-start(bf16[2,12,12]{2,0,1:T(2,128)(2,1)} %param.15) | copy-start | bytes 1732
  52.6 5.5 %copy-start.5 = (bf16[1,1,64,12,12]{2,4,3,1,0:T(8,128)(2,1)S(1)}, bf16[1,1,64,12,12]{2,4,3,1,0:T(8,128)(2,1)}, u32[]{:S(2)}) copy-start(bf16[1,1,64,12,12]{2,4,3,1,0:T(8,128)(2,1)} %param.14) | copy-start | bytes 55300
  52.6 33.6 %all-to-all-start.1 = ((bf16[2,64,12,384]{3,0,2,1:T(2,128)(2,1)}), bf16[2,64,12,384]{3,0,2,1:T(2,128)(2,1)S(1)}, u32[]{:S(2)}, u32[]{:S(2)}) async-start(bf16[2,64,12,384]{3,0,2,1:T(2,128)(2,1)} %copy.22), calls=%async_computation.1 | async-start | bytes 2359296 | tf_op jit(solution)/shard_map/all_to_all | solution.py:103
  59.7 1.3 copy-start.8
  61.0 2.2 %copy-start = (bf16[768,768]{0,1:T(8,128)(2,1)}, bf16[768,768]{0,1:T(8,128)(2,1)S(1)}, u32[]{:S(2)}) copy-start(bf16[768,768]{0,1:T(8,128)(2,1)S(1)} %fusion.12) | copy-start | bytes 3538948
  63.2 41.7 %collective-permute-start = (bf16[768,384]{1,0:T(8,128)(2,1)S(1)}, bf16[768,384]{1,0:T(8,128)(2,1)}, u32[]{:S(2)}, u32[]{:S(2)}) collective-permute-start(bf16[768,384]{1,0:T(8,128)(2,1)S(1)} %fusion.14), channel_id=1, source_target_pairs={{0,1},{1,0},{2,3},{3,2},{4,5},{5,4},{6,7},{7,6},{8,9},{9,8},{10,11... | collective-permute-start | bytes 1769480 | tf_op jit(solution)/shard_map/ppermute | solution.py:16
  86.4 1.7 %copy-start.1 = (bf16[768,768]{0,1:T(8,128)(2,1)S(1)}, bf16[768,768]{0,1:T(8,128)(2,1)}, u32[]{:S(2)}) copy-start(bf16[768,768]{0,1:T(8,128)(2,1)} %fusion.8) | copy-start | bytes 3538948
  88.1 4.1 %copy-start.3 = (bf16[768,768]{1,0:T(8,128)(2,1)S(1)}, bf16[768,768]{1,0:T(8,128)(2,1)}, u32[]{:S(2)}) copy-start(bf16[768,768]{1,0:T(8,128)(2,1)} %convolution_convert_fusion.3) | copy-start | bytes 3538948
  88.1 4.1 %copy-start.9 = (bf16[1,1,768,768]{3,2,1,0:T(8,128)(2,1)S(1)}, bf16[1,1,768,768]{3,2,1,0:T(8,128)(2,1)}, u32[]{:S(2)}) copy-start(bf16[1,1,768,768]{3,2,1,0:T(8,128)(2,1)} %param.13) | copy-start | bytes 3538948
  92.2 2.5 %copy-start.12 = (f32[4]{0:T(128)S(1)}, f32[4]{0:T(128)}, u32[]{:S(2)}) copy-start(f32[4]{0:T(128)} %constant.78.clone..sunk.2) | copy-start | bytes 52
  92.2 3.1 %copy-start.11 = (f32[4]{0:T(128)S(1)}, f32[4]{0:T(128)}, u32[]{:S(2)}) copy-start(f32[4]{0:T(128)} %constant.77.clone..sunk.2) | copy-start | bytes 52
  92.2 25.3 %collective-permute-start.1 = (bf16[768,384]{1,0:T(8,128)(2,1)}, bf16[768,384]{1,0:T(8,128)(2,1)}, u32[]{:S(2)}, u32[]{:S(2)}) collective-permute-start(bf16[768,384]{1,0:T(8,128)(2,1)} %fusion.15), channel_id=1, source_target_pairs={{0,1},{1,0},{2,3},{3,2},{4,5},{5,4},{6,7},{7,6},{8,9},{9,8},{10,11... | collective-permute-start | bytes 1769480 | tf_op jit(solution)/shard_map/ppermute | solution.py:16
  124.3 2.5 %copy-start.10 = (bf16[1,1,768,768]{3,2,1,0:T(8,128)(2,1)S(1)}, bf16[1,1,768,768]{3,2,1,0:T(8,128)(2,1)}, u32[]{:S(2)}) copy-start(bf16[1,1,768,768]{3,2,1,0:T(8,128)(2,1)} %param.13) | copy-start | bytes 3538948
  124.3 2.5 %copy-start.13 = (bf16[768,768]{1,0:T(8,128)(2,1)S(1)}, bf16[768,768]{1,0:T(8,128)(2,1)}, u32[]{:S(2)}) copy-start(bf16[768,768]{1,0:T(8,128)(2,1)} %convolution_convert_fusion.2) | copy-start | bytes 3538948

commit v8 on v3

--- a/solution.py
+++ b/solution.py
@@ -79,7 +79,7 @@
         packs.append(jnp.take(blocks, send_order, axis=0))
         mixes.append(mix_matrix(recv_slots, form_mix[r], freqs, expand, forms_expand))
     stacked = jnp.stack(packs)
-    mix = jnp.concatenate(mixes, axis=1)
+    mix4 = jnp.concatenate(mixes, axis=1).reshape(order_len, 2, freqs, forms)
 
     bubble_tall = bubble_mat.reshape(order_len, forms)
     block_mask = exact_dot(expand, expand.T)
@@ -96,8 +96,8 @@
     pieces = [stacked[..., k * width:(k + 1) * width] for k in range(NCHUNK)]
     for k in range(NCHUNK):
         received = lax.all_to_all(pieces[k], "mom", split_axis=1, concat_axis=1, tiled=True)
-        summed = jnp.dot(
-            mix, received.reshape(2 * order_len, width), preferred_element_type=jnp.float32
+        summed = jnp.einsum(
+            "frqm,rqmb->fb", mix4, received, preferred_element_type=jnp.float32
         ).astype(jnp.bfloat16)
         if k + 1 < NCHUNK:
             summed, pieces[k + 1] = lax.optimization_barrier((summed, pieces[k + 1]))

time: 125 us -> 127 us (1.016)
  other arithmetic: 5.6 us -> 10.5 us
  local copies, waits for them, and re-layouts: 17.9 us -> 15.6 us
  waiting for transfers between devices: 46.1 us -> 44.8 us
    all_to_all x2, waiting for transfers between devices: 29.3 us -> 25.8 us  [local(): lax.all_to_all(pieces[k], 'mom', split_axis=1, concat_axis=1, tiled=True)]
    ppermute x2, waiting for transfers between devices: 16.9 us -> 19 us  [partner_2(): return lax.ppermute(value, axis, pairs)]
    all_to_all x2 -> x0, local copies, waits for them, and re-layouts: 1.74 us -> none  [local(): lax.all_to_all(pieces[k], 'mom', split_axis=1, concat_axis=1, tiled=True)]
    concatenate x0 -> x1, other arithmetic: none -> 1.42 us  [local(): mix4 = jnp.concatenate(mixes, axis=1).reshape(order_len, 2, freqs, forms)]
    dot_general x8, matrix products: 18.2 us -> 16.8 us  [exact_dot(): jnp.dot(a, b, preferred_element_type=jnp.float32).astype(jnp.bfloat16)]
  transfers between devices with their start and end apart: 4 -> 4, of which waited for: 4 -> 4; matrix products, arithmetic and copies ran while one was open for 22% -> 23% of each run, Pallas kernels for 0% -> 0%
where the time goes in v8:
time: 127 us; the launch traced here: 126 us
  waiting for transfers between devices  44.8 us (35%)
  matrix products  34.1 us (27%)
  starting transfers between devices  19.4 us (15%)
  local copies, waits for them, and re-layouts  15.6 us (12%)
  other arithmetic  10.5 us (8%)
  between operations  1.56 us (1%)
    all_to_all x2, waiting for transfers between devices, local(): lax.all_to_all(pieces[k], 'mom', split_axis=1, concat_axis=1, tiled=True)  25.8 us
    ppermute x2, waiting for transfers between devices, partner_2(): return lax.ppermute(value, axis, pairs)  19 us
    dot_general x8, matrix products, exact_dot(): jnp.dot(a, b, preferred_element_type=jnp.float32).astype(jnp.bfloat16)  16.8 us
    all_to_all x2, starting transfers between devices, local(): lax.all_to_all(pieces[k], 'mom', split_axis=1, concat_axis=1, tiled=True)  16.4 us
    dot_general x2, matrix products, local(): jnp.einsum('frqm,rqmb->fb', mix4, received, preferred_element_type=jnp.fl...  8.21 us
    convert_element_type x2, other arithmetic, local(): (coef_self * summed.astype(jnp.float32) + coef_pair * other.astype(jnp.fl...  3.58 us
    another operation x3, other arithmetic, local(): stacked = jnp.stack(packs)  3.44 us
    ppermute x2, starting transfers between devices, partner_2(): return lax.ppermute(value, axis, pairs)  2.98 us
  transfers between devices with their start and end apart: 4, of which 4 were waited for; matrix products, arithmetic and copies ran while one was open for 23% of the time, Pallas kernels for 0%

profile of v8, /device:TPU:1, one launch (start us, length us, event | category | flops | bytes accessed | tf_op | source)
XLA Modules:
  0.0 126.0 jit_solution(3047942962806641963)
XLA Ops:
  0.0 0.8 slice_bitcast_fusion
  0.8 0.1 select_reduce_fusion
  0.9 0.1 select_reduce_fusion.1
  1.1 2.2 %reshape_squeeze.6 = bf16[64,12,768]{2,1,0:T(8,128)(2,1)S(1)} reshape(bf16[1,1,768,768]{3,2,1,0:T(8,128)(2,1)} %param.14) | data formatting | bytes 2359296 | tf_op jit(solution)/shard_map/reshape;squeeze | solution.py:72
  3.3 1.8 %gather_fusion.3 = bf16[64,12,768]{2,1,0:T(8,128)(2,1)} fusion(bf16[64,12,768]{2,1,0:T(8,128)(2,1)S(1)} %reshape_squeeze.6, s32[1024]{0:T(1024)S(1)} %pad_clamp_fusion), kind=kCustom, calls=%fused_computation.3.clone | custom fusion | bytes 2359552 | tf_op jit(solution)/shard_map/jit(_take)/gather | solution.py:79
  5.1 0.6 gather_fusion.2
  5.7 1.6 %select_bitcast_fusion = bf16[1,64,12,768]{3,2,1,0:T(8,128)(2,1)S(1)} fusion(bf16[64,12,768]{2,1,0:T(8,128)(2,1)} %gather_fusion.3, pred[64]{0:T(512)(128)(4,1)S(1)} %get-tuple-element.81), kind=kLoop, calls=%fused_computation.21 | loop fusion | flops 589824 | bytes 2359360 | tf_op jit(solution)/shard_map/stack | solution.py:81
  7.4 0.2 select_bitcast_fusion.1
  7.6 1.6 %pad_maximum_fusion.1 = (bf16[2,64,12,384]{3,2,1,0:T(8,128)(2,1)}, bf16[2,64,12,384]{3,2,1,0:T(8,128)(2,1)S(1)}) fusion(bf16[1,64,12,768]{3,2,1,0:T(8,128)(2,1)S(1)} %select_bitcast_fusion, bf16[1,64,12,768]{3,2,1,0:T(8,128)(2,1)S(1)} %select_bitcast_fusion.1), kind=kLoop, calls=%fused_computation.20 | loop fusion | flops 4718592 | bytes 4718592 | tf_op jit(solution)/shard_map/stack | solution.py:81
  9.2 2.3 %copy.26 = bf16[2,64,12,384]{3,0,2,1:T(2,128)(2,1)} copy(bf16[2,64,12,384]{3,2,1,0:T(8,128)(2,1)S(1)} %get-tuple-element.66) | data formatting | bytes 2359296 | tf_op jit(solution)/shard_map/slice | solution.py:96
  11.5 10.6 %all-to-all-start = ((bf16[2,64,12,384]{3,0,2,1:T(2,128)(2,1)}), bf16[2,64,12,384]{3,0,2,1:T(2,128)(2,1)}, u32[]{:S(2)}, u32[]{:S(2)}) async-start(bf16[2,64,12,384]{3,0,2,1:T(2,128)(2,1)} %copy.26), calls=%async_computation | async-start | bytes 2359296 | tf_op jit(solution)/shard_map/all_to_all | solution.py:98
  22.1 0.0 copy-done.6
  22.1 0.0 copy-done.12
  22.2 0.0 copy-start.9
  22.2 0.1 select_reduce_fusion.2
  22.3 0.6 fusion.76
  22.9 0.8 gather_fusion
  23.7 0.8 gather_fusion.1
  24.5 0.5 and_select_fusion.1
  25.0 0.5 and_select_fusion
  25.5 0.0 copy-done.11
  25.6 1.0 convolution_convert_fusion.7
  26.6 1.0 convolution_convert_fusion.6
  27.6 0.0 copy-done.9
  27.6 1.8 %fusion.11 = bf16[768,768]{0,1:T(8,128)(2,1)S(1)} fusion(bf16[768,768]{0,1:T(8,128)(2,1)S(1)} %convolution_convert_fusion.7, s32[768]{0:T(1024)S(1)} %get-tuple-element.75, s32[768]{0:T(1024)S(1)} %get-tuple-element.76, pred[768]{0:T(1024)(128)(4,1)} %fusion.76, s32[64]{0:T(128)} %and_select_fusion.1), kind=kOutput, calls=%fused_computation.32 | convolution fusion | flops 84987904 | bytes 2366464 | tf_op jit(solution)/shard_map/dot_general | solution.py:48
  29.4 2.8 %fusion.12 = bf16[768,768]{0,1:T(8,128)(2,1)} fusion(bf16[768,768]{0,1:T(8,128)(2,1)S(1)} %convolution_convert_fusion.6, s32[768]{0:T(1024)S(1)} %get-tuple-element.75, s32[768]{0:T(1024)S(1)} %get-tuple-element.76, pred[768]{0:T(1024)(128)(4,1)} %fusion.76, s32[64]{0:T(128)} %and_select_fusion), kind=kOutput, calls=%fused_computation.33 | convolution fusion | flops 84987904 | bytes 2366464 | tf_op jit(solution)/shard_map/dot_general | solution.py:48
  32.3 1.4 %pad_maximum_fusion = bf16[768,1536]{0,1:T(8,128)(2,1)S(1)} fusion(bf16[768,768]{0,1:T(8,128)(2,1)} %fusion.12, bf16[768,768]{0,1:T(8,128)(2,1)S(1)} %fusion.11), kind=kLoop, calls=%fused_computation.6 | loop fusion | flops 4718592 | bytes 4718592 | tf_op jit(solution)/shard_map/concatenate | solution.py:82
  33.7 2.3 %reshape.19 = bf16[768,2,64,12]{0,3,2,1:T(8,128)(2,1)} reshape(bf16[768,1536]{0,1:T(8,128)(2,1)S(1)} %pad_maximum_fusion) | data formatting | bytes 4718592 | tf_op jit(solution)/shard_map/reshape | solution.py:82
  36.0 5.7 %all-to-all-done = bf16[2,64,12,384]{3,0,2,1:T(2,128)(2,1)} async-done(((bf16[2,64,12,384]{3,0,2,1:T(2,128)(2,1)}), bf16[2,64,12,384]{3,0,2,1:T(2,128)(2,1)}, u32[]{:S(2)}, u32[]{:S(2)}) %all-to-all-start) | async-done | bytes 1179680 | tf_op jit(solution)/shard_map/all_to_all | solution.py:98
  41.7 4.5 %fusion.24 = bf16[768,384]{1,0:T(8,128)(2,1)} fusion(bf16[768,2,64,12]{0,3,2,1:T(8,128)(2,1)} %reshape.19, bf16[2,64,12,384]{3,0,2,1:T(2,128)(2,1)} %all-to-all-done), kind=kOutput, calls=%fused_computation.39 | convolution fusion | flops 906264576 | bytes 4128768 | tf_op jit(solution)/shard_map/frqm,rqmb->fb/dot_general | solution.py:99
  46.2 0.0 copy-done
  46.2 2.3 %copy.29 = bf16[2,64,12,384]{3,0,2,1:T(2,128)(2,1)} copy(bf16[2,64,12,384]{3,2,1,0:T(8,128)(2,1)S(1)} %copy-done) | data formatting | bytes 2359296 | tf_op jit(solution)/shard_map/optimization_barrier | solution.py:103
  48.5 5.8 %all-to-all-start.1 = ((bf16[2,64,12,384]{3,0,2,1:T(2,128)(2,1)}), bf16[2,64,12,384]{3,0,2,1:T(2,128)(2,1)}, u32[]{:S(2)}, u32[]{:S(2)}) async-start(bf16[2,64,12,384]{3,0,2,1:T(2,128)(2,1)} %copy.29), calls=%async_computation.1 | async-start | bytes 2359296 | tf_op jit(solution)/shard_map/all_to_all | solution.py:98
  54.3 0.0 copy-done.7
  54.3 0.2 copy.33
  54.5 0.3 reshape_squeeze.7
  54.7 0.0 copy-done.10
  54.8 0.0 copy-start.3
  54.8 1.1 fusion.10
  55.9 0.0 copy-done.8
  55.9 1.0 fusion.13
  56.9 0.0 copy-done.3
  57.0 0.0 copy-start.2
  57.0 0.0 copy-start.1
  57.0 2.2 %convolution_convert_fusion.1 = bf16[768,768]{1,0:T(8,128)(2,1)} fusion(bf16[768,768]{0,1:T(8,128)(2,1)S(1)} %fusion.13, bf16[1,1,768,768]{3,2,1,0:T(8,128)(2,1)S(1)} %copy-done.3), kind=kOutput, calls=%fused_computation.24 | convolution fusion | flops 906559488 | bytes 3538944 | tf_op jit(solution)/shard_map/dot_general | solution.py:48
  59.1 0.0 copy-done.2
  59.1 3.0 %collective-permute-start = (bf16[768,384]{1,0:T(8,128)(2,1)}, bf16[768,384]{1,0:T(8,128)(2,1)}, u32[]{:S(2)}, u32[]{:S(2)}) collective-permute-start(bf16[768,384]{1,0:T(8,128)(2,1)} %fusion.24), channel_id=1, source_target_pairs={{0,1},{1,0},{2,3},{3,2},{4,5},{5,4},{6,7},{7,6},{8,9},{9,8},{10,11... | collective-permute-start | bytes 1769480 | tf_op jit(solution)/shard_map/ppermute | solution.py:16
  62.1 20.1 %all-to-all-done.1 = bf16[2,64,12,384]{3,0,2,1:T(2,128)(2,1)} async-done(((bf16[2,64,12,384]{3,0,2,1:T(2,128)(2,1)}), bf16[2,64,12,384]{3,0,2,1:T(2,128)(2,1)}, u32[]{:S(2)}, u32[]{:S(2)}) %all-to-all-start.1) | async-done | bytes 1179680 | tf_op jit(solution)/shard_map/all_to_all | solution.py:98
  82.3 0.0 copy-done.1
  82.3 3.7 %fusion.21 = bf16[768,384]{1,0:T(8,128)(2,1)} fusion(bf16[768,2,64,12]{0,3,2,1:T(8,128)(2,1)S(1)} %copy-done.1, bf16[2,64,12,384]{3,0,2,1:T(2,128)(2,1)} %all-to-all-done.1), kind=kOutput, calls=%fused_computation.38 | convolution fusion | flops 906264576 | bytes 4128768 | tf_op jit(solution)/shard_map/frqm,rqmb->fb/dot_general | solution.py:99
  86.0 0.0 collective-permute-start.1
  86.0 2.5 %fusion.28 = f32[768,768]{0,1:T(8,128)} fusion(bf16[768,768]{1,0:T(8,128)(2,1)S(1)} %copy-done.5, bf16[1,1,768,768]{3,2,1,0:T(8,128)(2,1)S(1)} %copy-done.13), kind=kOutput, calls=%fused_computation.42 | convolution fusion | flops 905969664 | bytes 4718592 | tf_op jit(solution)/shard_map/dot_general | solution.py:92
  88.5 0.6 dynamic-slice.14
  89.1 0.0 copy-done.15
  89.1 0.7 dynamic-slice.13
  91.0 9.8 %collective-permute-done = bf16[768,384]{1,0:T(8,128)(2,1)} collective-permute-done((bf16[768,384]{1,0:T(8,128)(2,1)}, bf16[768,384]{1,0:T(8,128)(2,1)}, u32[]{:S(2)}, u32[]{:S(2)}) %collective-permute-start) | collective-permute-done | bytes 589856 | tf_op jit(solution)/shard_map/ppermute | solution.py:16
  100.8 1.5 %add_convert_fusion.1 = bf16[768,384]{1,0:T(8,128)(2,1)S(1)} fusion(bf16[768,384]{1,0:T(8,128)(2,1)} %collective-permute-done, bf16[768,384]{1,0:T(8,128)(2,1)} %fusion.24, f32[]{:T(128)} %bitcast.15, f32[]{:T(128)} %bitcast.2), kind=kLoop, calls=%fused_computation.48 | loop fusion | flops 1769472 | bytes 1769480 | tf_op jit(solution)/shard_map/convert_element_type | solution.py:106
  102.3 1.8 %fusion.36 = f32[768,768]{1,0:T(8,128)S(1)} fusion(bf16[768,384]{1,0:T(8,128)(2,1)S(1)} %add_convert_fusion.1, bf16[768,768]{1,0:T(8,128)(2,1)} %convolution_convert_fusion.1), kind=kOutput, calls=%fused_computation.55 | convolution fusion | flops 452984832 | bytes 3538944 | tf_op jit(solution)/shard_map/dot_general | solution.py:116
  104.1 9.2 %collective-permute-done.1 = bf16[768,384]{1,0:T(8,128)(2,1)S(1)} collective-permute-done((bf16[768,384]{1,0:T(8,128)(2,1)}, bf16[768,384]{1,0:T(8,128)(2,1)S(1)}, u32[]{:S(2)}, u32[]{:S(2)}) %collective-permute-start.1) | collective-permute-done | bytes 589856 | tf_op jit(solution)/shard_map/ppermute | solution.py:16
  113.4 2.1 %add_convert_fusion = bf16[768,384]{1,0:T(8,128)(2,1)} fusion(bf16[768,384]{1,0:T(8,128)(2,1)S(1)} %collective-permute-done.1, bf16[768,384]{1,0:T(8,128)(2,1)} %fusion.21, f32[]{:T(128)} %bitcast.15, f32[]{:T(128)} %bitcast.2), kind=kLoop, calls=%fused_computation.47 | loop fusion | flops 1769472 | bytes 1769480 | tf_op jit(solution)/shard_map/convert_element_type | solution.py:106
  115.5 5.8 %convolution_convert_fusion = bf16[768,768]{1,0:T(8,128)(2,1)} fusion(bf16[768,768]{0,1:T(8,128)(2,1)} %copy-done.2, f32[768,768]{1,0:T(8,128)S(1)} %fusion.36, f32[768,768]{0,1:T(8,128)} %fusion.28, bf16[768,384]{1,0:T(8,128)(2,1)} %add_convert_fusion, bf16[1,1,768,768]{3,2,1,0:T(8,128)(2,1)} %param.15, bf16[768,384]{1,0:T(8,128)(2,1)S(1)} %add_convert_fusion.1, ...), kind=kOutput, calls=%fused_computation.23 | convolution fusion | flops 1365442560 | bytes 10616832 | tf_op jit(solution)/shard_map/dot_general | solution.py:48
  121.3 0.0 copy-done.4
  121.3 2.5 %fusion.33 = f32[768,768]{1,0:T(8,128)S(1)} fusion(bf16[768,768]{1,0:T(8,128)(2,1)} %convolution_convert_fusion, bf16[768,384]{1,0:T(8,128)(2,1)S(1)} %copy-done.4, bf16[768,384]{1,0:T(8,128)(2,1)S(1)} %add_convert_fusion.1), kind=kOutput, calls=%fused_computation.53 | convolution fusion | flops 908328960 | bytes 4718592 | tf_op jit(solution)/shard_map/dot_general | solution.py:121
  123.8 2.2 %fusion.20 = bf16[1,1,768,768]{3,2,1,0:T(8,128)(2,1)} fusion(f32[768,768]{1,0:T(8,128)S(1)} %fusion.33, bf16[768,768]{1,0:T(8,128)(2,1)S(1)} %copy-done.17, bf16[1,1,768,768]{3,2,1,0:T(8,128)(2,1)S(1)} %copy-done.14, bf16[768,384]{1,0:T(8,128)(2,1)S(1)} %copy-done.4, bf16[768,384]{1,0:T(8,128)(2,1)S(1)} %add_convert_fusion.1), kind=kOutput, calls=%fused_computation.37 | convolution fusion | flops 911278080 | bytes 7077888 | tf_op jit(solution)/shard_map/dot_general | solution.py:120
  (35 shorter events, 0.2 us)
Async XLA Ops:
  11.5 10.6 %copy-start.6 = (s32[2,64,64]{2,1,0:T(8,128)S(1)}, s32[2,64,64]{2,1,0:T(8,128)}, u32[]{:S(2)}) copy-start(s32[2,64,64]{2,1,0:T(8,128)} %param.18) | copy-start | bytes 98308
  11.5 10.7 %copy-start.12 = (s32[2,64]{1,0:T(2,128)S(1)}, s32[2,64]{1,0:T(2,128)}, u32[]{:S(2)}) copy-start(s32[2,64]{1,0:T(2,128)} %param.19) | copy-start | bytes 1540
  11.5 14.1 %copy-start.11 = (bf16[2,12,12]{2,0,1:T(2,128)(2,1)S(1)}, bf16[2,12,12]{2,0,1:T(2,128)(2,1)}, u32[]{:S(2)}) copy-start(bf16[2,12,12]{2,0,1:T(2,128)(2,1)} %param.17) | copy-start | bytes 1732
  11.5 30.3 %all-to-all-start = ((bf16[2,64,12,384]{3,0,2,1:T(2,128)(2,1)}), bf16[2,64,12,384]{3,0,2,1:T(2,128)(2,1)}, u32[]{:S(2)}, u32[]{:S(2)}) async-start(bf16[2,64,12,384]{3,0,2,1:T(2,128)(2,1)} %copy.26), calls=%async_computation | async-start | bytes 2359296 | tf_op jit(solution)/shard_map/all_to_all | solution.py:98
  22.2 5.5 %copy-start.9 = (pred[768]{0:T(1024)(128)(4,1)}, pred[768]{0:T(1024)(128)(4,1)S(1)}, u32[]{:S(2)}) copy-start(pred[768]{0:T(1024)(128)(4,1)S(1)} %fusion.75) | copy-start | bytes 2308
  36.0 10.2 %copy-start = (bf16[2,64,12,384]{3,2,1,0:T(8,128)(2,1)S(1)}, bf16[2,64,12,384]{3,2,1,0:T(8,128)(2,1)}, u32[]{:S(2)}) copy-start(bf16[2,64,12,384]{3,2,1,0:T(8,128)(2,1)} %get-tuple-element.11) | copy-start | bytes 3538948
  48.5 5.8 %copy-start.7 = (bf16[1,1,64,12,12]{2,4,3,1,0:T(8,128)(2,1)S(1)}, bf16[1,1,64,12,12]{2,4,3,1,0:T(8,128)(2,1)}, u32[]{:S(2)}) copy-start(bf16[1,1,64,12,12]{2,4,3,1,0:T(8,128)(2,1)} %param.16) | copy-start | bytes 55300
  48.5 6.3 %copy-start.10 = (pred[768]{0:T(1024)(128)(4,1)S(1)}, pred[768]{0:T(1024)(128)(4,1)}, u32[]{:S(2)}) copy-start(pred[768]{0:T(1024)(128)(4,1)} %copy-done.9) | copy-start | bytes 2308
  48.5 7.4 %copy-start.8 = (pred[768]{0:T(1024)(128)(4,1)S(1)}, pred[768]{0:T(1024)(128)(4,1)}, u32[]{:S(2)}) copy-start(pred[768]{0:T(1024)(128)(4,1)} %fusion.76) | copy-start | bytes 2308
  48.5 33.8 %all-to-all-start.1 = ((bf16[2,64,12,384]{3,0,2,1:T(2,128)(2,1)}), bf16[2,64,12,384]{3,0,2,1:T(2,128)(2,1)}, u32[]{:S(2)}, u32[]{:S(2)}) async-start(bf16[2,64,12,384]{3,0,2,1:T(2,128)(2,1)} %copy.29), calls=%async_computation.1 | async-start | bytes 2359296 | tf_op jit(solution)/shard_map/all_to_all | solution.py:98
  54.8 2.2 %copy-start.3 = (bf16[1,1,768,768]{3,2,1,0:T(8,128)(2,1)S(1)}, bf16[1,1,768,768]{3,2,1,0:T(8,128)(2,1)}, u32[]{:S(2)}) copy-start(bf16[1,1,768,768]{3,2,1,0:T(8,128)(2,1)} %param.14) | copy-start | bytes 3538948
  57.0 2.2 %copy-start.2 = (bf16[768,768]{0,1:T(8,128)(2,1)}, bf16[768,768]{0,1:T(8,128)(2,1)S(1)}, u32[]{:S(2)}) copy-start(bf16[768,768]{0,1:T(8,128)(2,1)S(1)} %fusion.13) | copy-start | bytes 3538948
  57.0 25.3 %copy-start.1 = (bf16[768,2,64,12]{0,3,2,1:T(8,128)(2,1)S(1)}, bf16[768,2,64,12]{0,3,2,1:T(8,128)(2,1)}, u32[]{:S(2)}) copy-start(bf16[768,2,64,12]{0,3,2,1:T(8,128)(2,1)} %reshape.19) | copy-start | bytes 7077892
  59.1 41.7 %collective-permute-start = (bf16[768,384]{1,0:T(8,128)(2,1)}, bf16[768,384]{1,0:T(8,128)(2,1)}, u32[]{:S(2)}, u32[]{:S(2)}) collective-permute-start(bf16[768,384]{1,0:T(8,128)(2,1)} %fusion.24), channel_id=1, source_target_pairs={{0,1},{1,0},{2,3},{3,2},{4,5},{5,4},{6,7},{7,6},{8,9},{9,8},{10,11... | collective-permute-start | bytes 1769480 | tf_op jit(solution)/shard_map/ppermute | solution.py:16
  82.3 3.7 %copy-start.5 = (bf16[768,768]{1,0:T(8,128)(2,1)S(1)}, bf16[768,768]{1,0:T(8,128)(2,1)}, u32[]{:S(2)}) copy-start(bf16[768,768]{1,0:T(8,128)(2,1)} %convolution_convert_fusion.1) | copy-start | bytes 3538948
  82.3 3.7 %copy-start.13 = (bf16[1,1,768,768]{3,2,1,0:T(8,128)(2,1)S(1)}, bf16[1,1,768,768]{3,2,1,0:T(8,128)(2,1)}, u32[]{:S(2)}) copy-start(bf16[1,1,768,768]{3,2,1,0:T(8,128)(2,1)} %param.15) | copy-start | bytes 3538948
  86.0 2.6 %copy-start.16 = (f32[4]{0:T(128)S(1)}, f32[4]{0:T(128)}, u32[]{:S(2)}) copy-start(f32[4]{0:T(128)} %constant.88.clone..sunk.2) | copy-start | bytes 52
  86.0 3.1 %copy-start.15 = (f32[4]{0:T(128)S(1)}, f32[4]{0:T(128)}, u32[]{:S(2)}) copy-start(f32[4]{0:T(128)} %constant.87.clone..sunk.2) | copy-start | bytes 52
  86.0 27.4 %collective-permute-start.1 = (bf16[768,384]{1,0:T(8,128)(2,1)}, bf16[768,384]{1,0:T(8,128)(2,1)S(1)}, u32[]{:S(2)}, u32[]{:S(2)}) collective-permute-start(bf16[768,384]{1,0:T(8,128)(2,1)} %fusion.21), channel_id=1, source_target_pairs={{0,1},{1,0},{2,3},{3,2},{4,5},{5,4},{6,7},{7,6},{8,9},{9,8},{10,11... | collective-permute-start | bytes 1769480 | tf_op jit(solution)/shard_map/ppermute | solution.py:16
  115.5 5.8 %copy-start.4 = (bf16[768,384]{1,0:T(8,128)(2,1)S(1)}, bf16[768,384]{1,0:T(8,128)(2,1)}, u32[]{:S(2)}) copy-start(bf16[768,384]{1,0:T(8,128)(2,1)} %add_convert_fusion) | copy-start | bytes 1769476
  121.3 2.5 %copy-start.14 = (bf16[1,1,768,768]{3,2,1,0:T(8,128)(2,1)S(1)}, bf16[1,1,768,768]{3,2,1,0:T(8,128)(2,1)}, u32[]{:S(2)}) copy-start(bf16[1,1,768,768]{3,2,1,0:T(8,128)(2,1)} %param.15) | copy-start | bytes 3538948
  121.3 2.5 %copy-start.17 = (bf16[768,768]{1,0:T(8,128)(2,1)S(1)}, bf16[768,768]{1,0:T(8,128)(2,1)}, u32[]{:S(2)}) copy-start(bf16[768,768]{1,0:T(8,128)(2,1)} %convolution_convert_fusion) | copy-start | bytes 3538948

commit v9 on v6

--- a/solution.py
+++ b/solution.py
@@ -4,7 +4,8 @@
 from jax.sharding import PartitionSpec as P
 
 INNER = 2
-NCHUNK = 2
+WIDTHS = (512, 256)
+NCHUNK = len(WIDTHS)
 
 COEF_SELF = (-0.5, 0.5, 0.5, 0.5)
 COEF_PAIR = (-1.5, -0.5, 1.5, -0.5)
@@ -88,13 +89,14 @@
         return bubble_full, exact_dot(bubble_full, mat)
 
 
-    width = order_len // NCHUNK
+    assert sum(WIDTHS) == order_len
+    starts = [sum(WIDTHS[:k]) for k in range(NCHUNK)]
     red_chunks = []
-    pieces = [stacked[..., k * width:(k + 1) * width] for k in range(NCHUNK)]
+    pieces = [stacked[..., starts[k]:starts[k] + WIDTHS[k]] for k in range(NCHUNK)]
     for k in range(NCHUNK):
         received = lax.all_to_all(pieces[k], "mom", split_axis=1, concat_axis=1, tiled=True)
         summed = jnp.dot(
-            mix, received.reshape(2 * order_len, width), preferred_element_type=jnp.float32
+            mix, received.reshape(2 * order_len, WIDTHS[k]), preferred_element_type=jnp.float32
         ).astype(jnp.bfloat16)
         if k + 1 == NCHUNK:
             sums = [pair[0] for pair in red_chunks]
@@ -118,7 +120,7 @@
 
     total = base_sum + bare_part
     for k in range(NCHUNK):
-        rows = slice(k * width, (k + 1) * width)
+        rows = slice(starts[k], starts[k] + WIDTHS[k])
         total = total + jnp.dot(red_chunks[k], carried[rows], preferred_element_type=jnp.float32)
     current = total.astype(jnp.bfloat16)
     for inner_step in range(1, INNER):

time: 129 us -> 125 us (0.969)
  waiting for transfers between devices: 53.9 us -> 51.1 us
  matrix products: 32.5 us -> 30.3 us
    all_to_all x2, waiting for transfers between devices: 38.2 us -> 32.8 us  [local(): lax.all_to_all(pieces[k], 'mom', split_axis=1, concat_axis=1, tiled=True)]
    ppermute x2, waiting for transfers between devices: 15.7 us -> 18.3 us  [partner_2(): return lax.ppermute(value, axis, pairs)]
  transfers between devices with their start and end apart: 4 -> 4, of which waited for: 3 -> 4; matrix products, arithmetic and copies ran while one was open for 19% -> 19% of each run, Pallas kernels for 0% -> 0%
where the time goes in v9:
time: 125 us; the launch traced here: 124 us
  waiting for transfers between devices  51.1 us (41%)
  matrix products  30.3 us (24%)
  starting transfers between devices  18.6 us (15%)
  local copies, waits for them, and re-layouts  17.2 us (14%)
  other arithmetic  6.56 us (5%)
    all_to_all x2, waiting for transfers between devices, local(): lax.all_to_all(pieces[k], 'mom', split_axis=1, concat_axis=1, tiled=True)  32.8 us
    ppermute x2, waiting for transfers between devices, partner_2(): return lax.ppermute(value, axis, pairs)  18.3 us
    dot_general x8, matrix products, exact_dot(): jnp.dot(a, b, preferred_element_type=jnp.float32).astype(jnp.bfloat16)  16.1 us
    all_to_all x2, starting transfers between devices, local(): lax.all_to_all(pieces[k], 'mom', split_axis=1, concat_axis=1, tiled=True)  15.3 us
    dot_general x2, matrix products, local(): jnp.dot(mix, received.reshape(2 * order_len, WIDTHS[k]), preferred_elemen...  6.23 us
    ppermute x2, starting transfers between devices, partner_2(): return lax.ppermute(value, axis, pairs)  3.35 us
    slice x1, local copies, waits for them, and re-layouts, local(): stacked[..., starts[k]:starts[k] + WIDTHS[k]]  2.76 us
    convert_element_type x2, other arithmetic, local(): (coef_self * summed.astype(jnp.float32) + coef_pair * other.astype(jnp.fl...  2.57 us
  transfers between devices with their start and end apart: 4, of which 4 were waited for; matrix products, arithmetic and copies ran while one was open for 19% of the time, Pallas kernels for 0%

profile of v9, /device:TPU:1, one launch (start us, length us, event | category | flops | bytes accessed | tf_op | source)
XLA Modules:
  0.0 124.2 jit_solution(7930723383482372740)
XLA Ops:
  0.0 0.8 slice_bitcast_fusion
  0.8 0.1 select_reduce_fusion.1
  0.9 0.1 select_reduce_fusion
  1.1 2.2 %reshape_squeeze.3 = bf16[64,12,768]{2,1,0:T(8,128)(2,1)S(1)} reshape(bf16[1,1,768,768]{3,2,1,0:T(8,128)(2,1)} %param.12) | data formatting | bytes 2359296 | tf_op jit(solution)/shard_map/reshape;squeeze | solution.py:73
  3.3 1.8 %gather_fusion.3 = bf16[64,12,768]{2,1,0:T(8,128)(2,1)} fusion(bf16[64,12,768]{2,1,0:T(8,128)(2,1)S(1)} %reshape_squeeze.3, s32[1024]{0:T(1024)S(1)} %pad_clamp_fusion), kind=kCustom, calls=%fused_computation.3.clone | custom fusion | bytes 2359552 | tf_op jit(solution)/shard_map/jit(_take)/gather | solution.py:80
  5.1 0.6 gather_fusion.2
  5.7 0.0 copy-start
  5.7 0.2 select_bitcast_fusion.1
  6.0 1.2 copy-done
  7.1 0.2 select_bitcast_fusion
  7.4 0.3 fusion.5
  7.6 2.8 %copy.14 = bf16[2,64,12,512]{3,0,2,1:T(2,128)(2,1)} copy(bf16[2,64,12,512]{3,2,1,0:T(8,128)(2,1)S(1)} %fusion.5) | data formatting | bytes 3145728 | tf_op jit(solution)/shard_map/slice | solution.py:95
  10.4 10.6 %all-to-all-start = ((bf16[2,64,12,512]{3,0,2,1:T(2,128)(2,1)}), bf16[2,64,12,512]{3,0,2,1:T(2,128)(2,1)}, u32[]{:S(2)}, u32[]{:S(2)}) async-start(bf16[2,64,12,512]{3,0,2,1:T(2,128)(2,1)} %copy.14), calls=%async_computation | async-start | bytes 3145728 | tf_op jit(solution)/shard_map/all_to_all | solution.py:97
  21.0 0.0 copy-done.12
  21.1 0.1 select_reduce_fusion.4
  21.2 0.1 select_reduce_fusion.2
  21.3 0.0 copy-done.6
  21.4 0.8 gather_fusion.1
  22.1 0.8 gather_fusion
  22.9 0.6 fusion.60
  23.5 0.0 copy-start.11
  23.6 1.1 pad_maximum_fusion.8
  24.7 0.5 and_select_fusion
  25.2 0.5 and_select_fusion.1
  25.7 0.0 copy-done.11
  25.7 0.0 copy-done.9
  25.7 1.0 convolution_convert_fusion.7
  26.8 1.8 %convolution_convert_fusion.6 = bf16[768,768]{0,1:T(8,128)(2,1)S(1)} fusion(s32[768]{0:T(1024)S(1)} %get-tuple-element.45, s32[768]{0:T(1024)S(1)} %get-tuple-element.46, pred[768]{0:T(1024)(128)(4,1)} %copy-done.9, bf16[1,12,12]{2,0,1:T(2,128)(2,1)S(1)} %get-tuple-element.36), kind=kOutput, calls=%fused_computation.25 | convolution fusion | flops 15012864 | bytes 1186848 | tf_op jit(solution)/shard_map/dot_general | solution.py:49
  28.5 1.8 %fusion.8 = bf16[768,768]{0,1:T(8,128)(2,1)S(1)} fusion(bf16[768,768]{0,1:T(8,128)(2,1)S(1)} %convolution_convert_fusion.7, s32[768]{0:T(1024)S(1)} %get-tuple-element.47, s32[768]{0:T(1024)S(1)} %get-tuple-element.48, pred[768]{0:T(1024)(128)(4,1)} %fusion.60, s32[64]{0:T(128)} %and_select_fusion.1), kind=kOutput, calls=%fused_computation.29 | convolution fusion | flops 84987904 | bytes 2366464 | tf_op jit(solution)/shard_map/dot_general | solution.py:49
  30.3 2.8 %fusion.9 = bf16[768,768]{0,1:T(8,128)(2,1)} fusion(bf16[768,768]{0,1:T(8,128)(2,1)S(1)} %convolution_convert_fusion.6, s32[768]{0:T(1024)S(1)} %get-tuple-element.47, s32[768]{0:T(1024)S(1)} %get-tuple-element.48, pred[768]{0:T(1024)(128)(4,1)} %fusion.60, s32[64]{0:T(128)} %and_select_fusion), kind=kOutput, calls=%fused_computation.30 | convolution fusion | flops 84987904 | bytes 2366464 | tf_op jit(solution)/shard_map/dot_general | solution.py:49
  33.1 11.7 %all-to-all-done = bf16[2,64,12,512]{3,0,2,1:T(2,128)(2,1)} async-done(((bf16[2,64,12,512]{3,0,2,1:T(2,128)(2,1)}), bf16[2,64,12,512]{3,0,2,1:T(2,128)(2,1)}, u32[]{:S(2)}, u32[]{:S(2)}) %all-to-all-start) | async-done | bytes 1572896 | tf_op jit(solution)/shard_map/all_to_all | solution.py:97
  44.8 1.9 %copy.15 = bf16[2,64,12,512]{3,2,1,0:T(8,128)(2,1)S(1)} copy(bf16[2,64,12,512]{3,0,2,1:T(2,128)(2,1)} %all-to-all-done) | data formatting | bytes 3145728 | tf_op jit(solution)/shard_map/all_to_all | solution.py:97
  46.7 1.4 %reshape.24 = bf16[1536,512]{1,0:T(8,128)(2,1)} reshape(bf16[2,64,12,512]{3,2,1,0:T(8,128)(2,1)S(1)} %copy.15) | data formatting | bytes 3145728 | tf_op jit(solution)/shard_map/reshape | solution.py:99
  48.0 4.1 %fusion.11 = bf16[768,512]{1,0:T(8,128)(2,1)} fusion(bf16[1536,512]{1,0:T(8,128)(2,1)} %reshape.24, bf16[768,768]{0,1:T(8,128)(2,1)} %fusion.9, bf16[768,768]{0,1:T(8,128)(2,1)S(1)} %fusion.8), kind=kOutput, calls=%fused_computation.32 | convolution fusion | flops 1213071360 | bytes 4718592 | tf_op jit(solution)/shard_map/dot_general | solution.py:98
  52.2 1.7 %copy.16 = bf16[2,64,12,256]{3,0,2,1:T(2,128)(2,1)} copy(bf16[2,64,12,256]{3,2,1,0:T(8,128)(2,1)S(1)} %copy-done.1) | data formatting | bytes 1572864 | tf_op jit(solution)/shard_map/optimization_barrier | solution.py:110
  53.9 4.6 %all-to-all-start.1 = ((bf16[2,64,12,256]{3,0,2,1:T(2,128)(2,1)}), bf16[2,64,12,256]{3,0,2,1:T(2,128)(2,1)S(1)}, u32[]{:S(2)}, u32[]{:S(2)}) async-start(bf16[2,64,12,256]{3,0,2,1:T(2,128)(2,1)} %copy.16), calls=%async_computation.1 | async-start | bytes 1572864 | tf_op jit(solution)/shard_map/all_to_all | solution.py:97
  58.6 3.3 %collective-permute-start = (bf16[768,512]{1,0:T(8,128)(2,1)}, bf16[768,512]{1,0:T(8,128)(2,1)}, u32[]{:S(2)}, u32[]{:S(2)}) collective-permute-start(bf16[768,512]{1,0:T(8,128)(2,1)} %fusion.11), channel_id=1, source_target_pairs={{0,1},{1,0},{2,3},{3,2},{4,5},{5,4},{6,7},{7,6},{8,9},{9,8},{10,11... | collective-permute-start | bytes 2359304 | tf_op jit(solution)/shard_map/ppermute | solution.py:17
  61.9 21.1 %all-to-all-done.1 = bf16[2,64,12,256]{3,0,2,1:T(2,128)(2,1)S(1)} async-done(((bf16[2,64,12,256]{3,0,2,1:T(2,128)(2,1)}), bf16[2,64,12,256]{3,0,2,1:T(2,128)(2,1)S(1)}, u32[]{:S(2)}, u32[]{:S(2)}) %all-to-all-start.1) | async-done | bytes 786464 | tf_op jit(solution)/shard_map/all_to_all | solution.py:97
  82.9 0.2 copy.17
  83.1 0.2 reshape.25
  83.3 0.0 copy-start.7
  83.3 2.1 %fusion.13 = bf16[768,256]{1,0:T(8,128)(2,1)S(1)} fusion(bf16[1536,256]{1,0:T(8,128)(2,1)S(1)} %reshape.25, bf16[768,768]{0,1:T(8,128)(2,1)} %fusion.9, bf16[768,768]{0,1:T(8,128)(2,1)S(1)} %fusion.8), kind=kOutput, calls=%fused_computation.34 | convolution fusion | flops 608894976 | bytes 3538944 | tf_op jit(solution)/shard_map/dot_general | solution.py:98
  85.4 0.2 copy.18
  85.6 0.3 reshape.26
  85.9 0.0 copy-start.3
  85.9 0.1 collective-permute-start.1
  86.0 1.3 %convolution_convert_fusion.5 = bf16[768,768]{1,0:T(8,128)(2,1)S(1)} fusion(bf16[768,12]{0,1:T(8,128)(2,1)S(1)} %reshape.26, s32[768]{0:T(1024)S(1)} %get-tuple-element.45, s32[768]{0:T(1024)S(1)} %get-tuple-element.46, pred[768]{0:T(1024)(128)(4,1)S(1)} %copy-done.10), kind=kOutput, calls=%fused_computation.24 | convolution fusion | flops 14764032 | bytes 1204992 | tf_op jit(solution)/shard_map/dot_general | solution.py:49
  87.3 1.0 fusion.10
  88.3 0.0 copy-done.3
  88.3 0.0 copy-start.2
  88.3 1.1 convolution_convert_fusion.1
  89.4 0.0 copy-done.2
  89.4 0.0 copy-start.4
  89.4 15.4 %collective-permute-done = bf16[768,512]{1,0:T(8,128)(2,1)} collective-permute-done((bf16[768,512]{1,0:T(8,128)(2,1)}, bf16[768,512]{1,0:T(8,128)(2,1)}, u32[]{:S(2)}, u32[]{:S(2)}) %collective-permute-start) | collective-permute-done | bytes 786464 | tf_op jit(solution)/shard_map/ppermute | solution.py:17
  104.8 1.7 %add_convert_fusion = bf16[768,512]{1,0:T(8,128)(2,1)S(1)} fusion(bf16[768,512]{1,0:T(8,128)(2,1)} %collective-permute-done, bf16[768,512]{1,0:T(8,128)(2,1)} %fusion.11, f32[]{:T(128)S(6)} %add.80, f32[]{:T(128)S(6)} %add.76), kind=kLoop, calls=%fused_computation.18 | loop fusion | flops 2359296 | bytes 2359304 | tf_op jit(solution)/shard_map/convert_element_type | solution.py:113
  106.5 0.0 copy-start.13
  106.5 0.8 fusion.17
  107.3 0.5 copy-done.13
  107.8 2.5 %fusion.14 = f32[768,768]{0,1:T(8,128)} fusion(bf16[768,768]{1,0:T(8,128)(2,1)S(1)} %convolution_convert_fusion.1, bf16[1,1,768,768]{3,2,1,0:T(8,128)(2,1)S(1)} %copy-done.13), kind=kOutput, calls=%fused_computation.36 | convolution fusion | flops 905969664 | bytes 4718592 | tf_op jit(solution)/shard_map/dot_general | solution.py:108
  110.3 2.9 %collective-permute-done.1 = bf16[768,256]{1,0:T(8,128)(2,1)S(1)} collective-permute-done((bf16[768,256]{1,0:T(8,128)(2,1)S(1)}, bf16[768,256]{1,0:T(8,128)(2,1)S(1)}, u32[]{:S(2)}, u32[]{:S(2)}) %collective-permute-start.1) | collective-permute-done | bytes 393248 | tf_op jit(solution)/shard_map/ppermute | solution.py:17
  113.2 0.9 add_convert_fusion.1
  114.1 5.3 %convolution_convert_fusion = bf16[768,768]{1,0:T(8,128)(2,1)} fusion(bf16[768,768]{1,0:T(8,128)(2,1)} %copy-done.2, f32[768,768]{1,0:T(8,128)S(1)} %fusion.17, f32[768,768]{0,1:T(8,128)} %fusion.14, bf16[768,256]{1,0:T(8,128)(2,1)} %add_convert_fusion.1, bf16[1,1,768,768]{3,2,1,0:T(8,128)(2,1)} %param.13, bf16[768,512]{1,0:T(8,128)(2,1)S(1)} %add_convert_fusion, ...), kind=kOutput, calls=%fused_computation.19 | convolution fusion | flops 1214447616 | bytes 10223616 | tf_op jit(solution)/shard_map/dot_general | solution.py:49
  119.4 2.5 %fusion.19 = f32[768,768]{1,0:T(8,128)S(1)} fusion(bf16[768,768]{1,0:T(8,128)(2,1)} %convolution_convert_fusion, bf16[768,256]{1,0:T(8,128)(2,1)S(1)} %copy-done.5, bf16[768,512]{1,0:T(8,128)(2,1)S(1)} %add_convert_fusion), kind=kOutput, calls=%fused_computation.47 | convolution fusion | flops 908328960 | bytes 4718592 | tf_op jit(solution)/shard_map/dot_general | solution.py:129
  122.0 2.2 %fusion.12 = bf16[1,1,768,768]{3,2,1,0:T(8,128)(2,1)} fusion(f32[768,768]{1,0:T(8,128)S(1)} %fusion.19, bf16[768,768]{1,0:T(8,128)(2,1)S(1)} %copy-done.15, bf16[1,1,768,768]{3,2,1,0:T(8,128)(2,1)S(1)} %copy-done.14, bf16[768,256]{1,0:T(8,128)(2,1)S(1)} %copy-done.5, bf16[768,512]{1,0:T(8,128)(2,1)S(1)} %add_convert_fusion), kind=kOutput, calls=%fused_computation.33 | convolution fusion | flops 911278080 | bytes 7077888 | tf_op jit(solution)/shard_map/dot_general | solution.py:128
  (32 shorter events, 0.2 us)
Async XLA Ops:
  5.7 1.4 %copy-start = (bf16[64,12,768]{2,1,0:T(8,128)(2,1)S(1)}, bf16[64,12,768]{2,1,0:T(8,128)(2,1)}, u32[]{:S(2)}) copy-start(bf16[64,12,768]{2,1,0:T(8,128)(2,1)} %gather_fusion.3) | copy-start | bytes 3538948
  10.4 10.6 %copy-start.12 = (s32[2,64]{1,0:T(2,128)S(1)}, s32[2,64]{1,0:T(2,128)}, u32[]{:S(2)}) copy-start(s32[2,64]{1,0:T(2,128)} %param.17) | copy-start | bytes 1540
  10.4 10.9 %copy-start.6 = (s32[2,64,64]{2,1,0:T(8,128)S(1)}, s32[2,64,64]{2,1,0:T(8,128)}, u32[]{:S(2)}) copy-start(s32[2,64,64]{2,1,0:T(8,128)} %param.16) | copy-start | bytes 98308
  10.4 34.4 %all-to-all-start = ((bf16[2,64,12,512]{3,0,2,1:T(2,128)(2,1)}), bf16[2,64,12,512]{3,0,2,1:T(2,128)(2,1)}, u32[]{:S(2)}, u32[]{:S(2)}) async-start(bf16[2,64,12,512]{3,0,2,1:T(2,128)(2,1)} %copy.14), calls=%async_computation | async-start | bytes 3145728 | tf_op jit(solution)/shard_map/all_to_all | solution.py:97
  23.5 2.2 %copy-start.9 = (pred[768]{0:T(1024)(128)(4,1)}, pred[768]{0:T(1024)(128)(4,1)S(1)}, u32[]{:S(2)}) copy-start(pred[768]{0:T(1024)(128)(4,1)S(1)} %fusion.59) | copy-start | bytes 2308
  23.5 2.2 %copy-start.11 = (bf16[2,12,12]{2,0,1:T(2,128)(2,1)S(1)}, bf16[2,12,12]{2,0,1:T(2,128)(2,1)}, u32[]{:S(2)}) copy-start(bf16[2,12,12]{2,0,1:T(2,128)(2,1)} %param.15) | copy-start | bytes 1732
  48.0 4.1 %copy-start.1 = (bf16[2,64,12,256]{3,2,1,0:T(8,128)(2,1)S(1)}, bf16[2,64,12,256]{3,2,1,0:T(8,128)(2,1)}, u32[]{:S(2)}) copy-start(bf16[2,64,12,256]{3,2,1,0:T(8,128)(2,1)} %pad_maximum_fusion.8) | copy-start | bytes 2359300
  53.9 29.0 %all-to-all-start.1 = ((bf16[2,64,12,256]{3,0,2,1:T(2,128)(2,1)}), bf16[2,64,12,256]{3,0,2,1:T(2,128)(2,1)S(1)}, u32[]{:S(2)}, u32[]{:S(2)}) async-start(bf16[2,64,12,256]{3,0,2,1:T(2,128)(2,1)} %copy.16), calls=%async_computation.1 | async-start | bytes 1572864 | tf_op jit(solution)/shard_map/all_to_all | solution.py:97
  58.6 46.3 %collective-permute-start = (bf16[768,512]{1,0:T(8,128)(2,1)}, bf16[768,512]{1,0:T(8,128)(2,1)}, u32[]{:S(2)}, u32[]{:S(2)}) collective-permute-start(bf16[768,512]{1,0:T(8,128)(2,1)} %fusion.11), channel_id=1, source_target_pairs={{0,1},{1,0},{2,3},{3,2},{4,5},{5,4},{6,7},{7,6},{8,9},{9,8},{10,11... | collective-permute-start | bytes 2359304 | tf_op jit(solution)/shard_map/ppermute | solution.py:17
  83.3 2.1 %copy-start.7 = (bf16[1,1,64,12,12]{2,4,3,1,0:T(8,128)(2,1)S(1)}, bf16[1,1,64,12,12]{2,4,3,1,0:T(8,128)(2,1)}, u32[]{:S(2)}) copy-start(bf16[1,1,64,12,12]{2,4,3,1,0:T(8,128)(2,1)} %param.14) | copy-start | bytes 55300
  83.3 2.7 %copy-start.10 = (pred[768]{0:T(1024)(128)(4,1)S(1)}, pred[768]{0:T(1024)(128)(4,1)}, u32[]{:S(2)}) copy-start(pred[768]{0:T(1024)(128)(4,1)} %copy-done.9) | copy-start | bytes 2308
  85.4 1.9 %copy-start.8 = (pred[768]{0:T(1024)(128)(4,1)S(1)}, pred[768]{0:T(1024)(128)(4,1)}, u32[]{:S(2)}) copy-start(pred[768]{0:T(1024)(128)(4,1)} %fusion.60) | copy-start | bytes 2308
  85.9 2.4 %copy-start.3 = (bf16[1,1,768,768]{3,2,1,0:T(8,128)(2,1)S(1)}, bf16[1,1,768,768]{3,2,1,0:T(8,128)(2,1)}, u32[]{:S(2)}) copy-start(bf16[1,1,768,768]{3,2,1,0:T(8,128)(2,1)} %param.12) | copy-start | bytes 3538948
  85.9 27.3 %collective-permute-start.1 = (bf16[768,256]{1,0:T(8,128)(2,1)S(1)}, bf16[768,256]{1,0:T(8,128)(2,1)S(1)}, u32[]{:S(2)}, u32[]{:S(2)}) collective-permute-start(bf16[768,256]{1,0:T(8,128)(2,1)S(1)} %fusion.13), channel_id=1, source_target_pairs={{0,1},{1,0},{2,3},{3,2},{4,5},{5,4},{6,7},{7,6},{8,9},{9,8},{10,11... | collective-permute-start | bytes 1179656 | tf_op jit(solution)/shard_map/ppermute | solution.py:17
  88.3 1.1 copy-start.2
  89.4 17.9 %copy-start.4 = (bf16[768,768]{1,0:T(8,128)(2,1)}, bf16[768,768]{1,0:T(8,128)(2,1)S(1)}, u32[]{:S(2)}) copy-start(bf16[768,768]{1,0:T(8,128)(2,1)S(1)} %convolution_convert_fusion.1) | copy-start | bytes 3538948
  106.5 1.3 %copy-start.13 = (bf16[1,1,768,768]{3,2,1,0:T(8,128)(2,1)S(1)}, bf16[1,1,768,768]{3,2,1,0:T(8,128)(2,1)}, u32[]{:S(2)}) copy-start(bf16[1,1,768,768]{3,2,1,0:T(8,128)(2,1)} %param.13) | copy-start | bytes 3538948
  114.1 5.3 %copy-start.5 = (bf16[768,256]{1,0:T(8,128)(2,1)S(1)}, bf16[768,256]{1,0:T(8,128)(2,1)}, u32[]{:S(2)}) copy-start(bf16[768,256]{1,0:T(8,128)(2,1)} %add_convert_fusion.1) | copy-start | bytes 1179652
  119.4 2.5 %copy-start.14 = (bf16[1,1,768,768]{3,2,1,0:T(8,128)(2,1)S(1)}, bf16[1,1,768,768]{3,2,1,0:T(8,128)(2,1)}, u32[]{:S(2)}) copy-start(bf16[1,1,768,768]{3,2,1,0:T(8,128)(2,1)} %param.13) | copy-start | bytes 3538948
  119.4 2.5 %copy-start.15 = (bf16[768,768]{1,0:T(8,128)(2,1)S(1)}, bf16[768,768]{1,0:T(8,128)(2,1)}, u32[]{:S(2)}) copy-start(bf16[768,768]{1,0:T(8,128)(2,1)} %convolution_convert_fusion) | copy-start | bytes 3538948

commit v10 on v9

--- a/solution.py
+++ b/solution.py
@@ -70,16 +70,14 @@
     coef_self = sum(jnp.where(channel == c, jnp.float32(v), 0.0) for c, v in enumerate(COEF_SELF))
     coef_pair = sum(jnp.where(channel == c, jnp.float32(v), 0.0) for c, v in enumerate(COEF_PAIR))
 
-    blocks = current.reshape(freqs, forms, order_len)
     expand = block_rows(order_len, freqs)
     forms_expand = form_rows(order_len, forms)
     packs = []
     mixes = []
     for r in range(2):
         send_order, recv_slots = crossing_plan(cross_tables[r], freq_perm[r], momentum, freqs)
-        packs.append(jnp.take(blocks, send_order, axis=0))
+        packs.append(send_order)
         mixes.append(mix_matrix(recv_slots, form_mix[r], freqs, expand, forms_expand))
-    stacked = jnp.stack(packs)
     mix = jnp.concatenate(mixes, axis=1)
 
     def carry_of(mat, bubble_mat):
@@ -92,7 +90,10 @@
     assert sum(WIDTHS) == order_len
     starts = [sum(WIDTHS[:k]) for k in range(NCHUNK)]
     red_chunks = []
-    pieces = [stacked[..., starts[k]:starts[k] + WIDTHS[k]] for k in range(NCHUNK)]
+    pieces = []
+    for k in range(NCHUNK):
+        blocks = current[:, starts[k]:starts[k] + WIDTHS[k]].reshape(freqs, forms, WIDTHS[k])
+        pieces.append(jnp.stack([jnp.take(blocks, order, axis=0) for order in packs]))
     for k in range(NCHUNK):
         received = lax.all_to_all(pieces[k], "mom", split_axis=1, concat_axis=1, tiled=True)
         summed = jnp.dot(

time: 125 us -> 122 us (0.976)
  other arithmetic: 6.56 us -> 4.16 us
    slice x1 -> x2, local copies, waits for them, and re-layouts: 2.76 us -> 2.21 us  [local(): current[:, starts[k]:starts[k] + WIDTHS[k]].reshape(freqs, forms, WIDTHS[k])]
  transfers between devices with their start and end apart: 4 -> 4, of which waited for: 4 -> 4; matrix products, arithmetic and copies ran while one was open for 19% -> 18% of each run, Pallas kernels for 0% -> 0%
where the time goes in v10:
time: 122 us; the launch traced here: 121 us
  waiting for transfers between devices  51.8 us (42%)
  matrix products  29.4 us (24%)
  starting transfers between devices  18.6 us (15%)
  local copies, waits for them, and re-layouts  16.6 us (14%)
  other arithmetic  4.16 us (3%)
    all_to_all x2, waiting for transfers between devices, local(): lax.all_to_all(pieces[k], 'mom', split_axis=1, concat_axis=1, tiled=True)  33.8 us
    ppermute x2, waiting for transfers between devices, partner_2(): return lax.ppermute(value, axis, pairs)  17.9 us
    all_to_all x2, starting transfers between devices, local(): lax.all_to_all(pieces[k], 'mom', split_axis=1, concat_axis=1, tiled=True)  15.4 us
    dot_general x8, matrix products, exact_dot(): jnp.dot(a, b, preferred_element_type=jnp.float32).astype(jnp.bfloat16)  14.9 us
    dot_general x2, matrix products, local(): jnp.dot(mix, received.reshape(2 * order_len, WIDTHS[k]), preferred_elemen...  6.51 us
    ppermute x2, starting transfers between devices, partner_2(): return lax.ppermute(value, axis, pairs)  3.17 us
    another operation x1, local copies, waits for them, and re-layouts, local(): jnp.stack([jnp.take(blocks, order, axis=0) for order in packs])  2.76 us
    convert_element_type x2, other arithmetic, local(): (coef_self * summed.astype(jnp.float32) + coef_pair * other.astype(jnp.fl...  2.57 us
  transfers between devices with their start and end apart: 4, of which 4 were waited for; matrix products, arithmetic and copies ran while one was open for 18% of the time, Pallas kernels for 0%

profile of v10, /device:TPU:1, one launch (start us, length us, event | category | flops | bytes accessed | tf_op | source)
XLA Modules:
  0.0 121.1 jit_solution(272126947946886480)
XLA Ops:
  0.0 0.8 slice_bitcast_fusion.1
  0.8 0.1 select_reduce_fusion
  0.9 0.1 select_reduce_fusion.1
  1.1 1.2 slice.59
  2.3 0.2 reshape.35
  2.5 0.6 gather_fusion.3
  3.1 0.6 gather_fusion.2
  3.7 0.2 select_bitcast_fusion.1
  3.9 0.2 select_bitcast_fusion
  4.1 0.3 pad_maximum_fusion.1
  4.3 2.8 %copy.14 = bf16[2,64,12,512]{3,0,2,1:T(2,128)(2,1)} copy(bf16[2,64,12,512]{3,2,1,0:T(8,128)(2,1)S(1)} %pad_maximum_fusion.1) | data formatting | bytes 3145728 | tf_op jit(solution)/shard_map/stack | solution.py:96
  7.1 10.6 %all-to-all-start = ((bf16[2,64,12,512]{3,0,2,1:T(2,128)(2,1)}), bf16[2,64,12,512]{3,0,2,1:T(2,128)(2,1)}, u32[]{:S(2)}, u32[]{:S(2)}) async-start(bf16[2,64,12,512]{3,0,2,1:T(2,128)(2,1)} %copy.14), calls=%async_computation | async-start | bytes 3145728 | tf_op jit(solution)/shard_map/all_to_all | solution.py:98
  17.8 0.1 select_reduce_fusion.4
  17.9 0.1 select_reduce_fusion.2
  18.0 1.0 slice.60
  19.0 0.0 copy-start.5
  19.1 0.1 reshape.37
  19.1 0.6 gather_fusion.5
  19.8 0.6 gather_fusion.4
  20.4 0.8 gather_fusion.1
  21.2 0.8 gather_fusion
  22.0 0.1 select_bitcast_fusion.3
  22.2 0.0 copy-start.11
  22.2 0.1 select_bitcast_fusion.2
  22.3 0.1 pad_maximum_fusion.9
  22.5 0.4 copy-done.11
  22.9 1.0 convolution_convert_fusion.7
  23.9 1.0 convolution_convert_fusion.6
  24.9 2.1 %fusion.7 = bf16[768,768]{0,1:T(8,128)(2,1)} fusion(bf16[768,768]{0,1:T(8,128)(2,1)S(1)} %convolution_convert_fusion.7, s32[768]{0:T(1024)S(1)} %get-tuple-element.48, s32[768]{0:T(1024)S(1)} %get-tuple-element.49, pred[768]{0:T(1024)(128)(4,1)S(1)} %fusion.59, s32[64]{0:T(128)S(1)} %and_select_fusion.1), kind=kOutput, calls=%fused_computation.27 | convolution fusion | flops 84987904 | bytes 2366464 | tf_op jit(solution)/shard_map/dot_general | solution.py:49
  27.0 2.1 %fusion.8 = bf16[768,768]{0,1:T(8,128)(2,1)} fusion(bf16[768,768]{0,1:T(8,128)(2,1)S(1)} %convolution_convert_fusion.6, s32[768]{0:T(1024)S(1)} %get-tuple-element.48, s32[768]{0:T(1024)S(1)} %get-tuple-element.49, pred[768]{0:T(1024)(128)(4,1)S(1)} %fusion.59, s32[64]{0:T(128)S(1)} %and_select_fusion), kind=kOutput, calls=%fused_computation.28 | convolution fusion | flops 84987904 | bytes 2366464 | tf_op jit(solution)/shard_map/dot_general | solution.py:49
  29.1 12.4 %all-to-all-done = bf16[2,64,12,512]{3,0,2,1:T(2,128)(2,1)} async-done(((bf16[2,64,12,512]{3,0,2,1:T(2,128)(2,1)}), bf16[2,64,12,512]{3,0,2,1:T(2,128)(2,1)}, u32[]{:S(2)}, u32[]{:S(2)}) %all-to-all-start) | async-done | bytes 1572896 | tf_op jit(solution)/shard_map/all_to_all | solution.py:98
  41.5 1.9 %copy.15 = bf16[2,64,12,512]{3,2,1,0:T(8,128)(2,1)S(1)} copy(bf16[2,64,12,512]{3,0,2,1:T(2,128)(2,1)} %all-to-all-done) | data formatting | bytes 3145728 | tf_op jit(solution)/shard_map/all_to_all | solution.py:98
  43.4 1.4 %reshape.36 = bf16[1536,512]{1,0:T(8,128)(2,1)} reshape(bf16[2,64,12,512]{3,2,1,0:T(8,128)(2,1)S(1)} %copy.15) | data formatting | bytes 3145728 | tf_op jit(solution)/shard_map/reshape | solution.py:100
  44.7 4.4 %fusion.10 = bf16[768,512]{1,0:T(8,128)(2,1)} fusion(bf16[1536,512]{1,0:T(8,128)(2,1)} %reshape.36, bf16[768,768]{0,1:T(8,128)(2,1)} %fusion.8, bf16[768,768]{0,1:T(8,128)(2,1)} %fusion.7), kind=kOutput, calls=%fused_computation.30 | convolution fusion | flops 1213071360 | bytes 4718592 | tf_op jit(solution)/shard_map/dot_general | solution.py:99
  49.1 1.7 %copy.16 = bf16[2,64,12,256]{3,0,2,1:T(2,128)(2,1)} copy(bf16[2,64,12,256]{3,2,1,0:T(8,128)(2,1)S(1)} %pad_maximum_fusion.9) | data formatting | bytes 1572864 | tf_op jit(solution)/shard_map/optimization_barrier | solution.py:111
  50.9 4.8 %all-to-all-start.1 = ((bf16[2,64,12,256]{3,0,2,1:T(2,128)(2,1)}), bf16[2,64,12,256]{3,0,2,1:T(2,128)(2,1)S(1)}, u32[]{:S(2)}, u32[]{:S(2)}) async-start(bf16[2,64,12,256]{3,0,2,1:T(2,128)(2,1)} %copy.16), calls=%async_computation.1 | async-start | bytes 1572864 | tf_op jit(solution)/shard_map/all_to_all | solution.py:98
  55.7 3.1 %collective-permute-start = (bf16[768,512]{1,0:T(8,128)(2,1)}, bf16[768,512]{1,0:T(8,128)(2,1)}, u32[]{:S(2)}, u32[]{:S(2)}) collective-permute-start(bf16[768,512]{1,0:T(8,128)(2,1)} %fusion.10), channel_id=1, source_target_pairs={{0,1},{1,0},{2,3},{3,2},{4,5},{5,4},{6,7},{7,6},{8,9},{9,8},{10,11... | collective-permute-start | bytes 2359304 | tf_op jit(solution)/shard_map/ppermute | solution.py:17
  58.8 21.4 %all-to-all-done.1 = bf16[2,64,12,256]{3,0,2,1:T(2,128)(2,1)S(1)} async-done(((bf16[2,64,12,256]{3,0,2,1:T(2,128)(2,1)}), bf16[2,64,12,256]{3,0,2,1:T(2,128)(2,1)S(1)}, u32[]{:S(2)}, u32[]{:S(2)}) %all-to-all-start.1) | async-done | bytes 786464 | tf_op jit(solution)/shard_map/all_to_all | solution.py:98
  80.2 0.2 copy.17
  80.4 0.2 reshape.38
  80.6 0.0 copy-done.1
  80.6 0.0 copy-start.6
  80.6 2.1 %fusion.12 = bf16[768,256]{1,0:T(8,128)(2,1)S(1)} fusion(bf16[1536,256]{1,0:T(8,128)(2,1)S(1)} %reshape.38, bf16[768,768]{0,1:T(8,128)(2,1)} %fusion.8, bf16[768,768]{0,1:T(8,128)(2,1)S(1)} %copy-done.1), kind=kOutput, calls=%fused_computation.32 | convolution fusion | flops 608894976 | bytes 3538944 | tf_op jit(solution)/shard_map/dot_general | solution.py:99
  82.7 0.2 copy.18
  82.9 0.3 reshape.39
  83.2 0.0 copy-start
  83.2 0.1 collective-permute-start.1
  83.3 0.0 copy-done.10
  83.3 1.3 %convolution_convert_fusion.5 = bf16[768,768]{1,0:T(8,128)(2,1)S(1)} fusion(bf16[768,12]{0,1:T(8,128)(2,1)S(1)} %reshape.39, s32[768]{0:T(1024)S(1)} %get-tuple-element.46, s32[768]{0:T(1024)S(1)} %get-tuple-element.47, pred[768]{0:T(1024)(128)(4,1)S(1)} %copy-done.10), kind=kOutput, calls=%fused_computation.22 | convolution fusion | flops 14764032 | bytes 1204992 | tf_op jit(solution)/shard_map/dot_general | solution.py:49
  84.6 1.0 fusion.9
  85.6 0.0 copy-done
  85.6 0.0 copy-start.2
  85.6 1.1 convolution_convert_fusion.1
  86.8 15.1 %collective-permute-done = bf16[768,512]{1,0:T(8,128)(2,1)} collective-permute-done((bf16[768,512]{1,0:T(8,128)(2,1)}, bf16[768,512]{1,0:T(8,128)(2,1)}, u32[]{:S(2)}, u32[]{:S(2)}) %collective-permute-start) | collective-permute-done | bytes 786464 | tf_op jit(solution)/shard_map/ppermute | solution.py:17
  101.8 1.7 %add_convert_fusion = bf16[768,512]{1,0:T(8,128)(2,1)S(1)} fusion(bf16[768,512]{1,0:T(8,128)(2,1)} %collective-permute-done, bf16[768,512]{1,0:T(8,128)(2,1)} %fusion.10, f32[]{:T(128)S(6)} %add.86, f32[]{:T(128)S(6)} %add.82), kind=kLoop, calls=%fused_computation.16 | loop fusion | flops 2359296 | bytes 2359304 | tf_op jit(solution)/shard_map/convert_element_type | solution.py:114
  103.5 0.0 copy-start.13
  103.5 0.8 fusion.16
  104.3 0.5 copy-done.13
  104.7 2.5 %fusion.13 = f32[768,768]{0,1:T(8,128)} fusion(bf16[768,768]{1,0:T(8,128)(2,1)S(1)} %convolution_convert_fusion.1, bf16[1,1,768,768]{3,2,1,0:T(8,128)(2,1)S(1)} %copy-done.13), kind=kOutput, calls=%fused_computation.34 | convolution fusion | flops 905969664 | bytes 4718592 | tf_op jit(solution)/shard_map/dot_general | solution.py:109
  107.3 2.9 %collective-permute-done.1 = bf16[768,256]{1,0:T(8,128)(2,1)S(1)} collective-permute-done((bf16[768,256]{1,0:T(8,128)(2,1)S(1)}, bf16[768,256]{1,0:T(8,128)(2,1)S(1)}, u32[]{:S(2)}, u32[]{:S(2)}) %collective-permute-start.1) | collective-permute-done | bytes 393248 | tf_op jit(solution)/shard_map/ppermute | solution.py:17
  110.1 0.9 add_convert_fusion.1
  111.1 5.3 %convolution_convert_fusion = bf16[768,768]{1,0:T(8,128)(2,1)} fusion(bf16[768,768]{1,0:T(8,128)(2,1)} %copy-done.2, f32[768,768]{1,0:T(8,128)S(1)} %fusion.16, f32[768,768]{0,1:T(8,128)} %fusion.13, bf16[768,256]{1,0:T(8,128)(2,1)} %add_convert_fusion.1, bf16[1,1,768,768]{3,2,1,0:T(8,128)(2,1)} %param.15, bf16[768,512]{1,0:T(8,128)(2,1)S(1)} %add_convert_fusion, ...), kind=kOutput, calls=%fused_computation.17 | convolution fusion | flops 1214447616 | bytes 10223616 | tf_op jit(solution)/shard_map/dot_general | solution.py:49
  116.4 2.5 %fusion.18 = f32[768,768]{1,0:T(8,128)S(1)} fusion(bf16[768,768]{1,0:T(8,128)(2,1)} %convolution_convert_fusion, bf16[768,256]{1,0:T(8,128)(2,1)S(1)} %copy-done.4, bf16[768,512]{1,0:T(8,128)(2,1)S(1)} %add_convert_fusion), kind=kOutput, calls=%fused_computation.47 | convolution fusion | flops 908328960 | bytes 4718592 | tf_op jit(solution)/shard_map/dot_general | solution.py:130
  118.9 2.2 %fusion.11 = bf16[1,1,768,768]{3,2,1,0:T(8,128)(2,1)} fusion(f32[768,768]{1,0:T(8,128)S(1)} %fusion.18, bf16[768,768]{1,0:T(8,128)(2,1)S(1)} %copy-done.15, bf16[1,1,768,768]{3,2,1,0:T(8,128)(2,1)S(1)} %copy-done.14, bf16[768,256]{1,0:T(8,128)(2,1)S(1)} %copy-done.4, bf16[768,512]{1,0:T(8,128)(2,1)S(1)} %add_convert_fusion), kind=kOutput, calls=%fused_computation.31 | convolution fusion | flops 911278080 | bytes 7077888 | tf_op jit(solution)/shard_map/dot_general | solution.py:129
  (39 shorter events, 0.2 us)
Async XLA Ops:
  7.1 10.6 %copy-start.12 = (s32[2,64]{1,0:T(2,128)S(1)}, s32[2,64]{1,0:T(2,128)}, u32[]{:S(2)}) copy-start(s32[2,64]{1,0:T(2,128)} %param.19) | copy-start | bytes 1540
  7.1 34.4 %all-to-all-start = ((bf16[2,64,12,512]{3,0,2,1:T(2,128)(2,1)}), bf16[2,64,12,512]{3,0,2,1:T(2,128)(2,1)}, u32[]{:S(2)}, u32[]{:S(2)}) async-start(bf16[2,64,12,512]{3,0,2,1:T(2,128)(2,1)} %copy.14), calls=%async_computation | async-start | bytes 3145728 | tf_op jit(solution)/shard_map/all_to_all | solution.py:98
  19.0 1.3 %copy-start.5 = (s32[2,64,64]{2,1,0:T(8,128)S(1)}, s32[2,64,64]{2,1,0:T(8,128)}, u32[]{:S(2)}) copy-start(s32[2,64,64]{2,1,0:T(8,128)} %param.18) | copy-start | bytes 98308
  22.0 5.1 %copy-start.7 = (pred[768]{0:T(1024)(128)(4,1)}, pred[768]{0:T(1024)(128)(4,1)S(1)}, u32[]{:S(2)}) copy-start(pred[768]{0:T(1024)(128)(4,1)S(1)} %fusion.59) | copy-start | bytes 2308
  22.0 1.9 %copy-start.9 = (pred[768]{0:T(1024)(128)(4,1)}, pred[768]{0:T(1024)(128)(4,1)S(1)}, u32[]{:S(2)}) copy-start(pred[768]{0:T(1024)(128)(4,1)S(1)} %fusion.58) | copy-start | bytes 2308
  22.2 0.7 copy-start.11
  50.9 29.4 %all-to-all-start.1 = ((bf16[2,64,12,256]{3,0,2,1:T(2,128)(2,1)}), bf16[2,64,12,256]{3,0,2,1:T(2,128)(2,1)S(1)}, u32[]{:S(2)}, u32[]{:S(2)}) async-start(bf16[2,64,12,256]{3,0,2,1:T(2,128)(2,1)} %copy.16), calls=%async_computation.1 | async-start | bytes 1572864 | tf_op jit(solution)/shard_map/all_to_all | solution.py:98
  55.7 24.8 %copy-start.1 = (bf16[768,768]{0,1:T(8,128)(2,1)S(1)}, bf16[768,768]{0,1:T(8,128)(2,1)}, u32[]{:S(2)}) copy-start(bf16[768,768]{0,1:T(8,128)(2,1)} %fusion.7) | copy-start | bytes 3538948
  55.7 46.1 %collective-permute-start = (bf16[768,512]{1,0:T(8,128)(2,1)}, bf16[768,512]{1,0:T(8,128)(2,1)}, u32[]{:S(2)}, u32[]{:S(2)}) collective-permute-start(bf16[768,512]{1,0:T(8,128)(2,1)} %fusion.10), channel_id=1, source_target_pairs={{0,1},{1,0},{2,3},{3,2},{4,5},{5,4},{6,7},{7,6},{8,9},{9,8},{10,11... | collective-permute-start | bytes 2359304 | tf_op jit(solution)/shard_map/ppermute | solution.py:17
  80.6 2.1 %copy-start.6 = (bf16[1,1,64,12,12]{2,4,3,1,0:T(8,128)(2,1)S(1)}, bf16[1,1,64,12,12]{2,4,3,1,0:T(8,128)(2,1)}, u32[]{:S(2)}) copy-start(bf16[1,1,64,12,12]{2,4,3,1,0:T(8,128)(2,1)} %param.16) | copy-start | bytes 55300
  80.6 2.7 %copy-start.10 = (pred[768]{0:T(1024)(128)(4,1)S(1)}, pred[768]{0:T(1024)(128)(4,1)}, u32[]{:S(2)}) copy-start(pred[768]{0:T(1024)(128)(4,1)} %copy-done.9) | copy-start | bytes 2308
  82.7 1.9 %copy-start.8 = (pred[768]{0:T(1024)(128)(4,1)S(1)}, pred[768]{0:T(1024)(128)(4,1)}, u32[]{:S(2)}) copy-start(pred[768]{0:T(1024)(128)(4,1)} %copy-done.7) | copy-start | bytes 2308
  83.2 2.4 %copy-start = (bf16[1,1,768,768]{3,2,1,0:T(8,128)(2,1)S(1)}, bf16[1,1,768,768]{3,2,1,0:T(8,128)(2,1)}, u32[]{:S(2)}) copy-start(bf16[1,1,768,768]{3,2,1,0:T(8,128)(2,1)} %param.14) | copy-start | bytes 3538948
  83.2 26.9 %collective-permute-start.1 = (bf16[768,256]{1,0:T(8,128)(2,1)S(1)}, bf16[768,256]{1,0:T(8,128)(2,1)S(1)}, u32[]{:S(2)}, u32[]{:S(2)}) collective-permute-start(bf16[768,256]{1,0:T(8,128)(2,1)S(1)} %fusion.12), channel_id=1, source_target_pairs={{0,1},{1,0},{2,3},{3,2},{4,5},{5,4},{6,7},{7,6},{8,9},{9,8},{10,11... | collective-permute-start | bytes 1179656 | tf_op jit(solution)/shard_map/ppermute | solution.py:17
  85.6 1.1 copy-start.2
  86.7 17.5 %copy-start.3 = (bf16[768,768]{1,0:T(8,128)(2,1)}, bf16[768,768]{1,0:T(8,128)(2,1)S(1)}, u32[]{:S(2)}) copy-start(bf16[768,768]{1,0:T(8,128)(2,1)S(1)} %convolution_convert_fusion.1) | copy-start | bytes 3538948
  103.5 1.3 %copy-start.13 = (bf16[1,1,768,768]{3,2,1,0:T(8,128)(2,1)S(1)}, bf16[1,1,768,768]{3,2,1,0:T(8,128)(2,1)}, u32[]{:S(2)}) copy-start(bf16[1,1,768,768]{3,2,1,0:T(8,128)(2,1)} %param.15) | copy-start | bytes 3538948
  111.0 5.3 %copy-start.4 = (bf16[768,256]{1,0:T(8,128)(2,1)S(1)}, bf16[768,256]{1,0:T(8,128)(2,1)}, u32[]{:S(2)}) copy-start(bf16[768,256]{1,0:T(8,128)(2,1)} %add_convert_fusion.1) | copy-start | bytes 1179652
  116.4 2.5 %copy-start.14 = (bf16[1,1,768,768]{3,2,1,0:T(8,128)(2,1)S(1)}, bf16[1,1,768,768]{3,2,1,0:T(8,128)(2,1)}, u32[]{:S(2)}) copy-start(bf16[1,1,768,768]{3,2,1,0:T(8,128)(2,1)} %param.15) | copy-start | bytes 3538948
  116.4 2.5 %copy-start.15 = (bf16[768,768]{1,0:T(8,128)(2,1)S(1)}, bf16[768,768]{1,0:T(8,128)(2,1)}, u32[]{:S(2)}) copy-start(bf16[768,768]{1,0:T(8,128)(2,1)} %convolution_convert_fusion) | copy-start | bytes 3538948

commit v11 on v10

--- a/solution.py
+++ b/solution.py
@@ -110,19 +110,22 @@
         if k + 1 < NCHUNK:
             summed, pieces[k + 1] = lax.optimization_barrier((summed, pieces[k + 1]))
         red_chunks.append((summed, partner_2(summed, "spin", 0)))
-    red_chunks = [
-        (coef_self * summed.astype(jnp.float32) + coef_pair * other.astype(jnp.float32)).astype(
-            jnp.bfloat16
-        )
-        for summed, other in red_chunks
-    ]
+    reduce_pair = lambda summed, other: (
+        coef_self * summed.astype(jnp.float32) + coef_pair * other.astype(jnp.float32)
+    ).astype(jnp.bfloat16)
+    red_chunks = [reduce_pair(*pair) for pair in red_chunks[:-1]] + [red_chunks[-1]]
+    early = bare_part
+    for k in range(NCHUNK - 1):
+        rows = slice(starts[k], starts[k] + WIDTHS[k])
+        early = early + jnp.dot(red_chunks[k], carried[rows], preferred_element_type=jnp.float32)
+    last_sum, last_other = red_chunks[-1]
+    last_other, early = lax.optimization_barrier((last_other, early))
+    red_chunks[-1] = reduce_pair(last_sum, last_other)
     reducible = jnp.concatenate(red_chunks, axis=1)
     base_sum = bare_mat.astype(jnp.float32) + reducible.astype(jnp.float32)
 
-    total = base_sum + bare_part
-    for k in range(NCHUNK):
-        rows = slice(starts[k], starts[k] + WIDTHS[k])
-        total = total + jnp.dot(red_chunks[k], carried[rows], preferred_element_type=jnp.float32)
+    rows = slice(starts[-1], order_len)
+    total = base_sum + early + jnp.dot(red_chunks[-1], carried[rows], preferred_element_type=jnp.float32)
     current = total.astype(jnp.bfloat16)
     for inner_step in range(1, INNER):
         carried = exact_dot(bubble_full, current)

time: 122 us -> 121 us (level)
  matrix products: 29.4 us -> 27.3 us
    dot_general x1, matrix products: 2.51 us -> 1.08 us  [local(): bare_part = jnp.dot(bare_mat, carried, preferred_element_type=jnp.float32)]
    ppermute x2, waiting for transfers between devices: 17.9 us -> 19.2 us  [partner_2(): return lax.ppermute(value, axis, pairs)]
  transfers between devices with their start and end apart: 4 -> 4, of which waited for: 4 -> 4; matrix products, arithmetic and copies ran while one was open for 18% -> 17% of each run, Pallas kernels for 0% -> 0%
where the time goes in v11:
time: 121 us; the launch traced here: 120 us
  waiting for transfers between devices  53 us (44%)
  matrix products  27.3 us (23%)
  starting transfers between devices  18.6 us (15%)
  local copies, waits for them, and re-layouts  16.7 us (14%)
  other arithmetic  4.15 us (3%)
    all_to_all x2, waiting for transfers between devices, local(): lax.all_to_all(pieces[k], 'mom', split_axis=1, concat_axis=1, tiled=True)  33.8 us
    ppermute x2, waiting for transfers between devices, partner_2(): return lax.ppermute(value, axis, pairs)  19.2 us
    all_to_all x2, starting transfers between devices, local(): lax.all_to_all(pieces[k], 'mom', split_axis=1, concat_axis=1, tiled=True)  15.4 us
    dot_general x8, matrix products, exact_dot(): jnp.dot(a, b, preferred_element_type=jnp.float32).astype(jnp.bfloat16)  14.2 us
    dot_general x2, matrix products, local(): jnp.dot(mix, received.reshape(2 * order_len, WIDTHS[k]), preferred_elemen...  6.51 us
    ppermute x2, starting transfers between devices, partner_2(): return lax.ppermute(value, axis, pairs)  3.17 us
    another operation x1, local copies, waits for them, and re-layouts, local(): jnp.stack([jnp.take(blocks, order, axis=0) for order in packs])  2.76 us
    convert_element_type x2, other arithmetic, local(): reduce_pair = lambda summed, other: (coef_self * summed.astype(jnp.float3...  2.56 us
  transfers between devices with their start and end apart: 4, of which 4 were waited for; matrix products, arithmetic and copies ran while one was open for 17% of the time, Pallas kernels for 0%

profile of v11, /device:TPU:1, one launch (start us, length us, event | category | flops | bytes accessed | tf_op | source)
XLA Modules:
  0.0 120.4 jit_solution(17366184313638369649)
XLA Ops:
  0.0 0.8 slice_bitcast_fusion.1
  0.8 0.1 select_reduce_fusion
  0.9 0.1 select_reduce_fusion.1
  1.1 1.2 slice.59
  2.3 0.2 reshape.35
  2.5 0.6 gather_fusion.3
  3.1 0.6 gather_fusion.2
  3.7 0.2 select_bitcast_fusion.1
  3.9 0.2 select_bitcast_fusion
  4.1 0.3 pad_maximum_fusion.1
  4.3 2.8 %copy.16 = bf16[2,64,12,512]{3,0,2,1:T(2,128)(2,1)} copy(bf16[2,64,12,512]{3,2,1,0:T(8,128)(2,1)S(1)} %pad_maximum_fusion.1) | data formatting | bytes 3145728 | tf_op jit(solution)/shard_map/stack | solution.py:96
  7.1 10.6 %all-to-all-start = ((bf16[2,64,12,512]{3,0,2,1:T(2,128)(2,1)}), bf16[2,64,12,512]{3,0,2,1:T(2,128)(2,1)}, u32[]{:S(2)}, u32[]{:S(2)}) async-start(bf16[2,64,12,512]{3,0,2,1:T(2,128)(2,1)} %copy.16), calls=%async_computation | async-start | bytes 3145728 | tf_op jit(solution)/shard_map/all_to_all | solution.py:98
  17.7 0.0 copy-done.12
  17.8 0.1 select_reduce_fusion.4
  17.9 0.1 select_reduce_fusion.2
  18.0 1.0 slice.60
  19.0 0.0 copy-start.5
  19.1 0.1 reshape.37
  19.1 0.6 gather_fusion.5
  19.8 0.6 gather_fusion.4
  20.4 0.0 copy-done.5
  20.4 0.8 gather_fusion.1
  21.2 0.8 gather_fusion
  22.0 0.1 select_bitcast_fusion.3
  22.2 0.0 copy-start.11
  22.2 0.1 select_bitcast_fusion.2
  22.3 0.1 pad_maximum_fusion.9
  22.5 0.4 copy-done.11
  22.9 1.0 convolution_convert_fusion.7
  23.9 1.0 convolution_convert_fusion.6
  24.9 2.1 %fusion.4 = bf16[768,768]{0,1:T(8,128)(2,1)} fusion(bf16[768,768]{0,1:T(8,128)(2,1)S(1)} %convolution_convert_fusion.7, s32[768]{0:T(1024)S(1)} %get-tuple-element.52, s32[768]{0:T(1024)S(1)} %get-tuple-element.53, pred[768]{0:T(1024)(128)(4,1)S(1)} %fusion.58, s32[64]{0:T(128)S(1)} %and_select_fusion.1), kind=kOutput, calls=%fused_computation.25 | convolution fusion | flops 84987904 | bytes 2366464 | tf_op jit(solution)/shard_map/dot_general | solution.py:49
  27.0 2.1 %fusion.5 = bf16[768,768]{0,1:T(8,128)(2,1)} fusion(bf16[768,768]{0,1:T(8,128)(2,1)S(1)} %convolution_convert_fusion.6, s32[768]{0:T(1024)S(1)} %get-tuple-element.52, s32[768]{0:T(1024)S(1)} %get-tuple-element.53, pred[768]{0:T(1024)(128)(4,1)S(1)} %fusion.58, s32[64]{0:T(128)S(1)} %and_select_fusion), kind=kOutput, calls=%fused_computation.26 | convolution fusion | flops 84987904 | bytes 2366464 | tf_op jit(solution)/shard_map/dot_general | solution.py:49
  29.1 12.4 %all-to-all-done = bf16[2,64,12,512]{3,0,2,1:T(2,128)(2,1)} async-done(((bf16[2,64,12,512]{3,0,2,1:T(2,128)(2,1)}), bf16[2,64,12,512]{3,0,2,1:T(2,128)(2,1)}, u32[]{:S(2)}, u32[]{:S(2)}) %all-to-all-start) | async-done | bytes 1572896 | tf_op jit(solution)/shard_map/all_to_all | solution.py:98
  41.5 1.9 %copy.17 = bf16[2,64,12,512]{3,2,1,0:T(8,128)(2,1)S(1)} copy(bf16[2,64,12,512]{3,0,2,1:T(2,128)(2,1)} %all-to-all-done) | data formatting | bytes 3145728 | tf_op jit(solution)/shard_map/all_to_all | solution.py:98
  43.4 1.4 %reshape.36 = bf16[1536,512]{1,0:T(8,128)(2,1)} reshape(bf16[2,64,12,512]{3,2,1,0:T(8,128)(2,1)S(1)} %copy.17) | data formatting | bytes 3145728 | tf_op jit(solution)/shard_map/reshape | solution.py:100
  44.7 4.4 %fusion.7 = bf16[768,512]{1,0:T(8,128)(2,1)} fusion(bf16[1536,512]{1,0:T(8,128)(2,1)} %reshape.36, bf16[768,768]{0,1:T(8,128)(2,1)} %fusion.5, bf16[768,768]{0,1:T(8,128)(2,1)} %fusion.4), kind=kOutput, calls=%fused_computation.28 | convolution fusion | flops 1213071360 | bytes 4718592 | tf_op jit(solution)/shard_map/dot_general | solution.py:99
  49.1 1.7 %copy.18 = bf16[2,64,12,256]{3,0,2,1:T(2,128)(2,1)} copy(bf16[2,64,12,256]{3,2,1,0:T(8,128)(2,1)S(1)} %pad_maximum_fusion.9) | data formatting | bytes 1572864 | tf_op jit(solution)/shard_map/optimization_barrier | solution.py:111
  50.9 4.8 %all-to-all-start.1 = ((bf16[2,64,12,256]{3,0,2,1:T(2,128)(2,1)}), bf16[2,64,12,256]{3,0,2,1:T(2,128)(2,1)S(1)}, u32[]{:S(2)}, u32[]{:S(2)}) async-start(bf16[2,64,12,256]{3,0,2,1:T(2,128)(2,1)} %copy.18), calls=%async_computation.1 | async-start | bytes 1572864 | tf_op jit(solution)/shard_map/all_to_all | solution.py:98
  55.7 3.1 %collective-permute-start = (bf16[768,512]{1,0:T(8,128)(2,1)}, bf16[768,512]{1,0:T(8,128)(2,1)}, u32[]{:S(2)}, u32[]{:S(2)}) collective-permute-start(bf16[768,512]{1,0:T(8,128)(2,1)} %fusion.7), channel_id=1, source_target_pairs={{0,1},{1,0},{2,3},{3,2},{4,5},{5,4},{6,7},{7,6},{8,9},{9,8},{10,11... | collective-permute-start | bytes 2359304 | tf_op jit(solution)/shard_map/ppermute | solution.py:17
  58.8 21.4 %all-to-all-done.1 = bf16[2,64,12,256]{3,0,2,1:T(2,128)(2,1)S(1)} async-done(((bf16[2,64,12,256]{3,0,2,1:T(2,128)(2,1)}), bf16[2,64,12,256]{3,0,2,1:T(2,128)(2,1)S(1)}, u32[]{:S(2)}, u32[]{:S(2)}) %all-to-all-start.1) | async-done | bytes 786464 | tf_op jit(solution)/shard_map/all_to_all | solution.py:98
  80.2 0.2 copy.19
  80.4 0.2 reshape.38
  80.6 0.0 copy-start.6
  80.6 2.1 %fusion.9 = bf16[768,256]{1,0:T(8,128)(2,1)S(1)} fusion(bf16[1536,256]{1,0:T(8,128)(2,1)S(1)} %reshape.38, bf16[768,768]{0,1:T(8,128)(2,1)} %fusion.5, bf16[768,768]{0,1:T(8,128)(2,1)S(1)} %copy-done.1), kind=kOutput, calls=%fused_computation.30 | convolution fusion | flops 608894976 | bytes 3538944 | tf_op jit(solution)/shard_map/dot_general | solution.py:99
  82.7 0.2 copy.20
  82.9 0.3 reshape.39
  83.2 0.0 copy-start
  83.2 0.1 collective-permute-start.1
  83.3 1.3 %convolution_convert_fusion.5 = bf16[768,768]{1,0:T(8,128)(2,1)S(1)} fusion(bf16[768,12]{0,1:T(8,128)(2,1)S(1)} %reshape.39, s32[768]{0:T(1024)S(1)} %get-tuple-element.50, s32[768]{0:T(1024)S(1)} %get-tuple-element.51, pred[768]{0:T(1024)(128)(4,1)S(1)} %copy-done.10), kind=kOutput, calls=%fused_computation.20 | convolution fusion | flops 14764032 | bytes 1204992 | tf_op jit(solution)/shard_map/dot_general | solution.py:49
  84.6 1.0 fusion.6
  85.6 0.0 copy-done
  85.6 0.0 copy-start.2
  85.6 0.0 copy-start.13
  85.6 1.1 convolution_convert_fusion.1
  86.7 0.6 copy-done.13
  87.3 1.1 fusion.12
  88.4 13.4 %collective-permute-done = bf16[768,512]{1,0:T(8,128)(2,1)} collective-permute-done((bf16[768,512]{1,0:T(8,128)(2,1)}, bf16[768,512]{1,0:T(8,128)(2,1)}, u32[]{:S(2)}, u32[]{:S(2)}) %collective-permute-start) | collective-permute-done | bytes 786464 | tf_op jit(solution)/shard_map/ppermute | solution.py:17
  101.8 1.7 %add_convert_fusion.1 = bf16[768,512]{1,0:T(8,128)(2,1)S(1)} fusion(bf16[768,512]{1,0:T(8,128)(2,1)} %collective-permute-done, bf16[768,512]{1,0:T(8,128)(2,1)} %fusion.7, f32[]{:T(128)S(6)} %add.86, f32[]{:T(128)S(6)} %add.82), kind=kLoop, calls=%fused_computation.14 | loop fusion | flops 2359296 | bytes 2359304 | tf_op jit(solution)/shard_map/convert_element_type | solution.py:115
  103.5 0.8 bitcast_add_fusion.1
  104.3 5.8 %collective-permute-done.1 = bf16[768,256]{1,0:T(8,128)(2,1)S(1)} collective-permute-done((bf16[768,256]{1,0:T(8,128)(2,1)S(1)}, bf16[768,256]{1,0:T(8,128)(2,1)S(1)}, u32[]{:S(2)}, u32[]{:S(2)}) %collective-permute-start.1) | collective-permute-done | bytes 393248 | tf_op jit(solution)/shard_map/ppermute | solution.py:17
  110.1 0.9 add_convert_fusion.3
  111.0 4.6 %convolution_convert_fusion = bf16[768,768]{1,0:T(8,128)(2,1)} fusion(bf16[768,768]{1,0:T(8,128)(2,1)} %copy-done.2, f32[768,768]{1,0:T(8,128)S(1)} %bitcast_add_fusion.1, bf16[768,256]{1,0:T(8,128)(2,1)} %add_convert_fusion.3, bf16[1,1,768,768]{3,2,1,0:T(8,128)(2,1)} %param.15, bf16[768,512]{1,0:T(8,128)(2,1)S(1)} %add_convert_fusion.1, ...), kind=kOutput, calls=%fused_computation.15 | convolution fusion | flops 1213857792 | bytes 7864320 | tf_op jit(solution)/shard_map/dot_general | solution.py:49
  115.6 2.5 %fusion.17 = f32[768,768]{1,0:T(8,128)S(1)} fusion(bf16[768,768]{1,0:T(8,128)(2,1)} %convolution_convert_fusion, bf16[768,256]{1,0:T(8,128)(2,1)S(1)} %copy-done.4, bf16[768,512]{1,0:T(8,128)(2,1)S(1)} %add_convert_fusion.1), kind=kOutput, calls=%fused_computation.46 | convolution fusion | flops 908328960 | bytes 4718592 | tf_op jit(solution)/shard_map/dot_general | solution.py:133
  118.2 2.2 %fusion.8 = bf16[1,1,768,768]{3,2,1,0:T(8,128)(2,1)} fusion(f32[768,768]{1,0:T(8,128)S(1)} %fusion.17, bf16[768,768]{1,0:T(8,128)(2,1)S(1)} %copy-done.15, bf16[1,1,768,768]{3,2,1,0:T(8,128)(2,1)S(1)} %copy-done.14, bf16[768,256]{1,0:T(8,128)(2,1)S(1)} %copy-done.4, bf16[768,512]{1,0:T(8,128)(2,1)S(1)} %add_convert_fusion.1), kind=kOutput, calls=%fused_computation.29 | convolution fusion | flops 911278080 | bytes 7077888 | tf_op jit(solution)/shard_map/dot_general | solution.py:132
  (39 shorter events, 0.2 us)
Async XLA Ops:
  7.1 10.6 %copy-start.12 = (s32[2,64]{1,0:T(2,128)S(1)}, s32[2,64]{1,0:T(2,128)}, u32[]{:S(2)}) copy-start(s32[2,64]{1,0:T(2,128)} %param.19) | copy-start | bytes 1540
  7.1 34.4 %all-to-all-start = ((bf16[2,64,12,512]{3,0,2,1:T(2,128)(2,1)}), bf16[2,64,12,512]{3,0,2,1:T(2,128)(2,1)}, u32[]{:S(2)}, u32[]{:S(2)}) async-start(bf16[2,64,12,512]{3,0,2,1:T(2,128)(2,1)} %copy.16), calls=%async_computation | async-start | bytes 3145728 | tf_op jit(solution)/shard_map/all_to_all | solution.py:98
  19.0 1.3 %copy-start.5 = (s32[2,64,64]{2,1,0:T(8,128)S(1)}, s32[2,64,64]{2,1,0:T(8,128)}, u32[]{:S(2)}) copy-start(s32[2,64,64]{2,1,0:T(8,128)} %param.18) | copy-start | bytes 98308
  22.0 5.1 %copy-start.7 = (pred[768]{0:T(1024)(128)(4,1)}, pred[768]{0:T(1024)(128)(4,1)S(1)}, u32[]{:S(2)}) copy-start(pred[768]{0:T(1024)(128)(4,1)S(1)} %fusion.58) | copy-start | bytes 2308
  22.0 1.9 %copy-start.9 = (pred[768]{0:T(1024)(128)(4,1)}, pred[768]{0:T(1024)(128)(4,1)S(1)}, u32[]{:S(2)}) copy-start(pred[768]{0:T(1024)(128)(4,1)S(1)} %fusion.57) | copy-start | bytes 2308
  22.2 0.7 copy-start.11
  50.9 29.4 %all-to-all-start.1 = ((bf16[2,64,12,256]{3,0,2,1:T(2,128)(2,1)}), bf16[2,64,12,256]{3,0,2,1:T(2,128)(2,1)S(1)}, u32[]{:S(2)}, u32[]{:S(2)}) async-start(bf16[2,64,12,256]{3,0,2,1:T(2,128)(2,1)} %copy.18), calls=%async_computation.1 | async-start | bytes 1572864 | tf_op jit(solution)/shard_map/all_to_all | solution.py:98
  55.7 24.8 %copy-start.1 = (bf16[768,768]{0,1:T(8,128)(2,1)S(1)}, bf16[768,768]{0,1:T(8,128)(2,1)}, u32[]{:S(2)}) copy-start(bf16[768,768]{0,1:T(8,128)(2,1)} %fusion.4) | copy-start | bytes 3538948
  55.7 46.1 %collective-permute-start = (bf16[768,512]{1,0:T(8,128)(2,1)}, bf16[768,512]{1,0:T(8,128)(2,1)}, u32[]{:S(2)}, u32[]{:S(2)}) collective-permute-start(bf16[768,512]{1,0:T(8,128)(2,1)} %fusion.7), channel_id=1, source_target_pairs={{0,1},{1,0},{2,3},{3,2},{4,5},{5,4},{6,7},{7,6},{8,9},{9,8},{10,11... | collective-permute-start | bytes 2359304 | tf_op jit(solution)/shard_map/ppermute | solution.py:17
  80.6 2.1 %copy-start.6 = (bf16[1,1,64,12,12]{2,4,3,1,0:T(8,128)(2,1)S(1)}, bf16[1,1,64,12,12]{2,4,3,1,0:T(8,128)(2,1)}, u32[]{:S(2)}) copy-start(bf16[1,1,64,12,12]{2,4,3,1,0:T(8,128)(2,1)} %param.16) | copy-start | bytes 55300
  80.6 2.7 %copy-start.10 = (pred[768]{0:T(1024)(128)(4,1)S(1)}, pred[768]{0:T(1024)(128)(4,1)}, u32[]{:S(2)}) copy-start(pred[768]{0:T(1024)(128)(4,1)} %copy-done.9) | copy-start | bytes 2308
  82.7 1.9 %copy-start.8 = (pred[768]{0:T(1024)(128)(4,1)S(1)}, pred[768]{0:T(1024)(128)(4,1)}, u32[]{:S(2)}) copy-start(pred[768]{0:T(1024)(128)(4,1)} %copy-done.7) | copy-start | bytes 2308
  83.2 2.4 %copy-start = (bf16[1,1,768,768]{3,2,1,0:T(8,128)(2,1)S(1)}, bf16[1,1,768,768]{3,2,1,0:T(8,128)(2,1)}, u32[]{:S(2)}) copy-start(bf16[1,1,768,768]{3,2,1,0:T(8,128)(2,1)} %param.14) | copy-start | bytes 3538948
  83.2 26.9 %collective-permute-start.1 = (bf16[768,256]{1,0:T(8,128)(2,1)S(1)}, bf16[768,256]{1,0:T(8,128)(2,1)S(1)}, u32[]{:S(2)}, u32[]{:S(2)}) collective-permute-start(bf16[768,256]{1,0:T(8,128)(2,1)S(1)} %fusion.9), channel_id=1, source_target_pairs={{0,1},{1,0},{2,3},{3,2},{4,5},{5,4},{6,7},{7,6},{8,9},{9,8},{10,11... | collective-permute-start | bytes 1179656 | tf_op jit(solution)/shard_map/ppermute | solution.py:17
  85.6 1.1 copy-start.2
  85.6 1.7 %copy-start.13 = (bf16[1,1,768,768]{3,2,1,0:T(8,128)(2,1)S(1)}, bf16[1,1,768,768]{3,2,1,0:T(8,128)(2,1)}, u32[]{:S(2)}) copy-start(bf16[1,1,768,768]{3,2,1,0:T(8,128)(2,1)} %param.15) | copy-start | bytes 3538948
  87.3 16.1 %copy-start.3 = (bf16[768,768]{1,0:T(8,128)(2,1)}, bf16[768,768]{1,0:T(8,128)(2,1)S(1)}, u32[]{:S(2)}) copy-start(bf16[768,768]{1,0:T(8,128)(2,1)S(1)} %convolution_convert_fusion.1) | copy-start | bytes 3538948
  111.0 4.6 %copy-start.4 = (bf16[768,256]{1,0:T(8,128)(2,1)S(1)}, bf16[768,256]{1,0:T(8,128)(2,1)}, u32[]{:S(2)}) copy-start(bf16[768,256]{1,0:T(8,128)(2,1)} %add_convert_fusion.3) | copy-start | bytes 1179652
  115.6 2.5 %copy-start.14 = (bf16[1,1,768,768]{3,2,1,0:T(8,128)(2,1)S(1)}, bf16[1,1,768,768]{3,2,1,0:T(8,128)(2,1)}, u32[]{:S(2)}) copy-start(bf16[1,1,768,768]{3,2,1,0:T(8,128)(2,1)} %param.15) | copy-start | bytes 3538948
  115.6 2.5 %copy-start.15 = (bf16[768,768]{1,0:T(8,128)(2,1)S(1)}, bf16[768,768]{1,0:T(8,128)(2,1)}, u32[]{:S(2)}) copy-start(bf16[768,768]{1,0:T(8,128)(2,1)} %convolution_convert_fusion) | copy-start | bytes 3538948

commit v12 on v11

--- a/solution.py
+++ b/solution.py
@@ -6,6 +6,7 @@
 INNER = 2
 WIDTHS = (512, 256)
 NCHUNK = len(WIDTHS)
+TILE = 192
 
 COEF_SELF = (-0.5, 0.5, 0.5, 0.5)
 COEF_PAIR = (-1.5, -0.5, 1.5, -0.5)
@@ -84,7 +85,14 @@
         bubble_tall = bubble_mat.reshape(order_len, forms)
         block_mask = exact_dot(expand, expand.T)
         bubble_full = exact_dot(bubble_tall, forms_expand.T) * block_mask
-        return bubble_full, exact_dot(bubble_full, mat)
+        return bubble_full, diagonal_dot(bubble_full, mat)
+
+    def diagonal_dot(full, mat):
+        tile = TILE if order_len % TILE == 0 and TILE % forms == 0 else order_len
+        parts = [
+            exact_dot(full[i:i + tile, i:i + tile], mat[i:i + tile]) for i in range(0, order_len, tile)
+        ]
+        return jnp.concatenate(parts, axis=0)
 
 
     assert sum(WIDTHS) == order_len
@@ -128,7 +136,7 @@
     total = base_sum + early + jnp.dot(red_chunks[-1], carried[rows], preferred_element_type=jnp.float32)
     current = total.astype(jnp.bfloat16)
     for inner_step in range(1, INNER):
-        carried = exact_dot(bubble_full, current)
+        carried = diagonal_dot(bubble_full, current)
         total = base_sum + jnp.dot(bare_mat, carried, preferred_element_type=jnp.float32)
         total = total + jnp.dot(reducible, carried, preferred_element_type=jnp.float32)
         current = total.astype(jnp.bfloat16)

time: 121 us -> 116 us (0.959)
  waiting for transfers between devices: 53 us -> 49.3 us
  other arithmetic: 4.15 us -> 6.03 us
  matrix products: 27.3 us -> 25.5 us
  local copies, waits for them, and re-layouts: 16.7 us -> 15.4 us
    all_to_all x2, waiting for transfers between devices: 33.8 us -> 29.8 us  [local(): lax.all_to_all(pieces[k], 'mom', split_axis=1, concat_axis=1, tiled=True)]
    dot_general x8 -> x14, matrix products: 14.2 us -> 12.8 us  [exact_dot(): jnp.dot(a, b, preferred_element_type=jnp.float32).astype(jnp.bfloat16)]
    dot_general x1, matrix products: 2.51 us -> 1.09 us  [local(): jnp.dot(reducible, carried, preferred_element_type=jnp.float32)]
  transfers between devices with their start and end apart: 4 -> 4, of which waited for: 4 -> 4; matrix products, arithmetic and copies ran while one was open for 17% -> 22% of each run, Pallas kernels for 0% -> 0%
where the time goes in v12:
time: 116 us; the launch traced here: 115 us
  waiting for transfers between devices  49.3 us (42%)
  matrix products  25.5 us (22%)
  starting transfers between devices  18.6 us (16%)
  local copies, waits for them, and re-layouts  15.4 us (13%)
  other arithmetic  6.03 us (5%)
    all_to_all x2, waiting for transfers between devices, local(): lax.all_to_all(pieces[k], 'mom', split_axis=1, concat_axis=1, tiled=True)  29.8 us
    ppermute x2, waiting for transfers between devices, partner_2(): return lax.ppermute(value, axis, pairs)  19.5 us
    all_to_all x2, starting transfers between devices, local(): lax.all_to_all(pieces[k], 'mom', split_axis=1, concat_axis=1, tiled=True)  15.4 us
    dot_general x14, matrix products, exact_dot(): jnp.dot(a, b, preferred_element_type=jnp.float32).astype(jnp.bfloat16)  12.8 us
    dot_general x2, matrix products, local(): jnp.dot(mix, received.reshape(2 * order_len, WIDTHS[k]), preferred_elemen...  6.96 us
    ppermute x2, starting transfers between devices, partner_2(): return lax.ppermute(value, axis, pairs)  3.17 us
    another operation x1, local copies, waits for them, and re-layouts, local(): jnp.stack([jnp.take(blocks, order, axis=0) for order in packs])  2.78 us
    gather x4, local copies, waits for them, and re-layouts, local(): jnp.take(blocks, order, axis=0)  2.42 us
  transfers between devices with their start and end apart: 4, of which 4 were waited for; matrix products, arithmetic and copies ran while one was open for 22% of the time, Pallas kernels for 0%

profile of v12, /device:TPU:1, one launch (start us, length us, event | category | flops | bytes accessed | tf_op | source)
XLA Modules:
  0.0 115.3 jit_solution(2375962899025209684)
XLA Ops:
  0.0 0.8 slice_bitcast_fusion.1
  0.8 0.1 select_reduce_fusion
  0.9 0.1 select_reduce_fusion.1
  1.1 1.2 %slice.113 = bf16[768,512]{1,0:T(8,128)(2,1)S(1)} slice(bf16[768,768]{1,0:T(8,128)(2,1)} %bitcast.59), slice={[0:768], [0:512]} | slice | bytes 1572864 | tf_op jit(solution)/shard_map/slice | solution.py:103
  2.3 0.2 reshape.35
  2.5 0.6 gather_fusion.3
  3.1 0.6 gather_fusion.2
  3.7 0.2 select_bitcast_fusion.1
  3.9 0.2 select_bitcast_fusion
  4.1 0.3 pad_maximum_fusion.1
  4.3 2.8 %copy.16 = bf16[2,64,12,512]{3,0,2,1:T(2,128)(2,1)} copy(bf16[2,64,12,512]{3,2,1,0:T(8,128)(2,1)S(1)} %pad_maximum_fusion.1) | data formatting | bytes 3145728 | tf_op jit(solution)/shard_map/stack | solution.py:104
  7.1 10.6 %all-to-all-start = ((bf16[2,64,12,512]{3,0,2,1:T(2,128)(2,1)}), bf16[2,64,12,512]{3,0,2,1:T(2,128)(2,1)}, u32[]{:S(2)}, u32[]{:S(2)}) async-start(bf16[2,64,12,512]{3,0,2,1:T(2,128)(2,1)} %copy.16), calls=%async_computation | async-start | bytes 3145728 | tf_op jit(solution)/shard_map/all_to_all | solution.py:106
  17.8 0.1 select_reduce_fusion.4
  17.9 0.1 select_reduce_fusion.2
  18.1 0.1 reshape.37
  18.2 0.6 gather_fusion.5
  18.8 0.6 gather_fusion.4
  19.4 0.8 gather_fusion.1
  20.2 0.8 gather_fusion
  21.0 0.6 fusion.78
  21.6 0.1 select_bitcast_fusion.3
  21.8 0.1 select_bitcast_fusion.2
  21.9 1.1 pad_maximum_fusion.10
  23.0 0.5 and_select_fusion
  23.5 0.6 and_select_fusion.1
  24.1 0.6 fusion.89
  24.7 1.0 convolution_convert_fusion.5
  25.7 1.8 %convolution_convert_fusion.4 = bf16[768,768]{0,1:T(8,128)(2,1)S(1)} fusion(s32[768]{0:T(1024)S(1)} %get-tuple-element.50, s32[768]{0:T(1024)S(1)} %get-tuple-element.51, pred[768]{0:T(1024)(128)(4,1)} %copy-done.6, bf16[1,12,12]{2,0,1:T(2,128)(2,1)} %get-tuple-element.41), kind=kOutput, calls=%fused_computation.19 | convolution fusion | flops 15012864 | bytes 1186848 | tf_op jit(solution)/shard_map/dot_general | solution.py:50
  27.5 2.8 %fusion.4 = bf16[768,768]{0,1:T(8,128)(2,1)} fusion(bf16[768,768]{0,1:T(8,128)(2,1)S(1)} %convolution_convert_fusion.5, s32[768]{0:T(1024)S(1)} %get-tuple-element.52, s32[768]{0:T(1024)S(1)} %get-tuple-element.53, pred[768]{0:T(1024)(128)(4,1)} %fusion.78, s32[64]{0:T(128)} %and_select_fusion.1), kind=kOutput, calls=%fused_computation.23 | convolution fusion | flops 84987904 | bytes 2366464 | tf_op jit(solution)/shard_map/dot_general | solution.py:50
  30.4 2.8 %fusion.5 = bf16[768,768]{0,1:T(8,128)(2,1)} fusion(bf16[768,768]{0,1:T(8,128)(2,1)S(1)} %convolution_convert_fusion.4, s32[768]{0:T(1024)S(1)} %get-tuple-element.52, s32[768]{0:T(1024)S(1)} %get-tuple-element.53, pred[768]{0:T(1024)(128)(4,1)} %fusion.78, s32[64]{0:T(128)} %and_select_fusion), kind=kOutput, calls=%fused_computation.24 | convolution fusion | flops 84987904 | bytes 2366464 | tf_op jit(solution)/shard_map/dot_general | solution.py:50
  33.2 8.4 %all-to-all-done = bf16[2,64,12,512]{3,0,2,1:T(2,128)(2,1)} async-done(((bf16[2,64,12,512]{3,0,2,1:T(2,128)(2,1)}), bf16[2,64,12,512]{3,0,2,1:T(2,128)(2,1)}, u32[]{:S(2)}, u32[]{:S(2)}) %all-to-all-start) | async-done | bytes 1572896 | tf_op jit(solution)/shard_map/all_to_all | solution.py:106
  41.5 1.9 %copy.17 = bf16[2,64,12,512]{3,2,1,0:T(8,128)(2,1)S(1)} copy(bf16[2,64,12,512]{3,0,2,1:T(2,128)(2,1)} %all-to-all-done) | data formatting | bytes 3145728 | tf_op jit(solution)/shard_map/all_to_all | solution.py:106
  43.4 1.3 %reshape.36 = bf16[1536,512]{1,0:T(8,128)(2,1)} reshape(bf16[2,64,12,512]{3,2,1,0:T(8,128)(2,1)S(1)} %copy.17) | data formatting | bytes 3145728 | tf_op jit(solution)/shard_map/reshape | solution.py:108
  44.7 4.5 %fusion.7 = bf16[768,512]{1,0:T(8,128)(2,1)} fusion(bf16[1536,512]{1,0:T(8,128)(2,1)} %reshape.36, bf16[768,768]{0,1:T(8,128)(2,1)} %fusion.5, bf16[768,768]{0,1:T(8,128)(2,1)} %fusion.4), kind=kOutput, calls=%fused_computation.26 | convolution fusion | flops 1213071360 | bytes 4718592 | tf_op jit(solution)/shard_map/dot_general | solution.py:107
  49.2 1.7 %copy.18 = bf16[2,64,12,256]{3,0,2,1:T(2,128)(2,1)} copy(bf16[2,64,12,256]{3,2,1,0:T(8,128)(2,1)S(1)} %copy-done.1) | data formatting | bytes 1572864 | tf_op jit(solution)/shard_map/optimization_barrier | solution.py:119
  50.9 4.8 %all-to-all-start.1 = ((bf16[2,64,12,256]{3,0,2,1:T(2,128)(2,1)}), bf16[2,64,12,256]{3,0,2,1:T(2,128)(2,1)S(1)}, u32[]{:S(2)}, u32[]{:S(2)}) async-start(bf16[2,64,12,256]{3,0,2,1:T(2,128)(2,1)} %copy.18), calls=%async_computation.1 | async-start | bytes 1572864 | tf_op jit(solution)/shard_map/all_to_all | solution.py:106
  55.8 3.1 %collective-permute-start = (bf16[768,512]{1,0:T(8,128)(2,1)}, bf16[768,512]{1,0:T(8,128)(2,1)}, u32[]{:S(2)}, u32[]{:S(2)}) collective-permute-start(bf16[768,512]{1,0:T(8,128)(2,1)} %fusion.7), channel_id=1, source_target_pairs={{0,1},{1,0},{2,3},{3,2},{4,5},{5,4},{6,7},{7,6},{8,9},{9,8},{10,11... | collective-permute-start | bytes 2359304 | tf_op jit(solution)/shard_map/ppermute | solution.py:18
  58.9 21.4 %all-to-all-done.1 = bf16[2,64,12,256]{3,0,2,1:T(2,128)(2,1)S(1)} async-done(((bf16[2,64,12,256]{3,0,2,1:T(2,128)(2,1)}), bf16[2,64,12,256]{3,0,2,1:T(2,128)(2,1)S(1)}, u32[]{:S(2)}, u32[]{:S(2)}) %all-to-all-start.1) | async-done | bytes 786464 | tf_op jit(solution)/shard_map/all_to_all | solution.py:106
  80.3 0.2 copy.19
  80.5 0.2 reshape.38
  80.7 2.5 %fusion.9 = bf16[768,256]{1,0:T(8,128)(2,1)S(1)} fusion(bf16[1536,256]{1,0:T(8,128)(2,1)S(1)} %reshape.38, bf16[768,768]{0,1:T(8,128)(2,1)} %fusion.5, bf16[768,768]{0,1:T(8,128)(2,1)} %fusion.4), kind=kOutput, calls=%fused_computation.28 | convolution fusion | flops 608894976 | bytes 3538944 | tf_op jit(solution)/shard_map/dot_general | solution.py:107
  83.1 0.2 copy.20
  83.3 0.3 reshape.39
  83.6 1.3 %convolution_convert_fusion.3 = bf16[768,768]{1,0:T(8,128)(2,1)S(1)} fusion(bf16[768,12]{0,1:T(8,128)(2,1)S(1)} %reshape.39, s32[768]{0:T(1024)S(1)} %get-tuple-element.50, s32[768]{0:T(1024)S(1)} %get-tuple-element.51, pred[768]{0:T(1024)(128)(4,1)S(1)} %copy-done.7), kind=kOutput, calls=%fused_computation.18 | convolution fusion | flops 14764032 | bytes 1204992 | tf_op jit(solution)/shard_map/dot_general | solution.py:50
  84.9 1.0 fusion.6
  85.9 0.2 convolution_convert_fusion.11
  86.2 0.3 convolution_convert_fusion.10
  86.5 0.1 collective-permute-start.1
  86.6 0.3 convolution_convert_fusion.12
  86.9 0.2 convolution_convert_fusion.13
  87.1 0.1 copy-done.2
  87.2 1.1 fusion.10
  88.3 13.6 %collective-permute-done = bf16[768,512]{1,0:T(8,128)(2,1)} collective-permute-done((bf16[768,512]{1,0:T(8,128)(2,1)}, bf16[768,512]{1,0:T(8,128)(2,1)}, u32[]{:S(2)}, u32[]{:S(2)}) %collective-permute-start) | collective-permute-done | bytes 786464 | tf_op jit(solution)/shard_map/ppermute | solution.py:18
  101.9 1.7 %add_convert_fusion.1 = bf16[768,512]{1,0:T(8,128)(2,1)S(1)} fusion(bf16[768,512]{1,0:T(8,128)(2,1)} %collective-permute-done, bf16[768,512]{1,0:T(8,128)(2,1)} %fusion.7, f32[]{:T(128)S(6)} %add.86, f32[]{:T(128)S(6)} %add.82), kind=kLoop, calls=%fused_computation.14 | loop fusion | flops 2359296 | bytes 2359304 | tf_op jit(solution)/shard_map/convert_element_type | solution.py:123
  103.5 0.8 bitcast_add_fusion.1
  104.3 5.9 %collective-permute-done.1 = bf16[768,256]{1,0:T(8,128)(2,1)S(1)} collective-permute-done((bf16[768,256]{1,0:T(8,128)(2,1)S(1)}, bf16[768,256]{1,0:T(8,128)(2,1)S(1)}, u32[]{:S(2)}, u32[]{:S(2)}) %collective-permute-start.1) | collective-permute-done | bytes 393248 | tf_op jit(solution)/shard_map/ppermute | solution.py:18
  110.2 0.2 add_convert_fusion.2
  110.3 0.6 add_convert_fusion
  111.0 0.3 convolution_convert_fusion.6
  111.3 0.2 convolution_convert_fusion.7
  111.5 0.3 convolution_convert_fusion.8
  111.8 0.2 convolution_convert_fusion.9
  112.0 1.1 fusion.23
  113.1 2.2 %fusion.8 = bf16[1,1,768,768]{3,2,1,0:T(8,128)(2,1)} fusion(f32[768,768]{1,0:T(8,128)S(1)} %fusion.23, bf16[1,1,768,768]{3,2,1,0:T(8,128)(2,1)S(1)} %copy-done.2, bf16[768,256]{1,0:T(8,128)(2,1)S(1)} %add_convert_fusion.2, bf16[768,512]{1,0:T(8,128)(2,1)S(1)} %add_convert_fusion.1, bf16[192,768]{1,0:T(8,128)(2,1)S(1)} %convolution_convert_fusion.6, ...), kind=kOutput, calls=%fused_computation.27 | convolution fusion | flops 915996672 | bytes 7077888 | tf_op jit(solution)/shard_map/dot_general | solution.py:140
  (34 shorter events, 0.2 us)
Async XLA Ops:
  7.1 10.6 %copy-start.9 = (s32[2,64]{1,0:T(2,128)S(1)}, s32[2,64]{1,0:T(2,128)}, u32[]{:S(2)}) copy-start(s32[2,64]{1,0:T(2,128)} %param.19) | copy-start | bytes 1540
  7.1 10.9 %copy-start = (bf16[1,1,768,768]{3,2,1,0:T(8,128)(2,1)S(1)}, bf16[1,1,768,768]{3,2,1,0:T(8,128)(2,1)}, u32[]{:S(2)}) copy-start(bf16[1,1,768,768]{3,2,1,0:T(8,128)(2,1)} %param.14) | copy-start | bytes 3538948
  7.1 34.4 %all-to-all-start = ((bf16[2,64,12,512]{3,0,2,1:T(2,128)(2,1)}), bf16[2,64,12,512]{3,0,2,1:T(2,128)(2,1)}, u32[]{:S(2)}, u32[]{:S(2)}) async-start(bf16[2,64,12,512]{3,0,2,1:T(2,128)(2,1)} %copy.16), calls=%async_computation | async-start | bytes 3145728 | tf_op jit(solution)/shard_map/all_to_all | solution.py:106
  18.1 1.3 %copy-start.3 = (s32[2,64,64]{2,1,0:T(8,128)S(1)}, s32[2,64,64]{2,1,0:T(8,128)}, u32[]{:S(2)}) copy-start(s32[2,64,64]{2,1,0:T(8,128)} %param.18) | copy-start | bytes 98308
  21.6 3.1 %copy-start.6 = (pred[768]{0:T(1024)(128)(4,1)}, pred[768]{0:T(1024)(128)(4,1)S(1)}, u32[]{:S(2)}) copy-start(pred[768]{0:T(1024)(128)(4,1)S(1)} %fusion.77) | copy-start | bytes 2308
  21.8 2.4 %copy-start.8 = (bf16[2,12,12]{2,0,1:T(2,128)(2,1)S(1)}, bf16[2,12,12]{2,0,1:T(2,128)(2,1)}, u32[]{:S(2)}) copy-start(bf16[2,12,12]{2,0,1:T(2,128)(2,1)} %param.17) | copy-start | bytes 1732
  44.7 4.5 %copy-start.1 = (bf16[2,64,12,256]{3,2,1,0:T(8,128)(2,1)S(1)}, bf16[2,64,12,256]{3,2,1,0:T(8,128)(2,1)}, u32[]{:S(2)}) copy-start(bf16[2,64,12,256]{3,2,1,0:T(8,128)(2,1)} %pad_maximum_fusion.10) | copy-start | bytes 2359300
  50.9 29.4 %all-to-all-start.1 = ((bf16[2,64,12,256]{3,0,2,1:T(2,128)(2,1)}), bf16[2,64,12,256]{3,0,2,1:T(2,128)(2,1)S(1)}, u32[]{:S(2)}, u32[]{:S(2)}) async-start(bf16[2,64,12,256]{3,0,2,1:T(2,128)(2,1)} %copy.18), calls=%async_computation.1 | async-start | bytes 1572864 | tf_op jit(solution)/shard_map/all_to_all | solution.py:106
  55.8 46.1 %collective-permute-start = (bf16[768,512]{1,0:T(8,128)(2,1)}, bf16[768,512]{1,0:T(8,128)(2,1)}, u32[]{:S(2)}, u32[]{:S(2)}) collective-permute-start(bf16[768,512]{1,0:T(8,128)(2,1)} %fusion.7), channel_id=1, source_target_pairs={{0,1},{1,0},{2,3},{3,2},{4,5},{5,4},{6,7},{7,6},{8,9},{9,8},{10,11... | collective-permute-start | bytes 2359304 | tf_op jit(solution)/shard_map/ppermute | solution.py:18
  80.6 2.5 %copy-start.4 = (bf16[1,1,64,12,12]{2,4,3,1,0:T(8,128)(2,1)S(1)}, bf16[1,1,64,12,12]{2,4,3,1,0:T(8,128)(2,1)}, u32[]{:S(2)}) copy-start(bf16[1,1,64,12,12]{2,4,3,1,0:T(8,128)(2,1)} %param.16) | copy-start | bytes 55300
  80.7 2.9 %copy-start.7 = (pred[768]{0:T(1024)(128)(4,1)S(1)}, pred[768]{0:T(1024)(128)(4,1)}, u32[]{:S(2)}) copy-start(pred[768]{0:T(1024)(128)(4,1)} %copy-done.6) | copy-start | bytes 2308
  83.1 1.8 %copy-start.5 = (pred[768]{0:T(1024)(128)(4,1)S(1)}, pred[768]{0:T(1024)(128)(4,1)}, u32[]{:S(2)}) copy-start(pred[768]{0:T(1024)(128)(4,1)} %fusion.78) | copy-start | bytes 2308
  85.9 1.3 %copy-start.2 = (bf16[1,1,768,768]{3,2,1,0:T(8,128)(2,1)S(1)}, bf16[1,1,768,768]{3,2,1,0:T(8,128)(2,1)}, u32[]{:S(2)}) copy-start(bf16[1,1,768,768]{3,2,1,0:T(8,128)(2,1)} %param.15) | copy-start | bytes 3538948
  86.5 23.7 %collective-permute-start.1 = (bf16[768,256]{1,0:T(8,128)(2,1)S(1)}, bf16[768,256]{1,0:T(8,128)(2,1)S(1)}, u32[]{:S(2)}, u32[]{:S(2)}) collective-permute-start(bf16[768,256]{1,0:T(8,128)(2,1)S(1)} %fusion.9), channel_id=1, source_target_pairs={{0,1},{1,0},{2,3},{3,2},{4,5},{5,4},{6,7},{7,6},{8,9},{9,8},{10,11... | collective-permute-start | bytes 1179656 | tf_op jit(solution)/shard_map/ppermute | solution.py:18

commit v13 on v12

--- a/solution.py
+++ b/solution.py
@@ -79,7 +79,7 @@
         send_order, recv_slots = crossing_plan(cross_tables[r], freq_perm[r], momentum, freqs)
         packs.append(send_order)
         mixes.append(mix_matrix(recv_slots, form_mix[r], freqs, expand, forms_expand))
-    mix = jnp.concatenate(mixes, axis=1)
+    mix4 = jnp.concatenate(mixes, axis=1).reshape(order_len, 2, freqs, forms)
 
     def carry_of(mat, bubble_mat):
         bubble_tall = bubble_mat.reshape(order_len, forms)
@@ -104,8 +104,8 @@
         pieces.append(jnp.stack([jnp.take(blocks, order, axis=0) for order in packs]))
     for k in range(NCHUNK):
         received = lax.all_to_all(pieces[k], "mom", split_axis=1, concat_axis=1, tiled=True)
-        summed = jnp.dot(
-            mix, received.reshape(2 * order_len, WIDTHS[k]), preferred_element_type=jnp.float32
+        summed = jnp.einsum(
+            "frqm,rqmb->fb", mix4, received, preferred_element_type=jnp.float32
         ).astype(jnp.bfloat16)
         if k + 1 == NCHUNK:
             sums = [pair[0] for pair in red_chunks]

time: 116 us -> 115 us (level)
  waiting for transfers between devices: 49.3 us -> 42.4 us
  other arithmetic: 6.03 us -> 8.59 us
  starting transfers between devices: 18.6 us -> 21.1 us
    all_to_all x2, waiting for transfers between devices: 29.8 us -> 23.2 us  [local(): lax.all_to_all(pieces[k], 'mom', split_axis=1, concat_axis=1, tiled=True)]
    all_to_all x2, starting transfers between devices: 15.4 us -> 18 us  [local(): lax.all_to_all(pieces[k], 'mom', split_axis=1, concat_axis=1, tiled=True)]
    all_to_all x2 -> x0, local copies, waits for them, and re-layouts: 2 us -> none  [local(): lax.all_to_all(pieces[k], 'mom', split_axis=1, concat_axis=1, tiled=True)]
    concatenate x0 -> x1, other arithmetic: none -> 1.78 us  [local(): mix4 = jnp.concatenate(mixes, axis=1).reshape(order_len, 2, freqs, forms)]
    gather x4, local copies, waits for them, and re-layouts: 2.42 us -> 4.03 us  [local(): jnp.take(blocks, order, axis=0)]
  transfers between devices with their start and end apart: 4 -> 4, of which waited for: 4 -> 4; matrix products, arithmetic and copies ran while one was open for 22% -> 28% of each run, Pallas kernels for 0% -> 0%
where the time goes in v13:
time: 115 us; the launch traced here: 114 us
  waiting for transfers between devices  42.4 us (37%)
  matrix products  26 us (23%)
  starting transfers between devices  21.1 us (18%)
  local copies, waits for them, and re-layouts  15.9 us (14%)
  other arithmetic  8.59 us (7%)
    all_to_all x2, waiting for transfers between devices, local(): lax.all_to_all(pieces[k], 'mom', split_axis=1, concat_axis=1, tiled=True)  23.2 us
    ppermute x2, waiting for transfers between devices, partner_2(): return lax.ppermute(value, axis, pairs)  19.3 us
    all_to_all x2, starting transfers between devices, local(): lax.all_to_all(pieces[k], 'mom', split_axis=1, concat_axis=1, tiled=True)  18 us
    dot_general x14, matrix products, exact_dot(): jnp.dot(a, b, preferred_element_type=jnp.float32).astype(jnp.bfloat16)  12.7 us
    dot_general x2, matrix products, local(): jnp.einsum('frqm,rqmb->fb', mix4, received, preferred_element_type=jnp.fl...  7.4 us
    gather x4, local copies, waits for them, and re-layouts, local(): jnp.take(blocks, order, axis=0)  4.03 us
    ppermute x2, starting transfers between devices, partner_2(): return lax.ppermute(value, axis, pairs)  3.18 us
    another operation x6, other arithmetic, local(): jnp.stack([jnp.take(blocks, order, axis=0) for order in packs])  3.1 us
  transfers between devices with their start and end apart: 4, of which 4 were waited for; matrix products, arithmetic and copies ran while one was open for 28% of the time, Pallas kernels for 0%

profile of v13, /device:TPU:1, one launch (start us, length us, event | category | flops | bytes accessed | tf_op | source)
XLA Modules:
  0.0 114.5 jit_solution(1091166862216975516)
XLA Ops:
  0.0 0.8 slice_bitcast_fusion.1
  0.8 0.1 select_reduce_fusion
  0.9 0.1 select_reduce_fusion.1
  1.1 1.2 %slice.113 = bf16[768,512]{1,0:T(8,128)(2,1)S(1)} slice(bf16[768,768]{1,0:T(8,128)(2,1)} %bitcast.69), slice={[0:768], [0:512]} | slice | bytes 1572864 | tf_op jit(solution)/shard_map/slice | solution.py:103
  2.3 0.2 reshape.33
  2.5 0.6 gather_fusion.3
  3.1 0.6 gather_fusion.2
  3.7 0.2 select_bitcast_fusion
  3.9 0.2 select_bitcast_fusion.1
  4.1 0.3 pad_maximum_fusion.1
  4.4 2.8 %copy.24 = bf16[2,64,12,512]{3,0,2,1:T(2,128)(2,1)} copy(bf16[2,64,12,512]{3,2,1,0:T(8,128)(2,1)S(1)} %pad_maximum_fusion.1) | data formatting | bytes 3145728 | tf_op jit(solution)/shard_map/stack | solution.py:104
  7.2 10.6 %all-to-all-start = ((bf16[2,64,12,512]{3,0,2,1:T(2,128)(2,1)}), bf16[2,64,12,512]{3,0,2,1:T(2,128)(2,1)}, u32[]{:S(2)}, u32[]{:S(2)}) async-start(bf16[2,64,12,512]{3,0,2,1:T(2,128)(2,1)} %copy.24), calls=%async_computation | async-start | bytes 3145728 | tf_op jit(solution)/shard_map/all_to_all | solution.py:106
  17.9 0.0 copy-start.10
  17.9 0.1 reshape.34
  18.0 0.0 copy-start.7
  18.0 1.4 %gather_fusion.5 = bf16[64,12,256]{2,1,0:T(8,128)(2,1)} fusion(bf16[64,12,256]{2,1,0:T(8,128)(2,1)S(1)} %reshape.34, s32[1024]{0:T(1024)S(1)} %pad_clamp_fusion), kind=kCustom, calls=%fused_computation.5.clone | custom fusion | bytes 786688 | tf_op jit(solution)/shard_map/jit(_take)/gather | solution.py:104
  19.4 1.4 %gather_fusion.4 = bf16[64,12,256]{2,1,0:T(8,128)(2,1)} fusion(bf16[64,12,256]{2,1,0:T(8,128)(2,1)S(1)} %reshape.34, s32[1024]{0:T(1024)S(1)} %pad_clamp_fusion.1), kind=kCustom, calls=%fused_computation.2.clone | custom fusion | bytes 786688 | tf_op jit(solution)/shard_map/jit(_take)/gather | solution.py:104
  20.8 0.1 select_reduce_fusion.2
  21.0 0.8 gather_fusion
  21.7 0.8 gather_fusion.1
  22.5 0.6 fusion.90
  23.1 0.6 and_select_fusion.1
  23.7 0.5 and_select_fusion
  24.3 0.6 fusion.99
  24.9 1.0 convolution_convert_fusion.5
  25.9 1.7 %convolution_convert_fusion.4 = bf16[768,768]{0,1:T(8,128)(2,1)S(1)} fusion(s32[768]{0:T(1024)S(1)} %get-tuple-element.44, s32[768]{0:T(1024)S(1)} %get-tuple-element.45, pred[768]{0:T(1024)(128)(4,1)} %copy-done.5, bf16[1,12,12]{2,0,1:T(2,128)(2,1)} %get-tuple-element.41), kind=kOutput, calls=%fused_computation.25 | convolution fusion | flops 15012864 | bytes 1186848 | tf_op jit(solution)/shard_map/dot_general | solution.py:50
  27.6 2.8 %fusion.7 = bf16[768,768]{0,1:T(8,128)(2,1)} fusion(bf16[768,768]{0,1:T(8,128)(2,1)S(1)} %convolution_convert_fusion.5, s32[768]{0:T(1024)S(1)} %get-tuple-element.52, s32[768]{0:T(1024)S(1)} %get-tuple-element.53, pred[768]{0:T(1024)(128)(4,1)} %fusion.90, s32[64]{0:T(128)} %and_select_fusion.1), kind=kOutput, calls=%fused_computation.27 | convolution fusion | flops 84987904 | bytes 2366464 | tf_op jit(solution)/shard_map/dot_general | solution.py:50
  30.5 2.8 %fusion.8 = bf16[768,768]{0,1:T(8,128)(2,1)} fusion(bf16[768,768]{0,1:T(8,128)(2,1)S(1)} %convolution_convert_fusion.4, s32[768]{0:T(1024)S(1)} %get-tuple-element.52, s32[768]{0:T(1024)S(1)} %get-tuple-element.53, pred[768]{0:T(1024)(128)(4,1)} %fusion.90, s32[64]{0:T(128)} %and_select_fusion), kind=kOutput, calls=%fused_computation.28 | convolution fusion | flops 84987904 | bytes 2366464 | tf_op jit(solution)/shard_map/dot_general | solution.py:50
  33.3 1.8 %pad_maximum_fusion = bf16[768,1536]{0,1:T(8,128)(2,1)S(1)} fusion(bf16[768,768]{0,1:T(8,128)(2,1)} %fusion.8, bf16[768,768]{0,1:T(8,128)(2,1)} %fusion.7), kind=kLoop, calls=%fused_computation.6 | loop fusion | flops 4718592 | bytes 4718592 | tf_op jit(solution)/shard_map/concatenate | solution.py:82
  35.1 2.3 %reshape.32 = bf16[768,2,64,12]{0,3,2,1:T(8,128)(2,1)} reshape(bf16[768,1536]{0,1:T(8,128)(2,1)S(1)} %pad_maximum_fusion) | data formatting | bytes 4718592 | tf_op jit(solution)/shard_map/reshape | solution.py:82
  37.4 1.2 %select_bitcast_fusion.2 = bf16[1,64,12,256]{3,2,1,0:T(8,128)(2,1)S(1)} fusion(bf16[64,12,256]{2,1,0:T(8,128)(2,1)} %gather_fusion.5, pred[64]{0:T(512)(128)(4,1)} %copy-done.9), kind=kLoop, calls=%fused_computation.65 | loop fusion | flops 196608 | bytes 786496 | tf_op jit(solution)/shard_map/stack | solution.py:104
  38.6 1.2 %select_bitcast_fusion.3 = bf16[1,64,12,256]{3,2,1,0:T(8,128)(2,1)S(1)} fusion(bf16[64,12,256]{2,1,0:T(8,128)(2,1)} %gather_fusion.4, pred[64]{0:T(512)(128)(4,1)} %copy-done.8), kind=kLoop, calls=%fused_computation.66 | loop fusion | flops 196608 | bytes 786496 | tf_op jit(solution)/shard_map/stack | solution.py:104
  39.8 0.1 pad_maximum_fusion.4
  39.9 1.7 %all-to-all-done = bf16[2,64,12,512]{3,0,2,1:T(2,128)(2,1)} async-done(((bf16[2,64,12,512]{3,0,2,1:T(2,128)(2,1)}), bf16[2,64,12,512]{3,0,2,1:T(2,128)(2,1)}, u32[]{:S(2)}, u32[]{:S(2)}) %all-to-all-start) | async-done | bytes 1572896 | tf_op jit(solution)/shard_map/all_to_all | solution.py:106
  41.6 4.3 %bitcast_convert_fusion = bf16[768,512]{1,0:T(8,128)(2,1)S(1)} fusion(bf16[2,64,12,512]{3,0,2,1:T(2,128)(2,1)} %all-to-all-done, bf16[768,2,64,12]{0,3,2,1:T(8,128)(2,1)} %reshape.32), kind=kOutput, calls=%fused_computation.18 | convolution fusion | flops 1208352768 | bytes 4718592 | tf_op jit(solution)/shard_map/frqm,rqmb->fb/dot_general | solution.py:107
  45.9 1.7 %copy.27 = bf16[2,64,12,256]{3,0,2,1:T(2,128)(2,1)} copy(bf16[2,64,12,256]{3,2,1,0:T(8,128)(2,1)S(1)} %pad_maximum_fusion.4) | data formatting | bytes 1572864 | tf_op jit(solution)/shard_map/optimization_barrier | solution.py:119
  47.6 7.3 %all-to-all-start.1 = ((bf16[2,64,12,256]{3,0,2,1:T(2,128)(2,1)}), bf16[2,64,12,256]{3,0,2,1:T(2,128)(2,1)S(1)}, u32[]{:S(2)}, u32[]{:S(2)}) async-start(bf16[2,64,12,256]{3,0,2,1:T(2,128)(2,1)} %copy.27), calls=%async_computation.1 | async-start | bytes 1572864 | tf_op jit(solution)/shard_map/all_to_all | solution.py:106
  55.0 0.0 copy-start.3
  55.0 3.1 %collective-permute-start = (bf16[768,512]{1,0:T(8,128)(2,1)S(1)}, bf16[768,512]{1,0:T(8,128)(2,1)}, u32[]{:S(2)}, u32[]{:S(2)}) collective-permute-start(bf16[768,512]{1,0:T(8,128)(2,1)S(1)} %bitcast_convert_fusion), channel_id=1, source_target_pairs={{0,1},{1,0},{2,3},{3,2},{4,5},{5,4},{6,7},{7,6},{8,9},{9,8},{10,11... | collective-permute-start | bytes 2359304 | tf_op jit(solution)/shard_map/ppermute | solution.py:18
  58.1 21.5 %all-to-all-done.1 = bf16[2,64,12,256]{3,0,2,1:T(2,128)(2,1)S(1)} async-done(((bf16[2,64,12,256]{3,0,2,1:T(2,128)(2,1)}), bf16[2,64,12,256]{3,0,2,1:T(2,128)(2,1)S(1)}, u32[]{:S(2)}, u32[]{:S(2)}) %all-to-all-start.1) | async-done | bytes 786464 | tf_op jit(solution)/shard_map/all_to_all | solution.py:106
  79.6 3.1 %fusion.18 = bf16[768,256]{1,0:T(8,128)(2,1)S(1)} fusion(bf16[768,2,64,12]{0,3,2,1:T(8,128)(2,1)} %reshape.32, bf16[2,64,12,256]{3,0,2,1:T(2,128)(2,1)S(1)} %all-to-all-done.1), kind=kOutput, calls=%fused_computation.32 | convolution fusion | flops 604176384 | bytes 3538944 | tf_op jit(solution)/shard_map/frqm,rqmb->fb/dot_general | solution.py:107
  82.7 0.2 copy.30
  82.9 0.3 reshape.35
  83.1 1.3 %convolution_convert_fusion.3 = bf16[768,768]{1,0:T(8,128)(2,1)S(1)} fusion(bf16[768,12]{0,1:T(8,128)(2,1)S(1)} %reshape.35, s32[768]{0:T(1024)S(1)} %get-tuple-element.44, s32[768]{0:T(1024)S(1)} %get-tuple-element.45, pred[768]{0:T(1024)(128)(4,1)S(1)} %copy-done.6), kind=kOutput, calls=%fused_computation.24 | convolution fusion | flops 14764032 | bytes 1204992 | tf_op jit(solution)/shard_map/dot_general | solution.py:50
  84.4 1.0 fusion.9
  85.5 0.2 convolution_convert_fusion.13
  85.7 0.3 convolution_convert_fusion.12
  86.0 0.1 collective-permute-start.1
  86.1 0.2 convolution_convert_fusion.11
  86.3 0.3 convolution_convert_fusion.10
  86.6 0.1 copy-done.1
  86.7 1.1 fusion.21
  87.8 13.2 %collective-permute-done = bf16[768,512]{1,0:T(8,128)(2,1)} collective-permute-done((bf16[768,512]{1,0:T(8,128)(2,1)S(1)}, bf16[768,512]{1,0:T(8,128)(2,1)}, u32[]{:S(2)}, u32[]{:S(2)}) %collective-permute-start) | collective-permute-done | bytes 786464 | tf_op jit(solution)/shard_map/ppermute | solution.py:18
  101.0 1.4 %add_convert_fusion.1 = bf16[768,512]{1,0:T(8,128)(2,1)S(1)} fusion(bf16[768,512]{1,0:T(8,128)(2,1)} %collective-permute-done, bf16[768,512]{1,0:T(8,128)(2,1)S(1)} %bitcast_convert_fusion, f32[]{:T(128)S(6)} %add.86, f32[]{:T(128)S(6)} %add.82), kind=kLoop, calls=%fused_computation.20 | loop fusion | flops 2359296 | bytes 2359304 | tf_op jit(solution)/shard_map/convert_element_type | solution.py:123
  102.4 0.8 bitcast_add_fusion.1
  103.2 6.1 %collective-permute-done.1 = bf16[768,256]{1,0:T(8,128)(2,1)S(1)} collective-permute-done((bf16[768,256]{1,0:T(8,128)(2,1)S(1)}, bf16[768,256]{1,0:T(8,128)(2,1)S(1)}, u32[]{:S(2)}, u32[]{:S(2)}) %collective-permute-start.1) | collective-permute-done | bytes 393248 | tf_op jit(solution)/shard_map/ppermute | solution.py:18
  109.3 0.2 add_convert_fusion.2
  109.5 0.7 add_convert_fusion
  110.1 0.2 convolution_convert_fusion.9
  110.4 0.3 convolution_convert_fusion.8
  110.7 0.2 convolution_convert_fusion.7
  110.9 0.3 convolution_convert_fusion.6
  111.2 1.1 fusion.35
  112.3 2.2 %fusion.14 = bf16[1,1,768,768]{3,2,1,0:T(8,128)(2,1)} fusion(f32[768,768]{1,0:T(8,128)S(1)} %fusion.35, bf16[1,1,768,768]{3,2,1,0:T(8,128)(2,1)S(1)} %copy-done.1, bf16[768,256]{1,0:T(8,128)(2,1)S(1)} %add_convert_fusion.2, bf16[768,512]{1,0:T(8,128)(2,1)S(1)} %add_convert_fusion.1, bf16[192,768]{1,0:T(8,128)(2,1)S(1)} %convolution_convert_fusion.6, ...), kind=kOutput, calls=%fused_computation.30 | convolution fusion | flops 915996672 | bytes 7077888 | tf_op jit(solution)/shard_map/dot_general | solution.py:140
  (34 shorter events, 0.2 us)
Async XLA Ops:
  1.1 2.7 %copy-start.9 = (pred[64]{0:T(512)(128)(4,1)}, pred[64]{0:T(512)(128)(4,1)S(1)}, u32[]{:S(2)}) copy-start(pred[64]{0:T(512)(128)(4,1)S(1)} %get-tuple-element.50) | copy-start | bytes 196
  1.1 2.8 %copy-start.8 = (pred[64]{0:T(512)(128)(4,1)}, pred[64]{0:T(512)(128)(4,1)S(1)}, u32[]{:S(2)}) copy-start(pred[64]{0:T(512)(128)(4,1)S(1)} %get-tuple-element.51) | copy-start | bytes 196
  7.2 10.6 %copy-start.2 = (s32[2,64,64]{2,1,0:T(8,128)S(1)}, s32[2,64,64]{2,1,0:T(8,128)}, u32[]{:S(2)}) copy-start(s32[2,64,64]{2,1,0:T(8,128)} %param.18) | copy-start | bytes 98308
  7.2 10.7 %copy-start = (bf16[1,1,768,768]{3,2,1,0:T(8,128)(2,1)S(1)}, bf16[1,1,768,768]{3,2,1,0:T(8,128)(2,1)}, u32[]{:S(2)}) copy-start(bf16[1,1,768,768]{3,2,1,0:T(8,128)(2,1)} %param.14) | copy-start | bytes 3538948
  7.2 34.4 %all-to-all-start = ((bf16[2,64,12,512]{3,0,2,1:T(2,128)(2,1)}), bf16[2,64,12,512]{3,0,2,1:T(2,128)(2,1)}, u32[]{:S(2)}, u32[]{:S(2)}) async-start(bf16[2,64,12,512]{3,0,2,1:T(2,128)(2,1)} %copy.24), calls=%async_computation | async-start | bytes 3145728 | tf_op jit(solution)/shard_map/all_to_all | solution.py:106
  17.9 2.9 %copy-start.10 = (s32[2,64]{1,0:T(2,128)S(1)}, s32[2,64]{1,0:T(2,128)}, u32[]{:S(2)}) copy-start(s32[2,64]{1,0:T(2,128)} %param.19) | copy-start | bytes 1540
  18.0 6.3 %copy-start.7 = (bf16[2,12,12]{2,0,1:T(2,128)(2,1)S(1)}, bf16[2,12,12]{2,0,1:T(2,128)(2,1)}, u32[]{:S(2)}) copy-start(bf16[2,12,12]{2,0,1:T(2,128)(2,1)} %param.17) | copy-start | bytes 1732
  22.5 3.3 %copy-start.5 = (pred[768]{0:T(1024)(128)(4,1)}, pred[768]{0:T(1024)(128)(4,1)S(1)}, u32[]{:S(2)}) copy-start(pred[768]{0:T(1024)(128)(4,1)S(1)} %fusion.89) | copy-start | bytes 2308
  47.6 32.0 %all-to-all-start.1 = ((bf16[2,64,12,256]{3,0,2,1:T(2,128)(2,1)}), bf16[2,64,12,256]{3,0,2,1:T(2,128)(2,1)S(1)}, u32[]{:S(2)}, u32[]{:S(2)}) async-start(bf16[2,64,12,256]{3,0,2,1:T(2,128)(2,1)} %copy.27), calls=%async_computation.1 | async-start | bytes 1572864 | tf_op jit(solution)/shard_map/all_to_all | solution.py:106
  55.0 27.7 %copy-start.3 = (bf16[1,1,64,12,12]{2,4,3,1,0:T(8,128)(2,1)S(1)}, bf16[1,1,64,12,12]{2,4,3,1,0:T(8,128)(2,1)}, u32[]{:S(2)}) copy-start(bf16[1,1,64,12,12]{2,4,3,1,0:T(8,128)(2,1)} %param.16) | copy-start | bytes 55300
  55.0 28.1 %copy-start.6 = (pred[768]{0:T(1024)(128)(4,1)S(1)}, pred[768]{0:T(1024)(128)(4,1)}, u32[]{:S(2)}) copy-start(pred[768]{0:T(1024)(128)(4,1)} %copy-done.5) | copy-start | bytes 2308
  55.0 46.0 %collective-permute-start = (bf16[768,512]{1,0:T(8,128)(2,1)S(1)}, bf16[768,512]{1,0:T(8,128)(2,1)}, u32[]{:S(2)}, u32[]{:S(2)}) collective-permute-start(bf16[768,512]{1,0:T(8,128)(2,1)S(1)} %bitcast_convert_fusion), channel_id=1, source_target_pairs={{0,1},{1,0},{2,3},{3,2},{4,5},{5,4},{6,7},{7,6},{8,9},{9,8},{10,11... | collective-permute-start | bytes 2359304 | tf_op jit(solution)/shard_map/ppermute | solution.py:18
  82.7 1.8 %copy-start.4 = (pred[768]{0:T(1024)(128)(4,1)S(1)}, pred[768]{0:T(1024)(128)(4,1)}, u32[]{:S(2)}) copy-start(pred[768]{0:T(1024)(128)(4,1)} %fusion.90) | copy-start | bytes 2308
  85.5 1.3 %copy-start.1 = (bf16[1,1,768,768]{3,2,1,0:T(8,128)(2,1)S(1)}, bf16[1,1,768,768]{3,2,1,0:T(8,128)(2,1)}, u32[]{:S(2)}) copy-start(bf16[1,1,768,768]{3,2,1,0:T(8,128)(2,1)} %param.15) | copy-start | bytes 3538948
  86.0 23.3 %collective-permute-start.1 = (bf16[768,256]{1,0:T(8,128)(2,1)S(1)}, bf16[768,256]{1,0:T(8,128)(2,1)S(1)}, u32[]{:S(2)}, u32[]{:S(2)}) collective-permute-start(bf16[768,256]{1,0:T(8,128)(2,1)S(1)} %fusion.18), channel_id=1, source_target_pairs={{0,1},{1,0},{2,3},{3,2},{4,5},{5,4},{6,7},{7,6},{8,9},{9,8},{10,11... | collective-permute-start | bytes 1179656 | tf_op jit(solution)/shard_map/ppermute | solution.py:18

commit v14 on v13

--- a/solution.py
+++ b/solution.py
@@ -6,7 +6,7 @@
 INNER = 2
 WIDTHS = (512, 256)
 NCHUNK = len(WIDTHS)
-TILE = 192
+TILE = 96
 
 COEF_SELF = (-0.5, 0.5, 0.5, 0.5)
 COEF_PAIR = (-1.5, -0.5, 1.5, -0.5)
@@ -135,10 +135,12 @@
     rows = slice(starts[-1], order_len)
     total = base_sum + early + jnp.dot(red_chunks[-1], carried[rows], preferred_element_type=jnp.float32)
     current = total.astype(jnp.bfloat16)
+    pair_left = jnp.concatenate([bare_mat, reducible], axis=1)
     for inner_step in range(1, INNER):
         carried = diagonal_dot(bubble_full, current)
-        total = base_sum + jnp.dot(bare_mat, carried, preferred_element_type=jnp.float32)
-        total = total + jnp.dot(reducible, carried, preferred_element_type=jnp.float32)
+        total = base_sum + jnp.dot(
+            pair_left, jnp.concatenate([carried, carried], axis=0), preferred_element_type=jnp.float32
+        )
         current = total.astype(jnp.bfloat16)
     return current[None, None]
 

time: 115 us -> 113 us (0.983)
  waiting for transfers between devices: 42.4 us -> 46.4 us
  other arithmetic: 8.59 us -> 5.04 us
  starting transfers between devices: 21.1 us -> 18.6 us
    all_to_all x2, waiting for transfers between devices: 23.2 us -> 26.9 us  [local(): lax.all_to_all(pieces[k], 'mom', split_axis=1, concat_axis=1, tiled=True)]
    all_to_all x2, starting transfers between devices: 18 us -> 15.5 us  [local(): lax.all_to_all(pieces[k], 'mom', split_axis=1, concat_axis=1, tiled=True)]
    another operation x6, other arithmetic: 3.1 us -> 1.01 us  [local(): jnp.stack([jnp.take(blocks, order, axis=0) for order in packs])]
    dot_general x2 -> x1, matrix products: 3.31 us -> 3.01 us  [local(): jnp.dot(pair_left, jnp.concatenate([carried, carried], axis=0), preferred...]
    dot_general x14 -> x22, matrix products: 12.7 us -> 12.6 us  [exact_dot(): jnp.dot(a, b, preferred_element_type=jnp.float32).astype(jnp.bfloat16)]
  transfers between devices with their start and end apart: 4 -> 4, of which waited for: 4 -> 4; matrix products, arithmetic and copies ran while one was open for 28% -> 25% of each run, Pallas kernels for 0% -> 0%
where the time goes in v14:
time: 113 us; the launch traced here: 112 us
  waiting for transfers between devices  46.4 us (41%)
  matrix products  25.5 us (23%)
  starting transfers between devices  18.6 us (16%)
  local copies, waits for them, and re-layouts  16.3 us (14%)
  other arithmetic  5.04 us (4%)
    all_to_all x2, waiting for transfers between devices, local(): lax.all_to_all(pieces[k], 'mom', split_axis=1, concat_axis=1, tiled=True)  26.9 us
    ppermute x2, waiting for transfers between devices, partner_2(): return lax.ppermute(value, axis, pairs)  19.5 us
    all_to_all x2, starting transfers between devices, local(): lax.all_to_all(pieces[k], 'mom', split_axis=1, concat_axis=1, tiled=True)  15.5 us
    dot_general x22, matrix products, exact_dot(): jnp.dot(a, b, preferred_element_type=jnp.float32).astype(jnp.bfloat16)  12.6 us
    dot_general x2, matrix products, local(): jnp.einsum('frqm,rqmb->fb', mix4, received, preferred_element_type=jnp.fl...  7.39 us
    gather x4, local copies, waits for them, and re-layouts, local(): jnp.take(blocks, order, axis=0)  4.04 us
    ppermute x2, starting transfers between devices, partner_2(): return lax.ppermute(value, axis, pairs)  3.17 us
    dot_general x1, matrix products, local(): jnp.dot(pair_left, jnp.concatenate([carried, carried], axis=0), preferred...  3.01 us
  transfers between devices with their start and end apart: 4, of which 4 were waited for; matrix products, arithmetic and copies ran while one was open for 25% of the time, Pallas kernels for 0%

profile of v14, /device:TPU:1, one launch (start us, length us, event | category | flops | bytes accessed | tf_op | source)
XLA Modules:
  0.0 112.5 jit_solution(2912503921756423446)
XLA Ops:
  0.0 0.8 slice_bitcast_fusion.1
  0.9 0.1 select_reduce_fusion.1
  1.1 1.2 %slice.165 = bf16[768,512]{1,0:T(8,128)(2,1)S(1)} slice(bf16[768,768]{1,0:T(8,128)(2,1)} %bitcast.61), slice={[0:768], [0:512]} | slice | bytes 1572864 | tf_op jit(solution)/shard_map/slice | solution.py:103
  2.3 0.2 reshape.33
  2.5 0.6 gather_fusion.3
  3.1 0.6 gather_fusion.2
  3.7 0.2 select_bitcast_fusion.1
  3.9 0.2 select_bitcast_fusion
  4.1 0.3 pad_maximum_fusion.1
  4.4 2.8 %copy.22 = bf16[2,64,12,512]{3,0,2,1:T(2,128)(2,1)} copy(bf16[2,64,12,512]{3,2,1,0:T(8,128)(2,1)S(1)} %pad_maximum_fusion.1) | data formatting | bytes 3145728 | tf_op jit(solution)/shard_map/stack | solution.py:104
  7.2 10.6 %all-to-all-start = ((bf16[2,64,12,512]{3,0,2,1:T(2,128)(2,1)}), bf16[2,64,12,512]{3,0,2,1:T(2,128)(2,1)}, u32[]{:S(2)}, u32[]{:S(2)}) async-start(bf16[2,64,12,512]{3,0,2,1:T(2,128)(2,1)} %copy.22), calls=%async_computation | async-start | bytes 3145728 | tf_op jit(solution)/shard_map/all_to_all | solution.py:106
  17.9 1.0 slice.166
  19.0 1.4 %gather_fusion.5 = bf16[64,12,256]{2,1,0:T(8,128)(2,1)} fusion(bf16[64,12,256]{2,1,0:T(8,128)(2,1)S(1)} %reshape.34, s32[1024]{0:T(1024)S(1)} %pad_clamp_fusion), kind=kCustom, calls=%fused_computation.5.clone | custom fusion | bytes 786688 | tf_op jit(solution)/shard_map/jit(_take)/gather | solution.py:104
  20.4 1.4 %gather_fusion.4 = bf16[64,12,256]{2,1,0:T(8,128)(2,1)} fusion(bf16[64,12,256]{2,1,0:T(8,128)(2,1)S(1)} %reshape.34, s32[1024]{0:T(1024)S(1)} %pad_clamp_fusion.1), kind=kCustom, calls=%fused_computation.2.clone | custom fusion | bytes 786688 | tf_op jit(solution)/shard_map/jit(_take)/gather | solution.py:104
  21.8 0.1 select_reduce_fusion.2
  22.0 0.8 gather_fusion
  22.8 0.8 gather_fusion.1
  23.6 0.6 fusion.103
  24.2 0.5 and_select_fusion.1
  24.7 0.6 and_select_fusion
  25.3 1.0 convolution_convert_fusion.5
  26.3 1.0 convolution_convert_fusion.4
  27.4 1.8 %fusion.13 = bf16[768,768]{0,1:T(8,128)(2,1)S(1)} fusion(bf16[768,768]{0,1:T(8,128)(2,1)S(1)} %convolution_convert_fusion.5, s32[768]{0:T(1024)S(1)} %get-tuple-element.85, s32[768]{0:T(1024)S(1)} %get-tuple-element.86, pred[768]{0:T(1024)(128)(4,1)} %fusion.103, s32[64]{0:T(128)} %and_select_fusion.1), kind=kOutput, calls=%fused_computation.31 | convolution fusion | flops 84987904 | bytes 2366464 | tf_op jit(solution)/shard_map/dot_general | solution.py:50
  29.2 2.8 %fusion.14 = bf16[768,768]{0,1:T(8,128)(2,1)} fusion(bf16[768,768]{0,1:T(8,128)(2,1)S(1)} %convolution_convert_fusion.4, s32[768]{0:T(1024)S(1)} %get-tuple-element.85, s32[768]{0:T(1024)S(1)} %get-tuple-element.86, pred[768]{0:T(1024)(128)(4,1)} %fusion.103, s32[64]{0:T(128)} %and_select_fusion), kind=kOutput, calls=%fused_computation.32 | convolution fusion | flops 84987904 | bytes 2366464 | tf_op jit(solution)/shard_map/dot_general | solution.py:50
  32.0 1.4 %pad_maximum_fusion = bf16[768,1536]{0,1:T(8,128)(2,1)S(1)} fusion(bf16[768,768]{0,1:T(8,128)(2,1)} %fusion.14, bf16[768,768]{0,1:T(8,128)(2,1)S(1)} %fusion.13), kind=kLoop, calls=%fused_computation.6 | loop fusion | flops 4718592 | bytes 4718592 | tf_op jit(solution)/shard_map/concatenate | solution.py:82
  33.5 2.3 %reshape.32 = bf16[768,2,64,12]{0,3,2,1:T(8,128)(2,1)} reshape(bf16[768,1536]{0,1:T(8,128)(2,1)S(1)} %pad_maximum_fusion) | data formatting | bytes 4718592 | tf_op jit(solution)/shard_map/reshape | solution.py:82
  35.8 0.1 select_bitcast_fusion.3
  36.0 0.1 select_bitcast_fusion.2
  36.2 0.1 pad_maximum_fusion.3
  36.3 5.3 %all-to-all-done = bf16[2,64,12,512]{3,0,2,1:T(2,128)(2,1)} async-done(((bf16[2,64,12,512]{3,0,2,1:T(2,128)(2,1)}), bf16[2,64,12,512]{3,0,2,1:T(2,128)(2,1)}, u32[]{:S(2)}, u32[]{:S(2)}) %all-to-all-start) | async-done | bytes 1572896 | tf_op jit(solution)/shard_map/all_to_all | solution.py:106
  41.6 4.3 %bitcast_convert_fusion = bf16[768,512]{1,0:T(8,128)(2,1)S(1)} fusion(bf16[2,64,12,512]{3,0,2,1:T(2,128)(2,1)} %all-to-all-done, bf16[768,2,64,12]{0,3,2,1:T(8,128)(2,1)} %reshape.32), kind=kOutput, calls=%fused_computation.22 | convolution fusion | flops 1208352768 | bytes 4718592 | tf_op jit(solution)/shard_map/frqm,rqmb->fb/dot_general | solution.py:107
  46.0 1.7 %copy.25 = bf16[2,64,12,256]{3,0,2,1:T(2,128)(2,1)} copy(bf16[2,64,12,256]{3,2,1,0:T(8,128)(2,1)S(1)} %pad_maximum_fusion.3) | data formatting | bytes 1572864 | tf_op jit(solution)/shard_map/optimization_barrier | solution.py:119
  47.6 4.8 %all-to-all-start.1 = ((bf16[2,64,12,256]{3,0,2,1:T(2,128)(2,1)}), bf16[2,64,12,256]{3,0,2,1:T(2,128)(2,1)S(1)}, u32[]{:S(2)}, u32[]{:S(2)}) async-start(bf16[2,64,12,256]{3,0,2,1:T(2,128)(2,1)} %copy.25), calls=%async_computation.1 | async-start | bytes 1572864 | tf_op jit(solution)/shard_map/all_to_all | solution.py:106
  52.5 3.1 %collective-permute-start = (bf16[768,512]{1,0:T(8,128)(2,1)S(1)}, bf16[768,512]{1,0:T(8,128)(2,1)S(1)}, u32[]{:S(2)}, u32[]{:S(2)}) collective-permute-start(bf16[768,512]{1,0:T(8,128)(2,1)S(1)} %bitcast_convert_fusion), channel_id=1, source_target_pairs={{0,1},{1,0},{2,3},{3,2},{4,5},{5,4},{6,7},{7,6},{8,9},{9,8},{10,11... | collective-permute-start | bytes 2359304 | tf_op jit(solution)/shard_map/ppermute | solution.py:18
  55.6 21.6 %all-to-all-done.1 = bf16[2,64,12,256]{3,0,2,1:T(2,128)(2,1)S(1)} async-done(((bf16[2,64,12,256]{3,0,2,1:T(2,128)(2,1)}), bf16[2,64,12,256]{3,0,2,1:T(2,128)(2,1)S(1)}, u32[]{:S(2)}, u32[]{:S(2)}) %all-to-all-start.1) | async-done | bytes 786464 | tf_op jit(solution)/shard_map/all_to_all | solution.py:106
  77.2 3.1 %fusion.26 = bf16[768,256]{1,0:T(8,128)(2,1)S(1)} fusion(bf16[768,2,64,12]{0,3,2,1:T(8,128)(2,1)} %reshape.32, bf16[2,64,12,256]{3,0,2,1:T(2,128)(2,1)S(1)} %all-to-all-done.1), kind=kOutput, calls=%fused_computation.36 | convolution fusion | flops 604176384 | bytes 3538944 | tf_op jit(solution)/shard_map/frqm,rqmb->fb/dot_general | solution.py:107
  80.3 0.2 copy.28
  80.5 0.3 reshape.35
  80.9 1.3 %convolution_convert_fusion.3 = bf16[768,768]{1,0:T(8,128)(2,1)S(1)} fusion(bf16[768,12]{0,1:T(8,128)(2,1)S(1)} %reshape.35, s32[768]{0:T(1024)S(1)} %get-tuple-element.77, s32[768]{0:T(1024)S(1)} %get-tuple-element.78, pred[768]{0:T(1024)(128)(4,1)S(1)} %copy-done.8), kind=kOutput, calls=%fused_computation.28 | convolution fusion | flops 14764032 | bytes 1204992 | tf_op jit(solution)/shard_map/dot_general | solution.py:50
  82.2 1.0 fusion.15
  83.2 0.2 constant_dynamic-update-slice_fusion.13
  83.4 0.2 constant_dynamic-update-slice_fusion.12
  83.6 0.2 constant_dynamic-update-slice_fusion.11
  83.9 0.2 constant_dynamic-update-slice_fusion.10
  84.1 0.2 constant_dynamic-update-slice_fusion.9
  84.3 0.2 constant_dynamic-update-slice_fusion.8
  84.5 0.2 constant_dynamic-update-slice_fusion.1
  84.8 0.2 constant_dynamic-update-slice_fusion
  85.0 1.1 fusion.109
  86.1 12.2 %collective-permute-done = bf16[768,512]{1,0:T(8,128)(2,1)S(1)} collective-permute-done((bf16[768,512]{1,0:T(8,128)(2,1)S(1)}, bf16[768,512]{1,0:T(8,128)(2,1)S(1)}, u32[]{:S(2)}, u32[]{:S(2)}) %collective-permute-start) | collective-permute-done | bytes 786464 | tf_op jit(solution)/shard_map/ppermute | solution.py:18
  98.3 0.3 add_convert_fusion.2
  98.6 0.8 bitcast_add_fusion
  99.4 7.3 %collective-permute-done.1 = bf16[768,256]{1,0:T(8,128)(2,1)S(1)} collective-permute-done((bf16[768,256]{1,0:T(8,128)(2,1)S(1)}, bf16[768,256]{1,0:T(8,128)(2,1)S(1)}, u32[]{:S(2)}, u32[]{:S(2)}) %collective-permute-start.1) | collective-permute-done | bytes 393248 | tf_op jit(solution)/shard_map/ppermute | solution.py:18
  106.7 0.2 add_convert_fusion.3
  106.9 0.6 add_convert_fusion.1
  107.5 0.2 constant_dynamic-update-slice_fusion.29
  107.7 0.2 constant_dynamic-update-slice_fusion.28
  107.9 0.2 constant_dynamic-update-slice_fusion.27
  108.2 0.2 constant_dynamic-update-slice_fusion.26
  108.4 0.2 constant_dynamic-update-slice_fusion.25
  108.6 0.2 constant_dynamic-update-slice_fusion.24
  108.8 0.2 constant_dynamic-update-slice_fusion.23
  109.1 0.2 constant_dynamic-update-slice_fusion.22
  109.5 3.0 %fusion.20 = bf16[1,1,768,768]{3,2,1,0:T(8,128)(2,1)} fusion(bf16[1536,768]{1,0:T(8,128)(2,1)S(1)} %constant_dynamic-update-slice_fusion.14, bf16[768,256]{1,0:T(8,128)(2,1)S(1)} %add_convert_fusion.3, bf16[768,512]{1,0:T(8,128)(2,1)S(1)} %add_convert_fusion.2, bf16[768,768]{1,0:T(8,128)(2,1)S(1)} %bitcast.71), kind=kOutput, calls=%fused_computation.34 | convolution fusion | flops 1823735808 | bytes 5898240 | tf_op jit(solution)/shard_map/dot_general | solution.py:141
  (57 shorter events, 0.6 us)
Async XLA Ops:
  1.1 2.7 %copy-start.12 = (pred[64]{0:T(512)(128)(4,1)}, pred[64]{0:T(512)(128)(4,1)S(1)}, u32[]{:S(2)}) copy-start(pred[64]{0:T(512)(128)(4,1)S(1)} %get-tuple-element.84) | copy-start | bytes 196
  1.1 2.9 %copy-start.10 = (pred[64]{0:T(512)(128)(4,1)}, pred[64]{0:T(512)(128)(4,1)S(1)}, u32[]{:S(2)}) copy-start(pred[64]{0:T(512)(128)(4,1)S(1)} %get-tuple-element.83) | copy-start | bytes 196
  7.2 10.6 %copy-start.4 = (s32[2,64,64]{2,1,0:T(8,128)S(1)}, s32[2,64,64]{2,1,0:T(8,128)}, u32[]{:S(2)}) copy-start(s32[2,64,64]{2,1,0:T(8,128)} %param.18) | copy-start | bytes 98308
  7.2 34.4 %all-to-all-start = ((bf16[2,64,12,512]{3,0,2,1:T(2,128)(2,1)}), bf16[2,64,12,512]{3,0,2,1:T(2,128)(2,1)}, u32[]{:S(2)}, u32[]{:S(2)}) async-start(bf16[2,64,12,512]{3,0,2,1:T(2,128)(2,1)} %copy.22), calls=%async_computation | async-start | bytes 3145728 | tf_op jit(solution)/shard_map/all_to_all | solution.py:106
  18.9 2.9 %copy-start.14 = (s32[2,64]{1,0:T(2,128)S(1)}, s32[2,64]{1,0:T(2,128)}, u32[]{:S(2)}) copy-start(s32[2,64]{1,0:T(2,128)} %param.19) | copy-start | bytes 1540
  19.0 6.3 %copy-start.9 = (bf16[2,12,12]{2,0,1:T(2,128)(2,1)S(1)}, bf16[2,12,12]{2,0,1:T(2,128)(2,1)}, u32[]{:S(2)}) copy-start(bf16[2,12,12]{2,0,1:T(2,128)(2,1)} %param.17) | copy-start | bytes 1732
  24.2 3.2 %copy-start.7 = (pred[768]{0:T(1024)(128)(4,1)}, pred[768]{0:T(1024)(128)(4,1)S(1)}, u32[]{:S(2)}) copy-start(pred[768]{0:T(1024)(128)(4,1)S(1)} %fusion.102) | copy-start | bytes 2308
  33.4 2.4 %copy-start.2 = (bf16[64,12,256]{2,1,0:T(8,128)(2,1)S(1)}, bf16[64,12,256]{2,1,0:T(8,128)(2,1)}, u32[]{:S(2)}) copy-start(bf16[64,12,256]{2,1,0:T(8,128)(2,1)} %gather_fusion.4) | copy-start | bytes 1179652
  33.5 2.4 %copy-start.13 = (pred[64]{0:T(512)(128)(4,1)S(1)}, pred[64]{0:T(512)(128)(4,1)}, u32[]{:S(2)}) copy-start(pred[64]{0:T(512)(128)(4,1)} %copy-done.12) | copy-start | bytes 196
  33.5 2.5 %copy-start.1 = (bf16[64,12,256]{2,1,0:T(8,128)(2,1)S(1)}, bf16[64,12,256]{2,1,0:T(8,128)(2,1)}, u32[]{:S(2)}) copy-start(bf16[64,12,256]{2,1,0:T(8,128)(2,1)} %gather_fusion.5) | copy-start | bytes 1179652
  33.5 2.5 %copy-start.11 = (pred[64]{0:T(512)(128)(4,1)S(1)}, pred[64]{0:T(512)(128)(4,1)}, u32[]{:S(2)}) copy-start(pred[64]{0:T(512)(128)(4,1)} %copy-done.10) | copy-start | bytes 196
  47.6 29.6 %all-to-all-start.1 = ((bf16[2,64,12,256]{3,0,2,1:T(2,128)(2,1)}), bf16[2,64,12,256]{3,0,2,1:T(2,128)(2,1)S(1)}, u32[]{:S(2)}, u32[]{:S(2)}) async-start(bf16[2,64,12,256]{3,0,2,1:T(2,128)(2,1)} %copy.25), calls=%async_computation.1 | async-start | bytes 1572864 | tf_op jit(solution)/shard_map/all_to_all | solution.py:106
  52.5 27.8 %copy-start.5 = (bf16[1,1,64,12,12]{2,4,3,1,0:T(8,128)(2,1)S(1)}, bf16[1,1,64,12,12]{2,4,3,1,0:T(8,128)(2,1)}, u32[]{:S(2)}) copy-start(bf16[1,1,64,12,12]{2,4,3,1,0:T(8,128)(2,1)} %param.16) | copy-start | bytes 55300
  52.5 28.3 %copy-start.8 = (pred[768]{0:T(1024)(128)(4,1)S(1)}, pred[768]{0:T(1024)(128)(4,1)}, u32[]{:S(2)}) copy-start(pred[768]{0:T(1024)(128)(4,1)} %copy-done.7) | copy-start | bytes 2308
  52.5 45.8 %collective-permute-start = (bf16[768,512]{1,0:T(8,128)(2,1)S(1)}, bf16[768,512]{1,0:T(8,128)(2,1)S(1)}, u32[]{:S(2)}, u32[]{:S(2)}) collective-permute-start(bf16[768,512]{1,0:T(8,128)(2,1)S(1)} %bitcast_convert_fusion), channel_id=1, source_target_pairs={{0,1},{1,0},{2,3},{3,2},{4,5},{5,4},{6,7},{7,6},{8,9},{9,8},{10,11... | collective-permute-start | bytes 2359304 | tf_op jit(solution)/shard_map/ppermute | solution.py:18
  80.3 1.9 %copy-start.6 = (pred[768]{0:T(1024)(128)(4,1)S(1)}, pred[768]{0:T(1024)(128)(4,1)}, u32[]{:S(2)}) copy-start(pred[768]{0:T(1024)(128)(4,1)} %fusion.103) | copy-start | bytes 2308
  80.8 2.4 %copy-start = (bf16[1,1,768,768]{3,2,1,0:T(8,128)(2,1)S(1)}, bf16[1,1,768,768]{3,2,1,0:T(8,128)(2,1)}, u32[]{:S(2)}) copy-start(bf16[1,1,768,768]{3,2,1,0:T(8,128)(2,1)} %param.14) | copy-start | bytes 3538948
  80.8 25.9 %collective-permute-start.1 = (bf16[768,256]{1,0:T(8,128)(2,1)S(1)}, bf16[768,256]{1,0:T(8,128)(2,1)S(1)}, u32[]{:S(2)}, u32[]{:S(2)}) collective-permute-start(bf16[768,256]{1,0:T(8,128)(2,1)S(1)} %fusion.26), channel_id=1, source_target_pairs={{0,1},{1,0},{2,3},{3,2},{4,5},{5,4},{6,7},{7,6},{8,9},{9,8},{10,11... | collective-permute-start | bytes 1179656 | tf_op jit(solution)/shard_map/ppermute | solution.py:18
  83.6 1.4 %copy-start.3 = (bf16[1,1,768,768]{3,2,1,0:T(8,128)(2,1)S(1)}, bf16[1,1,768,768]{3,2,1,0:T(8,128)(2,1)}, u32[]{:S(2)}) copy-start(bf16[1,1,768,768]{3,2,1,0:T(8,128)(2,1)} %param.15) | copy-start | bytes 3538948

commit v15 on v14

--- a/solution.py
+++ b/solution.py
@@ -6,7 +6,7 @@
 INNER = 2
 WIDTHS = (512, 256)
 NCHUNK = len(WIDTHS)
-TILE = 96
+TILE = 48
 
 COEF_SELF = (-0.5, 0.5, 0.5, 0.5)
 COEF_PAIR = (-1.5, -0.5, 1.5, -0.5)

time: 113 us -> 115 us (1.018)
  matrix products: 25.5 us -> 28.3 us
  waiting for transfers between devices: 46.4 us -> 43.9 us
  local copies, waits for them, and re-layouts: 16.3 us -> 17.5 us
    dot_general x22 -> x38, matrix products: 12.6 us -> 15.4 us  [exact_dot(): jnp.dot(a, b, preferred_element_type=jnp.float32).astype(jnp.bfloat16)]
    ppermute x2, waiting for transfers between devices: 19.5 us -> 17.8 us  [partner_2(): return lax.ppermute(value, axis, pairs)]
    unnamed x37 -> x45, local copies, waits for them, and re-layouts: 0.16 us -> 1.31 us
  transfers between devices with their start and end apart: 4 -> 4, of which waited for: 4 -> 4; matrix products, arithmetic and copies ran while one was open for 25% -> 26% of each run, Pallas kernels for 0% -> 0%
where the time goes in v15:
time: 115 us; the launch traced here: 114 us
  waiting for transfers between devices  43.9 us (38%)
  matrix products  28.3 us (25%)
  starting transfers between devices  18.6 us (16%)
  local copies, waits for them, and re-layouts  17.5 us (15%)
  other arithmetic  4.97 us (4%)
    all_to_all x2, waiting for transfers between devices, local(): lax.all_to_all(pieces[k], 'mom', split_axis=1, concat_axis=1, tiled=True)  26.2 us
    ppermute x2, waiting for transfers between devices, partner_2(): return lax.ppermute(value, axis, pairs)  17.8 us
    all_to_all x2, starting transfers between devices, local(): lax.all_to_all(pieces[k], 'mom', split_axis=1, concat_axis=1, tiled=True)  15.4 us
    dot_general x38, matrix products, exact_dot(): jnp.dot(a, b, preferred_element_type=jnp.float32).astype(jnp.bfloat16)  15.4 us
    dot_general x2, matrix products, local(): jnp.einsum('frqm,rqmb->fb', mix4, received, preferred_element_type=jnp.fl...  7.4 us
    gather x4, local copies, waits for them, and re-layouts, local(): jnp.take(blocks, order, axis=0)  4 us
    ppermute x2, starting transfers between devices, partner_2(): return lax.ppermute(value, axis, pairs)  3.17 us
    dot_general x1, matrix products, local(): jnp.dot(pair_left, jnp.concatenate([carried, carried], axis=0), preferred...  3.01 us
  transfers between devices with their start and end apart: 4, of which 4 were waited for; matrix products, arithmetic and copies ran while one was open for 26% of the time, Pallas kernels for 0%

profile of v15, /device:TPU:1, one launch (start us, length us, event | category | flops | bytes accessed | tf_op | source)
XLA Modules:
  0.0 114.1 jit_solution(7266935314349074343)
XLA Ops:
  0.0 0.8 slice_bitcast_fusion.1
  1.1 1.2 %slice.269 = bf16[768,512]{1,0:T(8,128)(2,1)S(1)} slice(bf16[768,768]{1,0:T(8,128)(2,1)} %bitcast.61), slice={[0:768], [0:512]} | slice | bytes 1572864 | tf_op jit(solution)/shard_map/slice | solution.py:103
  2.5 0.6 gather_fusion.3
  3.1 0.6 gather_fusion.2
  4.1 0.3 pad_maximum_fusion.1
  4.4 2.8 %copy.22 = bf16[2,64,12,512]{3,0,2,1:T(2,128)(2,1)} copy(bf16[2,64,12,512]{3,2,1,0:T(8,128)(2,1)S(1)} %pad_maximum_fusion.1) | data formatting | bytes 3145728 | tf_op jit(solution)/shard_map/stack | solution.py:104
  7.2 10.6 %all-to-all-start = ((bf16[2,64,12,512]{3,0,2,1:T(2,128)(2,1)}), bf16[2,64,12,512]{3,0,2,1:T(2,128)(2,1)}, u32[]{:S(2)}, u32[]{:S(2)}) async-start(bf16[2,64,12,512]{3,0,2,1:T(2,128)(2,1)} %copy.22), calls=%async_computation | async-start | bytes 3145728 | tf_op jit(solution)/shard_map/all_to_all | solution.py:106
  17.9 1.0 slice.270
  19.0 1.4 %gather_fusion.5 = bf16[64,12,256]{2,1,0:T(8,128)(2,1)} fusion(bf16[64,12,256]{2,1,0:T(8,128)(2,1)S(1)} %reshape.34, s32[1024]{0:T(1024)S(1)} %pad_clamp_fusion), kind=kCustom, calls=%fused_computation.5.clone | custom fusion | bytes 786688 | tf_op jit(solution)/shard_map/jit(_take)/gather | solution.py:104
  20.4 1.4 %gather_fusion.4 = bf16[64,12,256]{2,1,0:T(8,128)(2,1)} fusion(bf16[64,12,256]{2,1,0:T(8,128)(2,1)S(1)} %reshape.34, s32[1024]{0:T(1024)S(1)} %pad_clamp_fusion.1), kind=kCustom, calls=%fused_computation.2.clone | custom fusion | bytes 786688 | tf_op jit(solution)/shard_map/jit(_take)/gather | solution.py:104
  21.9 0.8 gather_fusion
  22.7 0.8 gather_fusion.1
  23.5 0.6 fusion.137
  24.1 0.5 and_select_fusion.1
  24.7 0.5 and_select_fusion
  25.2 1.0 convolution_convert_fusion.5
  26.2 1.0 convolution_convert_fusion.4
  27.3 1.8 %fusion.13 = bf16[768,768]{0,1:T(8,128)(2,1)S(1)} fusion(bf16[768,768]{0,1:T(8,128)(2,1)S(1)} %convolution_convert_fusion.5, s32[768]{0:T(1024)S(1)} %get-tuple-element.117, s32[768]{0:T(1024)S(1)} %get-tuple-element.118, pred[768]{0:T(1024)(128)(4,1)} %fusion.137, s32[64]{0:T(128)} %and_select_fusion.1), kind=kOutput, calls=%fused_computation.31 | convolution fusion | flops 84987904 | bytes 2366464 | tf_op jit(solution)/shard_map/dot_general | solution.py:50
  29.1 2.8 %fusion.14 = bf16[768,768]{0,1:T(8,128)(2,1)} fusion(bf16[768,768]{0,1:T(8,128)(2,1)S(1)} %convolution_convert_fusion.4, s32[768]{0:T(1024)S(1)} %get-tuple-element.117, s32[768]{0:T(1024)S(1)} %get-tuple-element.118, pred[768]{0:T(1024)(128)(4,1)} %fusion.137, s32[64]{0:T(128)} %and_select_fusion), kind=kOutput, calls=%fused_computation.32 | convolution fusion | flops 84987904 | bytes 2366464 | tf_op jit(solution)/shard_map/dot_general | solution.py:50
  31.9 1.4 %pad_maximum_fusion = bf16[768,1536]{0,1:T(8,128)(2,1)S(1)} fusion(bf16[768,768]{0,1:T(8,128)(2,1)} %fusion.14, bf16[768,768]{0,1:T(8,128)(2,1)S(1)} %fusion.13), kind=kLoop, calls=%fused_computation.6 | loop fusion | flops 4718592 | bytes 4718592 | tf_op jit(solution)/shard_map/concatenate | solution.py:82
  33.4 2.4 %reshape.32 = bf16[768,2,64,12]{0,3,2,1:T(8,128)(2,1)} reshape(bf16[768,1536]{0,1:T(8,128)(2,1)S(1)} %pad_maximum_fusion) | data formatting | bytes 4718592 | tf_op jit(solution)/shard_map/reshape | solution.py:82
  35.9 0.9 copy-done.1
  37.1 4.6 %all-to-all-done = bf16[2,64,12,512]{3,0,2,1:T(2,128)(2,1)} async-done(((bf16[2,64,12,512]{3,0,2,1:T(2,128)(2,1)}), bf16[2,64,12,512]{3,0,2,1:T(2,128)(2,1)}, u32[]{:S(2)}, u32[]{:S(2)}) %all-to-all-start) | async-done | bytes 1572896 | tf_op jit(solution)/shard_map/all_to_all | solution.py:106
  41.6 4.3 %bitcast_convert_fusion = bf16[768,512]{1,0:T(8,128)(2,1)S(1)} fusion(bf16[2,64,12,512]{3,0,2,1:T(2,128)(2,1)} %all-to-all-done, bf16[768,2,64,12]{0,3,2,1:T(8,128)(2,1)} %reshape.32), kind=kOutput, calls=%fused_computation.22 | convolution fusion | flops 1208352768 | bytes 4718592 | tf_op jit(solution)/shard_map/frqm,rqmb->fb/dot_general | solution.py:107
  46.0 1.7 %copy.25 = bf16[2,64,12,256]{3,0,2,1:T(2,128)(2,1)} copy(bf16[2,64,12,256]{3,2,1,0:T(8,128)(2,1)S(1)} %pad_maximum_fusion.3) | data formatting | bytes 1572864 | tf_op jit(solution)/shard_map/optimization_barrier | solution.py:119
  47.7 4.8 %all-to-all-start.1 = ((bf16[2,64,12,256]{3,0,2,1:T(2,128)(2,1)}), bf16[2,64,12,256]{3,0,2,1:T(2,128)(2,1)S(1)}, u32[]{:S(2)}, u32[]{:S(2)}) async-start(bf16[2,64,12,256]{3,0,2,1:T(2,128)(2,1)} %copy.25), calls=%async_computation.1 | async-start | bytes 1572864 | tf_op jit(solution)/shard_map/all_to_all | solution.py:106
  52.5 3.1 %collective-permute-start = (bf16[768,512]{1,0:T(8,128)(2,1)S(1)}, bf16[768,512]{1,0:T(8,128)(2,1)S(1)}, u32[]{:S(2)}, u32[]{:S(2)}) collective-permute-start(bf16[768,512]{1,0:T(8,128)(2,1)S(1)} %bitcast_convert_fusion), channel_id=1, source_target_pairs={{0,1},{1,0},{2,3},{3,2},{4,5},{5,4},{6,7},{7,6},{8,9},{9,8},{10,11... | collective-permute-start | bytes 2359304 | tf_op jit(solution)/shard_map/ppermute | solution.py:18
  55.6 21.6 %all-to-all-done.1 = bf16[2,64,12,256]{3,0,2,1:T(2,128)(2,1)S(1)} async-done(((bf16[2,64,12,256]{3,0,2,1:T(2,128)(2,1)}), bf16[2,64,12,256]{3,0,2,1:T(2,128)(2,1)S(1)}, u32[]{:S(2)}, u32[]{:S(2)}) %all-to-all-start.1) | async-done | bytes 786464 | tf_op jit(solution)/shard_map/all_to_all | solution.py:106
  77.2 3.1 %fusion.26 = bf16[768,256]{1,0:T(8,128)(2,1)S(1)} fusion(bf16[768,2,64,12]{0,3,2,1:T(8,128)(2,1)} %reshape.32, bf16[2,64,12,256]{3,0,2,1:T(2,128)(2,1)S(1)} %all-to-all-done.1), kind=kOutput, calls=%fused_computation.36 | convolution fusion | flops 604176384 | bytes 3538944 | tf_op jit(solution)/shard_map/frqm,rqmb->fb/dot_general | solution.py:107
  80.5 0.3 reshape.35
  80.9 1.3 %convolution_convert_fusion.3 = bf16[768,768]{1,0:T(8,128)(2,1)S(1)} fusion(bf16[768,12]{0,1:T(8,128)(2,1)S(1)} %reshape.35, s32[768]{0:T(1024)S(1)} %get-tuple-element.109, s32[768]{0:T(1024)S(1)} %get-tuple-element.110, pred[768]{0:T(1024)(128)(4,1)S(1)} %copy-done.8), kind=kOutput, calls=%fused_computation.28 | convolution fusion | flops 14764032 | bytes 1204992 | tf_op jit(solution)/shard_map/dot_general | solution.py:50
  82.2 1.0 fusion.15
  83.2 0.2 copy-done
  83.6 0.2 constant_dynamic-update-slice_fusion.25
  83.8 0.2 constant_dynamic-update-slice_fusion.24
  84.0 0.2 constant_dynamic-update-slice_fusion.23
  84.2 0.2 constant_dynamic-update-slice_fusion.22
  84.4 0.2 constant_dynamic-update-slice_fusion.21
  84.7 0.2 constant_dynamic-update-slice_fusion.20
  85.2 0.2 constant_dynamic-update-slice_fusion.17
  85.5 0.2 constant_dynamic-update-slice_fusion.32
  85.9 0.2 constant_dynamic-update-slice_fusion.30
  86.1 0.2 constant_dynamic-update-slice_fusion.29
  86.3 0.2 constant_dynamic-update-slice_fusion.28
  86.5 0.2 constant_dynamic-update-slice_fusion.27
  86.8 1.1 fusion.142
  87.8 10.4 %collective-permute-done = bf16[768,512]{1,0:T(8,128)(2,1)S(1)} collective-permute-done((bf16[768,512]{1,0:T(8,128)(2,1)S(1)}, bf16[768,512]{1,0:T(8,128)(2,1)S(1)}, u32[]{:S(2)}, u32[]{:S(2)}) %collective-permute-start) | collective-permute-done | bytes 786464 | tf_op jit(solution)/shard_map/ppermute | solution.py:18
  98.3 0.3 add_convert_fusion.2
  98.6 0.8 bitcast_add_fusion
  99.4 7.3 %collective-permute-done.1 = bf16[768,256]{1,0:T(8,128)(2,1)S(1)} collective-permute-done((bf16[768,256]{1,0:T(8,128)(2,1)S(1)}, bf16[768,256]{1,0:T(8,128)(2,1)S(1)}, u32[]{:S(2)}, u32[]{:S(2)}) %collective-permute-start.1) | collective-permute-done | bytes 393248 | tf_op jit(solution)/shard_map/ppermute | solution.py:18
  106.9 0.6 add_convert_fusion.1
  107.7 0.2 constant_dynamic-update-slice_fusion.63
  107.9 0.2 constant_dynamic-update-slice_fusion.62
  108.3 0.2 constant_dynamic-update-slice_fusion.60
  108.5 0.2 constant_dynamic-update-slice_fusion.59
  108.7 0.2 constant_dynamic-update-slice_fusion.58
  108.9 0.2 constant_dynamic-update-slice_fusion.57
  109.3 0.2 constant_dynamic-update-slice_fusion.55
  109.5 0.2 constant_dynamic-update-slice_fusion.54
  109.9 0.2 constant_dynamic-update-slice_fusion.52
  110.2 0.2 constant_dynamic-update-slice_fusion.51
  110.4 0.2 constant_dynamic-update-slice_fusion.50
  110.6 0.2 constant_dynamic-update-slice_fusion.49
  111.1 3.0 %fusion.20 = bf16[1,1,768,768]{3,2,1,0:T(8,128)(2,1)} fusion(bf16[1536,768]{1,0:T(8,128)(2,1)S(1)} %constant_dynamic-update-slice_fusion.33, bf16[768,256]{1,0:T(8,128)(2,1)S(1)} %add_convert_fusion.3, bf16[768,512]{1,0:T(8,128)(2,1)S(1)} %add_convert_fusion.2, bf16[768,768]{1,0:T(8,128)(2,1)S(1)} %bitcast.79), kind=kOutput, calls=%fused_computation.34 | convolution fusion | flops 1823735808 | bytes 5898240 | tf_op jit(solution)/shard_map/dot_general | solution.py:141
  (81 shorter events, 3.5 us)
Async XLA Ops:
  1.1 2.7 %copy-start.12 = (pred[64]{0:T(512)(128)(4,1)}, pred[64]{0:T(512)(128)(4,1)S(1)}, u32[]{:S(2)}) copy-start(pred[64]{0:T(512)(128)(4,1)S(1)} %get-tuple-element.116) | copy-start | bytes 196
  1.1 2.9 %copy-start.10 = (pred[64]{0:T(512)(128)(4,1)}, pred[64]{0:T(512)(128)(4,1)S(1)}, u32[]{:S(2)}) copy-start(pred[64]{0:T(512)(128)(4,1)S(1)} %get-tuple-element.115) | copy-start | bytes 196
  7.2 10.6 %copy-start.4 = (s32[2,64,64]{2,1,0:T(8,128)S(1)}, s32[2,64,64]{2,1,0:T(8,128)}, u32[]{:S(2)}) copy-start(s32[2,64,64]{2,1,0:T(8,128)} %param.18) | copy-start | bytes 98308
  7.2 34.4 %all-to-all-start = ((bf16[2,64,12,512]{3,0,2,1:T(2,128)(2,1)}), bf16[2,64,12,512]{3,0,2,1:T(2,128)(2,1)}, u32[]{:S(2)}, u32[]{:S(2)}) async-start(bf16[2,64,12,512]{3,0,2,1:T(2,128)(2,1)} %copy.22), calls=%async_computation | async-start | bytes 3145728 | tf_op jit(solution)/shard_map/all_to_all | solution.py:106
  19.0 2.8 %copy-start.14 = (s32[2,64]{1,0:T(2,128)S(1)}, s32[2,64]{1,0:T(2,128)}, u32[]{:S(2)}) copy-start(s32[2,64]{1,0:T(2,128)} %param.19) | copy-start | bytes 1540
  20.4 4.8 %copy-start.9 = (bf16[2,12,12]{2,0,1:T(2,128)(2,1)S(1)}, bf16[2,12,12]{2,0,1:T(2,128)(2,1)}, u32[]{:S(2)}) copy-start(bf16[2,12,12]{2,0,1:T(2,128)(2,1)} %param.17) | copy-start | bytes 1732
  24.1 3.1 %copy-start.7 = (pred[768]{0:T(1024)(128)(4,1)}, pred[768]{0:T(1024)(128)(4,1)S(1)}, u32[]{:S(2)}) copy-start(pred[768]{0:T(1024)(128)(4,1)S(1)} %fusion.136) | copy-start | bytes 2308
  33.3 2.4 %copy-start.2 = (bf16[64,12,256]{2,1,0:T(8,128)(2,1)S(1)}, bf16[64,12,256]{2,1,0:T(8,128)(2,1)}, u32[]{:S(2)}) copy-start(bf16[64,12,256]{2,1,0:T(8,128)(2,1)} %gather_fusion.4) | copy-start | bytes 1179652
  33.4 2.4 %copy-start.13 = (pred[64]{0:T(512)(128)(4,1)S(1)}, pred[64]{0:T(512)(128)(4,1)}, u32[]{:S(2)}) copy-start(pred[64]{0:T(512)(128)(4,1)} %copy-done.12) | copy-start | bytes 196
  33.4 2.5 %copy-start.11 = (pred[64]{0:T(512)(128)(4,1)S(1)}, pred[64]{0:T(512)(128)(4,1)}, u32[]{:S(2)}) copy-start(pred[64]{0:T(512)(128)(4,1)} %copy-done.10) | copy-start | bytes 196
  35.7 1.0 copy-start.1
  47.7 29.6 %all-to-all-start.1 = ((bf16[2,64,12,256]{3,0,2,1:T(2,128)(2,1)}), bf16[2,64,12,256]{3,0,2,1:T(2,128)(2,1)S(1)}, u32[]{:S(2)}, u32[]{:S(2)}) async-start(bf16[2,64,12,256]{3,0,2,1:T(2,128)(2,1)} %copy.25), calls=%async_computation.1 | async-start | bytes 1572864 | tf_op jit(solution)/shard_map/all_to_all | solution.py:106
  52.5 27.8 %copy-start.5 = (bf16[1,1,64,12,12]{2,4,3,1,0:T(8,128)(2,1)S(1)}, bf16[1,1,64,12,12]{2,4,3,1,0:T(8,128)(2,1)}, u32[]{:S(2)}) copy-start(bf16[1,1,64,12,12]{2,4,3,1,0:T(8,128)(2,1)} %param.16) | copy-start | bytes 55300
  52.5 28.3 %copy-start.8 = (pred[768]{0:T(1024)(128)(4,1)S(1)}, pred[768]{0:T(1024)(128)(4,1)}, u32[]{:S(2)}) copy-start(pred[768]{0:T(1024)(128)(4,1)} %copy-done.7) | copy-start | bytes 2308
  52.5 45.8 %collective-permute-start = (bf16[768,512]{1,0:T(8,128)(2,1)S(1)}, bf16[768,512]{1,0:T(8,128)(2,1)S(1)}, u32[]{:S(2)}, u32[]{:S(2)}) collective-permute-start(bf16[768,512]{1,0:T(8,128)(2,1)S(1)} %bitcast_convert_fusion), channel_id=1, source_target_pairs={{0,1},{1,0},{2,3},{3,2},{4,5},{5,4},{6,7},{7,6},{8,9},{9,8},{10,11... | collective-permute-start | bytes 2359304 | tf_op jit(solution)/shard_map/ppermute | solution.py:18
  80.3 1.9 %copy-start.6 = (pred[768]{0:T(1024)(128)(4,1)S(1)}, pred[768]{0:T(1024)(128)(4,1)}, u32[]{:S(2)}) copy-start(pred[768]{0:T(1024)(128)(4,1)} %fusion.137) | copy-start | bytes 2308
  80.8 26.0 %collective-permute-start.1 = (bf16[768,256]{1,0:T(8,128)(2,1)S(1)}, bf16[768,256]{1,0:T(8,128)(2,1)S(1)}, u32[]{:S(2)}, u32[]{:S(2)}) collective-permute-start(bf16[768,256]{1,0:T(8,128)(2,1)S(1)} %fusion.26), channel_id=1, source_target_pairs={{0,1},{1,0},{2,3},{3,2},{4,5},{5,4},{6,7},{7,6},{8,9},{9,8},{10,11... | collective-permute-start | bytes 1179656 | tf_op jit(solution)/shard_map/ppermute | solution.py:18
  82.2 1.3 %copy-start = (bf16[1,1,768,768]{3,2,1,0:T(8,128)(2,1)S(1)}, bf16[1,1,768,768]{3,2,1,0:T(8,128)(2,1)}, u32[]{:S(2)}) copy-start(bf16[1,1,768,768]{3,2,1,0:T(8,128)(2,1)} %param.14) | copy-start | bytes 3538948
  84.7 2.1 %copy-start.3 = (bf16[1,1,768,768]{3,2,1,0:T(8,128)(2,1)S(1)}, bf16[1,1,768,768]{3,2,1,0:T(8,128)(2,1)}, u32[]{:S(2)}) copy-start(bf16[1,1,768,768]{3,2,1,0:T(8,128)(2,1)} %param.15) | copy-start | bytes 3538948
